TPU v7x, 512 devices: a whole 4x8x8 slice. The times are simulated.
512 devices in a mesh: section: 64 (over y_hi, z, x), rep: 8 (over y_lo, core).
Axes of the slice: x: 4, y: 8 (y_hi: 2, y_lo: 4; y = y_hi * 4 + y_lo), z: 8, core: 2. Of those that a mesh axis runs over, the one named last changes fastest.
Arguments:
- features: bfloat16 [65536, 512], P(('section', 'rep')), may hold values from -6 to 6
- col_panels: int32 [512, 8, 12], P('section', 'rep'), may hold values from 0 to 511, as said below
- block_counts: int32 [512, 8], P('section', 'rep'), may hold values from 1 to 12, as said below
- block_values: bfloat16 [512, 8, 12, 128, 128], P('section', 'rep'), may hold values from 0.0019989014 to 0.019897461
- weight: bfloat16 [512, 512], replicated, may hold values from -0.25 to 0.25
- bias: float32 [512], replicated, may hold values from -3 to 3
- cotangent: bfloat16 [65536, 512], P(('section', 'rep')), may hold values from -6 to 6
Outputs:
- hidden: bfloat16 [65536, 512], P(('section', 'rep'))
- weight_grad: float32 [512, 512], replicated
- bias_grad: float32 [512], replicated
Inputs may be any that keep to these rules, and one draw needn't show every extreme that they name: Column group r holds the column panels c with (c) % 8 == r; col_panels[p, r, k] lies in column group r, and the 12 entries of one list are distinct. Only the first block_counts[p, r] slots of a list are nonzero blocks; later slots are ignored. The count 12 occurs in every draw.
All inputs are finite; a program needn't handle non-finite values.
Results may differ from a plain program's by a relative error of at most 0.0055.
Values may be sent and summed in bfloat16 or wider, within the bound.
No kernel may reach another device: no remote copies, remote signals or barrier semaphores. Data moves between devices by JAX's collectives and lax.ppermute only.
A program may use at most 64 MiB of HBM per device.

v0:
```python
import math

import jax
import jax.numpy as jnp
from jax import lax
from jax.sharding import PartitionSpec as P


def shards(features, col_panels, block_counts, block_values, weight, bias, cotangent):
    rep_count = lax.axis_size("rep")
    rep_index = lax.axis_index("rep")
    tile_size = block_values.shape[-1]
    feat_width = features.shape[1]
    own_panels = features.shape[0] // tile_size
    row_panels = col_panels.shape[0]
    slot_count = col_panels.shape[2]
    global_cols = col_panels[:, 0, :]
    local_cols = global_cols // (own_panels * rep_count) * own_panels + global_cols % own_panels
    live_counts = block_counts[:, 0]
    slot_mask = jnp.arange(slot_count, dtype=jnp.int32)[None, :] < live_counts[:, None]
    tiles = block_values[:, 0]
    empty = jnp.zeros((row_panels, tile_size, feat_width), jnp.float32)
    gathered = lax.all_gather(features, "section", axis=0, tiled=True)
    all_panels = gathered.reshape(-1, tile_size, feat_width)
    slot_step = 4
    turn_count = (jnp.max(live_counts) + slot_step - 1) // slot_step

    def one_turn(turn, running):
        begin_slot = turn * slot_step
        step_cols = lax.dynamic_slice_in_dim(local_cols, begin_slot, slot_step, 1)
        step_mask = lax.dynamic_slice_in_dim(slot_mask, begin_slot, slot_step, 1)
        step_tiles = lax.dynamic_slice_in_dim(tiles, begin_slot, slot_step, 1)
        step_tiles = jnp.where(step_mask[:, :, None, None], step_tiles, jnp.zeros((), jnp.bfloat16))
        picked = all_panels[step_cols]
        return running + jnp.einsum(
            "gkab,gkbf->gaf", step_tiles, picked, preferred_element_type=jnp.float32
        )

    gathered_sum = lax.fori_loop(0, turn_count, one_turn, empty)
    partial_value = gathered_sum.reshape(row_panels * tile_size, feat_width)
    own_rows = own_panels * tile_size
    summed_all = lax.psum(partial_value, "rep")
    summed_own = lax.dynamic_slice_in_dim(summed_all, rep_index * own_rows, own_rows, 0)
    aggregated = summed_own.astype(jnp.bfloat16)
    pre = jnp.dot(aggregated, weight, preferred_element_type=jnp.float32) + bias
    hidden = jax.nn.silu(pre).astype(jnp.bfloat16)
    sigmoid_pre = jax.nn.sigmoid(pre)
    slope = (
        cotangent.astype(jnp.float32) * (sigmoid_pre * (1.0 + pre * (1.0 - sigmoid_pre)))
    ).astype(jnp.bfloat16)
    local_weight = jnp.einsum("nd,nf->df", aggregated, slope, preferred_element_type=jnp.float32)
    local_bias = jnp.sum(slope.astype(jnp.float32), axis=0)
    weight_sum, bias_sum = lax.psum((local_weight, local_bias), ("section", "rep"))
    node_total = lax.axis_size("section") * rep_count * own_rows
    factor = 1.0 / math.sqrt(node_total)
    return (hidden, weight_sum * factor, bias_sum * factor)


def solution(mesh):
    in_specs = (
        P(("section", "rep"), None),
        P("section", "rep", None),
        P("section", "rep"),
        P("section", "rep", None, None, None),
        P(),
        P(),
        P(("section", "rep"), None),
    )
    out_specs = (P(("section", "rep"), None), P(), P())
    return jax.shard_map(shards, mesh=mesh, in_specs=in_specs, out_specs=out_specs, check_vma=False)
```

profile of v0, /device:TPU:1, one launch (start us, length us, event | category | flops | bytes accessed | tf_op | source)
XLA Modules:
  0.0 583.5 jit_solution(16949796323749232449)
XLA Ops:
  7.2 0.0 copy-start
  7.2 0.0 all-gather.2.cloned.1.call-start
  7.2 0.7 all-gather.2.cloned.1.call-update
  7.9 0.0 all-reduce.3.cloned.1.call-start
  8.0 1.3 reduce_max.9
  9.9 0.7 iota_compare_fusion
  10.7 0.7 add_select_fusion
  11.4 182.3 %all-gather.2.cloned.1.call-done = bf16[8192,512]{1,0:T(8,128)(2,1)} async-done(((bf16[128,512]{1,0:T(8,128)(2,1)}), bf16[8192,512]{1,0:T(8,128)(2,1)}) %all-gather.2.cloned.1.call-update) | async-done | bytes 8388624 | tf_op jit(solution)/shard_map/all_gather | solution.py:23
  193.6 0.2 broadcast_in_dim.21
  193.9 10.1 %while.10 = (s32[]{:T(128)}, f32[8,128,512]{2,1,0:T(8,128)S(1)}, s32[]{:T(128)}, pred[8,12]{1,0:T(8,128)(4,1)S(1)}, bf16[8,12,128,128]{3,2,1,0:T(8,128)(2,1)}, /...) while((s32[]{:T(128)}, f32[8,128,512]{2,1,0:T(8,128)S(1)}, ...), condition=%wide.region_2.3_spmd, body=%wide.region_1.2_spmd.sunk | while | flops 537920640 | bytes 17830920 | solution.py:39
  193.9 0.1 compare_select_fusion.2
  194.0 0.1 reshape.32
  194.1 6.2 %gather_fusion = bf16[32,128,512]{2,1,0:T(8,128)(2,1)} fusion(bf16[64,128,512]{2,1,0:T(8,128)(2,1)} %get-tuple-element.131, s32[1024]{0:T(1024)S(1)} %pad_clamp_fusion.2), kind=kCustom, calls=%fused_computation.clone.1 | custom fusion | bytes 8388736 | tf_op jit(solution)/shard_map/while/body/gather | solution.py:34
  200.3 0.1 constant_dynamic-slice_fusion.2
  200.3 3.7 bitcast_add_fusion.2
  204.0 0.0 copy-start.1
  204.0 0.0 copy-start.2
  204.0 73.0 %all-reduce.4 = bf16[1024,512]{1,0:T(8,128)(2,1)} all-reduce(f32[1024,512]{1,0:T(8,128)S(1)} %bitcast.19), channel_id=1, replica_groups=mesh['section'=64,'rep'=8] {'rep'}, use_global_device_ids=true, to_apply=%region_3.4 | all-reduce | flops 524288 | bytes 3145728 | tf_op jit(solution)/shard_map/psum | solution.py:42
  277.0 0.0 copy-done
  277.0 0.0 copy-done.1
  277.0 0.0 copy-done.2
  277.0 1.9 convert_reduce_fusion
  278.9 2.3 fusion.6
  281.2 0.0 all-reduce.3.cloned.1.call-update
  281.2 118.4 %psum.23 = f32[512]{0:T(512)S(1)} all-reduce(f32[512]{0:T(512)S(1)} %get-tuple-element.56), channel_id=1, replica_groups=mesh['section'=64,'rep'=8] {'section','rep'}, use_global_device_ids=true, to_apply=%region_6.7 | all-reduce | flops 512 | bytes 4096 | tf_op jit(solution)/shard_map/psum | solution.py:53
  399.6 0.6 broadcast_multiply_fusion.1
  400.2 174.2 %all-reduce.3.cloned.1.call-done = f32[512,512]{1,0:T(8,128)} async-done(((f32[512,512]{1,0:T(8,128)}), f32[512,512]{1,0:T(8,128)}) %all-reduce.3.cloned.1.call-update) | async-done | bytes 1048592 | tf_op jit(solution)/shard_map/psum | solution.py:53
  574.4 2.3 broadcast_multiply_fusion
  (1 shorter events, 0.0 us)
Async XLA Ops:
  7.2 269.9 %copy-start = (bf16[512,512]{1,0:T(8,128)(2,1)S(1)}, bf16[512,512]{1,0:T(8,128)(2,1)}, u32[]{:S(2)}) copy-start(bf16[512,512]{1,0:T(8,128)(2,1)} %param.13) | copy-start | bytes 1572868
  7.2 186.5 %all-gather.2.cloned.1.call-start = ((), (), s32[]{:S(2)}) async-start(), calls=%async_computation | async-start | bytes 8519680 | tf_op jit(solution)/shard_map/all_gather | solution.py:23
  7.9 566.5 %all-reduce.3.cloned.1.call-start = ((), (), s32[]{:S(2)}) async-start(), calls=%async_computation.1 | async-start | bytes 2097152 | tf_op jit(solution)/shard_map/psum | solution.py:53
  204.0 73.0 %copy-start.1 = (bf16[128,512]{1,0:T(8,128)(2,1)S(1)}, bf16[128,512]{1,0:T(8,128)(2,1)}, u32[]{:S(2)}) copy-start(bf16[128,512]{1,0:T(8,128)(2,1)} %param.15) | copy-start | bytes 393220
  204.0 73.0 %copy-start.2 = (f32[512]{0:T(512)S(1)}, f32[512]{0:T(512)}, u32[]{:S(2)}) copy-start(f32[512]{0:T(512)} %param.14) | copy-start | bytes 6148
Sparse Core Ops, SparseCore 0:
  12.3 181.2 all-gather.1
  281.3 293.0 all-reduce.2
where the time goes:
time: 584 us
  waiting for transfers between devices  357 us (61%)
  blocking collectives  191 us (33%)
  between operations  14.8 us (3%)
  matrix products  7.8 us (1%)
  local copies, waits for them, and re-layouts  6.6 us (1%)
    all_gather x1, waiting for transfers between devices, shards(): gathered = lax.all_gather(features, 'section', axis=0, tiled=True)  182 us
    psum x1, waiting for transfers between devices, shards(): lax.psum((local_weight, local_bias), ('section', 'rep'))  174 us
    psum x1, blocking collectives, shards(): lax.psum((local_weight, local_bias), ('section', 'rep'))  118 us
    psum x1, blocking collectives, shards(): summed_all = lax.psum(partial_value, 'rep')  73 us
  transfers between devices with their start and end apart: 2, of which 2 were waited for; matrix products, arithmetic and copies ran while one was open for 1% of the time, Pallas kernels for 0%

commit v1 on v0

v1 whole, which is shorter than its diff:
```python
import math

import jax
import jax.numpy as jnp
from jax import lax
from jax.sharding import Mesh
from jax.sharding import PartitionSpec as P

SECTION_AXES = ("y_hi", "z", "x")
REP_AXES = ("y_lo", "core")
ALL_AXES = SECTION_AXES + REP_AXES


def _shift_perm(n, k):
    return [(i, (i + k) % n) for i in range(n)]


def _reduce_scatter(blocks, axis, n):
    me = lax.axis_index(axis)
    acc = lax.dynamic_index_in_dim(blocks, me, 0, keepdims=False)
    for k in range(1, n):
        send = lax.dynamic_index_in_dim(blocks, (me + k) % n, 0, keepdims=False)
        acc = acc + lax.ppermute(send, axis, _shift_perm(n, k))
    return acc


def _all_gather(piece, axis, n):
    me = lax.axis_index(axis)
    pieces = [piece] + [lax.ppermute(piece, axis, _shift_perm(n, k)) for k in range(1, n)]
    stacked = jnp.stack(pieces)
    order = (me - jnp.arange(n, dtype=jnp.int32)) % n
    return jnp.take(stacked, order, axis=0)


def _all_reduce_direct(piece, axes, n):
    gathered = _all_gather(piece, axes, n)
    total = gathered[0]
    for j in range(1, n):
        total = total + gathered[j]
    return total


def shards(features, col_panels, block_counts, block_values, weight, bias, cotangent):
    sizes = {name: lax.axis_size(name) for name in ALL_AXES}
    rep_count = sizes["y_lo"] * sizes["core"]
    tile_size = block_values.shape[-1]
    feat_width = features.shape[1]
    own_panels = features.shape[0] // tile_size
    row_panels = col_panels.shape[0]
    slot_count = col_panels.shape[2]
    global_cols = col_panels[:, 0, :]
    section_of = global_cols // (own_panels * rep_count)
    low = sizes["z"] * sizes["x"]
    gathered_pos = (section_of % low) * sizes["y_hi"] + section_of // low
    local_cols = gathered_pos * own_panels + global_cols % own_panels
    live_counts = block_counts[:, 0]
    slot_mask = jnp.arange(slot_count, dtype=jnp.int32)[None, :] < live_counts[:, None]
    tiles = block_values[:, 0]
    empty = jnp.zeros((row_panels, tile_size, feat_width), jnp.float32)
    gathered = lax.all_gather(features, "y_hi", axis=0, tiled=True)
    gathered = lax.all_gather(gathered, ("z", "x"), axis=0, tiled=True)
    all_panels = gathered.reshape(-1, tile_size, feat_width)
    slot_step = 4
    turn_count = (jnp.max(live_counts) + slot_step - 1) // slot_step

    def one_turn(turn, running):
        begin_slot = turn * slot_step
        step_cols = lax.dynamic_slice_in_dim(local_cols, begin_slot, slot_step, 1)
        step_mask = lax.dynamic_slice_in_dim(slot_mask, begin_slot, slot_step, 1)
        step_tiles = lax.dynamic_slice_in_dim(tiles, begin_slot, slot_step, 1)
        step_tiles = jnp.where(step_mask[:, :, None, None], step_tiles, jnp.zeros((), jnp.bfloat16))
        picked = all_panels[step_cols]
        return running + jnp.einsum(
            "gkab,gkbf->gaf", step_tiles, picked, preferred_element_type=jnp.float32
        )

    gathered_sum = lax.fori_loop(0, turn_count, one_turn, empty)
    cores = sizes["core"]
    by_core = gathered_sum.reshape(row_panels // cores, cores, tile_size, feat_width)
    by_core = jnp.moveaxis(by_core, 1, 0)
    half = _reduce_scatter(by_core, "core", cores)
    summed_own = _reduce_scatter(half, "y_lo", sizes["y_lo"])
    own_rows = own_panels * tile_size
    aggregated = summed_own.reshape(own_rows, feat_width).astype(jnp.bfloat16)
    pre = jnp.dot(aggregated, weight, preferred_element_type=jnp.float32) + bias
    hidden = jax.nn.silu(pre).astype(jnp.bfloat16)
    sigmoid_pre = jax.nn.sigmoid(pre)
    slope = (
        cotangent.astype(jnp.float32) * (sigmoid_pre * (1.0 + pre * (1.0 - sigmoid_pre)))
    ).astype(jnp.bfloat16)
    local_weight = jnp.einsum("nd,nf->df", aggregated, slope, preferred_element_type=jnp.float32)
    local_bias = jnp.sum(slope.astype(jnp.float32), axis=0)
    width = weight.shape[0]
    scatter_ways = sizes["core"] * sizes["x"] * sizes["y_lo"]
    padded_rows = -(-(width + 1) // scatter_ways) * scatter_ways
    combined = jnp.zeros((padded_rows, feat_width), jnp.float32)
    combined = combined.at[:width].set(local_weight).at[width].set(local_bias)
    chunk = combined
    for name in ("core", "x", "y_lo"):
        chunk = _reduce_scatter(chunk.reshape(sizes[name], -1, feat_width), name, sizes[name])
    outer = sizes["z"] * sizes["y_hi"]
    chunk = _all_reduce_direct(chunk, ("y_hi", "z"), outer)
    for name in ("y_lo", "x", "core"):
        chunk = _all_gather(chunk, name, sizes[name]).reshape(-1, feat_width)
    node_total = lax.axis_size(SECTION_AXES) * rep_count * own_rows
    factor = 1.0 / math.sqrt(node_total)
    weight_sum = chunk[:width]
    bias_sum = chunk[width]
    return (hidden, weight_sum * factor, bias_sum * factor)


def solution(mesh):
    section_size, rep_size = mesh.devices.shape
    fine = Mesh(mesh.devices.reshape(2, section_size // 8, 4, rep_size // 2, 2), ALL_AXES)
    in_specs = (
        P(ALL_AXES, None),
        P(SECTION_AXES, REP_AXES, None),
        P(SECTION_AXES, REP_AXES),
        P(SECTION_AXES, REP_AXES, None, None, None),
        P(),
        P(),
        P(ALL_AXES, None),
    )
    out_specs = (P(ALL_AXES, None), P(), P())
    return jax.shard_map(shards, mesh=fine, in_specs=in_specs, out_specs=out_specs, check_vma=False)
```

time: 584 us -> 359 us (0.61)
  waiting for transfers between devices: 357 us -> 148 us
  blocking collectives: 191 us -> 12.4 us
  starting transfers between devices: 0.08 us -> 137 us
  local copies, waits for them, and re-layouts: 6.6 us -> 24.9 us
    psum x2 -> x0, blocking collectives: 191 us -> none  [the longest x1 118 us: shards(): lax.psum((local_weight, local_bias), ('section', 'rep'))]
    psum x1 -> x0, waiting for transfers between devices: 174 us -> none  [shards(): lax.psum((local_weight, local_bias), ('section', 'rep'))]
    ppermute x0 -> x33, starting transfers between devices: none -> 137 us  [the longest x22 103 us: _all_gather(): lax.ppermute(piece, axis, _shift_perm(n, k))]
    all_gather x1, waiting for transfers between devices: 182 us -> 106 us  [shards(): gathered = lax.all_gather(gathered, ('z', 'x'), axis=0, tiled=True)]
    ppermute x0 -> x33, waiting for transfers between devices: none -> 41.9 us  [the longest x11 30.5 us: _reduce_scatter(): acc = acc + lax.ppermute(send, axis, _shift_perm(n, k))]
    gather x1 -> x3, local copies, waits for them, and re-layouts: 6.17 us -> 18.6 us  [one_turn(): picked = all_panels[step_cols]]
    all_gather x0 -> x1, blocking collectives: none -> 12.4 us  [shards(): gathered = lax.all_gather(features, 'y_hi', axis=0, tiled=True)]
    dot_general x1 -> x3, matrix products: 3.65 us -> 10.9 us  [one_turn(): jnp.einsum('gkab,gkbf->gaf', step_tiles, picked, preferred_element_type=j...]
  transfers between devices with their start and end apart: 2 -> 34, of which waited for: 2 -> 14; matrix products, arithmetic and copies ran while one was open for 1% -> 1% of each run, Pallas kernels for 0% -> 0%
where the time goes in v1:
time: 359 us; the launch traced here: 358 us
  waiting for transfers between devices  148 us (41%)
  starting transfers between devices  137 us (38%)
  local copies, waits for them, and re-layouts  24.9 us (7%)
  between operations  15.7 us (4%)
  blocking collectives  12.4 us (3%)
  matrix products  12.2 us (3%)
  other arithmetic  8.24 us (2%)
    all_gather x1, waiting for transfers between devices, shards(): gathered = lax.all_gather(gathered, ('z', 'x'), axis=0, tiled=True)  106 us
    ppermute x22, starting transfers between devices, _all_gather(): lax.ppermute(piece, axis, _shift_perm(n, k))  103 us
    ppermute x11, starting transfers between devices, _reduce_scatter(): acc = acc + lax.ppermute(send, axis, _shift_perm(n, k))  33.6 us
    ppermute x11, waiting for transfers between devices, _reduce_scatter(): acc = acc + lax.ppermute(send, axis, _shift_perm(n, k))  30.5 us
    gather x3, local copies, waits for them, and re-layouts, one_turn(): picked = all_panels[step_cols]  18.6 us
    all_gather x1, blocking collectives, shards(): gathered = lax.all_gather(features, 'y_hi', axis=0, tiled=True)  12.4 us
    ppermute x22, waiting for transfers between devices, _all_gather(): lax.ppermute(piece, axis, _shift_perm(n, k))  11.3 us
    dot_general x3, matrix products, one_turn(): jnp.einsum('gkab,gkbf->gaf', step_tiles, picked, preferred_element_type=j...  10.9 us
  transfers between devices with their start and end apart: 34, of which 14 were waited for; matrix products, arithmetic and copies ran while one was open for 1% of the time, Pallas kernels for 0%

profile of v1, /device:TPU:1, one launch (start us, length us, event | category | flops | bytes accessed | tf_op | source)
XLA Modules:
  0.0 358.1 jit_solution(10029851802086631331)
XLA Ops:
  7.2 12.4 %all_gather.6 = bf16[256,512]{1,0:T(8,128)(2,1)} all-gather(bf16[128,512]{1,0:T(8,128)(2,1)} %param.13), channel_id=1, replica_groups=mesh['y_hi'=2,'z'=8,'x'=4,'y_lo'=4,'core'=2] {'y_hi'}, dimensions={0}, use_global_device_ids=true | all-gather | bytes 393216 | tf_op jit(solution)/shard_map/all_gather | solution.py:60
  23.1 106.0 %all-gather.2.cloned.1.call-done = bf16[8192,512]{1,0:T(8,128)(2,1)} async-done(((bf16[256,512]{1,0:T(8,128)(2,1)}), bf16[8192,512]{1,0:T(8,128)(2,1)}) %all-gather.2.cloned.1.call-update) | async-done | bytes 8388624 | tf_op jit(solution)/shard_map/all_gather | solution.py:61
  129.3 30.4 %while.12 = (s32[]{:T(128)}, f32[8,128,512]{2,1,0:T(8,128)S(1)}, s32[]{:T(128)}, pred[8,12]{1,0:T(8,128)(4,1)S(1)}, bf16[8,12,128,128]{3,2,1,0:T(8,128)(2,1)}, /...) while((s32[]{:T(128)}, f32[8,128,512]{2,1,0:T(8,128)S(1)}, ...), condition=%wide.region_2.3_spmd, body=%wide.region_1.2_spmd.sunk | while | flops 537920640 | bytes 17830928 | solution.py:77
  129.5 6.2 %gather_fusion = bf16[32,128,512]{2,1,0:T(8,128)(2,1)} fusion(bf16[64,128,512]{2,1,0:T(8,128)(2,1)} %get-tuple-element.168, s32[1024]{0:T(1024)S(1)} %pad_clamp_fusion.6), kind=kCustom, calls=%fused_computation.clone.1 | custom fusion | bytes 8388736 | tf_op jit(solution)/shard_map/while/body/gather | solution.py:72
  135.8 3.6 %bitcast_add_fusion.7 = f32[8,128,512]{2,1,0:T(8,128)S(1)} fusion(f32[8,128,512]{2,1,0:T(8,128)S(1)} %get-tuple-element.152, bf16[8,4,128,512]{3,2,1,0:T(8,128)(2,1)} %bitcast.121, bf16[8,12,128,128]{3,2,1,0:T(8,128)(2,1)} %get-tuple-element.166, s32[]{:T(128)S(6)} %select_n.410, pred[8,4]{1,0:T(8,128)(4,1)S(1)} %constant_dynamic-slice_fusion.2), kind=kOutput, calls=%fused_computation.5.clone.1 | convolution fusion | flops 537919488 | bytes 9437220 | tf_op jit(solution)/shard_map/while/body/gkab,gkbf->gaf/dot_general | solution.py:73
  139.6 6.2 %gather_fusion = bf16[32,128,512]{2,1,0:T(8,128)(2,1)} fusion(bf16[64,128,512]{2,1,0:T(8,128)(2,1)} %get-tuple-element.168, s32[1024]{0:T(1024)S(1)} %pad_clamp_fusion.6), kind=kCustom, calls=%fused_computation.clone.1 | custom fusion | bytes 8388736 | tf_op jit(solution)/shard_map/while/body/gather | solution.py:72
  145.9 3.6 %bitcast_add_fusion.7 = f32[8,128,512]{2,1,0:T(8,128)S(1)} fusion(f32[8,128,512]{2,1,0:T(8,128)S(1)} %get-tuple-element.152, bf16[8,4,128,512]{3,2,1,0:T(8,128)(2,1)} %bitcast.121, bf16[8,12,128,128]{3,2,1,0:T(8,128)(2,1)} %get-tuple-element.166, s32[]{:T(128)S(6)} %select_n.410, pred[8,4]{1,0:T(8,128)(4,1)S(1)} %constant_dynamic-slice_fusion.2), kind=kOutput, calls=%fused_computation.5.clone.1 | convolution fusion | flops 537919488 | bytes 9437220 | tf_op jit(solution)/shard_map/while/body/gkab,gkbf->gaf/dot_general | solution.py:73
  149.8 6.2 %gather_fusion = bf16[32,128,512]{2,1,0:T(8,128)(2,1)} fusion(bf16[64,128,512]{2,1,0:T(8,128)(2,1)} %get-tuple-element.168, s32[1024]{0:T(1024)S(1)} %pad_clamp_fusion.6), kind=kCustom, calls=%fused_computation.clone.1 | custom fusion | bytes 8388736 | tf_op jit(solution)/shard_map/while/body/gather | solution.py:72
  156.1 3.6 %bitcast_add_fusion.7 = f32[8,128,512]{2,1,0:T(8,128)S(1)} fusion(f32[8,128,512]{2,1,0:T(8,128)S(1)} %get-tuple-element.152, bf16[8,4,128,512]{3,2,1,0:T(8,128)(2,1)} %bitcast.121, bf16[8,12,128,128]{3,2,1,0:T(8,128)(2,1)} %get-tuple-element.166, s32[]{:T(128)S(6)} %select_n.410, pred[8,4]{1,0:T(8,128)(4,1)S(1)} %constant_dynamic-slice_fusion.2), kind=kOutput, calls=%fused_computation.5.clone.1 | convolution fusion | flops 537919488 | bytes 9437220 | tf_op jit(solution)/shard_map/while/body/gkab,gkbf->gaf/dot_general | solution.py:73
  160.8 3.3 collective-permute-start
  169.1 5.0 %collective-permute-start.3 = (f32[128,512]{1,0:T(8,128)S(1)}, f32[128,512]{1,0:T(8,128)S(1)}, u32[]{:S(2)}, u32[]{:S(2)}) collective-permute-start(f32[128,512]{1,0:T(8,128)S(1)} %get-tuple-element.85), channel_id=1, source_target_pairs={{0,6},{2,0},{4,2},{6,4},{1,7},{3,1},{5,3},{7,5},{8,14},{10,8},{12,... | collective-permute-start | bytes 786440 | tf_op jit(solution)/shard_map/ppermute | solution.py:23
  179.4 17.0 %collective-permute-done.2 = f32[128,512]{1,0:T(8,128)S(1)} collective-permute-done((f32[128,512]{1,0:T(8,128)S(1)}, f32[128,512]{1,0:T(8,128)S(1)}, u32[]{:S(2)}, u32[]{:S(2)}) %collective-permute-start.2) | collective-permute-done | bytes 262176 | tf_op jit(solution)/shard_map/ppermute | solution.py:23
  199.1 3.0 collective-permute-start.4
  205.7 3.6 %collective-permute-start.6 = (f32[68,512]{1,0:T(8,128)S(1)}, f32[68,512]{1,0:T(8,128)S(1)}, u32[]{:S(2)}, u32[]{:S(2)}) collective-permute-start(f32[68,512]{1,0:T(8,128)S(1)} %get-tuple-element.89), channel_id=1, source_target_pairs={{0,16},{8,24},{16,0},{24,8},{1,17},{9,25},{17,1},{25,9},{2,18},{10... | collective-permute-start | bytes 417800 | tf_op jit(solution)/shard_map/ppermute | solution.py:23
  219.0 4.9 %collective-permute-start.9 = (f32[17,512]{1,0:T(8,128)S(1)}, f32[17,512]{1,0:T(8,128)S(1)}, u32[]{:S(2)}, u32[]{:S(2)}) collective-permute-start(f32[17,512]{1,0:T(8,128)S(1)} %get-tuple-element.93), channel_id=1, source_target_pairs={{0,4},{2,6},{4,0},{6,2},{1,5},{3,7},{5,1},{7,3},{8,12},{10,14},{12... | collective-permute-start | bytes 104456 | tf_op jit(solution)/shard_map/ppermute | solution.py:23
  223.9 3.4 collective-permute-start.8
  227.3 3.2 collective-permute-done.8
  235.7 6.5 %collective-permute-start.13 = (f32[17,512]{1,0:T(8,128)S(1)}, f32[17,512]{1,0:T(8,128)S(1)}, u32[]{:S(2)}, u32[]{:S(2)}) collective-permute-start(f32[17,512]{1,0:T(8,128)S(1)} %get-tuple-element.81), channel_id=1, source_target_pairs={{0,96},{32,128},{64,160},{96,192},{128,224},{160,256},{192,288},{2... | collective-permute-start | bytes 104456 | tf_op jit(solution)/shard_map/ppermute | solution.py:29
  242.2 4.9 %collective-permute-start.14 = (f32[17,512]{1,0:T(8,128)S(1)}, f32[17,512]{1,0:T(8,128)S(1)}, u32[]{:S(2)}, u32[]{:S(2)}) collective-permute-start(f32[17,512]{1,0:T(8,128)S(1)} %get-tuple-element.81), channel_id=1, source_target_pairs={{0,128},{32,160},{64,192},{96,224},{128,256},{160,288},{192,320},{... | collective-permute-start | bytes 104456 | tf_op jit(solution)/shard_map/ppermute | solution.py:29
  247.1 4.5 %collective-permute-start.15 = (f32[17,512]{1,0:T(8,128)S(1)}, f32[17,512]{1,0:T(8,128)S(1)}, u32[]{:S(2)}, u32[]{:S(2)}) collective-permute-start(f32[17,512]{1,0:T(8,128)S(1)} %get-tuple-element.81), channel_id=1, source_target_pairs={{0,160},{32,192},{64,224},{96,256},{128,288},{160,320},{192,352},{... | collective-permute-start | bytes 104456 | tf_op jit(solution)/shard_map/ppermute | solution.py:29
  251.6 7.6 %collective-permute-start.16 = (f32[17,512]{1,0:T(8,128)S(1)}, f32[17,512]{1,0:T(8,128)S(1)}, u32[]{:S(2)}, u32[]{:S(2)}) collective-permute-start(f32[17,512]{1,0:T(8,128)S(1)} %get-tuple-element.81), channel_id=1, source_target_pairs={{0,192},{32,224},{64,256},{96,288},{128,320},{160,352},{192,384},{... | collective-permute-start | bytes 104456 | tf_op jit(solution)/shard_map/ppermute | solution.py:29
  259.2 5.7 %collective-permute-start.17 = (f32[17,512]{1,0:T(8,128)S(1)}, f32[17,512]{1,0:T(8,128)S(1)}, u32[]{:S(2)}, u32[]{:S(2)}) collective-permute-start(f32[17,512]{1,0:T(8,128)S(1)} %get-tuple-element.81), channel_id=1, source_target_pairs={{0,224},{32,256},{64,288},{96,320},{128,352},{160,384},{192,416},{... | collective-permute-start | bytes 104456 | tf_op jit(solution)/shard_map/ppermute | solution.py:29
  265.0 4.6 %collective-permute-start.18 = (f32[17,512]{1,0:T(8,128)S(1)}, f32[17,512]{1,0:T(8,128)S(1)}, u32[]{:S(2)}, u32[]{:S(2)}) collective-permute-start(f32[17,512]{1,0:T(8,128)S(1)} %get-tuple-element.81), channel_id=1, source_target_pairs={{0,256},{32,288},{64,320},{96,352},{128,384},{160,416},{192,448},{... | collective-permute-start | bytes 104456 | tf_op jit(solution)/shard_map/ppermute | solution.py:29
  269.7 4.3 %collective-permute-start.19 = (f32[17,512]{1,0:T(8,128)S(1)}, f32[17,512]{1,0:T(8,128)S(1)}, u32[]{:S(2)}, u32[]{:S(2)}) collective-permute-start(f32[17,512]{1,0:T(8,128)S(1)} %get-tuple-element.81), channel_id=1, source_target_pairs={{0,288},{32,320},{64,352},{96,384},{128,416},{160,448},{192,480},{... | collective-permute-start | bytes 104456 | tf_op jit(solution)/shard_map/ppermute | solution.py:29
  274.0 4.4 %collective-permute-start.20 = (f32[17,512]{1,0:T(8,128)S(1)}, f32[17,512]{1,0:T(8,128)S(1)}, u32[]{:S(2)}, u32[]{:S(2)}) collective-permute-start(f32[17,512]{1,0:T(8,128)S(1)} %get-tuple-element.81), channel_id=1, source_target_pairs={{0,320},{32,352},{64,384},{96,416},{128,448},{160,480},{192,0},{22... | collective-permute-start | bytes 104456 | tf_op jit(solution)/shard_map/ppermute | solution.py:29
  278.4 8.0 %collective-permute-start.21 = (f32[17,512]{1,0:T(8,128)S(1)}, f32[17,512]{1,0:T(8,128)S(1)}, u32[]{:S(2)}, u32[]{:S(2)}) collective-permute-start(f32[17,512]{1,0:T(8,128)S(1)} %get-tuple-element.81), channel_id=1, source_target_pairs={{0,352},{32,384},{64,416},{96,448},{128,480},{160,0},{192,32},{224... | collective-permute-start | bytes 104456 | tf_op jit(solution)/shard_map/ppermute | solution.py:29
  289.1 11.1 %collective-permute-start.23 = (f32[17,512]{1,0:T(8,128)S(1)}, f32[17,512]{1,0:T(8,128)S(1)}, u32[]{:S(2)}, u32[]{:S(2)}) collective-permute-start(f32[17,512]{1,0:T(8,128)S(1)} %get-tuple-element.81), channel_id=1, source_target_pairs={{0,416},{32,448},{64,480},{96,0},{128,32},{160,64},{192,96},{224,1... | collective-permute-start | bytes 104456 | tf_op jit(solution)/shard_map/ppermute | solution.py:29
  300.2 3.3 collective-permute-start.24
  303.5 3.0 collective-permute-start.25
  323.9 3.3 collective-permute-start.30
  331.3 3.0 collective-permute-done.29
  335.1 12.1 %collective-permute-start.32 = (f32[272,512]{1,0:T(8,128)S(1)}, f32[272,512]{1,0:T(8,128)S(1)}, u32[]{:S(2)}, u32[]{:S(2)}) collective-permute-start(f32[272,512]{1,0:T(8,128)S(1)} %broadcast_select_fusion.1), channel_id=1, source_target_pairs={{0,1},{1,0},{2,3},{3,2},{4,5},{5,4},{6,7},{7,6},{8,9},{9,8},{10,11... | collective-permute-start | bytes 1671176 | tf_op jit(solution)/shard_map/ppermute | solution.py:29
  (138 shorter events, 64.7 us)
Async XLA Ops:
  7.2 121.9 %all-gather.2.cloned.1.call-start = ((), (), s32[]{:S(2)}) async-start(), calls=%async_computation | async-start | bytes 8650752 | tf_op jit(solution)/shard_map/all_gather | solution.py:61
  160.8 5.9 %collective-permute-start = (f32[4,128,512]{2,1,0:T(8,128)}, f32[4,128,512]{2,1,0:T(8,128)}, u32[]{:S(2)}, u32[]{:S(2)}) collective-permute-start(f32[4,128,512]{2,1,0:T(8,128)} %dynamic-slice_bitcast_fusion), channel_id=1, source_target_pairs={{0,1},{1,0},{2,3},{3,2},{4,5},{5,4},{6,7},{7,6},{8,9},{9,8},{10,11... | collective-permute-start | bytes 3145736 | tf_op jit(solution)/shard_map/ppermute | solution.py:23
  169.1 10.3 %collective-permute-start.3 = (f32[128,512]{1,0:T(8,128)S(1)}, f32[128,512]{1,0:T(8,128)S(1)}, u32[]{:S(2)}, u32[]{:S(2)}) collective-permute-start(f32[128,512]{1,0:T(8,128)S(1)} %get-tuple-element.85), channel_id=1, source_target_pairs={{0,6},{2,0},{4,2},{6,4},{1,7},{3,1},{5,3},{7,5},{8,14},{10,8},{12,... | collective-permute-start | bytes 786440 | tf_op jit(solution)/shard_map/ppermute | solution.py:23
  174.1 22.4 %collective-permute-start.2 = (f32[128,512]{1,0:T(8,128)S(1)}, f32[128,512]{1,0:T(8,128)S(1)}, u32[]{:S(2)}, u32[]{:S(2)}) collective-permute-start(f32[128,512]{1,0:T(8,128)S(1)} %get-tuple-element.86), channel_id=1, source_target_pairs={{0,4},{2,6},{4,0},{6,2},{1,5},{3,7},{5,1},{7,3},{8,12},{10,14},{12... | collective-permute-start | bytes 786440 | tf_op jit(solution)/shard_map/ppermute | solution.py:23
  176.0 20.4 %collective-permute-start.1 = (f32[128,512]{1,0:T(8,128)S(1)}, f32[128,512]{1,0:T(8,128)S(1)}, u32[]{:S(2)}, u32[]{:S(2)}) collective-permute-start(f32[128,512]{1,0:T(8,128)S(1)} %get-tuple-element.84), channel_id=1, source_target_pairs={{0,2},{2,4},{4,6},{6,0},{1,3},{3,5},{5,7},{7,1},{8,10},{10,12},{12... | collective-permute-start | bytes 786440 | tf_op jit(solution)/shard_map/ppermute | solution.py:23
  203.8 7.8 %collective-permute-start.7 = (f32[68,512]{1,0:T(8,128)S(1)}, f32[68,512]{1,0:T(8,128)S(1)}, u32[]{:S(2)}, u32[]{:S(2)}) collective-permute-start(f32[68,512]{1,0:T(8,128)S(1)} %get-tuple-element.88), channel_id=1, source_target_pairs={{0,24},{8,0},{16,8},{24,16},{1,25},{9,1},{17,9},{25,17},{2,26},{10... | collective-permute-start | bytes 417800 | tf_op jit(solution)/shard_map/ppermute | solution.py:23
  205.7 8.4 %collective-permute-start.6 = (f32[68,512]{1,0:T(8,128)S(1)}, f32[68,512]{1,0:T(8,128)S(1)}, u32[]{:S(2)}, u32[]{:S(2)}) collective-permute-start(f32[68,512]{1,0:T(8,128)S(1)} %get-tuple-element.89), channel_id=1, source_target_pairs={{0,16},{8,24},{16,0},{24,8},{1,17},{9,25},{17,1},{25,9},{2,18},{10... | collective-permute-start | bytes 417800 | tf_op jit(solution)/shard_map/ppermute | solution.py:23
  209.4 7.6 %collective-permute-start.5 = (f32[68,512]{1,0:T(8,128)S(1)}, f32[68,512]{1,0:T(8,128)S(1)}, u32[]{:S(2)}, u32[]{:S(2)}) collective-permute-start(f32[68,512]{1,0:T(8,128)S(1)} %get-tuple-element.87), channel_id=1, source_target_pairs={{0,8},{8,16},{16,24},{24,0},{1,9},{9,17},{17,25},{25,1},{2,10},{10... | collective-permute-start | bytes 417800 | tf_op jit(solution)/shard_map/ppermute | solution.py:23
  217.1 10.3 %collective-permute-start.10 = (f32[17,512]{1,0:T(8,128)S(1)}, f32[17,512]{1,0:T(8,128)S(1)}, u32[]{:S(2)}, u32[]{:S(2)}) collective-permute-start(f32[17,512]{1,0:T(8,128)S(1)} %get-tuple-element.92), channel_id=1, source_target_pairs={{0,6},{2,0},{4,2},{6,4},{1,7},{3,1},{5,3},{7,5},{8,14},{10,8},{12,... | collective-permute-start | bytes 104456 | tf_op jit(solution)/shard_map/ppermute | solution.py:23
  219.0 8.3 %collective-permute-start.9 = (f32[17,512]{1,0:T(8,128)S(1)}, f32[17,512]{1,0:T(8,128)S(1)}, u32[]{:S(2)}, u32[]{:S(2)}) collective-permute-start(f32[17,512]{1,0:T(8,128)S(1)} %get-tuple-element.93), channel_id=1, source_target_pairs={{0,4},{2,6},{4,0},{6,2},{1,5},{3,7},{5,1},{7,3},{8,12},{10,14},{12... | collective-permute-start | bytes 104456 | tf_op jit(solution)/shard_map/ppermute | solution.py:23
  223.9 6.6 %collective-permute-start.8 = (f32[17,512]{1,0:T(8,128)S(1)}, f32[17,512]{1,0:T(8,128)S(1)}, u32[]{:S(2)}, u32[]{:S(2)}) collective-permute-start(f32[17,512]{1,0:T(8,128)S(1)} %get-tuple-element.91), channel_id=1, source_target_pairs={{0,2},{2,4},{4,6},{6,0},{1,3},{3,5},{5,7},{7,1},{8,10},{10,12},{12... | collective-permute-start | bytes 104456 | tf_op jit(solution)/shard_map/ppermute | solution.py:23
  230.6 21.0 %collective-permute-start.11 = (f32[17,512]{1,0:T(8,128)S(1)}, f32[17,512]{1,0:T(8,128)S(1)}, u32[]{:S(2)}, u32[]{:S(2)}) collective-permute-start(f32[17,512]{1,0:T(8,128)S(1)} %get-tuple-element.81), channel_id=1, source_target_pairs={{0,32},{32,64},{64,96},{96,128},{128,160},{160,192},{192,224},{224... | collective-permute-start | bytes 104456 | tf_op jit(solution)/shard_map/ppermute | solution.py:29
  232.9 26.4 %collective-permute-start.12 = (f32[17,512]{1,0:T(8,128)S(1)}, f32[17,512]{1,0:T(8,128)S(1)}, u32[]{:S(2)}, u32[]{:S(2)}) collective-permute-start(f32[17,512]{1,0:T(8,128)S(1)} %get-tuple-element.81), channel_id=1, source_target_pairs={{0,64},{32,96},{64,128},{96,160},{128,192},{160,224},{192,256},{22... | collective-permute-start | bytes 104456 | tf_op jit(solution)/shard_map/ppermute | solution.py:29
  235.7 29.3 %collective-permute-start.13 = (f32[17,512]{1,0:T(8,128)S(1)}, f32[17,512]{1,0:T(8,128)S(1)}, u32[]{:S(2)}, u32[]{:S(2)}) collective-permute-start(f32[17,512]{1,0:T(8,128)S(1)} %get-tuple-element.81), channel_id=1, source_target_pairs={{0,96},{32,128},{64,160},{96,192},{128,224},{160,256},{192,288},{2... | collective-permute-start | bytes 104456 | tf_op jit(solution)/shard_map/ppermute | solution.py:29
  242.2 27.5 %collective-permute-start.14 = (f32[17,512]{1,0:T(8,128)S(1)}, f32[17,512]{1,0:T(8,128)S(1)}, u32[]{:S(2)}, u32[]{:S(2)}) collective-permute-start(f32[17,512]{1,0:T(8,128)S(1)} %get-tuple-element.81), channel_id=1, source_target_pairs={{0,128},{32,160},{64,192},{96,224},{128,256},{160,288},{192,320},{... | collective-permute-start | bytes 104456 | tf_op jit(solution)/shard_map/ppermute | solution.py:29
  247.1 26.9 %collective-permute-start.15 = (f32[17,512]{1,0:T(8,128)S(1)}, f32[17,512]{1,0:T(8,128)S(1)}, u32[]{:S(2)}, u32[]{:S(2)}) collective-permute-start(f32[17,512]{1,0:T(8,128)S(1)} %get-tuple-element.81), channel_id=1, source_target_pairs={{0,160},{32,192},{64,224},{96,256},{128,288},{160,320},{192,352},{... | collective-permute-start | bytes 104456 | tf_op jit(solution)/shard_map/ppermute | solution.py:29
  251.6 26.9 %collective-permute-start.16 = (f32[17,512]{1,0:T(8,128)S(1)}, f32[17,512]{1,0:T(8,128)S(1)}, u32[]{:S(2)}, u32[]{:S(2)}) collective-permute-start(f32[17,512]{1,0:T(8,128)S(1)} %get-tuple-element.81), channel_id=1, source_target_pairs={{0,192},{32,224},{64,256},{96,288},{128,320},{160,352},{192,384},{... | collective-permute-start | bytes 104456 | tf_op jit(solution)/shard_map/ppermute | solution.py:29
  259.2 27.2 %collective-permute-start.17 = (f32[17,512]{1,0:T(8,128)S(1)}, f32[17,512]{1,0:T(8,128)S(1)}, u32[]{:S(2)}, u32[]{:S(2)}) collective-permute-start(f32[17,512]{1,0:T(8,128)S(1)} %get-tuple-element.81), channel_id=1, source_target_pairs={{0,224},{32,256},{64,288},{96,320},{128,352},{160,384},{192,416},{... | collective-permute-start | bytes 104456 | tf_op jit(solution)/shard_map/ppermute | solution.py:29
  265.0 24.1 %collective-permute-start.18 = (f32[17,512]{1,0:T(8,128)S(1)}, f32[17,512]{1,0:T(8,128)S(1)}, u32[]{:S(2)}, u32[]{:S(2)}) collective-permute-start(f32[17,512]{1,0:T(8,128)S(1)} %get-tuple-element.81), channel_id=1, source_target_pairs={{0,256},{32,288},{64,320},{96,352},{128,384},{160,416},{192,448},{... | collective-permute-start | bytes 104456 | tf_op jit(solution)/shard_map/ppermute | solution.py:29
  269.7 30.5 %collective-permute-start.19 = (f32[17,512]{1,0:T(8,128)S(1)}, f32[17,512]{1,0:T(8,128)S(1)}, u32[]{:S(2)}, u32[]{:S(2)}) collective-permute-start(f32[17,512]{1,0:T(8,128)S(1)} %get-tuple-element.81), channel_id=1, source_target_pairs={{0,288},{32,320},{64,352},{96,384},{128,416},{160,448},{192,480},{... | collective-permute-start | bytes 104456 | tf_op jit(solution)/shard_map/ppermute | solution.py:29
  274.0 29.5 %collective-permute-start.20 = (f32[17,512]{1,0:T(8,128)S(1)}, f32[17,512]{1,0:T(8,128)S(1)}, u32[]{:S(2)}, u32[]{:S(2)}) collective-permute-start(f32[17,512]{1,0:T(8,128)S(1)} %get-tuple-element.81), channel_id=1, source_target_pairs={{0,320},{32,352},{64,384},{96,416},{128,448},{160,480},{192,0},{22... | collective-permute-start | bytes 104456 | tf_op jit(solution)/shard_map/ppermute | solution.py:29
  278.4 28.1 %collective-permute-start.21 = (f32[17,512]{1,0:T(8,128)S(1)}, f32[17,512]{1,0:T(8,128)S(1)}, u32[]{:S(2)}, u32[]{:S(2)}) collective-permute-start(f32[17,512]{1,0:T(8,128)S(1)} %get-tuple-element.81), channel_id=1, source_target_pairs={{0,352},{32,384},{64,416},{96,448},{128,480},{160,0},{192,32},{224... | collective-permute-start | bytes 104456 | tf_op jit(solution)/shard_map/ppermute | solution.py:29
  286.5 20.1 %collective-permute-start.22 = (f32[17,512]{1,0:T(8,128)S(1)}, f32[17,512]{1,0:T(8,128)S(1)}, u32[]{:S(2)}, u32[]{:S(2)}) collective-permute-start(f32[17,512]{1,0:T(8,128)S(1)} %get-tuple-element.81), channel_id=1, source_target_pairs={{0,384},{32,416},{64,448},{96,480},{128,0},{160,32},{192,64},{224,... | collective-permute-start | bytes 104456 | tf_op jit(solution)/shard_map/ppermute | solution.py:29
  289.1 17.5 %collective-permute-start.23 = (f32[17,512]{1,0:T(8,128)S(1)}, f32[17,512]{1,0:T(8,128)S(1)}, u32[]{:S(2)}, u32[]{:S(2)}) collective-permute-start(f32[17,512]{1,0:T(8,128)S(1)} %get-tuple-element.81), channel_id=1, source_target_pairs={{0,416},{32,448},{64,480},{96,0},{128,32},{160,64},{192,96},{224,1... | collective-permute-start | bytes 104456 | tf_op jit(solution)/shard_map/ppermute | solution.py:29
  300.2 6.4 %collective-permute-start.24 = (f32[17,512]{1,0:T(8,128)S(1)}, f32[17,512]{1,0:T(8,128)S(1)}, u32[]{:S(2)}, u32[]{:S(2)}) collective-permute-start(f32[17,512]{1,0:T(8,128)S(1)} %get-tuple-element.81), channel_id=1, source_target_pairs={{0,448},{32,480},{64,0},{96,32},{128,64},{160,96},{192,128},{224,1... | collective-permute-start | bytes 104456 | tf_op jit(solution)/shard_map/ppermute | solution.py:29
  309.2 7.3 %collective-permute-start.28 = (f32[17,512]{1,0:T(8,128)S(1)}, f32[17,512]{1,0:T(8,128)S(1)}, u32[]{:S(2)}, u32[]{:S(2)}) collective-permute-start(f32[17,512]{1,0:T(8,128)S(1)} %fusion.40), channel_id=1, source_target_pairs={{0,6},{2,0},{4,2},{6,4},{1,7},{3,1},{5,3},{7,5},{8,14},{10,8},{12,... | collective-permute-start | bytes 104456 | tf_op jit(solution)/shard_map/ppermute | solution.py:29
  312.0 6.7 %collective-permute-start.27 = (f32[17,512]{1,0:T(8,128)S(1)}, f32[17,512]{1,0:T(8,128)S(1)}, u32[]{:S(2)}, u32[]{:S(2)}) collective-permute-start(f32[17,512]{1,0:T(8,128)S(1)} %fusion.40), channel_id=1, source_target_pairs={{0,4},{2,6},{4,0},{6,2},{1,5},{3,7},{5,1},{7,3},{8,12},{10,14},{12... | collective-permute-start | bytes 104456 | tf_op jit(solution)/shard_map/ppermute | solution.py:29
  314.0 6.6 %collective-permute-start.26 = (f32[17,512]{1,0:T(8,128)S(1)}, f32[17,512]{1,0:T(8,128)S(1)}, u32[]{:S(2)}, u32[]{:S(2)}) collective-permute-start(f32[17,512]{1,0:T(8,128)S(1)} %fusion.40), channel_id=1, source_target_pairs={{0,2},{2,4},{4,6},{6,0},{1,3},{3,5},{5,7},{7,1},{8,10},{10,12},{12... | collective-permute-start | bytes 104456 | tf_op jit(solution)/shard_map/ppermute | solution.py:29
  321.3 8.7 %collective-permute-start.31 = (f32[68,512]{1,0:T(8,128)S(1)}, f32[68,512]{1,0:T(8,128)S(1)}, u32[]{:S(2)}, u32[]{:S(2)}) collective-permute-start(f32[68,512]{1,0:T(8,128)S(1)} %broadcast_select_fusion.3), channel_id=1, source_target_pairs={{0,24},{8,0},{16,8},{24,16},{1,25},{9,1},{17,9},{25,17},{2,26},{10... | collective-permute-start | bytes 417800 | tf_op jit(solution)/shard_map/ppermute | solution.py:29
  323.9 7.4 %collective-permute-start.30 = (f32[68,512]{1,0:T(8,128)S(1)}, f32[68,512]{1,0:T(8,128)S(1)}, u32[]{:S(2)}, u32[]{:S(2)}) collective-permute-start(f32[68,512]{1,0:T(8,128)S(1)} %broadcast_select_fusion.3), channel_id=1, source_target_pairs={{0,16},{8,24},{16,0},{24,8},{1,17},{9,25},{17,1},{25,9},{2,18},{10... | collective-permute-start | bytes 417800 | tf_op jit(solution)/shard_map/ppermute | solution.py:29
  327.2 7.1 %collective-permute-start.29 = (f32[68,512]{1,0:T(8,128)S(1)}, f32[68,512]{1,0:T(8,128)S(1)}, u32[]{:S(2)}, u32[]{:S(2)}) collective-permute-start(f32[68,512]{1,0:T(8,128)S(1)} %broadcast_select_fusion.3), channel_id=1, source_target_pairs={{0,8},{8,16},{16,24},{24,0},{1,9},{9,17},{17,25},{25,1},{2,10},{10... | collective-permute-start | bytes 417800 | tf_op jit(solution)/shard_map/ppermute | solution.py:29
  335.1 13.6 %collective-permute-start.32 = (f32[272,512]{1,0:T(8,128)S(1)}, f32[272,512]{1,0:T(8,128)S(1)}, u32[]{:S(2)}, u32[]{:S(2)}) collective-permute-start(f32[272,512]{1,0:T(8,128)S(1)} %broadcast_select_fusion.1), channel_id=1, source_target_pairs={{0,1},{1,0},{2,3},{3,2},{4,5},{5,4},{6,7},{7,6},{8,9},{9,8},{10,11... | collective-permute-start | bytes 1671176 | tf_op jit(solution)/shard_map/ppermute | solution.py:29
  (6 other events, 257.6 us)
Sparse Core Ops, SparseCore 0:
  19.8 109.2 all-gather.1

commit v2 on v1

--- a/solution.py
+++ b/solution.py
@@ -11,33 +11,42 @@
 ALL_AXES = SECTION_AXES + REP_AXES
 
 
-def _shift_perm(n, k):
-    return [(i, (i + k) % n) for i in range(n)]
+def _xor_perm(n, bit):
+    return [(i, i ^ bit) for i in range(n)]
 
 
-def _reduce_scatter(blocks, axis, n):
+def _halving_scatter(blocks, axis, n):
     me = lax.axis_index(axis)
-    acc = lax.dynamic_index_in_dim(blocks, me, 0, keepdims=False)
-    for k in range(1, n):
-        send = lax.dynamic_index_in_dim(blocks, (me + k) % n, 0, keepdims=False)
-        acc = acc + lax.ppermute(send, axis, _shift_perm(n, k))
-    return acc
+    bit = n // 2
+    while bit >= 1:
+        pairs = blocks.reshape((2, blocks.shape[0] // 2) + blocks.shape[1:])
+        mine = (me // bit) % 2
+        keep = lax.dynamic_index_in_dim(pairs, mine, 0, keepdims=False)
+        send = lax.dynamic_index_in_dim(pairs, 1 - mine, 0, keepdims=False)
+        blocks = keep + lax.ppermute(send, axis, _xor_perm(n, bit))
+        bit //= 2
+    return blocks[0]
 
 
-def _all_gather(piece, axis, n):
+def _doubling_gather(piece, axis, n):
     me = lax.axis_index(axis)
-    pieces = [piece] + [lax.ppermute(piece, axis, _shift_perm(n, k)) for k in range(1, n)]
-    stacked = jnp.stack(pieces)
-    order = (me - jnp.arange(n, dtype=jnp.int32)) % n
-    return jnp.take(stacked, order, axis=0)
+    bit = 1
+    while bit < n:
+        other = lax.ppermute(piece, axis, _xor_perm(n, bit))
+        upper = (me // bit) % 2 == 1
+        low = jnp.where(upper, other, piece)
+        high = jnp.where(upper, piece, other)
+        piece = jnp.concatenate([low, high], axis=0)
+        bit *= 2
+    return piece
 
 
-def _all_reduce_direct(piece, axes, n):
-    gathered = _all_gather(piece, axes, n)
-    total = gathered[0]
-    for j in range(1, n):
-        total = total + gathered[j]
-    return total
+def _doubling_sum(piece, axis, n):
+    bit = 1
+    while bit < n:
+        piece = piece + lax.ppermute(piece, axis, _xor_perm(n, bit))
+        bit *= 2
+    return piece
 
 
 def shards(features, col_panels, block_counts, block_values, weight, bias, cotangent):
@@ -78,8 +87,8 @@
     cores = sizes["core"]
     by_core = gathered_sum.reshape(row_panels // cores, cores, tile_size, feat_width)
     by_core = jnp.moveaxis(by_core, 1, 0)
-    half = _reduce_scatter(by_core, "core", cores)
-    summed_own = _reduce_scatter(half, "y_lo", sizes["y_lo"])
+    half = _halving_scatter(by_core, "core", cores)
+    summed_own = _halving_scatter(half.reshape((sizes["y_lo"], 1) + half.shape[1:]), "y_lo", sizes["y_lo"])
     own_rows = own_panels * tile_size
     aggregated = summed_own.reshape(own_rows, feat_width).astype(jnp.bfloat16)
     pre = jnp.dot(aggregated, weight, preferred_element_type=jnp.float32) + bias
@@ -91,17 +100,16 @@
     local_weight = jnp.einsum("nd,nf->df", aggregated, slope, preferred_element_type=jnp.float32)
     local_bias = jnp.sum(slope.astype(jnp.float32), axis=0)
     width = weight.shape[0]
-    scatter_ways = sizes["core"] * sizes["x"] * sizes["y_lo"]
-    padded_rows = -(-(width + 1) // scatter_ways) * scatter_ways
+    scatter_ways = sizes["core"] * sizes["x"]
+    padded_rows = -(-(width + 1) // (scatter_ways * 8)) * scatter_ways * 8
     combined = jnp.zeros((padded_rows, feat_width), jnp.float32)
     combined = combined.at[:width].set(local_weight).at[width].set(local_bias)
-    chunk = combined
-    for name in ("core", "x", "y_lo"):
-        chunk = _reduce_scatter(chunk.reshape(sizes[name], -1, feat_width), name, sizes[name])
-    outer = sizes["z"] * sizes["y_hi"]
-    chunk = _all_reduce_direct(chunk, ("y_hi", "z"), outer)
-    for name in ("y_lo", "x", "core"):
-        chunk = _all_gather(chunk, name, sizes[name]).reshape(-1, feat_width)
+    chunk = _halving_scatter(combined.reshape(sizes["core"], -1, feat_width), "core", sizes["core"])
+    chunk = _halving_scatter(chunk.reshape(sizes["x"], -1, feat_width), "x", sizes["x"])
+    for name in ("y_lo", "z", "y_hi"):
+        chunk = _doubling_sum(chunk, name, sizes[name])
+    chunk = _doubling_gather(chunk, "x", sizes["x"])
+    chunk = _doubling_gather(chunk, "core", sizes["core"])
     node_total = lax.axis_size(SECTION_AXES) * rep_count * own_rows
     factor = 1.0 / math.sqrt(node_total)
     weight_sum = chunk[:width]

time: 359 us -> 322 us (0.90)
  starting transfers between devices: 137 us -> 56.4 us
  waiting for transfers between devices: 148 us -> 195 us
    ppermute x33 -> x15, starting transfers between devices: 137 us -> 56.4 us  [the longest x6 21.1 us: _doubling_sum(): piece = piece + lax.ppermute(piece, axis, _xor_perm(n, bit))]
    ppermute x33 -> x15, waiting for transfers between devices: 41.9 us -> 89.2 us  [the longest x6 45.3 us: _halving_scatter(): blocks = keep + lax.ppermute(send, axis, _xor_perm(n, bit))]
  transfers between devices with their start and end apart: 34 -> 16, of which waited for: 14 -> 16; matrix products, arithmetic and copies ran while one was open for 1% -> 1% of each run, Pallas kernels for 0% -> 0%
where the time goes in v2:
time: 322 us; the launch traced here: 321 us
  waiting for transfers between devices  195 us (61%)
  starting transfers between devices  56.4 us (18%)
  local copies, waits for them, and re-layouts  21.5 us (7%)
  between operations  15.2 us (5%)
  blocking collectives  12.4 us (4%)
  matrix products  12.2 us (4%)
  other arithmetic  7.77 us (2%)
    all_gather x1, waiting for transfers between devices, shards(): gathered = lax.all_gather(gathered, ('z', 'x'), axis=0, tiled=True)  106 us
    ppermute x6, waiting for transfers between devices, _halving_scatter(): blocks = keep + lax.ppermute(send, axis, _xor_perm(n, bit))  45.3 us
    ppermute x6, waiting for transfers between devices, _doubling_sum(): piece = piece + lax.ppermute(piece, axis, _xor_perm(n, bit))  30 us
    ppermute x6, starting transfers between devices, _doubling_sum(): piece = piece + lax.ppermute(piece, axis, _xor_perm(n, bit))  21.1 us
    ppermute x6, starting transfers between devices, _halving_scatter(): blocks = keep + lax.ppermute(send, axis, _xor_perm(n, bit))  19.2 us
    gather x3, local copies, waits for them, and re-layouts, one_turn(): picked = all_panels[step_cols]  18.5 us
    ppermute x3, starting transfers between devices, _doubling_gather(): other = lax.ppermute(piece, axis, _xor_perm(n, bit))  16 us
    ppermute x3, waiting for transfers between devices, _doubling_gather(): other = lax.ppermute(piece, axis, _xor_perm(n, bit))  14 us
  transfers between devices with their start and end apart: 16, of which 16 were waited for; matrix products, arithmetic and copies ran while one was open for 1% of the time, Pallas kernels for 0%

profile of v2, /device:TPU:1, one launch (start us, length us, event | category | flops | bytes accessed | tf_op | source)
XLA Modules:
  0.0 320.9 jit_solution(3849501572358321335)
XLA Ops:
  7.2 12.4 %all_gather.6 = bf16[256,512]{1,0:T(8,128)(2,1)} all-gather(bf16[128,512]{1,0:T(8,128)(2,1)} %param.13), channel_id=1, replica_groups=mesh['y_hi'=2,'z'=8,'x'=4,'y_lo'=4,'core'=2] {'y_hi'}, dimensions={0}, use_global_device_ids=true | all-gather | bytes 393216 | tf_op jit(solution)/shard_map/all_gather | solution.py:69
  23.1 106.0 %all-gather.2.cloned.1.call-done = bf16[8192,512]{1,0:T(8,128)(2,1)} async-done(((bf16[256,512]{1,0:T(8,128)(2,1)}), bf16[8192,512]{1,0:T(8,128)(2,1)}) %all-gather.2.cloned.1.call-update) | async-done | bytes 8388624 | tf_op jit(solution)/shard_map/all_gather | solution.py:70
  129.3 30.2 %while.12 = (s32[]{:T(128)}, f32[8,128,512]{2,1,0:T(8,128)S(1)}, s32[]{:T(128)}, pred[8,12]{1,0:T(8,128)(4,1)S(1)}, bf16[8,12,128,128]{3,2,1,0:T(8,128)(2,1)}, /...) while((s32[]{:T(128)}, f32[8,128,512]{2,1,0:T(8,128)S(1)}, ...), condition=%wide.region_2.3_spmd, body=%wide.region_1.2_spmd.sunk | while | flops 537920640 | bytes 17830928 | solution.py:86
  129.5 6.2 %gather_fusion = bf16[32,128,512]{2,1,0:T(8,128)(2,1)} fusion(bf16[64,128,512]{2,1,0:T(8,128)(2,1)} %get-tuple-element.161, s32[1024]{0:T(1024)S(1)} %pad_clamp_fusion.2), kind=kCustom, calls=%fused_computation.clone.1 | custom fusion | bytes 8388736 | tf_op jit(solution)/shard_map/while/body/gather | solution.py:81
  135.8 3.6 %bitcast_add_fusion.6 = f32[8,128,512]{2,1,0:T(8,128)S(1)} fusion(f32[8,128,512]{2,1,0:T(8,128)S(1)} %get-tuple-element.145, bf16[8,4,128,512]{3,2,1,0:T(8,128)(2,1)} %bitcast.45, bf16[8,12,128,128]{3,2,1,0:T(8,128)(2,1)} %get-tuple-element.159, s32[]{:T(128)S(6)} %select_n.211, pred[8,4]{1,0:T(8,128)(4,1)S(1)} %constant_dynamic-slice_fusion.4), kind=kOutput, calls=%fused_computation.1.clone.1 | convolution fusion | flops 537919488 | bytes 9437220 | tf_op jit(solution)/shard_map/while/body/gkab,gkbf->gaf/dot_general | solution.py:82
  139.6 6.2 %gather_fusion = bf16[32,128,512]{2,1,0:T(8,128)(2,1)} fusion(bf16[64,128,512]{2,1,0:T(8,128)(2,1)} %get-tuple-element.161, s32[1024]{0:T(1024)S(1)} %pad_clamp_fusion.2), kind=kCustom, calls=%fused_computation.clone.1 | custom fusion | bytes 8388736 | tf_op jit(solution)/shard_map/while/body/gather | solution.py:81
  145.8 3.6 %bitcast_add_fusion.6 = f32[8,128,512]{2,1,0:T(8,128)S(1)} fusion(f32[8,128,512]{2,1,0:T(8,128)S(1)} %get-tuple-element.145, bf16[8,4,128,512]{3,2,1,0:T(8,128)(2,1)} %bitcast.45, bf16[8,12,128,128]{3,2,1,0:T(8,128)(2,1)} %get-tuple-element.159, s32[]{:T(128)S(6)} %select_n.211, pred[8,4]{1,0:T(8,128)(4,1)S(1)} %constant_dynamic-slice_fusion.4), kind=kOutput, calls=%fused_computation.1.clone.1 | convolution fusion | flops 537919488 | bytes 9437220 | tf_op jit(solution)/shard_map/while/body/gkab,gkbf->gaf/dot_general | solution.py:82
  149.7 6.2 %gather_fusion = bf16[32,128,512]{2,1,0:T(8,128)(2,1)} fusion(bf16[64,128,512]{2,1,0:T(8,128)(2,1)} %get-tuple-element.161, s32[1024]{0:T(1024)S(1)} %pad_clamp_fusion.2), kind=kCustom, calls=%fused_computation.clone.1 | custom fusion | bytes 8388736 | tf_op jit(solution)/shard_map/while/body/gather | solution.py:81
  155.9 3.6 %bitcast_add_fusion.6 = f32[8,128,512]{2,1,0:T(8,128)S(1)} fusion(f32[8,128,512]{2,1,0:T(8,128)S(1)} %get-tuple-element.145, bf16[8,4,128,512]{3,2,1,0:T(8,128)(2,1)} %bitcast.45, bf16[8,12,128,128]{3,2,1,0:T(8,128)(2,1)} %get-tuple-element.159, s32[]{:T(128)S(6)} %select_n.211, pred[8,4]{1,0:T(8,128)(4,1)S(1)} %constant_dynamic-slice_fusion.4), kind=kOutput, calls=%fused_computation.1.clone.1 | convolution fusion | flops 537919488 | bytes 9437220 | tf_op jit(solution)/shard_map/while/body/gkab,gkbf->gaf/dot_general | solution.py:82
  160.6 3.3 %collective-permute-start = (f32[1,4,128,512]{3,2,1,0:T(8,128)}, f32[1,4,128,512]{3,2,1,0:T(8,128)}, u32[]{:S(2)}, u32[]{:S(2)}) collective-permute-start(f32[1,4,128,512]{3,2,1,0:T(8,128)} %dynamic-slice_bitcast_fusion), channel_id=1, source_target_pairs={{0,1},{1,0},{2,3},{3,2},{4,5},{5,4},{6,7},{7,6},{8,9},{9,8},{10,11... | collective-permute-start | bytes 3145736 | tf_op jit(solution)/shard_map/ppermute | solution.py:26
  164.0 2.6 collective-permute-done
  169.0 4.1 %collective-permute-start.1 = (f32[2,1,128,512]{3,2,0,1:T(8,128)S(1)}, f32[2,1,128,512]{3,2,0,1:T(8,128)S(1)}, u32[]{:S(2)}, u32[]{:S(2)}) collective-permute-start(f32[2,1,128,512]{3,2,0,1:T(8,128)S(1)} %dynamic-slice_bitcast_fusion.2), channel_id=1, source_target_pairs={{0,4},{2,6},{4,0},{6,2},{1,5},{3,7},{5,1},{7,3},{8,12},{10,14},{12... | collective-permute-start | bytes 1572872 | tf_op jit(solution)/shard_map/ppermute | solution.py:26
  173.1 23.1 %collective-permute-done.1 = f32[2,1,128,512]{3,2,0,1:T(8,128)S(1)} collective-permute-done((f32[2,1,128,512]{3,2,0,1:T(8,128)S(1)}, f32[2,1,128,512]{3,2,0,1:T(8,128)S(1)}, u32[]{:S(2)}, u32[]{:S(2)}) %collective-permute-start.1) | collective-permute-done | bytes 524320 | tf_op jit(solution)/shard_map/ppermute | solution.py:26
  197.3 2.9 collective-permute-start.2
  200.2 5.6 %collective-permute-done.2 = f32[1,1,128,512]{3,2,0,1:T(8,128)S(1)} collective-permute-done((f32[1,1,128,512]{3,2,0,1:T(8,128)S(1)}, f32[1,1,128,512]{3,2,0,1:T(8,128)S(1)}, u32[]{:S(2)}, u32[]{:S(2)}) %collective-permute-start.2) | collective-permute-done | bytes 262176 | tf_op jit(solution)/shard_map/ppermute | solution.py:26
  207.4 4.0 %collective-permute-start.3 = (f32[1,288,512]{2,1,0:T(8,128)S(1)}, f32[1,288,512]{2,1,0:T(8,128)S(1)}, u32[]{:S(2)}, u32[]{:S(2)}) collective-permute-start(f32[1,288,512]{2,1,0:T(8,128)S(1)} %dynamic-slice_bitcast_fusion.1), channel_id=1, source_target_pairs={{0,1},{1,0},{2,3},{3,2},{4,5},{5,4},{6,7},{7,6},{8,9},{9,8},{10,11... | collective-permute-start | bytes 1769480 | tf_op jit(solution)/shard_map/ppermute | solution.py:26
  213.2 3.1 collective-permute-start.4
  216.3 8.5 %collective-permute-done.4 = f32[2,72,512]{2,1,0:T(8,128)S(1)} collective-permute-done((f32[2,72,512]{2,1,0:T(8,128)S(1)}, f32[2,72,512]{2,1,0:T(8,128)S(1)}, u32[]{:S(2)}, u32[]{:S(2)}) %collective-permute-start.4) | collective-permute-done | bytes 294944 | tf_op jit(solution)/shard_map/ppermute | solution.py:26
  226.8 4.0 %collective-permute-done.5 = f32[1,72,512]{2,1,0:T(8,128)S(1)} collective-permute-done((f32[1,72,512]{2,1,0:T(8,128)S(1)}, f32[1,72,512]{2,1,0:T(8,128)S(1)}, u32[]{:S(2)}, u32[]{:S(2)}) %collective-permute-start.5) | collective-permute-done | bytes 147488 | tf_op jit(solution)/shard_map/ppermute | solution.py:26
  230.7 2.9 collective-permute-start.6
  233.6 3.0 collective-permute-done.6
  236.7 4.5 %collective-permute-start.7 = (f32[72,512]{1,0:T(8,128)S(1)}, f32[72,512]{1,0:T(8,128)S(1)}, u32[]{:S(2)}, u32[]{:S(2)}) collective-permute-start(f32[72,512]{1,0:T(8,128)S(1)} %add.186), channel_id=1, source_target_pairs={{0,4},{2,6},{4,0},{6,2},{1,5},{3,7},{5,1},{7,3},{8,12},{10,14},{12... | collective-permute-start | bytes 442376 | tf_op jit(solution)/shard_map/ppermute | solution.py:47
  241.2 4.1 %collective-permute-done.7 = f32[72,512]{1,0:T(8,128)S(1)} collective-permute-done((f32[72,512]{1,0:T(8,128)S(1)}, f32[72,512]{1,0:T(8,128)S(1)}, u32[]{:S(2)}, u32[]{:S(2)}) %collective-permute-start.7) | collective-permute-done | bytes 147488 | tf_op jit(solution)/shard_map/ppermute | solution.py:47
  247.3 4.0 %collective-permute-done.8 = f32[72,512]{1,0:T(8,128)S(1)} collective-permute-done((f32[72,512]{1,0:T(8,128)S(1)}, f32[72,512]{1,0:T(8,128)S(1)}, u32[]{:S(2)}, u32[]{:S(2)}) %collective-permute-start.8) | collective-permute-done | bytes 147488 | tf_op jit(solution)/shard_map/ppermute | solution.py:47
  253.4 6.0 %collective-permute-done.9 = f32[72,512]{1,0:T(8,128)S(1)} collective-permute-done((f32[72,512]{1,0:T(8,128)S(1)}, f32[72,512]{1,0:T(8,128)S(1)}, u32[]{:S(2)}, u32[]{:S(2)}) %collective-permute-start.9) | collective-permute-done | bytes 147488 | tf_op jit(solution)/shard_map/ppermute | solution.py:47
  259.4 3.7 %collective-permute-start.10 = (f32[72,512]{1,0:T(8,128)S(1)}, f32[72,512]{1,0:T(8,128)S(1)}, u32[]{:S(2)}, u32[]{:S(2)}) collective-permute-start(f32[72,512]{1,0:T(8,128)S(1)} %add.189), channel_id=1, source_target_pairs={{0,128},{32,160},{64,192},{96,224},{128,0},{160,32},{192,64},{224,... | collective-permute-start | bytes 442376 | tf_op jit(solution)/shard_map/ppermute | solution.py:47
  263.1 7.5 %collective-permute-done.10 = f32[72,512]{1,0:T(8,128)S(1)} collective-permute-done((f32[72,512]{1,0:T(8,128)S(1)}, f32[72,512]{1,0:T(8,128)S(1)}, u32[]{:S(2)}, u32[]{:S(2)}) %collective-permute-start.10) | collective-permute-done | bytes 147488 | tf_op jit(solution)/shard_map/ppermute | solution.py:47
  270.7 5.9 %collective-permute-start.11 = (f32[72,512]{1,0:T(8,128)S(1)}, f32[72,512]{1,0:T(8,128)S(1)}, u32[]{:S(2)}, u32[]{:S(2)}) collective-permute-start(f32[72,512]{1,0:T(8,128)S(1)} %add.190), channel_id=1, source_target_pairs={{0,256},{256,0},{1,257},{257,1},{2,258},{258,2},{3,259},{259,3},{4... | collective-permute-start | bytes 442376 | tf_op jit(solution)/shard_map/ppermute | solution.py:47
  276.6 5.4 %collective-permute-done.11 = f32[72,512]{1,0:T(8,128)S(1)} collective-permute-done((f32[72,512]{1,0:T(8,128)S(1)}, f32[72,512]{1,0:T(8,128)S(1)}, u32[]{:S(2)}, u32[]{:S(2)}) %collective-permute-start.11) | collective-permute-done | bytes 147488 | tf_op jit(solution)/shard_map/ppermute | solution.py:47
  284.2 3.8 %collective-permute-done.12 = f32[72,512]{1,0:T(8,128)S(1)} collective-permute-done((f32[72,512]{1,0:T(8,128)S(1)}, f32[72,512]{1,0:T(8,128)S(1)}, u32[]{:S(2)}, u32[]{:S(2)}) %collective-permute-start.12) | collective-permute-done | bytes 147488 | tf_op jit(solution)/shard_map/ppermute | solution.py:35
  290.0 8.6 %collective-permute-done.13 = f32[144,512]{1,0:T(8,128)S(1)} collective-permute-done((f32[144,512]{1,0:T(8,128)S(1)}, f32[144,512]{1,0:T(8,128)S(1)}, u32[]{:S(2)}, u32[]{:S(2)}) %collective-permute-start.13) | collective-permute-done | bytes 294944 | tf_op jit(solution)/shard_map/ppermute | solution.py:35
  298.7 12.0 %collective-permute-start.14 = (f32[288,512]{1,0:T(8,128)S(1)}, f32[288,512]{1,0:T(8,128)S(1)}, u32[]{:S(2)}, u32[]{:S(2)}) collective-permute-start(f32[288,512]{1,0:T(8,128)S(1)} %pad_maximum_fusion.1), channel_id=1, source_target_pairs={{0,1},{1,0},{2,3},{3,2},{4,5},{5,4},{6,7},{7,6},{8,9},{9,8},{10,11... | collective-permute-start | bytes 1769480 | tf_op jit(solution)/shard_map/ppermute | solution.py:35
  (62 shorter events, 25.4 us)
Async XLA Ops:
  7.2 198.7 %copy-start = (bf16[512,512]{1,0:T(8,128)(2,1)S(1)}, bf16[512,512]{1,0:T(8,128)(2,1)}, u32[]{:S(2)}) copy-start(bf16[512,512]{1,0:T(8,128)(2,1)} %param.17) | copy-start | bytes 1572868
  7.2 121.9 %all-gather.2.cloned.1.call-start = ((), (), s32[]{:S(2)}) async-start(), calls=%async_computation | async-start | bytes 8650752 | tf_op jit(solution)/shard_map/all_gather | solution.py:70
  160.6 5.9 %collective-permute-start = (f32[1,4,128,512]{3,2,1,0:T(8,128)}, f32[1,4,128,512]{3,2,1,0:T(8,128)}, u32[]{:S(2)}, u32[]{:S(2)}) collective-permute-start(f32[1,4,128,512]{3,2,1,0:T(8,128)} %dynamic-slice_bitcast_fusion), channel_id=1, source_target_pairs={{0,1},{1,0},{2,3},{3,2},{4,5},{5,4},{6,7},{7,6},{8,9},{9,8},{10,11... | collective-permute-start | bytes 3145736 | tf_op jit(solution)/shard_map/ppermute | solution.py:26
  168.0 1.0 copy-start.1
  168.0 37.9 %copy-start.2 = (bf16[128,512]{1,0:T(8,128)(2,1)S(1)}, bf16[128,512]{1,0:T(8,128)(2,1)}, u32[]{:S(2)}) copy-start(bf16[128,512]{1,0:T(8,128)(2,1)} %param.19) | copy-start | bytes 393220
  168.0 37.9 %copy-start.3 = (f32[512]{0:T(512)S(1)}, f32[512]{0:T(512)}, u32[]{:S(2)}) copy-start(f32[512]{0:T(512)} %param.18) | copy-start | bytes 6148
  169.0 27.1 %collective-permute-start.1 = (f32[2,1,128,512]{3,2,0,1:T(8,128)S(1)}, f32[2,1,128,512]{3,2,0,1:T(8,128)S(1)}, u32[]{:S(2)}, u32[]{:S(2)}) collective-permute-start(f32[2,1,128,512]{3,2,0,1:T(8,128)S(1)} %dynamic-slice_bitcast_fusion.2), channel_id=1, source_target_pairs={{0,4},{2,6},{4,0},{6,2},{1,5},{3,7},{5,1},{7,3},{8,12},{10,14},{12... | collective-permute-start | bytes 1572872 | tf_op jit(solution)/shard_map/ppermute | solution.py:26
  197.3 8.5 %collective-permute-start.2 = (f32[1,1,128,512]{3,2,0,1:T(8,128)S(1)}, f32[1,1,128,512]{3,2,0,1:T(8,128)S(1)}, u32[]{:S(2)}, u32[]{:S(2)}) collective-permute-start(f32[1,1,128,512]{3,2,0,1:T(8,128)S(1)} %constant_dynamic-slice_fusion.2), channel_id=1, source_target_pairs={{0,2},{2,0},{4,6},{6,4},{1,3},{3,1},{5,7},{7,5},{8,10},{10,8},{12,... | collective-permute-start | bytes 786440 | tf_op jit(solution)/shard_map/ppermute | solution.py:26
  207.4 5.6 %collective-permute-start.3 = (f32[1,288,512]{2,1,0:T(8,128)S(1)}, f32[1,288,512]{2,1,0:T(8,128)S(1)}, u32[]{:S(2)}, u32[]{:S(2)}) collective-permute-start(f32[1,288,512]{2,1,0:T(8,128)S(1)} %dynamic-slice_bitcast_fusion.1), channel_id=1, source_target_pairs={{0,1},{1,0},{2,3},{3,2},{4,5},{5,4},{6,7},{7,6},{8,9},{9,8},{10,11... | collective-permute-start | bytes 1769480 | tf_op jit(solution)/shard_map/ppermute | solution.py:26
  213.2 11.6 %collective-permute-start.4 = (f32[2,72,512]{2,1,0:T(8,128)S(1)}, f32[2,72,512]{2,1,0:T(8,128)S(1)}, u32[]{:S(2)}, u32[]{:S(2)}) collective-permute-start(f32[2,72,512]{2,1,0:T(8,128)S(1)} %dynamic-slice_bitcast_fusion.3), channel_id=1, source_target_pairs={{0,16},{8,24},{16,0},{24,8},{1,17},{9,25},{17,1},{25,9},{2,18},{10... | collective-permute-start | bytes 884744 | tf_op jit(solution)/shard_map/ppermute | solution.py:26
  224.8 5.9 %collective-permute-start.5 = (f32[1,72,512]{2,1,0:T(8,128)S(1)}, f32[1,72,512]{2,1,0:T(8,128)S(1)}, u32[]{:S(2)}, u32[]{:S(2)}) collective-permute-start(f32[1,72,512]{2,1,0:T(8,128)S(1)} %constant_dynamic-slice_fusion.1), channel_id=1, source_target_pairs={{0,8},{8,0},{16,24},{24,16},{1,9},{9,1},{17,25},{25,17},{2,10},{10... | collective-permute-start | bytes 442376 | tf_op jit(solution)/shard_map/ppermute | solution.py:26
  230.7 5.9 %collective-permute-start.6 = (f32[72,512]{1,0:T(8,128)S(1)}, f32[72,512]{1,0:T(8,128)S(1)}, u32[]{:S(2)}, u32[]{:S(2)}) collective-permute-start(f32[72,512]{1,0:T(8,128)S(1)} %add_bitcast_fusion), channel_id=1, source_target_pairs={{0,2},{2,0},{4,6},{6,4},{1,3},{3,1},{5,7},{7,5},{8,10},{10,8},{12,... | collective-permute-start | bytes 442376 | tf_op jit(solution)/shard_map/ppermute | solution.py:47
  236.7 8.6 %collective-permute-start.7 = (f32[72,512]{1,0:T(8,128)S(1)}, f32[72,512]{1,0:T(8,128)S(1)}, u32[]{:S(2)}, u32[]{:S(2)}) collective-permute-start(f32[72,512]{1,0:T(8,128)S(1)} %add.186), channel_id=1, source_target_pairs={{0,4},{2,6},{4,0},{6,2},{1,5},{3,7},{5,1},{7,3},{8,12},{10,14},{12... | collective-permute-start | bytes 442376 | tf_op jit(solution)/shard_map/ppermute | solution.py:47
  245.3 5.9 %collective-permute-start.8 = (f32[72,512]{1,0:T(8,128)S(1)}, f32[72,512]{1,0:T(8,128)S(1)}, u32[]{:S(2)}, u32[]{:S(2)}) collective-permute-start(f32[72,512]{1,0:T(8,128)S(1)} %add.187), channel_id=1, source_target_pairs={{0,32},{32,0},{64,96},{96,64},{128,160},{160,128},{192,224},{224,1... | collective-permute-start | bytes 442376 | tf_op jit(solution)/shard_map/ppermute | solution.py:47
  251.2 8.1 %collective-permute-start.9 = (f32[72,512]{1,0:T(8,128)S(1)}, f32[72,512]{1,0:T(8,128)S(1)}, u32[]{:S(2)}, u32[]{:S(2)}) collective-permute-start(f32[72,512]{1,0:T(8,128)S(1)} %add.188), channel_id=1, source_target_pairs={{0,64},{32,96},{64,0},{96,32},{128,192},{160,224},{192,128},{224,1... | collective-permute-start | bytes 442376 | tf_op jit(solution)/shard_map/ppermute | solution.py:47
  259.4 11.3 %collective-permute-start.10 = (f32[72,512]{1,0:T(8,128)S(1)}, f32[72,512]{1,0:T(8,128)S(1)}, u32[]{:S(2)}, u32[]{:S(2)}) collective-permute-start(f32[72,512]{1,0:T(8,128)S(1)} %add.189), channel_id=1, source_target_pairs={{0,128},{32,160},{64,192},{96,224},{128,0},{160,32},{192,64},{224,... | collective-permute-start | bytes 442376 | tf_op jit(solution)/shard_map/ppermute | solution.py:47
  270.7 11.4 %collective-permute-start.11 = (f32[72,512]{1,0:T(8,128)S(1)}, f32[72,512]{1,0:T(8,128)S(1)}, u32[]{:S(2)}, u32[]{:S(2)}) collective-permute-start(f32[72,512]{1,0:T(8,128)S(1)} %add.190), channel_id=1, source_target_pairs={{0,256},{256,0},{1,257},{257,1},{2,258},{258,2},{3,259},{259,3},{4... | collective-permute-start | bytes 442376 | tf_op jit(solution)/shard_map/ppermute | solution.py:47
  282.1 5.9 %collective-permute-start.12 = (f32[72,512]{1,0:T(8,128)S(1)}, f32[72,512]{1,0:T(8,128)S(1)}, u32[]{:S(2)}, u32[]{:S(2)}) collective-permute-start(f32[72,512]{1,0:T(8,128)S(1)} %add.191), channel_id=1, source_target_pairs={{0,8},{8,0},{16,24},{24,16},{1,9},{9,1},{17,25},{25,17},{2,10},{10... | collective-permute-start | bytes 442376 | tf_op jit(solution)/shard_map/ppermute | solution.py:35
  288.0 10.6 %collective-permute-start.13 = (f32[144,512]{1,0:T(8,128)S(1)}, f32[144,512]{1,0:T(8,128)S(1)}, u32[]{:S(2)}, u32[]{:S(2)}) collective-permute-start(f32[144,512]{1,0:T(8,128)S(1)} %pad_maximum_fusion.2), channel_id=1, source_target_pairs={{0,16},{8,24},{16,0},{24,8},{1,17},{9,25},{17,1},{25,9},{2,18},{10... | collective-permute-start | bytes 884744 | tf_op jit(solution)/shard_map/ppermute | solution.py:35
  298.7 13.6 %collective-permute-start.14 = (f32[288,512]{1,0:T(8,128)S(1)}, f32[288,512]{1,0:T(8,128)S(1)}, u32[]{:S(2)}, u32[]{:S(2)}) collective-permute-start(f32[288,512]{1,0:T(8,128)S(1)} %pad_maximum_fusion.1), channel_id=1, source_target_pairs={{0,1},{1,0},{2,3},{3,2},{4,5},{5,4},{6,7},{7,6},{8,9},{9,8},{10,11... | collective-permute-start | bytes 1769480 | tf_op jit(solution)/shard_map/ppermute | solution.py:35
Sparse Core Ops, SparseCore 0:
  19.8 109.2 all-gather.1

commit v3 on v2

--- a/solution.py
+++ b/solution.py
@@ -3,6 +3,8 @@
 import jax
 import jax.numpy as jnp
 from jax import lax
+from jax.experimental import pallas as pl
+from jax.experimental.pallas import tpu as pltpu
 from jax.sharding import Mesh
 from jax.sharding import PartitionSpec as P
 
@@ -49,6 +51,43 @@
     return piece
 
 
+def _aggregate_kernel(cols_ref, counts_ref, tiles_ref, panels_ref, out_ref):
+    groups, slots = tiles_ref.shape[0], tiles_ref.shape[1]
+    for g in range(groups):
+        out_ref[g] = jnp.zeros(out_ref.shape[1:], jnp.float32)
+
+        def body(k, carry, g=g):
+            col = cols_ref[g * slots + k]
+            out_ref[g] += jnp.dot(tiles_ref[g, k], panels_ref[col], preferred_element_type=jnp.float32)
+            return carry
+
+        lax.fori_loop(0, counts_ref[g], body, 0)
+
+
+def _aggregate(cols, counts, tiles, panels):
+    groups, slots, tile_size, _ = tiles.shape
+    feat_width = panels.shape[-1]
+    flops = 2 * groups * slots * tile_size * tile_size * feat_width
+    moved = tiles.size * 2 + panels.size * 2 + groups * tile_size * feat_width * 4
+    return pl.pallas_call(
+        _aggregate_kernel,
+        out_shape=jax.ShapeDtypeStruct((groups, tile_size, feat_width), jnp.float32),
+        in_specs=[
+            pl.BlockSpec(memory_space=pltpu.SMEM),
+            pl.BlockSpec(memory_space=pltpu.SMEM),
+            pl.BlockSpec(memory_space=pltpu.VMEM),
+            pl.BlockSpec(memory_space=pltpu.VMEM),
+        ],
+        out_specs=pl.BlockSpec(memory_space=pltpu.VMEM),
+        cost_estimate=pl.CostEstimate(flops=flops, bytes_accessed=moved, transcendentals=0),
+    )(
+        jnp.clip(cols, 0, panels.shape[0] - 1).reshape(-1),
+        jnp.clip(counts, 0, slots),
+        tiles,
+        panels,
+    )
+
+
 def shards(features, col_panels, block_counts, block_values, weight, bias, cotangent):
     sizes = {name: lax.axis_size(name) for name in ALL_AXES}
     rep_count = sizes["y_lo"] * sizes["core"]
@@ -56,34 +95,17 @@
     feat_width = features.shape[1]
     own_panels = features.shape[0] // tile_size
     row_panels = col_panels.shape[0]
-    slot_count = col_panels.shape[2]
     global_cols = col_panels[:, 0, :]
     section_of = global_cols // (own_panels * rep_count)
     low = sizes["z"] * sizes["x"]
     gathered_pos = (section_of % low) * sizes["y_hi"] + section_of // low
     local_cols = gathered_pos * own_panels + global_cols % own_panels
     live_counts = block_counts[:, 0]
-    slot_mask = jnp.arange(slot_count, dtype=jnp.int32)[None, :] < live_counts[:, None]
     tiles = block_values[:, 0]
-    empty = jnp.zeros((row_panels, tile_size, feat_width), jnp.float32)
     gathered = lax.all_gather(features, "y_hi", axis=0, tiled=True)
     gathered = lax.all_gather(gathered, ("z", "x"), axis=0, tiled=True)
     all_panels = gathered.reshape(-1, tile_size, feat_width)
-    slot_step = 4
-    turn_count = (jnp.max(live_counts) + slot_step - 1) // slot_step
-
-    def one_turn(turn, running):
-        begin_slot = turn * slot_step
-        step_cols = lax.dynamic_slice_in_dim(local_cols, begin_slot, slot_step, 1)
-        step_mask = lax.dynamic_slice_in_dim(slot_mask, begin_slot, slot_step, 1)
-        step_tiles = lax.dynamic_slice_in_dim(tiles, begin_slot, slot_step, 1)
-        step_tiles = jnp.where(step_mask[:, :, None, None], step_tiles, jnp.zeros((), jnp.bfloat16))
-        picked = all_panels[step_cols]
-        return running + jnp.einsum(
-            "gkab,gkbf->gaf", step_tiles, picked, preferred_element_type=jnp.float32
-        )
-
-    gathered_sum = lax.fori_loop(0, turn_count, one_turn, empty)
+    gathered_sum = _aggregate(local_cols, live_counts, tiles, all_panels)
     cores = sizes["core"]
     by_core = gathered_sum.reshape(row_panels // cores, cores, tile_size, feat_width)
     by_core = jnp.moveaxis(by_core, 1, 0)

time: 322 us -> 306 us (0.950)
  local copies, waits for them, and re-layouts: 21.5 us -> 4.3 us
  Pallas kernels: 0 us -> 11.7 us
  matrix products: 12.2 us -> 1.31 us
  starting transfers between devices: 56.4 us -> 60 us
    gather x3 -> x0, local copies, waits for them, and re-layouts: 18.5 us -> none  [one_turn(): picked = all_panels[step_cols]]
    pallas_call x0 -> x1, Pallas kernels: none -> 11.7 us  [_aggregate(): pl.pallas_call(_aggregate_kernel, out_shape=jax.ShapeDtypeStruct((groups,...]
    dot_general x3 -> x0, matrix products: 10.9 us -> none  [one_turn(): jnp.einsum('gkab,gkbf->gaf', step_tiles, picked, preferred_element_type=j...]
    ppermute x3, starting transfers between devices: 16 us -> 20.5 us  [_doubling_gather(): other = lax.ppermute(piece, axis, _xor_perm(n, bit))]
    ppermute x3, waiting for transfers between devices: 14 us -> 10.3 us  [_doubling_gather(): other = lax.ppermute(piece, axis, _xor_perm(n, bit))]
where the time goes in v3:
time: 306 us
  waiting for transfers between devices  194 us (63%)
  starting transfers between devices  60 us (20%)
  between operations  14.5 us (5%)
  blocking collectives  12.4 us (4%)
  Pallas kernels  11.7 us (4%)
  other arithmetic  7.84 us (3%)
  local copies, waits for them, and re-layouts  4.3 us (1%)
    all_gather x1, waiting for transfers between devices, shards(): gathered = lax.all_gather(gathered, ('z', 'x'), axis=0, tiled=True)  106 us
    ppermute x6, waiting for transfers between devices, _halving_scatter(): blocks = keep + lax.ppermute(send, axis, _xor_perm(n, bit))  47.1 us
    ppermute x6, waiting for transfers between devices, _doubling_sum(): piece = piece + lax.ppermute(piece, axis, _xor_perm(n, bit))  30.5 us
    ppermute x3, starting transfers between devices, _doubling_gather(): other = lax.ppermute(piece, axis, _xor_perm(n, bit))  20.5 us
    ppermute x6, starting transfers between devices, _doubling_sum(): piece = piece + lax.ppermute(piece, axis, _xor_perm(n, bit))  20.4 us
    ppermute x6, starting transfers between devices, _halving_scatter(): blocks = keep + lax.ppermute(send, axis, _xor_perm(n, bit))  19.1 us
    all_gather x1, blocking collectives, shards(): gathered = lax.all_gather(features, 'y_hi', axis=0, tiled=True)  12.4 us
    pallas_call x1, Pallas kernels, _aggregate(): pl.pallas_call(_aggregate_kernel, out_shape=jax.ShapeDtypeStruct((groups,...  11.7 us
  transfers between devices with their start and end apart: 16, of which 16 were waited for; matrix products, arithmetic and copies ran while one was open for 1% of the time, Pallas kernels for 0%

profile of v3, /device:TPU:1, one launch (start us, length us, event | category | flops | bytes accessed | tf_op | source)
XLA Modules:
  0.0 305.7 jit_solution(10619134777912737056)
XLA Ops:
  7.2 12.4 %all_gather.6 = bf16[256,512]{1,0:T(8,128)(2,1)} all-gather(bf16[128,512]{1,0:T(8,128)(2,1)} %param.11), channel_id=1, replica_groups=mesh['y_hi'=2,'z'=8,'x'=4,'y_lo'=4,'core'=2] {'y_hi'}, dimensions={0}, use_global_device_ids=true | all-gather | bytes 393216 | tf_op jit(solution)/shard_map/all_gather | solution.py:105
  23.3 105.7 %all-gather.2.cloned.1.call-done = bf16[8192,512]{1,0:T(8,128)(2,1)} async-done(((bf16[256,512]{1,0:T(8,128)(2,1)}), bf16[8192,512]{1,0:T(8,128)(2,1)}) %all-gather.2.cloned.1.call-update) | async-done | bytes 8388624 | tf_op jit(solution)/shard_map/all_gather | solution.py:106
  129.1 11.7 %shard_map.94 = f32[8,128,512]{2,1,0:T(8,128)} custom-call(s32[96]{0:T(128)} %fusion.4.cols_ref, s32[8]{0:T(128)} %clamp_bitcast_fusion.counts_ref, bf16[8,12,128,128]{3,2,1,0:T(8,128)(2,1)} %bitcast.41, bf16[64,128,512]{2,1,0:T(8,128)(2,1)} %bitcast.34), custom_call_target="tpu_custom_call" | custom-call | flops 1610612736 | bytes 13631488 | tf_op jit(solution)/shard_map/pallas_call | solution.py:72
  140.8 2.4 dynamic-slice_bitcast_fusion
  143.2 3.3 %collective-permute-start = (f32[1,4,128,512]{3,2,1,0:T(8,128)}, f32[1,4,128,512]{3,2,1,0:T(8,128)}, u32[]{:S(2)}, u32[]{:S(2)}) collective-permute-start(f32[1,4,128,512]{3,2,1,0:T(8,128)} %dynamic-slice_bitcast_fusion), channel_id=1, source_target_pairs={{0,1},{1,0},{2,3},{3,2},{4,5},{5,4},{6,7},{7,6},{8,9},{9,8},{10,11... | collective-permute-start | bytes 3145736 | tf_op jit(solution)/shard_map/ppermute | solution.py:28
  146.5 2.6 collective-permute-done
  151.6 4.7 %collective-permute-start.1 = (f32[2,1,128,512]{3,2,0,1:T(8,128)S(1)}, f32[2,1,128,512]{3,2,0,1:T(8,128)S(1)}, u32[]{:S(2)}, u32[]{:S(2)}) collective-permute-start(f32[2,1,128,512]{3,2,0,1:T(8,128)S(1)} %dynamic-slice_bitcast_fusion.2), channel_id=1, source_target_pairs={{0,4},{2,6},{4,0},{6,2},{1,5},{3,7},{5,1},{7,3},{8,12},{10,14},{12... | collective-permute-start | bytes 1572872 | tf_op jit(solution)/shard_map/ppermute | solution.py:28
  156.3 23.2 %collective-permute-done.1 = f32[2,1,128,512]{3,2,0,1:T(8,128)S(1)} collective-permute-done((f32[2,1,128,512]{3,2,0,1:T(8,128)S(1)}, f32[2,1,128,512]{3,2,0,1:T(8,128)S(1)}, u32[]{:S(2)}, u32[]{:S(2)}) %collective-permute-start.1) | collective-permute-done | bytes 524320 | tf_op jit(solution)/shard_map/ppermute | solution.py:28
  180.7 1.9 collective-permute-start.2
  182.6 7.4 %collective-permute-done.2 = f32[1,1,128,512]{3,2,0,1:T(8,128)S(1)} collective-permute-done((f32[1,1,128,512]{3,2,0,1:T(8,128)S(1)}, f32[1,1,128,512]{3,2,0,1:T(8,128)S(1)}, u32[]{:S(2)}, u32[]{:S(2)}) %collective-permute-start.2) | collective-permute-done | bytes 262176 | tf_op jit(solution)/shard_map/ppermute | solution.py:28
  191.6 3.2 %collective-permute-start.3 = (f32[1,288,512]{2,1,0:T(8,128)S(1)}, f32[1,288,512]{2,1,0:T(8,128)S(1)}, u32[]{:S(2)}, u32[]{:S(2)}) collective-permute-start(f32[1,288,512]{2,1,0:T(8,128)S(1)} %dynamic-slice_bitcast_fusion.1), channel_id=1, source_target_pairs={{0,1},{1,0},{2,3},{3,2},{4,5},{5,4},{6,7},{7,6},{8,9},{9,8},{10,11... | collective-permute-start | bytes 1769480 | tf_op jit(solution)/shard_map/ppermute | solution.py:28
  196.6 2.1 collective-permute-start.4
  198.7 9.4 %collective-permute-done.4 = f32[2,72,512]{2,1,0:T(8,128)S(1)} collective-permute-done((f32[2,72,512]{2,1,0:T(8,128)S(1)}, f32[2,72,512]{2,1,0:T(8,128)S(1)}, u32[]{:S(2)}, u32[]{:S(2)}) %collective-permute-start.4) | collective-permute-done | bytes 294944 | tf_op jit(solution)/shard_map/ppermute | solution.py:28
  208.2 3.7 %collective-permute-start.5 = (f32[1,72,512]{2,1,0:T(8,128)S(1)}, f32[1,72,512]{2,1,0:T(8,128)S(1)}, u32[]{:S(2)}, u32[]{:S(2)}) collective-permute-start(f32[1,72,512]{2,1,0:T(8,128)S(1)} %constant_dynamic-slice_fusion), channel_id=1, source_target_pairs={{0,8},{8,0},{16,24},{24,16},{1,9},{9,1},{17,25},{25,17},{2,10},{10... | collective-permute-start | bytes 442376 | tf_op jit(solution)/shard_map/ppermute | solution.py:28
  212.0 3.0 collective-permute-done.5
  215.0 1.9 collective-permute-start.6
  216.9 4.0 %collective-permute-done.6 = f32[72,512]{1,0:T(8,128)S(1)} collective-permute-done((f32[72,512]{1,0:T(8,128)S(1)}, f32[72,512]{1,0:T(8,128)S(1)}, u32[]{:S(2)}, u32[]{:S(2)}) %collective-permute-start.6) | collective-permute-done | bytes 147488 | tf_op jit(solution)/shard_map/ppermute | solution.py:49
  220.9 2.3 collective-permute-start.7
  223.2 5.8 %collective-permute-done.7 = f32[72,512]{1,0:T(8,128)S(1)} collective-permute-done((f32[72,512]{1,0:T(8,128)S(1)}, f32[72,512]{1,0:T(8,128)S(1)}, u32[]{:S(2)}, u32[]{:S(2)}) %collective-permute-start.7) | collective-permute-done | bytes 147488 | tf_op jit(solution)/shard_map/ppermute | solution.py:49
  229.0 4.9 %collective-permute-start.8 = (f32[72,512]{1,0:T(8,128)S(1)}, f32[72,512]{1,0:T(8,128)S(1)}, u32[]{:S(2)}, u32[]{:S(2)}) collective-permute-start(f32[72,512]{1,0:T(8,128)S(1)} %add.174), channel_id=1, source_target_pairs={{0,32},{32,0},{64,96},{96,64},{128,160},{160,128},{192,224},{224,1... | collective-permute-start | bytes 442376 | tf_op jit(solution)/shard_map/ppermute | solution.py:49
  233.9 2.5 collective-permute-done.8
  236.4 3.0 collective-permute-start.9
  239.5 5.3 %collective-permute-done.9 = f32[72,512]{1,0:T(8,128)S(1)} collective-permute-done((f32[72,512]{1,0:T(8,128)S(1)}, f32[72,512]{1,0:T(8,128)S(1)}, u32[]{:S(2)}, u32[]{:S(2)}) %collective-permute-start.9) | collective-permute-done | bytes 147488 | tf_op jit(solution)/shard_map/ppermute | solution.py:49
  244.8 4.8 %collective-permute-start.10 = (f32[72,512]{1,0:T(8,128)S(1)}, f32[72,512]{1,0:T(8,128)S(1)}, u32[]{:S(2)}, u32[]{:S(2)}) collective-permute-start(f32[72,512]{1,0:T(8,128)S(1)} %add.176), channel_id=1, source_target_pairs={{0,128},{32,160},{64,192},{96,224},{128,0},{160,32},{192,64},{224,... | collective-permute-start | bytes 442376 | tf_op jit(solution)/shard_map/ppermute | solution.py:49
  249.6 6.6 %collective-permute-done.10 = f32[72,512]{1,0:T(8,128)S(1)} collective-permute-done((f32[72,512]{1,0:T(8,128)S(1)}, f32[72,512]{1,0:T(8,128)S(1)}, u32[]{:S(2)}, u32[]{:S(2)}) %collective-permute-start.10) | collective-permute-done | bytes 147488 | tf_op jit(solution)/shard_map/ppermute | solution.py:49
  256.2 3.4 %collective-permute-start.11 = (f32[72,512]{1,0:T(8,128)S(1)}, f32[72,512]{1,0:T(8,128)S(1)}, u32[]{:S(2)}, u32[]{:S(2)}) collective-permute-start(f32[72,512]{1,0:T(8,128)S(1)} %add.177), channel_id=1, source_target_pairs={{0,256},{256,0},{1,257},{257,1},{2,258},{258,2},{3,259},{259,3},{4... | collective-permute-start | bytes 442376 | tf_op jit(solution)/shard_map/ppermute | solution.py:49
  259.6 6.4 %collective-permute-done.11 = f32[72,512]{1,0:T(8,128)S(1)} collective-permute-done((f32[72,512]{1,0:T(8,128)S(1)}, f32[72,512]{1,0:T(8,128)S(1)}, u32[]{:S(2)}, u32[]{:S(2)}) %collective-permute-start.11) | collective-permute-done | bytes 147488 | tf_op jit(solution)/shard_map/ppermute | solution.py:49
  266.0 2.9 collective-permute-start.12
  268.9 3.0 collective-permute-done.12
  271.9 5.6 %collective-permute-start.13 = (f32[144,512]{1,0:T(8,128)S(1)}, f32[144,512]{1,0:T(8,128)S(1)}, u32[]{:S(2)}, u32[]{:S(2)}) collective-permute-start(f32[144,512]{1,0:T(8,128)S(1)} %pad_maximum_fusion.2), channel_id=1, source_target_pairs={{0,16},{8,24},{16,0},{24,8},{1,17},{9,25},{17,1},{25,9},{2,18},{10... | collective-permute-start | bytes 884744 | tf_op jit(solution)/shard_map/ppermute | solution.py:37
  277.6 5.7 %collective-permute-done.13 = f32[144,512]{1,0:T(8,128)S(1)} collective-permute-done((f32[144,512]{1,0:T(8,128)S(1)}, f32[144,512]{1,0:T(8,128)S(1)}, u32[]{:S(2)}, u32[]{:S(2)}) %collective-permute-start.13) | collective-permute-done | bytes 294944 | tf_op jit(solution)/shard_map/ppermute | solution.py:37
  283.4 12.1 %collective-permute-start.14 = (f32[288,512]{1,0:T(8,128)S(1)}, f32[288,512]{1,0:T(8,128)S(1)}, u32[]{:S(2)}, u32[]{:S(2)}) collective-permute-start(f32[288,512]{1,0:T(8,128)S(1)} %pad_maximum_fusion.1), channel_id=1, source_target_pairs={{0,1},{1,0},{2,3},{3,2},{4,5},{5,4},{6,7},{7,6},{8,9},{9,8},{10,11... | collective-permute-start | bytes 1769480 | tf_op jit(solution)/shard_map/ppermute | solution.py:37
  (47 shorter events, 14.3 us)
Async XLA Ops:
  7.2 182.9 %copy-start = (bf16[512,512]{1,0:T(8,128)(2,1)S(1)}, bf16[512,512]{1,0:T(8,128)(2,1)}, u32[]{:S(2)}) copy-start(bf16[512,512]{1,0:T(8,128)(2,1)} %param.15) | copy-start | bytes 1572868
  7.2 121.9 %all-gather.2.cloned.1.call-start = ((), (), s32[]{:S(2)}) async-start(), calls=%async_computation | async-start | bytes 8650752 | tf_op jit(solution)/shard_map/all_gather | solution.py:106
  140.8 8.3 %copy-start.1 = (f32[8,128,512]{2,1,0:T(8,128)S(1)}, f32[8,128,512]{2,1,0:T(8,128)}, u32[]{:S(2)}) copy-start(f32[8,128,512]{2,1,0:T(8,128)} %shard_map.94) | copy-start | bytes 6291460
  143.2 5.9 %collective-permute-start = (f32[1,4,128,512]{3,2,1,0:T(8,128)}, f32[1,4,128,512]{3,2,1,0:T(8,128)}, u32[]{:S(2)}, u32[]{:S(2)}) collective-permute-start(f32[1,4,128,512]{3,2,1,0:T(8,128)} %dynamic-slice_bitcast_fusion), channel_id=1, source_target_pairs={{0,1},{1,0},{2,3},{3,2},{4,5},{5,4},{6,7},{7,6},{8,9},{9,8},{10,11... | collective-permute-start | bytes 3145736 | tf_op jit(solution)/shard_map/ppermute | solution.py:28
  150.5 1.0 copy-start.2
  150.6 39.5 %copy-start.3 = (bf16[128,512]{1,0:T(8,128)(2,1)S(1)}, bf16[128,512]{1,0:T(8,128)(2,1)}, u32[]{:S(2)}) copy-start(bf16[128,512]{1,0:T(8,128)(2,1)} %param.17) | copy-start | bytes 393220
  150.6 39.5 %copy-start.4 = (f32[512]{0:T(512)S(1)}, f32[512]{0:T(512)}, u32[]{:S(2)}) copy-start(f32[512]{0:T(512)} %param.16) | copy-start | bytes 6148
  151.6 28.0 %collective-permute-start.1 = (f32[2,1,128,512]{3,2,0,1:T(8,128)S(1)}, f32[2,1,128,512]{3,2,0,1:T(8,128)S(1)}, u32[]{:S(2)}, u32[]{:S(2)}) collective-permute-start(f32[2,1,128,512]{3,2,0,1:T(8,128)S(1)} %dynamic-slice_bitcast_fusion.2), channel_id=1, source_target_pairs={{0,4},{2,6},{4,0},{6,2},{1,5},{3,7},{5,1},{7,3},{8,12},{10,14},{12... | collective-permute-start | bytes 1572872 | tf_op jit(solution)/shard_map/ppermute | solution.py:28
  180.7 9.3 %collective-permute-start.2 = (f32[1,1,128,512]{3,2,0,1:T(8,128)S(1)}, f32[1,1,128,512]{3,2,0,1:T(8,128)S(1)}, u32[]{:S(2)}, u32[]{:S(2)}) collective-permute-start(f32[1,1,128,512]{3,2,0,1:T(8,128)S(1)} %constant_dynamic-slice_fusion.1), channel_id=1, source_target_pairs={{0,2},{2,0},{4,6},{6,4},{1,3},{3,1},{5,7},{7,5},{8,10},{10,8},{12,... | collective-permute-start | bytes 786440 | tf_op jit(solution)/shard_map/ppermute | solution.py:28
  191.6 4.8 %collective-permute-start.3 = (f32[1,288,512]{2,1,0:T(8,128)S(1)}, f32[1,288,512]{2,1,0:T(8,128)S(1)}, u32[]{:S(2)}, u32[]{:S(2)}) collective-permute-start(f32[1,288,512]{2,1,0:T(8,128)S(1)} %dynamic-slice_bitcast_fusion.1), channel_id=1, source_target_pairs={{0,1},{1,0},{2,3},{3,2},{4,5},{5,4},{6,7},{7,6},{8,9},{9,8},{10,11... | collective-permute-start | bytes 1769480 | tf_op jit(solution)/shard_map/ppermute | solution.py:28
  196.6 11.6 %collective-permute-start.4 = (f32[2,72,512]{2,1,0:T(8,128)S(1)}, f32[2,72,512]{2,1,0:T(8,128)S(1)}, u32[]{:S(2)}, u32[]{:S(2)}) collective-permute-start(f32[2,72,512]{2,1,0:T(8,128)S(1)} %dynamic-slice_bitcast_fusion.3), channel_id=1, source_target_pairs={{0,16},{8,24},{16,0},{24,8},{1,17},{9,25},{17,1},{25,9},{2,18},{10... | collective-permute-start | bytes 884744 | tf_op jit(solution)/shard_map/ppermute | solution.py:28
  208.2 6.7 %collective-permute-start.5 = (f32[1,72,512]{2,1,0:T(8,128)S(1)}, f32[1,72,512]{2,1,0:T(8,128)S(1)}, u32[]{:S(2)}, u32[]{:S(2)}) collective-permute-start(f32[1,72,512]{2,1,0:T(8,128)S(1)} %constant_dynamic-slice_fusion), channel_id=1, source_target_pairs={{0,8},{8,0},{16,24},{24,16},{1,9},{9,1},{17,25},{25,17},{2,10},{10... | collective-permute-start | bytes 442376 | tf_op jit(solution)/shard_map/ppermute | solution.py:28
  215.0 5.9 %collective-permute-start.6 = (f32[72,512]{1,0:T(8,128)S(1)}, f32[72,512]{1,0:T(8,128)S(1)}, u32[]{:S(2)}, u32[]{:S(2)}) collective-permute-start(f32[72,512]{1,0:T(8,128)S(1)} %add_bitcast_fusion), channel_id=1, source_target_pairs={{0,2},{2,0},{4,6},{6,4},{1,3},{3,1},{5,7},{7,5},{8,10},{10,8},{12,... | collective-permute-start | bytes 442376 | tf_op jit(solution)/shard_map/ppermute | solution.py:49
  220.9 8.1 %collective-permute-start.7 = (f32[72,512]{1,0:T(8,128)S(1)}, f32[72,512]{1,0:T(8,128)S(1)}, u32[]{:S(2)}, u32[]{:S(2)}) collective-permute-start(f32[72,512]{1,0:T(8,128)S(1)} %add.173), channel_id=1, source_target_pairs={{0,4},{2,6},{4,0},{6,2},{1,5},{3,7},{5,1},{7,3},{8,12},{10,14},{12... | collective-permute-start | bytes 442376 | tf_op jit(solution)/shard_map/ppermute | solution.py:49
  229.0 7.4 %collective-permute-start.8 = (f32[72,512]{1,0:T(8,128)S(1)}, f32[72,512]{1,0:T(8,128)S(1)}, u32[]{:S(2)}, u32[]{:S(2)}) collective-permute-start(f32[72,512]{1,0:T(8,128)S(1)} %add.174), channel_id=1, source_target_pairs={{0,32},{32,0},{64,96},{96,64},{128,160},{160,128},{192,224},{224,1... | collective-permute-start | bytes 442376 | tf_op jit(solution)/shard_map/ppermute | solution.py:49
  236.4 8.4 %collective-permute-start.9 = (f32[72,512]{1,0:T(8,128)S(1)}, f32[72,512]{1,0:T(8,128)S(1)}, u32[]{:S(2)}, u32[]{:S(2)}) collective-permute-start(f32[72,512]{1,0:T(8,128)S(1)} %add.175), channel_id=1, source_target_pairs={{0,64},{32,96},{64,0},{96,32},{128,192},{160,224},{192,128},{224,1... | collective-permute-start | bytes 442376 | tf_op jit(solution)/shard_map/ppermute | solution.py:49
  244.8 11.3 %collective-permute-start.10 = (f32[72,512]{1,0:T(8,128)S(1)}, f32[72,512]{1,0:T(8,128)S(1)}, u32[]{:S(2)}, u32[]{:S(2)}) collective-permute-start(f32[72,512]{1,0:T(8,128)S(1)} %add.176), channel_id=1, source_target_pairs={{0,128},{32,160},{64,192},{96,224},{128,0},{160,32},{192,64},{224,... | collective-permute-start | bytes 442376 | tf_op jit(solution)/shard_map/ppermute | solution.py:49
  256.2 9.8 %collective-permute-start.11 = (f32[72,512]{1,0:T(8,128)S(1)}, f32[72,512]{1,0:T(8,128)S(1)}, u32[]{:S(2)}, u32[]{:S(2)}) collective-permute-start(f32[72,512]{1,0:T(8,128)S(1)} %add.177), channel_id=1, source_target_pairs={{0,256},{256,0},{1,257},{257,1},{2,258},{258,2},{3,259},{259,3},{4... | collective-permute-start | bytes 442376 | tf_op jit(solution)/shard_map/ppermute | solution.py:49
  266.0 5.9 %collective-permute-start.12 = (f32[72,512]{1,0:T(8,128)S(1)}, f32[72,512]{1,0:T(8,128)S(1)}, u32[]{:S(2)}, u32[]{:S(2)}) collective-permute-start(f32[72,512]{1,0:T(8,128)S(1)} %add.178), channel_id=1, source_target_pairs={{0,8},{8,0},{16,24},{24,16},{1,9},{9,1},{17,25},{25,17},{2,10},{10... | collective-permute-start | bytes 442376 | tf_op jit(solution)/shard_map/ppermute | solution.py:37
  271.9 11.3 %collective-permute-start.13 = (f32[144,512]{1,0:T(8,128)S(1)}, f32[144,512]{1,0:T(8,128)S(1)}, u32[]{:S(2)}, u32[]{:S(2)}) collective-permute-start(f32[144,512]{1,0:T(8,128)S(1)} %pad_maximum_fusion.2), channel_id=1, source_target_pairs={{0,16},{8,24},{16,0},{24,8},{1,17},{9,25},{17,1},{25,9},{2,18},{10... | collective-permute-start | bytes 884744 | tf_op jit(solution)/shard_map/ppermute | solution.py:37
  283.4 13.7 %collective-permute-start.14 = (f32[288,512]{1,0:T(8,128)S(1)}, f32[288,512]{1,0:T(8,128)S(1)}, u32[]{:S(2)}, u32[]{:S(2)}) collective-permute-start(f32[288,512]{1,0:T(8,128)S(1)} %pad_maximum_fusion.1), channel_id=1, source_target_pairs={{0,1},{1,0},{2,3},{3,2},{4,5},{5,4},{6,7},{7,6},{8,9},{9,8},{10,11... | collective-permute-start | bytes 1769480 | tf_op jit(solution)/shard_map/ppermute | solution.py:37
Sparse Core Ops, SparseCore 0:
  19.8 109.2 all-gather.1

commit v4 on v3

--- a/solution.py
+++ b/solution.py
@@ -51,41 +51,55 @@
     return piece
 
 
-def _aggregate_kernel(cols_ref, counts_ref, tiles_ref, panels_ref, out_ref):
-    groups, slots = tiles_ref.shape[0], tiles_ref.shape[1]
+def _aggregate_kernel(cols_ref, tiles_ref, panels_hbm, out_ref, buf, sems):
+    groups, slots = out_ref.shape[0], buf.shape[1]
+
+    def copies(g, slot):
+        return [
+            pltpu.make_async_copy(panels_hbm.at[cols_ref[g * slots + k]], buf.at[slot, k], sems.at[slot, k])
+            for k in range(slots)
+        ]
+
+    pending = copies(0, 0)
+    for c in pending:
+        c.start()
     for g in range(groups):
-        out_ref[g] = jnp.zeros(out_ref.shape[1:], jnp.float32)
-
-        def body(k, carry, g=g):
-            col = cols_ref[g * slots + k]
-            out_ref[g] += jnp.dot(tiles_ref[g, k], panels_ref[col], preferred_element_type=jnp.float32)
-            return carry
-
-        lax.fori_loop(0, counts_ref[g], body, 0)
+        slot = g % 2
+        if g + 1 < groups:
+            ahead = copies(g + 1, 1 - slot)
+            for c in ahead:
+                c.start()
+        for c in pending:
+            c.wait()
+        rhs = buf[slot].reshape(slots * buf.shape[2], buf.shape[3])
+        out_ref[g] = jnp.dot(tiles_ref[g], rhs, preferred_element_type=jnp.float32)
+        if g + 1 < groups:
+            pending = ahead
 
 
 def _aggregate(cols, counts, tiles, panels):
     groups, slots, tile_size, _ = tiles.shape
     feat_width = panels.shape[-1]
+    live = jnp.arange(slots, dtype=jnp.int32)[None, :] < counts[:, None]
+    wide = jnp.where(live[:, :, None, None], tiles, jnp.zeros((), tiles.dtype))
+    wide = wide.transpose(0, 2, 1, 3).reshape(groups, tile_size, slots * tile_size)
     flops = 2 * groups * slots * tile_size * tile_size * feat_width
-    moved = tiles.size * 2 + panels.size * 2 + groups * tile_size * feat_width * 4
+    moved = tiles.size * 2 + groups * slots * tile_size * feat_width * 2 + groups * tile_size * feat_width * 4
     return pl.pallas_call(
         _aggregate_kernel,
         out_shape=jax.ShapeDtypeStruct((groups, tile_size, feat_width), jnp.float32),
         in_specs=[
             pl.BlockSpec(memory_space=pltpu.SMEM),
-            pl.BlockSpec(memory_space=pltpu.SMEM),
             pl.BlockSpec(memory_space=pltpu.VMEM),
-            pl.BlockSpec(memory_space=pltpu.VMEM),
+            pl.BlockSpec(memory_space=pl.ANY),
         ],
         out_specs=pl.BlockSpec(memory_space=pltpu.VMEM),
+        scratch_shapes=[
+            pltpu.VMEM((2, slots, tile_size, feat_width), panels.dtype),
+            pltpu.SemaphoreType.DMA((2, slots)),
+        ],
         cost_estimate=pl.CostEstimate(flops=flops, bytes_accessed=moved, transcendentals=0),
-    )(
-        jnp.clip(cols, 0, panels.shape[0] - 1).reshape(-1),
-        jnp.clip(counts, 0, slots),
-        tiles,
-        panels,
-    )
+    )(jnp.clip(cols, 0, panels.shape[0] - 1).reshape(-1), wide, panels)
 
 
 def shards(features, col_panels, block_counts, block_values, weight, bias, cotangent):

time: 306 us -> 299 us (0.977)
  waiting for transfers between devices: 194 us -> 174 us
  local copies, waits for them, and re-layouts: 4.3 us -> 11.7 us
  starting transfers between devices: 60 us -> 63.6 us
    all_gather x1, waiting for transfers between devices: 106 us -> 93.5 us  [shards(): gathered = lax.all_gather(gathered, ('z', 'x'), axis=0, tiled=True)]
    ppermute x6, waiting for transfers between devices: 30.5 us -> 24.7 us  [_doubling_sum(): piece = piece + lax.ppermute(piece, axis, _xor_perm(n, bit))]
    reshape x0 -> x1, local copies, waits for them, and re-layouts: none -> 4.73 us  [_aggregate(): wide.transpose(0, 2, 1, 3).reshape(groups, tile_size, slots * tile_size)]
    select_n x0 -> x1, other arithmetic: none -> 3.92 us  [_aggregate(): wide = jnp.where(live[:, :, None, None], tiles, jnp.zeros((), tiles.dtype))]
    unnamed x11 -> x10, local copies, waits for them, and re-layouts: 1.48 us -> 5.24 us
    ppermute x6, starting transfers between devices: 20.4 us -> 23.9 us  [_doubling_sum(): piece = piece + lax.ppermute(piece, axis, _xor_perm(n, bit))]
  transfers between devices with their start and end apart: 16 -> 16, of which waited for: 16 -> 16; matrix products, arithmetic and copies ran while one was open for 1% -> 5% of each run, Pallas kernels for 0% -> 0%
where the time goes in v4:
time: 299 us; the launch traced here: 298 us
  waiting for transfers between devices  174 us (58%)
  starting transfers between devices  63.6 us (21%)
  between operations  14.5 us (5%)
  blocking collectives  12.4 us (4%)
  local copies, waits for them, and re-layouts  11.7 us (4%)
  Pallas kernels  11 us (4%)
  other arithmetic  9.63 us (3%)
    all_gather x1, waiting for transfers between devices, shards(): gathered = lax.all_gather(gathered, ('z', 'x'), axis=0, tiled=True)  93.5 us
    ppermute x6, waiting for transfers between devices, _halving_scatter(): blocks = keep + lax.ppermute(send, axis, _xor_perm(n, bit))  44.9 us
    ppermute x6, waiting for transfers between devices, _doubling_sum(): piece = piece + lax.ppermute(piece, axis, _xor_perm(n, bit))  24.7 us
    ppermute x6, starting transfers between devices, _doubling_sum(): piece = piece + lax.ppermute(piece, axis, _xor_perm(n, bit))  23.9 us
    ppermute x3, starting transfers between devices, _doubling_gather(): other = lax.ppermute(piece, axis, _xor_perm(n, bit))  20.4 us
    ppermute x6, starting transfers between devices, _halving_scatter(): blocks = keep + lax.ppermute(send, axis, _xor_perm(n, bit))  19.2 us
    all_gather x1, blocking collectives, shards(): gathered = lax.all_gather(features, 'y_hi', axis=0, tiled=True)  12.4 us
    pallas_call x1, Pallas kernels, _aggregate(): pl.pallas_call(_aggregate_kernel, out_shape=jax.ShapeDtypeStruct((groups,...  11 us
  transfers between devices with their start and end apart: 16, of which 16 were waited for; matrix products, arithmetic and copies ran while one was open for 5% of the time, Pallas kernels for 0%

profile of v4, /device:TPU:1, one launch (start us, length us, event | category | flops | bytes accessed | tf_op | source)
XLA Modules:
  0.0 297.7 jit_solution(2611678084442230159)
XLA Ops:
  7.2 12.4 %all_gather.6 = bf16[256,512]{1,0:T(8,128)(2,1)} all-gather(bf16[128,512]{1,0:T(8,128)(2,1)} %param.11), channel_id=1, replica_groups=mesh['y_hi'=2,'z'=8,'x'=4,'y_lo'=4,'core'=2] {'y_hi'}, dimensions={0}, use_global_device_ids=true | all-gather | bytes 393216 | tf_op jit(solution)/shard_map/all_gather | solution.py:119
  21.6 4.7 %copy.11 = bf16[8,1,12,128,128]{3,4,2,0,1:T(8,128)(2,1)} copy(bf16[8,1,12,128,128]{4,3,2,1,0:T(8,128)(2,1)} %param.14) | data formatting | bytes 6291456 | tf_op args[3]
  26.4 3.9 %bitcast_select_fusion = bf16[8,12,128,128]{2,3,1,0:T(8,128)(2,1)} fusion(bf16[8,1,12,128,128]{3,4,2,0,1:T(8,128)(2,1)} %copy.11, pred[8,12]{1,0:T(8,128)(4,1)S(1)} %iota_compare_fusion), kind=kLoop, calls=%fused_computation | loop fusion | flops 1572864 | bytes 6291552 | tf_op jit(solution)/shard_map/jit(_where)/select_n | solution.py:84
  30.3 4.7 %copy.12.tiles_ref = bf16[8,128,1536]{2,1,0:T(8,128)(2,1)} copy(bf16[8,128,1536]{1,2,0:T(8,128)(2,1)} %bitcast.37) | data formatting | bytes 6291456 | tf_op jit(solution)/shard_map/reshape | solution.py:85
  35.6 93.5 %all-gather.2.cloned.1.call-done = bf16[8192,512]{1,0:T(8,128)(2,1)} async-done(((bf16[256,512]{1,0:T(8,128)(2,1)}), bf16[8192,512]{1,0:T(8,128)(2,1)}) %all-gather.2.cloned.1.call-update) | async-done | bytes 8388624 | tf_op jit(solution)/shard_map/all_gather | solution.py:120
  129.1 11.0 %shard_map.97 = f32[8,128,512]{2,1,0:T(8,128)} custom-call(s32[96]{0:T(128)} %fusion.4.cols_ref, bf16[8,128,1536]{2,1,0:T(8,128)(2,1)} %copy.12.tiles_ref, bf16[64,128,512]{2,1,0:T(8,128)(2,1)} %bitcast.38), custom_call_target="tpu_custom_call" | custom-call | flops 1610612736 | bytes 17825792 | tf_op jit(solution)/shard_map/pallas_call | solution.py:88
  141.4 3.1 %collective-permute-start = (f32[1,4,128,512]{3,2,1,0:T(8,128)S(1)}, f32[1,4,128,512]{3,2,1,0:T(8,128)S(1)}, u32[]{:S(2)}, u32[]{:S(2)}) collective-permute-start(f32[1,4,128,512]{3,2,1,0:T(8,128)S(1)} %dynamic-slice_bitcast_fusion), channel_id=1, source_target_pairs={{0,1},{1,0},{2,3},{3,2},{4,5},{5,4},{6,7},{7,6},{8,9},{9,8},{10,11... | collective-permute-start | bytes 3145736 | tf_op jit(solution)/shard_map/ppermute | solution.py:28
  144.6 2.2 collective-permute-done
  148.2 4.3 %collective-permute-start.1 = (f32[2,1,128,512]{3,2,0,1:T(8,128)S(1)}, f32[2,1,128,512]{3,2,0,1:T(8,128)S(1)}, u32[]{:S(2)}, u32[]{:S(2)}) collective-permute-start(f32[2,1,128,512]{3,2,0,1:T(8,128)S(1)} %dynamic-slice_bitcast_fusion.2), channel_id=1, source_target_pairs={{0,4},{2,6},{4,0},{6,2},{1,5},{3,7},{5,1},{7,3},{8,12},{10,14},{12... | collective-permute-start | bytes 1572872 | tf_op jit(solution)/shard_map/ppermute | solution.py:28
  152.6 22.9 %collective-permute-done.1 = f32[2,1,128,512]{3,2,0,1:T(8,128)S(1)} collective-permute-done((f32[2,1,128,512]{3,2,0,1:T(8,128)S(1)}, f32[2,1,128,512]{3,2,0,1:T(8,128)S(1)}, u32[]{:S(2)}, u32[]{:S(2)}) %collective-permute-start.1) | collective-permute-done | bytes 524320 | tf_op jit(solution)/shard_map/ppermute | solution.py:28
  175.7 3.0 %collective-permute-start.2 = (f32[1,1,128,512]{3,2,0,1:T(8,128)S(1)}, f32[1,1,128,512]{3,2,0,1:T(8,128)S(1)}, u32[]{:S(2)}, u32[]{:S(2)}) collective-permute-start(f32[1,1,128,512]{3,2,0,1:T(8,128)S(1)} %constant_dynamic-slice_fusion.1), channel_id=1, source_target_pairs={{0,2},{2,0},{4,6},{6,4},{1,3},{3,1},{5,7},{7,5},{8,10},{10,8},{12,... | collective-permute-start | bytes 786440 | tf_op jit(solution)/shard_map/ppermute | solution.py:28
  178.7 5.6 %collective-permute-done.2 = f32[1,1,128,512]{3,2,0,1:T(8,128)S(1)} collective-permute-done((f32[1,1,128,512]{3,2,0,1:T(8,128)S(1)}, f32[1,1,128,512]{3,2,0,1:T(8,128)S(1)}, u32[]{:S(2)}, u32[]{:S(2)}) %collective-permute-start.2) | collective-permute-done | bytes 262176 | tf_op jit(solution)/shard_map/ppermute | solution.py:28
  185.9 3.9 %collective-permute-start.3 = (f32[1,288,512]{2,1,0:T(8,128)S(1)}, f32[1,288,512]{2,1,0:T(8,128)S(1)}, u32[]{:S(2)}, u32[]{:S(2)}) collective-permute-start(f32[1,288,512]{2,1,0:T(8,128)S(1)} %dynamic-slice_bitcast_fusion.1), channel_id=1, source_target_pairs={{0,1},{1,0},{2,3},{3,2},{4,5},{5,4},{6,7},{7,6},{8,9},{9,8},{10,11... | collective-permute-start | bytes 1769480 | tf_op jit(solution)/shard_map/ppermute | solution.py:28
  191.6 2.9 collective-permute-start.4
  194.5 8.6 %collective-permute-done.4 = f32[2,72,512]{2,1,0:T(8,128)S(1)} collective-permute-done((f32[2,72,512]{2,1,0:T(8,128)S(1)}, f32[2,72,512]{2,1,0:T(8,128)S(1)}, u32[]{:S(2)}, u32[]{:S(2)}) %collective-permute-start.4) | collective-permute-done | bytes 294944 | tf_op jit(solution)/shard_map/ppermute | solution.py:28
  205.2 4.0 %collective-permute-done.5 = f32[1,72,512]{2,1,0:T(8,128)S(1)} collective-permute-done((f32[1,72,512]{2,1,0:T(8,128)S(1)}, f32[1,72,512]{2,1,0:T(8,128)S(1)}, u32[]{:S(2)}, u32[]{:S(2)}) %collective-permute-start.5) | collective-permute-done | bytes 147488 | tf_op jit(solution)/shard_map/ppermute | solution.py:28
  209.1 3.0 %collective-permute-start.6 = (f32[72,512]{1,0:T(8,128)S(1)}, f32[72,512]{1,0:T(8,128)S(1)}, u32[]{:S(2)}, u32[]{:S(2)}) collective-permute-start(f32[72,512]{1,0:T(8,128)S(1)} %add_bitcast_fusion), channel_id=1, source_target_pairs={{0,2},{2,0},{4,6},{6,4},{1,3},{3,1},{5,7},{7,5},{8,10},{10,8},{12,... | collective-permute-start | bytes 442376 | tf_op jit(solution)/shard_map/ppermute | solution.py:49
  212.2 2.9 collective-permute-done.6
  215.1 4.7 %collective-permute-start.7 = (f32[72,512]{1,0:T(8,128)S(1)}, f32[72,512]{1,0:T(8,128)S(1)}, u32[]{:S(2)}, u32[]{:S(2)}) collective-permute-start(f32[72,512]{1,0:T(8,128)S(1)} %add.173), channel_id=1, source_target_pairs={{0,4},{2,6},{4,0},{6,2},{1,5},{3,7},{5,1},{7,3},{8,12},{10,14},{12... | collective-permute-start | bytes 442376 | tf_op jit(solution)/shard_map/ppermute | solution.py:49
  219.7 4.1 %collective-permute-done.7 = f32[72,512]{1,0:T(8,128)S(1)} collective-permute-done((f32[72,512]{1,0:T(8,128)S(1)}, f32[72,512]{1,0:T(8,128)S(1)}, u32[]{:S(2)}, u32[]{:S(2)}) %collective-permute-start.7) | collective-permute-done | bytes 147488 | tf_op jit(solution)/shard_map/ppermute | solution.py:49
  225.8 4.0 %collective-permute-done.8 = f32[72,512]{1,0:T(8,128)S(1)} collective-permute-done((f32[72,512]{1,0:T(8,128)S(1)}, f32[72,512]{1,0:T(8,128)S(1)}, u32[]{:S(2)}, u32[]{:S(2)}) %collective-permute-start.8) | collective-permute-done | bytes 147488 | tf_op jit(solution)/shard_map/ppermute | solution.py:49
  229.8 3.1 %collective-permute-start.9 = (f32[72,512]{1,0:T(8,128)S(1)}, f32[72,512]{1,0:T(8,128)S(1)}, u32[]{:S(2)}, u32[]{:S(2)}) collective-permute-start(f32[72,512]{1,0:T(8,128)S(1)} %add.175), channel_id=1, source_target_pairs={{0,64},{32,96},{64,0},{96,32},{128,192},{160,224},{192,128},{224,1... | collective-permute-start | bytes 442376 | tf_op jit(solution)/shard_map/ppermute | solution.py:49
  232.9 5.3 %collective-permute-done.9 = f32[72,512]{1,0:T(8,128)S(1)} collective-permute-done((f32[72,512]{1,0:T(8,128)S(1)}, f32[72,512]{1,0:T(8,128)S(1)}, u32[]{:S(2)}, u32[]{:S(2)}) %collective-permute-start.9) | collective-permute-done | bytes 147488 | tf_op jit(solution)/shard_map/ppermute | solution.py:49
  238.2 4.3 %collective-permute-start.10 = (f32[72,512]{1,0:T(8,128)S(1)}, f32[72,512]{1,0:T(8,128)S(1)}, u32[]{:S(2)}, u32[]{:S(2)}) collective-permute-start(f32[72,512]{1,0:T(8,128)S(1)} %add.176), channel_id=1, source_target_pairs={{0,128},{32,160},{64,192},{96,224},{128,0},{160,32},{192,64},{224,... | collective-permute-start | bytes 442376 | tf_op jit(solution)/shard_map/ppermute | solution.py:49
  242.4 5.6 %collective-permute-done.10 = f32[72,512]{1,0:T(8,128)S(1)} collective-permute-done((f32[72,512]{1,0:T(8,128)S(1)}, f32[72,512]{1,0:T(8,128)S(1)}, u32[]{:S(2)}, u32[]{:S(2)}) %collective-permute-start.10) | collective-permute-done | bytes 147488 | tf_op jit(solution)/shard_map/ppermute | solution.py:49
  248.1 7.0 %collective-permute-start.11 = (f32[72,512]{1,0:T(8,128)S(1)}, f32[72,512]{1,0:T(8,128)S(1)}, u32[]{:S(2)}, u32[]{:S(2)}) collective-permute-start(f32[72,512]{1,0:T(8,128)S(1)} %add.177), channel_id=1, source_target_pairs={{0,256},{256,0},{1,257},{257,1},{2,258},{258,2},{3,259},{259,3},{4... | collective-permute-start | bytes 442376 | tf_op jit(solution)/shard_map/ppermute | solution.py:49
  255.1 2.9 collective-permute-done.11
  258.0 2.9 collective-permute-start.12
  260.9 3.0 collective-permute-done.12
  263.9 3.1 %collective-permute-start.13 = (f32[144,512]{1,0:T(8,128)S(1)}, f32[144,512]{1,0:T(8,128)S(1)}, u32[]{:S(2)}, u32[]{:S(2)}) collective-permute-start(f32[144,512]{1,0:T(8,128)S(1)} %pad_maximum_fusion.2), channel_id=1, source_target_pairs={{0,16},{8,24},{16,0},{24,8},{1,17},{9,25},{17,1},{25,9},{2,18},{10... | collective-permute-start | bytes 884744 | tf_op jit(solution)/shard_map/ppermute | solution.py:37
  267.0 5.9 %collective-permute-done.13 = f32[144,512]{1,0:T(8,128)S(1)} collective-permute-done((f32[144,512]{1,0:T(8,128)S(1)}, f32[144,512]{1,0:T(8,128)S(1)}, u32[]{:S(2)}, u32[]{:S(2)}) %collective-permute-start.13) | collective-permute-done | bytes 294944 | tf_op jit(solution)/shard_map/ppermute | solution.py:37
  273.0 14.4 %collective-permute-start.14 = (f32[288,512]{1,0:T(8,128)S(1)}, f32[288,512]{1,0:T(8,128)S(1)}, u32[]{:S(2)}, u32[]{:S(2)}) collective-permute-start(f32[288,512]{1,0:T(8,128)S(1)} %pad_maximum_fusion.1), channel_id=1, source_target_pairs={{0,1},{1,0},{2,3},{3,2},{4,5},{5,4},{6,7},{7,6},{8,9},{9,8},{10,11... | collective-permute-start | bytes 1769480 | tf_op jit(solution)/shard_map/ppermute | solution.py:37
  (48 shorter events, 16.3 us)
Async XLA Ops:
  7.2 177.2 %copy-start = (bf16[512,512]{1,0:T(8,128)(2,1)S(1)}, bf16[512,512]{1,0:T(8,128)(2,1)}, u32[]{:S(2)}) copy-start(bf16[512,512]{1,0:T(8,128)(2,1)} %param.15) | copy-start | bytes 1572868
  7.2 121.9 %all-gather.2.cloned.1.call-start = ((), (), s32[]{:S(2)}) async-start(), calls=%async_computation | async-start | bytes 8650752 | tf_op jit(solution)/shard_map/all_gather | solution.py:120
  21.6 4.7 %copy-start.3 = (s32[8,1]{0,1:T(1,128)S(1)}, s32[8,1]{0,1:T(1,128)}, u32[]{:S(2)}) copy-start(s32[8,1]{0,1:T(1,128)} %param.13) | copy-start | bytes 100
  141.4 5.4 %collective-permute-start = (f32[1,4,128,512]{3,2,1,0:T(8,128)S(1)}, f32[1,4,128,512]{3,2,1,0:T(8,128)S(1)}, u32[]{:S(2)}, u32[]{:S(2)}) collective-permute-start(f32[1,4,128,512]{3,2,1,0:T(8,128)S(1)} %dynamic-slice_bitcast_fusion), channel_id=1, source_target_pairs={{0,1},{1,0},{2,3},{3,2},{4,5},{5,4},{6,7},{7,6},{8,9},{9,8},{10,11... | collective-permute-start | bytes 3145736 | tf_op jit(solution)/shard_map/ppermute | solution.py:28
  144.5 39.8 %copy-start.1 = (bf16[128,512]{1,0:T(8,128)(2,1)S(1)}, bf16[128,512]{1,0:T(8,128)(2,1)}, u32[]{:S(2)}) copy-start(bf16[128,512]{1,0:T(8,128)(2,1)} %param.17) | copy-start | bytes 393220
  144.5 39.8 %copy-start.2 = (f32[512]{0:T(512)S(1)}, f32[512]{0:T(512)}, u32[]{:S(2)}) copy-start(f32[512]{0:T(512)} %param.16) | copy-start | bytes 6148
  148.2 27.3 %collective-permute-start.1 = (f32[2,1,128,512]{3,2,0,1:T(8,128)S(1)}, f32[2,1,128,512]{3,2,0,1:T(8,128)S(1)}, u32[]{:S(2)}, u32[]{:S(2)}) collective-permute-start(f32[2,1,128,512]{3,2,0,1:T(8,128)S(1)} %dynamic-slice_bitcast_fusion.2), channel_id=1, source_target_pairs={{0,4},{2,6},{4,0},{6,2},{1,5},{3,7},{5,1},{7,3},{8,12},{10,14},{12... | collective-permute-start | bytes 1572872 | tf_op jit(solution)/shard_map/ppermute | solution.py:28
  175.7 8.6 %collective-permute-start.2 = (f32[1,1,128,512]{3,2,0,1:T(8,128)S(1)}, f32[1,1,128,512]{3,2,0,1:T(8,128)S(1)}, u32[]{:S(2)}, u32[]{:S(2)}) collective-permute-start(f32[1,1,128,512]{3,2,0,1:T(8,128)S(1)} %constant_dynamic-slice_fusion.1), channel_id=1, source_target_pairs={{0,2},{2,0},{4,6},{6,4},{1,3},{3,1},{5,7},{7,5},{8,10},{10,8},{12,... | collective-permute-start | bytes 786440 | tf_op jit(solution)/shard_map/ppermute | solution.py:28
  185.9 5.5 %collective-permute-start.3 = (f32[1,288,512]{2,1,0:T(8,128)S(1)}, f32[1,288,512]{2,1,0:T(8,128)S(1)}, u32[]{:S(2)}, u32[]{:S(2)}) collective-permute-start(f32[1,288,512]{2,1,0:T(8,128)S(1)} %dynamic-slice_bitcast_fusion.1), channel_id=1, source_target_pairs={{0,1},{1,0},{2,3},{3,2},{4,5},{5,4},{6,7},{7,6},{8,9},{9,8},{10,11... | collective-permute-start | bytes 1769480 | tf_op jit(solution)/shard_map/ppermute | solution.py:28
  191.6 11.6 %collective-permute-start.4 = (f32[2,72,512]{2,1,0:T(8,128)S(1)}, f32[2,72,512]{2,1,0:T(8,128)S(1)}, u32[]{:S(2)}, u32[]{:S(2)}) collective-permute-start(f32[2,72,512]{2,1,0:T(8,128)S(1)} %dynamic-slice_bitcast_fusion.3), channel_id=1, source_target_pairs={{0,16},{8,24},{16,0},{24,8},{1,17},{9,25},{17,1},{25,9},{2,18},{10... | collective-permute-start | bytes 884744 | tf_op jit(solution)/shard_map/ppermute | solution.py:28
  203.2 5.9 %collective-permute-start.5 = (f32[1,72,512]{2,1,0:T(8,128)S(1)}, f32[1,72,512]{2,1,0:T(8,128)S(1)}, u32[]{:S(2)}, u32[]{:S(2)}) collective-permute-start(f32[1,72,512]{2,1,0:T(8,128)S(1)} %constant_dynamic-slice_fusion), channel_id=1, source_target_pairs={{0,8},{8,0},{16,24},{24,16},{1,9},{9,1},{17,25},{25,17},{2,10},{10... | collective-permute-start | bytes 442376 | tf_op jit(solution)/shard_map/ppermute | solution.py:28
  209.1 5.9 %collective-permute-start.6 = (f32[72,512]{1,0:T(8,128)S(1)}, f32[72,512]{1,0:T(8,128)S(1)}, u32[]{:S(2)}, u32[]{:S(2)}) collective-permute-start(f32[72,512]{1,0:T(8,128)S(1)} %add_bitcast_fusion), channel_id=1, source_target_pairs={{0,2},{2,0},{4,6},{6,4},{1,3},{3,1},{5,7},{7,5},{8,10},{10,8},{12,... | collective-permute-start | bytes 442376 | tf_op jit(solution)/shard_map/ppermute | solution.py:49
  215.1 8.8 %collective-permute-start.7 = (f32[72,512]{1,0:T(8,128)S(1)}, f32[72,512]{1,0:T(8,128)S(1)}, u32[]{:S(2)}, u32[]{:S(2)}) collective-permute-start(f32[72,512]{1,0:T(8,128)S(1)} %add.173), channel_id=1, source_target_pairs={{0,4},{2,6},{4,0},{6,2},{1,5},{3,7},{5,1},{7,3},{8,12},{10,14},{12... | collective-permute-start | bytes 442376 | tf_op jit(solution)/shard_map/ppermute | solution.py:49
  223.8 5.9 %collective-permute-start.8 = (f32[72,512]{1,0:T(8,128)S(1)}, f32[72,512]{1,0:T(8,128)S(1)}, u32[]{:S(2)}, u32[]{:S(2)}) collective-permute-start(f32[72,512]{1,0:T(8,128)S(1)} %add.174), channel_id=1, source_target_pairs={{0,32},{32,0},{64,96},{96,64},{128,160},{160,128},{192,224},{224,1... | collective-permute-start | bytes 442376 | tf_op jit(solution)/shard_map/ppermute | solution.py:49
  229.8 8.4 %collective-permute-start.9 = (f32[72,512]{1,0:T(8,128)S(1)}, f32[72,512]{1,0:T(8,128)S(1)}, u32[]{:S(2)}, u32[]{:S(2)}) collective-permute-start(f32[72,512]{1,0:T(8,128)S(1)} %add.175), channel_id=1, source_target_pairs={{0,64},{32,96},{64,0},{96,32},{128,192},{160,224},{192,128},{224,1... | collective-permute-start | bytes 442376 | tf_op jit(solution)/shard_map/ppermute | solution.py:49
  238.2 9.9 %collective-permute-start.10 = (f32[72,512]{1,0:T(8,128)S(1)}, f32[72,512]{1,0:T(8,128)S(1)}, u32[]{:S(2)}, u32[]{:S(2)}) collective-permute-start(f32[72,512]{1,0:T(8,128)S(1)} %add.176), channel_id=1, source_target_pairs={{0,128},{32,160},{64,192},{96,224},{128,0},{160,32},{192,64},{224,... | collective-permute-start | bytes 442376 | tf_op jit(solution)/shard_map/ppermute | solution.py:49
  248.1 9.9 %collective-permute-start.11 = (f32[72,512]{1,0:T(8,128)S(1)}, f32[72,512]{1,0:T(8,128)S(1)}, u32[]{:S(2)}, u32[]{:S(2)}) collective-permute-start(f32[72,512]{1,0:T(8,128)S(1)} %add.177), channel_id=1, source_target_pairs={{0,256},{256,0},{1,257},{257,1},{2,258},{258,2},{3,259},{259,3},{4... | collective-permute-start | bytes 442376 | tf_op jit(solution)/shard_map/ppermute | solution.py:49
  258.0 5.9 %collective-permute-start.12 = (f32[72,512]{1,0:T(8,128)S(1)}, f32[72,512]{1,0:T(8,128)S(1)}, u32[]{:S(2)}, u32[]{:S(2)}) collective-permute-start(f32[72,512]{1,0:T(8,128)S(1)} %add.178), channel_id=1, source_target_pairs={{0,8},{8,0},{16,24},{24,16},{1,9},{9,1},{17,25},{25,17},{2,10},{10... | collective-permute-start | bytes 442376 | tf_op jit(solution)/shard_map/ppermute | solution.py:37
  263.9 9.0 %collective-permute-start.13 = (f32[144,512]{1,0:T(8,128)S(1)}, f32[144,512]{1,0:T(8,128)S(1)}, u32[]{:S(2)}, u32[]{:S(2)}) collective-permute-start(f32[144,512]{1,0:T(8,128)S(1)} %pad_maximum_fusion.2), channel_id=1, source_target_pairs={{0,16},{8,24},{16,0},{24,8},{1,17},{9,25},{17,1},{25,9},{2,18},{10... | collective-permute-start | bytes 884744 | tf_op jit(solution)/shard_map/ppermute | solution.py:37
  273.0 16.0 %collective-permute-start.14 = (f32[288,512]{1,0:T(8,128)S(1)}, f32[288,512]{1,0:T(8,128)S(1)}, u32[]{:S(2)}, u32[]{:S(2)}) collective-permute-start(f32[288,512]{1,0:T(8,128)S(1)} %pad_maximum_fusion.1), channel_id=1, source_target_pairs={{0,1},{1,0},{2,3},{3,2},{4,5},{5,4},{6,7},{7,6},{8,9},{9,8},{10,11... | collective-permute-start | bytes 1769480 | tf_op jit(solution)/shard_map/ppermute | solution.py:37
Sparse Core Ops, SparseCore 0:
  19.8 109.2 all-gather.1

commit v5 on v4

--- a/solution.py
+++ b/solution.py
@@ -17,30 +17,36 @@
     return [(i, i ^ bit) for i in range(n)]
 
 
-def _halving_scatter(blocks, axis, n):
+def _halving_scatter(blocks, axis, n, bits):
     me = lax.axis_index(axis)
-    bit = n // 2
-    while bit >= 1:
-        pairs = blocks.reshape((2, blocks.shape[0] // 2) + blocks.shape[1:])
-        mine = (me // bit) % 2
-        keep = lax.dynamic_index_in_dim(pairs, mine, 0, keepdims=False)
-        send = lax.dynamic_index_in_dim(pairs, 1 - mine, 0, keepdims=False)
-        blocks = keep + lax.ppermute(send, axis, _xor_perm(n, bit))
-        bit //= 2
-    return blocks[0]
+    depth = n.bit_length() - 1
+    rest = blocks.shape[1:]
+    blocks = blocks.reshape((2,) * depth + rest)
+    left = list(range(depth - 1, -1, -1))
+    for bit in bits:
+        at = left.index(bit)
+        mine = (me // (1 << bit)) % 2
+        keep = lax.dynamic_index_in_dim(blocks, mine, at, keepdims=False)
+        send = lax.dynamic_index_in_dim(blocks, 1 - mine, at, keepdims=False)
+        blocks = keep + lax.ppermute(send, axis, _xor_perm(n, 1 << bit))
+        left.pop(at)
+    return blocks
 
 
-def _doubling_gather(piece, axis, n):
+def _doubling_gather(piece, axis, n, bits):
     me = lax.axis_index(axis)
-    bit = 1
-    while bit < n:
-        other = lax.ppermute(piece, axis, _xor_perm(n, bit))
-        upper = (me // bit) % 2 == 1
+    rest = piece.shape
+    got = []
+    for bit in bits:
+        other = lax.ppermute(piece, axis, _xor_perm(n, 1 << bit))
+        upper = (me // (1 << bit)) % 2 == 1
         low = jnp.where(upper, other, piece)
         high = jnp.where(upper, piece, other)
-        piece = jnp.concatenate([low, high], axis=0)
-        bit *= 2
-    return piece
+        piece = jnp.stack([low, high])
+        got = [bit] + got
+    order = sorted(range(len(got)), key=lambda i: -got[i])
+    piece = jnp.transpose(piece, order + list(range(len(got), piece.ndim)))
+    return piece.reshape((n * rest[0],) + rest[1:])
 
 
 def _doubling_sum(piece, axis, n):
@@ -123,8 +129,8 @@
     cores = sizes["core"]
     by_core = gathered_sum.reshape(row_panels // cores, cores, tile_size, feat_width)
     by_core = jnp.moveaxis(by_core, 1, 0)
-    half = _halving_scatter(by_core, "core", cores)
-    summed_own = _halving_scatter(half.reshape((sizes["y_lo"], 1) + half.shape[1:]), "y_lo", sizes["y_lo"])
+    half = _halving_scatter(by_core, "core", cores, (0,))
+    summed_own = _halving_scatter(half, "y_lo", sizes["y_lo"], (0, 1))
     own_rows = own_panels * tile_size
     aggregated = summed_own.reshape(own_rows, feat_width).astype(jnp.bfloat16)
     pre = jnp.dot(aggregated, weight, preferred_element_type=jnp.float32) + bias
@@ -140,12 +146,12 @@
     padded_rows = -(-(width + 1) // (scatter_ways * 8)) * scatter_ways * 8
     combined = jnp.zeros((padded_rows, feat_width), jnp.float32)
     combined = combined.at[:width].set(local_weight).at[width].set(local_bias)
-    chunk = _halving_scatter(combined.reshape(sizes["core"], -1, feat_width), "core", sizes["core"])
-    chunk = _halving_scatter(chunk.reshape(sizes["x"], -1, feat_width), "x", sizes["x"])
+    chunk = _halving_scatter(combined.reshape(sizes["core"], -1, feat_width), "core", sizes["core"], (0,))
+    chunk = _halving_scatter(chunk.reshape(sizes["x"], -1, feat_width), "x", sizes["x"], (0, 1))
     for name in ("y_lo", "z", "y_hi"):
         chunk = _doubling_sum(chunk, name, sizes[name])
-    chunk = _doubling_gather(chunk, "x", sizes["x"])
-    chunk = _doubling_gather(chunk, "core", sizes["core"])
+    chunk = _doubling_gather(chunk, "x", sizes["x"], (1, 0))
+    chunk = _doubling_gather(chunk, "core", sizes["core"], (0,))
     node_total = lax.axis_size(SECTION_AXES) * rep_count * own_rows
     factor = 1.0 / math.sqrt(node_total)
     weight_sum = chunk[:width]

time: 299 us -> 297 us (level)
  starting transfers between devices: 63.6 us -> 59.9 us
    ppermute x9, waiting for transfers between devices: 55.3 us -> 51.9 us  [the longest x6 39.8 us: _halving_scatter(): blocks = keep + lax.ppermute(send, axis, _xor_perm(n, 1 << bit))]
    unnamed x10 -> x14, local copies, waits for them, and re-layouts: 5.24 us -> 6.2 us
where the time goes in v5:
time: 297 us; the launch traced here: 296 us
  waiting for transfers between devices  172 us (58%)
  starting transfers between devices  59.9 us (20%)
  between operations  14.5 us (5%)
  local copies, waits for them, and re-layouts  13.7 us (5%)
  blocking collectives  12.4 us (4%)
  Pallas kernels  11.1 us (4%)
  other arithmetic  10.8 us (4%)
    all_gather x1, waiting for transfers between devices, shards(): gathered = lax.all_gather(gathered, ('z', 'x'), axis=0, tiled=True)  93.5 us
    ppermute x6, waiting for transfers between devices, _halving_scatter(): blocks = keep + lax.ppermute(send, axis, _xor_perm(n, 1 << bit))  39.8 us
    ppermute x6, waiting for transfers between devices, _doubling_sum(): piece = piece + lax.ppermute(piece, axis, _xor_perm(n, bit))  26.4 us
    ppermute x6, starting transfers between devices, _doubling_sum(): piece = piece + lax.ppermute(piece, axis, _xor_perm(n, bit))  22.1 us
    ppermute x6, starting transfers between devices, _halving_scatter(): blocks = keep + lax.ppermute(send, axis, _xor_perm(n, 1 << bit))  18.9 us
    ppermute x3, starting transfers between devices, _doubling_gather(): other = lax.ppermute(piece, axis, _xor_perm(n, 1 << bit))  18.9 us
    all_gather x1, blocking collectives, shards(): gathered = lax.all_gather(features, 'y_hi', axis=0, tiled=True)  12.4 us
    ppermute x3, waiting for transfers between devices, _doubling_gather(): other = lax.ppermute(piece, axis, _xor_perm(n, 1 << bit))  12.1 us
  transfers between devices with their start and end apart: 16, of which 16 were waited for; matrix products, arithmetic and copies ran while one was open for 5% of the time, Pallas kernels for 0%

profile of v5, /device:TPU:1, one launch (start us, length us, event | category | flops | bytes accessed | tf_op | source)
XLA Modules:
  0.0 295.6 jit_solution(12918398279519746932)
XLA Ops:
  7.2 12.4 %all_gather.6 = bf16[256,512]{1,0:T(8,128)(2,1)} all-gather(bf16[128,512]{1,0:T(8,128)(2,1)} %param.11), channel_id=1, replica_groups=mesh['y_hi'=2,'z'=8,'x'=4,'y_lo'=4,'core'=2] {'y_hi'}, dimensions={0}, use_global_device_ids=true | all-gather | bytes 393216 | tf_op jit(solution)/shard_map/all_gather | solution.py:125
  21.6 4.7 %copy.12 = bf16[8,1,12,128,128]{3,4,2,0,1:T(8,128)(2,1)} copy(bf16[8,1,12,128,128]{4,3,2,1,0:T(8,128)(2,1)} %param.14) | data formatting | bytes 6291456 | tf_op args[3]
  26.4 3.9 %bitcast_select_fusion = bf16[8,12,128,128]{2,3,1,0:T(8,128)(2,1)} fusion(bf16[8,1,12,128,128]{3,4,2,0,1:T(8,128)(2,1)} %copy.12, pred[8,12]{1,0:T(8,128)(4,1)S(1)} %iota_compare_fusion), kind=kLoop, calls=%fused_computation | loop fusion | flops 1572864 | bytes 6291552 | tf_op jit(solution)/shard_map/jit(_where)/select_n | solution.py:90
  30.3 4.7 %copy.13.tiles_ref = bf16[8,128,1536]{2,1,0:T(8,128)(2,1)} copy(bf16[8,128,1536]{1,2,0:T(8,128)(2,1)} %bitcast.63) | data formatting | bytes 6291456 | tf_op jit(solution)/shard_map/reshape | solution.py:91
  35.6 93.5 %all-gather.2.cloned.1.call-done = bf16[8192,512]{1,0:T(8,128)(2,1)} async-done(((bf16[256,512]{1,0:T(8,128)(2,1)}), bf16[8192,512]{1,0:T(8,128)(2,1)}) %all-gather.2.cloned.1.call-update) | async-done | bytes 8388624 | tf_op jit(solution)/shard_map/all_gather | solution.py:126
  129.1 11.1 %shard_map.97 = f32[8,128,512]{2,1,0:T(8,128)} custom-call(s32[96]{0:T(128)} %fusion.3.cols_ref, bf16[8,128,1536]{2,1,0:T(8,128)(2,1)} %copy.13.tiles_ref, bf16[64,128,512]{2,1,0:T(8,128)(2,1)} %bitcast.64), custom_call_target="tpu_custom_call" | custom-call | flops 1610612736 | bytes 17825792 | tf_op jit(solution)/shard_map/pallas_call | solution.py:94
  140.1 2.4 dynamic-slice_bitcast_fusion
  142.6 3.2 %collective-permute-start = (f32[4,128,512]{2,1,0:T(8,128)}, f32[4,128,512]{2,1,0:T(8,128)}, u32[]{:S(2)}, u32[]{:S(2)}) collective-permute-start(f32[4,128,512]{2,1,0:T(8,128)} %dynamic-slice_bitcast_fusion), channel_id=1, source_target_pairs={{0,1},{1,0},{2,3},{3,2},{4,5},{5,4},{6,7},{7,6},{8,9},{9,8},{10,11... | collective-permute-start | bytes 3145736 | tf_op jit(solution)/shard_map/ppermute | solution.py:31
  145.8 2.6 collective-permute-done
  150.8 3.2 %collective-permute-start.1 = (f32[2,128,512]{2,1,0:T(8,128)S(1)}, f32[2,128,512]{2,1,0:T(8,128)S(1)}, u32[]{:S(2)}, u32[]{:S(2)}) collective-permute-start(f32[2,128,512]{2,1,0:T(8,128)S(1)} %dynamic-slice_bitcast_fusion.2), channel_id=1, source_target_pairs={{0,2},{2,0},{4,6},{6,4},{1,3},{3,1},{5,7},{7,5},{8,10},{10,8},{12,... | collective-permute-start | bytes 1572872 | tf_op jit(solution)/shard_map/ppermute | solution.py:31
  154.0 11.8 %collective-permute-done.1 = f32[2,128,512]{2,1,0:T(8,128)S(1)} collective-permute-done((f32[2,128,512]{2,1,0:T(8,128)S(1)}, f32[2,128,512]{2,1,0:T(8,128)S(1)}, u32[]{:S(2)}, u32[]{:S(2)}) %collective-permute-start.1) | collective-permute-done | bytes 524320 | tf_op jit(solution)/shard_map/ppermute | solution.py:31
  167.0 4.2 %collective-permute-start.2 = (f32[128,512]{1,0:T(8,128)S(1)}, f32[128,512]{1,0:T(8,128)S(1)}, u32[]{:S(2)}, u32[]{:S(2)}) collective-permute-start(f32[128,512]{1,0:T(8,128)S(1)} %dynamic-slice_bitcast_fusion.4), channel_id=1, source_target_pairs={{0,4},{2,6},{4,0},{6,2},{1,5},{3,7},{5,1},{7,3},{8,12},{10,14},{12... | collective-permute-start | bytes 786440 | tf_op jit(solution)/shard_map/ppermute | solution.py:31
  171.2 11.4 %collective-permute-done.2 = f32[128,512]{1,0:T(8,128)S(1)} collective-permute-done((f32[128,512]{1,0:T(8,128)S(1)}, f32[128,512]{1,0:T(8,128)S(1)}, u32[]{:S(2)}, u32[]{:S(2)}) %collective-permute-start.2) | collective-permute-done | bytes 262176 | tf_op jit(solution)/shard_map/ppermute | solution.py:31
  184.2 3.4 %collective-permute-start.3 = (f32[288,512]{1,0:T(8,128)S(1)}, f32[288,512]{1,0:T(8,128)S(1)}, u32[]{:S(2)}, u32[]{:S(2)}) collective-permute-start(f32[288,512]{1,0:T(8,128)S(1)} %dynamic-slice_bitcast_fusion.1), channel_id=1, source_target_pairs={{0,1},{1,0},{2,3},{3,2},{4,5},{5,4},{6,7},{7,6},{8,9},{9,8},{10,11... | collective-permute-start | bytes 1769480 | tf_op jit(solution)/shard_map/ppermute | solution.py:31
  191.4 8.1 %collective-permute-done.4 = f32[2,72,512]{2,1,0:T(8,128)S(1)} collective-permute-done((f32[2,72,512]{2,1,0:T(8,128)S(1)}, f32[2,72,512]{2,1,0:T(8,128)S(1)}, u32[]{:S(2)}, u32[]{:S(2)}) %collective-permute-start.4) | collective-permute-done | bytes 294944 | tf_op jit(solution)/shard_map/ppermute | solution.py:31
  199.5 3.1 %collective-permute-start.5 = (f32[72,512]{1,0:T(8,128)S(1)}, f32[72,512]{1,0:T(8,128)S(1)}, u32[]{:S(2)}, u32[]{:S(2)}) collective-permute-start(f32[72,512]{1,0:T(8,128)S(1)} %dynamic-slice_bitcast_fusion.5), channel_id=1, source_target_pairs={{0,16},{8,24},{16,0},{24,8},{1,17},{9,25},{17,1},{25,9},{2,18},{10... | collective-permute-start | bytes 442376 | tf_op jit(solution)/shard_map/ppermute | solution.py:31
  202.6 4.3 %collective-permute-done.5 = f32[72,512]{1,0:T(8,128)S(1)} collective-permute-done((f32[72,512]{1,0:T(8,128)S(1)}, f32[72,512]{1,0:T(8,128)S(1)}, u32[]{:S(2)}, u32[]{:S(2)}) %collective-permute-start.5) | collective-permute-done | bytes 147488 | tf_op jit(solution)/shard_map/ppermute | solution.py:31
  207.0 2.2 collective-permute-start.6
  209.2 3.6 %collective-permute-done.6 = f32[72,512]{1,0:T(8,128)S(1)} collective-permute-done((f32[72,512]{1,0:T(8,128)S(1)}, f32[72,512]{1,0:T(8,128)S(1)}, u32[]{:S(2)}, u32[]{:S(2)}) %collective-permute-start.6) | collective-permute-done | bytes 147488 | tf_op jit(solution)/shard_map/ppermute | solution.py:55
  212.9 3.9 %collective-permute-start.7 = (f32[72,512]{1,0:T(8,128)S(1)}, f32[72,512]{1,0:T(8,128)S(1)}, u32[]{:S(2)}, u32[]{:S(2)}) collective-permute-start(f32[72,512]{1,0:T(8,128)S(1)} %add.173), channel_id=1, source_target_pairs={{0,4},{2,6},{4,0},{6,2},{1,5},{3,7},{5,1},{7,3},{8,12},{10,14},{12... | collective-permute-start | bytes 442376 | tf_op jit(solution)/shard_map/ppermute | solution.py:55
  216.8 4.5 %collective-permute-done.7 = f32[72,512]{1,0:T(8,128)S(1)} collective-permute-done((f32[72,512]{1,0:T(8,128)S(1)}, f32[72,512]{1,0:T(8,128)S(1)}, u32[]{:S(2)}, u32[]{:S(2)}) %collective-permute-start.7) | collective-permute-done | bytes 147488 | tf_op jit(solution)/shard_map/ppermute | solution.py:55
  223.2 4.0 %collective-permute-done.8 = f32[72,512]{1,0:T(8,128)S(1)} collective-permute-done((f32[72,512]{1,0:T(8,128)S(1)}, f32[72,512]{1,0:T(8,128)S(1)}, u32[]{:S(2)}, u32[]{:S(2)}) %collective-permute-start.8) | collective-permute-done | bytes 147488 | tf_op jit(solution)/shard_map/ppermute | solution.py:55
  227.2 3.3 %collective-permute-start.9 = (f32[72,512]{1,0:T(8,128)S(1)}, f32[72,512]{1,0:T(8,128)S(1)}, u32[]{:S(2)}, u32[]{:S(2)}) collective-permute-start(f32[72,512]{1,0:T(8,128)S(1)} %add.175), channel_id=1, source_target_pairs={{0,64},{32,96},{64,0},{96,32},{128,192},{160,224},{192,128},{224,1... | collective-permute-start | bytes 442376 | tf_op jit(solution)/shard_map/ppermute | solution.py:55
  230.5 5.0 %collective-permute-done.9 = f32[72,512]{1,0:T(8,128)S(1)} collective-permute-done((f32[72,512]{1,0:T(8,128)S(1)}, f32[72,512]{1,0:T(8,128)S(1)}, u32[]{:S(2)}, u32[]{:S(2)}) %collective-permute-start.9) | collective-permute-done | bytes 147488 | tf_op jit(solution)/shard_map/ppermute | solution.py:55
  235.6 4.4 %collective-permute-start.10 = (f32[72,512]{1,0:T(8,128)S(1)}, f32[72,512]{1,0:T(8,128)S(1)}, u32[]{:S(2)}, u32[]{:S(2)}) collective-permute-start(f32[72,512]{1,0:T(8,128)S(1)} %add.176), channel_id=1, source_target_pairs={{0,128},{32,160},{64,192},{96,224},{128,0},{160,32},{192,64},{224,... | collective-permute-start | bytes 442376 | tf_op jit(solution)/shard_map/ppermute | solution.py:55
  240.0 5.8 %collective-permute-done.10 = f32[72,512]{1,0:T(8,128)S(1)} collective-permute-done((f32[72,512]{1,0:T(8,128)S(1)}, f32[72,512]{1,0:T(8,128)S(1)}, u32[]{:S(2)}, u32[]{:S(2)}) %collective-permute-start.10) | collective-permute-done | bytes 147488 | tf_op jit(solution)/shard_map/ppermute | solution.py:55
  245.8 6.4 %collective-permute-start.11 = (f32[72,512]{1,0:T(8,128)S(1)}, f32[72,512]{1,0:T(8,128)S(1)}, u32[]{:S(2)}, u32[]{:S(2)}) collective-permute-start(f32[72,512]{1,0:T(8,128)S(1)} %add.177), channel_id=1, source_target_pairs={{0,256},{256,0},{1,257},{257,1},{2,258},{258,2},{3,259},{259,3},{4... | collective-permute-start | bytes 442376 | tf_op jit(solution)/shard_map/ppermute | solution.py:55
  252.2 3.4 %collective-permute-done.11 = f32[72,512]{1,0:T(8,128)S(1)} collective-permute-done((f32[72,512]{1,0:T(8,128)S(1)}, f32[72,512]{1,0:T(8,128)S(1)}, u32[]{:S(2)}, u32[]{:S(2)}) %collective-permute-start.11) | collective-permute-done | bytes 147488 | tf_op jit(solution)/shard_map/ppermute | solution.py:55
  255.7 2.8 collective-permute-start.12
  258.5 4.8 %collective-permute-done.12 = f32[72,512]{1,0:T(8,128)S(1)} collective-permute-done((f32[72,512]{1,0:T(8,128)S(1)}, f32[72,512]{1,0:T(8,128)S(1)}, u32[]{:S(2)}, u32[]{:S(2)}) %collective-permute-start.12) | collective-permute-done | bytes 147488 | tf_op jit(solution)/shard_map/ppermute | solution.py:41
  265.3 5.7 %collective-permute-done.13 = f32[2,72,512]{2,1,0:T(8,128)S(1)} collective-permute-done((f32[2,72,512]{2,1,0:T(8,128)S(1)}, f32[2,72,512]{2,1,0:T(8,128)S(1)}, u32[]{:S(2)}, u32[]{:S(2)}) %collective-permute-start.13) | collective-permute-done | bytes 294944 | tf_op jit(solution)/shard_map/ppermute | solution.py:41
  271.1 14.1 %collective-permute-start.14 = (f32[288,512]{1,0:T(8,128)S(1)}, f32[288,512]{1,0:T(8,128)S(1)}, u32[]{:S(2)}, u32[]{:S(2)}) collective-permute-start(f32[288,512]{1,0:T(8,128)S(1)} %bitcast.73), channel_id=1, source_target_pairs={{0,1},{1,0},{2,3},{3,2},{4,5},{5,4},{6,7},{7,6},{8,9},{9,8},{10,11... | collective-permute-start | bytes 1769480 | tf_op jit(solution)/shard_map/ppermute | solution.py:41
  (53 shorter events, 19.0 us)
Async XLA Ops:
  7.2 175.5 %copy-start = (bf16[512,512]{1,0:T(8,128)(2,1)S(1)}, bf16[512,512]{1,0:T(8,128)(2,1)}, u32[]{:S(2)}) copy-start(bf16[512,512]{1,0:T(8,128)(2,1)} %param.15) | copy-start | bytes 1572868
  7.2 121.9 %all-gather.2.cloned.1.call-start = ((), (), s32[]{:S(2)}) async-start(), calls=%async_computation | async-start | bytes 8650752 | tf_op jit(solution)/shard_map/all_gather | solution.py:126
  21.6 4.7 %copy-start.5 = (s32[8,1]{0,1:T(1,128)S(1)}, s32[8,1]{0,1:T(1,128)}, u32[]{:S(2)}) copy-start(s32[8,1]{0,1:T(1,128)} %param.13) | copy-start | bytes 100
  140.1 8.2 %copy-start.1 = (f32[8,128,512]{2,1,0:T(8,128)S(1)}, f32[8,128,512]{2,1,0:T(8,128)}, u32[]{:S(2)}) copy-start(f32[8,128,512]{2,1,0:T(8,128)} %shard_map.97) | copy-start | bytes 6291460
  142.6 5.8 %collective-permute-start = (f32[4,128,512]{2,1,0:T(8,128)}, f32[4,128,512]{2,1,0:T(8,128)}, u32[]{:S(2)}, u32[]{:S(2)}) collective-permute-start(f32[4,128,512]{2,1,0:T(8,128)} %dynamic-slice_bitcast_fusion), channel_id=1, source_target_pairs={{0,1},{1,0},{2,3},{3,2},{4,5},{5,4},{6,7},{7,6},{8,9},{9,8},{10,11... | collective-permute-start | bytes 3145736 | tf_op jit(solution)/shard_map/ppermute | solution.py:31
  149.8 1.0 copy-start.2
  149.8 32.9 %copy-start.3 = (bf16[128,512]{1,0:T(8,128)(2,1)S(1)}, bf16[128,512]{1,0:T(8,128)(2,1)}, u32[]{:S(2)}) copy-start(bf16[128,512]{1,0:T(8,128)(2,1)} %param.17) | copy-start | bytes 393220
  149.8 32.9 %copy-start.4 = (f32[512]{0:T(512)S(1)}, f32[512]{0:T(512)}, u32[]{:S(2)}) copy-start(f32[512]{0:T(512)} %param.16) | copy-start | bytes 6148
  150.8 15.0 %collective-permute-start.1 = (f32[2,128,512]{2,1,0:T(8,128)S(1)}, f32[2,128,512]{2,1,0:T(8,128)S(1)}, u32[]{:S(2)}, u32[]{:S(2)}) collective-permute-start(f32[2,128,512]{2,1,0:T(8,128)S(1)} %dynamic-slice_bitcast_fusion.2), channel_id=1, source_target_pairs={{0,2},{2,0},{4,6},{6,4},{1,3},{3,1},{5,7},{7,5},{8,10},{10,8},{12,... | collective-permute-start | bytes 1572872 | tf_op jit(solution)/shard_map/ppermute | solution.py:31
  167.0 15.7 %collective-permute-start.2 = (f32[128,512]{1,0:T(8,128)S(1)}, f32[128,512]{1,0:T(8,128)S(1)}, u32[]{:S(2)}, u32[]{:S(2)}) collective-permute-start(f32[128,512]{1,0:T(8,128)S(1)} %dynamic-slice_bitcast_fusion.4), channel_id=1, source_target_pairs={{0,4},{2,6},{4,0},{6,2},{1,5},{3,7},{5,1},{7,3},{8,12},{10,14},{12... | collective-permute-start | bytes 786440 | tf_op jit(solution)/shard_map/ppermute | solution.py:31
  184.2 5.0 %collective-permute-start.3 = (f32[288,512]{1,0:T(8,128)S(1)}, f32[288,512]{1,0:T(8,128)S(1)}, u32[]{:S(2)}, u32[]{:S(2)}) collective-permute-start(f32[288,512]{1,0:T(8,128)S(1)} %dynamic-slice_bitcast_fusion.1), channel_id=1, source_target_pairs={{0,1},{1,0},{2,3},{3,2},{4,5},{5,4},{6,7},{7,6},{8,9},{9,8},{10,11... | collective-permute-start | bytes 1769480 | tf_op jit(solution)/shard_map/ppermute | solution.py:31
  189.4 10.1 %collective-permute-start.4 = (f32[2,72,512]{2,1,0:T(8,128)S(1)}, f32[2,72,512]{2,1,0:T(8,128)S(1)}, u32[]{:S(2)}, u32[]{:S(2)}) collective-permute-start(f32[2,72,512]{2,1,0:T(8,128)S(1)} %dynamic-slice_bitcast_fusion.3), channel_id=1, source_target_pairs={{0,8},{8,0},{16,24},{24,16},{1,9},{9,1},{17,25},{25,17},{2,10},{10... | collective-permute-start | bytes 884744 | tf_op jit(solution)/shard_map/ppermute | solution.py:31
  199.5 7.4 %collective-permute-start.5 = (f32[72,512]{1,0:T(8,128)S(1)}, f32[72,512]{1,0:T(8,128)S(1)}, u32[]{:S(2)}, u32[]{:S(2)}) collective-permute-start(f32[72,512]{1,0:T(8,128)S(1)} %dynamic-slice_bitcast_fusion.5), channel_id=1, source_target_pairs={{0,16},{8,24},{16,0},{24,8},{1,17},{9,25},{17,1},{25,9},{2,18},{10... | collective-permute-start | bytes 442376 | tf_op jit(solution)/shard_map/ppermute | solution.py:31
  207.0 5.9 %collective-permute-start.6 = (f32[72,512]{1,0:T(8,128)S(1)}, f32[72,512]{1,0:T(8,128)S(1)}, u32[]{:S(2)}, u32[]{:S(2)}) collective-permute-start(f32[72,512]{1,0:T(8,128)S(1)} %bitcast_add_fusion.5), channel_id=1, source_target_pairs={{0,2},{2,0},{4,6},{6,4},{1,3},{3,1},{5,7},{7,5},{8,10},{10,8},{12,... | collective-permute-start | bytes 442376 | tf_op jit(solution)/shard_map/ppermute | solution.py:55
  212.9 8.4 %collective-permute-start.7 = (f32[72,512]{1,0:T(8,128)S(1)}, f32[72,512]{1,0:T(8,128)S(1)}, u32[]{:S(2)}, u32[]{:S(2)}) collective-permute-start(f32[72,512]{1,0:T(8,128)S(1)} %add.173), channel_id=1, source_target_pairs={{0,4},{2,6},{4,0},{6,2},{1,5},{3,7},{5,1},{7,3},{8,12},{10,14},{12... | collective-permute-start | bytes 442376 | tf_op jit(solution)/shard_map/ppermute | solution.py:55
  221.3 5.9 %collective-permute-start.8 = (f32[72,512]{1,0:T(8,128)S(1)}, f32[72,512]{1,0:T(8,128)S(1)}, u32[]{:S(2)}, u32[]{:S(2)}) collective-permute-start(f32[72,512]{1,0:T(8,128)S(1)} %add.174), channel_id=1, source_target_pairs={{0,32},{32,0},{64,96},{96,64},{128,160},{160,128},{192,224},{224,1... | collective-permute-start | bytes 442376 | tf_op jit(solution)/shard_map/ppermute | solution.py:55
  227.2 8.4 %collective-permute-start.9 = (f32[72,512]{1,0:T(8,128)S(1)}, f32[72,512]{1,0:T(8,128)S(1)}, u32[]{:S(2)}, u32[]{:S(2)}) collective-permute-start(f32[72,512]{1,0:T(8,128)S(1)} %add.175), channel_id=1, source_target_pairs={{0,64},{32,96},{64,0},{96,32},{128,192},{160,224},{192,128},{224,1... | collective-permute-start | bytes 442376 | tf_op jit(solution)/shard_map/ppermute | solution.py:55
  235.6 10.2 %collective-permute-start.10 = (f32[72,512]{1,0:T(8,128)S(1)}, f32[72,512]{1,0:T(8,128)S(1)}, u32[]{:S(2)}, u32[]{:S(2)}) collective-permute-start(f32[72,512]{1,0:T(8,128)S(1)} %add.176), channel_id=1, source_target_pairs={{0,128},{32,160},{64,192},{96,224},{128,0},{160,32},{192,64},{224,... | collective-permute-start | bytes 442376 | tf_op jit(solution)/shard_map/ppermute | solution.py:55
  245.8 9.8 %collective-permute-start.11 = (f32[72,512]{1,0:T(8,128)S(1)}, f32[72,512]{1,0:T(8,128)S(1)}, u32[]{:S(2)}, u32[]{:S(2)}) collective-permute-start(f32[72,512]{1,0:T(8,128)S(1)} %add.177), channel_id=1, source_target_pairs={{0,256},{256,0},{1,257},{257,1},{2,258},{258,2},{3,259},{259,3},{4... | collective-permute-start | bytes 442376 | tf_op jit(solution)/shard_map/ppermute | solution.py:55
  255.7 7.7 %collective-permute-start.12 = (f32[72,512]{1,0:T(8,128)S(1)}, f32[72,512]{1,0:T(8,128)S(1)}, u32[]{:S(2)}, u32[]{:S(2)}) collective-permute-start(f32[72,512]{1,0:T(8,128)S(1)} %add.178), channel_id=1, source_target_pairs={{0,16},{8,24},{16,0},{24,8},{1,17},{9,25},{17,1},{25,9},{2,18},{10... | collective-permute-start | bytes 442376 | tf_op jit(solution)/shard_map/ppermute | solution.py:41
  263.4 7.6 %collective-permute-start.13 = (f32[2,72,512]{2,1,0:T(8,128)S(1)}, f32[2,72,512]{2,1,0:T(8,128)S(1)}, u32[]{:S(2)}, u32[]{:S(2)}) collective-permute-start(f32[2,72,512]{2,1,0:T(8,128)S(1)} %pad_maximum_fusion.2), channel_id=1, source_target_pairs={{0,8},{8,0},{16,24},{24,16},{1,9},{9,1},{17,25},{25,17},{2,10},{10... | collective-permute-start | bytes 884744 | tf_op jit(solution)/shard_map/ppermute | solution.py:41
  271.1 15.7 %collective-permute-start.14 = (f32[288,512]{1,0:T(8,128)S(1)}, f32[288,512]{1,0:T(8,128)S(1)}, u32[]{:S(2)}, u32[]{:S(2)}) collective-permute-start(f32[288,512]{1,0:T(8,128)S(1)} %bitcast.73), channel_id=1, source_target_pairs={{0,1},{1,0},{2,3},{3,2},{4,5},{5,4},{6,7},{7,6},{8,9},{9,8},{10,11... | collective-permute-start | bytes 1769480 | tf_op jit(solution)/shard_map/ppermute | solution.py:41
Sparse Core Ops, SparseCore 0:
  19.8 109.2 all-gather.1

commit v6 on v5

--- a/solution.py
+++ b/solution.py
@@ -17,7 +17,7 @@
     return [(i, i ^ bit) for i in range(n)]
 
 
-def _halving_scatter(blocks, axis, n, bits):
+def _halving_scatter(blocks, axis, n, bits, wire=None):
     me = lax.axis_index(axis)
     depth = n.bit_length() - 1
     rest = blocks.shape[1:]
@@ -28,7 +28,9 @@
         mine = (me // (1 << bit)) % 2
         keep = lax.dynamic_index_in_dim(blocks, mine, at, keepdims=False)
         send = lax.dynamic_index_in_dim(blocks, 1 - mine, at, keepdims=False)
-        blocks = keep + lax.ppermute(send, axis, _xor_perm(n, 1 << bit))
+        if wire is not None:
+            send = send.astype(wire)
+        blocks = keep + lax.ppermute(send, axis, _xor_perm(n, 1 << bit)).astype(keep.dtype)
         left.pop(at)
     return blocks
 
@@ -130,7 +132,7 @@
     by_core = gathered_sum.reshape(row_panels // cores, cores, tile_size, feat_width)
     by_core = jnp.moveaxis(by_core, 1, 0)
     half = _halving_scatter(by_core, "core", cores, (0,))
-    summed_own = _halving_scatter(half, "y_lo", sizes["y_lo"], (0, 1))
+    summed_own = _halving_scatter(half, "y_lo", sizes["y_lo"], (0, 1), jnp.bfloat16)
     own_rows = own_panels * tile_size
     aggregated = summed_own.reshape(own_rows, feat_width).astype(jnp.bfloat16)
     pre = jnp.dot(aggregated, weight, preferred_element_type=jnp.float32) + bias
@@ -142,16 +144,19 @@
     local_weight = jnp.einsum("nd,nf->df", aggregated, slope, preferred_element_type=jnp.float32)
     local_bias = jnp.sum(slope.astype(jnp.float32), axis=0)
     width = weight.shape[0]
-    scatter_ways = sizes["core"] * sizes["x"]
-    padded_rows = -(-(width + 1) // (scatter_ways * 8)) * scatter_ways * 8
+    scatter_ways = sizes["core"] * sizes["x"] * sizes["y_lo"]
+    padded_rows = -(-(width + 1) // scatter_ways) * scatter_ways
     combined = jnp.zeros((padded_rows, feat_width), jnp.float32)
     combined = combined.at[:width].set(local_weight).at[width].set(local_bias)
-    chunk = _halving_scatter(combined.reshape(sizes["core"], -1, feat_width), "core", sizes["core"], (0,))
-    chunk = _halving_scatter(chunk.reshape(sizes["x"], -1, feat_width), "x", sizes["x"], (0, 1))
-    for name in ("y_lo", "z", "y_hi"):
+    chunk = combined
+    for name in ("core", "x", "y_lo"):
+        order = tuple(range(sizes[name].bit_length() - 1))
+        chunk = _halving_scatter(chunk.reshape(sizes[name], -1, feat_width), name, sizes[name], order)
+    for name in ("z", "y_hi"):
         chunk = _doubling_sum(chunk, name, sizes[name])
-    chunk = _doubling_gather(chunk, "x", sizes["x"], (1, 0))
-    chunk = _doubling_gather(chunk, "core", sizes["core"], (0,))
+    for name in ("y_lo", "x", "core"):
+        order = tuple(range(sizes[name].bit_length() - 2, -1, -1))
+        chunk = _doubling_gather(chunk, name, sizes[name], order)
     node_total = lax.axis_size(SECTION_AXES) * rep_count * own_rows
     factor = 1.0 / math.sqrt(node_total)
     weight_sum = chunk[:width]

time: 297 us -> 290 us (0.976)
  waiting for transfers between devices: 172 us -> 161 us
  starting transfers between devices: 59.9 us -> 64.4 us
    ppermute x6 -> x4, waiting for transfers between devices: 26.4 us -> 12.8 us  [_doubling_sum(): piece = piece + lax.ppermute(piece, axis, _xor_perm(n, bit))]
    ppermute x6 -> x4, starting transfers between devices: 22.1 us -> 15.6 us  [_doubling_sum(): piece = piece + lax.ppermute(piece, axis, _xor_perm(n, bit))]
    ppermute x3 -> x5, starting transfers between devices: 18.9 us -> 25.4 us  [_doubling_gather(): other = lax.ppermute(piece, axis, _xor_perm(n, 1 << bit))]
    ppermute x3 -> x5, waiting for transfers between devices: 12.1 us -> 18.4 us  [_doubling_gather(): other = lax.ppermute(piece, axis, _xor_perm(n, 1 << bit))]
    ppermute x6 -> x8, starting transfers between devices: 18.9 us -> 23.4 us  [_halving_scatter(): lax.ppermute(send, axis, _xor_perm(n, 1 << bit)).astype(keep.dtype)]
    ppermute x6 -> x8, waiting for transfers between devices: 39.8 us -> 35.9 us  [_halving_scatter(): lax.ppermute(send, axis, _xor_perm(n, 1 << bit)).astype(keep.dtype)]
  transfers between devices with their start and end apart: 16 -> 18, of which waited for: 16 -> 18; matrix products, arithmetic and copies ran while one was open for 5% -> 5% of each run, Pallas kernels for 0% -> 0%
where the time goes in v6:
time: 290 us; the launch traced here: 289 us
  waiting for transfers between devices  161 us (56%)
  starting transfers between devices  64.4 us (22%)
  between operations  14.6 us (5%)
  local copies, waits for them, and re-layouts  13.9 us (5%)
  blocking collectives  12.4 us (4%)
  Pallas kernels  11 us (4%)
  other arithmetic  10.7 us (4%)
    all_gather x1, waiting for transfers between devices, shards(): gathered = lax.all_gather(gathered, ('z', 'x'), axis=0, tiled=True)  93.5 us
    ppermute x8, waiting for transfers between devices, _halving_scatter(): lax.ppermute(send, axis, _xor_perm(n, 1 << bit)).astype(keep.dtype)  35.9 us
    ppermute x5, starting transfers between devices, _doubling_gather(): other = lax.ppermute(piece, axis, _xor_perm(n, 1 << bit))  25.4 us
    ppermute x8, starting transfers between devices, _halving_scatter(): lax.ppermute(send, axis, _xor_perm(n, 1 << bit)).astype(keep.dtype)  23.4 us
    ppermute x5, waiting for transfers between devices, _doubling_gather(): other = lax.ppermute(piece, axis, _xor_perm(n, 1 << bit))  18.4 us
    ppermute x4, starting transfers between devices, _doubling_sum(): piece = piece + lax.ppermute(piece, axis, _xor_perm(n, bit))  15.6 us
    ppermute x4, waiting for transfers between devices, _doubling_sum(): piece = piece + lax.ppermute(piece, axis, _xor_perm(n, bit))  12.8 us
    all_gather x1, blocking collectives, shards(): gathered = lax.all_gather(features, 'y_hi', axis=0, tiled=True)  12.4 us
  transfers between devices with their start and end apart: 18, of which 18 were waited for; matrix products, arithmetic and copies ran while one was open for 5% of the time, Pallas kernels for 0%

profile of v6, /device:TPU:1, one launch (start us, length us, event | category | flops | bytes accessed | tf_op | source)
XLA Modules:
  0.0 289.1 jit_solution(1681036581126230130)
XLA Ops:
  7.2 12.4 %all_gather.6 = bf16[256,512]{1,0:T(8,128)(2,1)} all-gather(bf16[128,512]{1,0:T(8,128)(2,1)} %param.11), channel_id=1, replica_groups=mesh['y_hi'=2,'z'=8,'x'=4,'y_lo'=4,'core'=2] {'y_hi'}, dimensions={0}, use_global_device_ids=true | all-gather | bytes 393216 | tf_op jit(solution)/shard_map/all_gather | solution.py:127
  21.6 4.7 %copy.13 = bf16[8,1,12,128,128]{3,4,2,0,1:T(8,128)(2,1)} copy(bf16[8,1,12,128,128]{4,3,2,1,0:T(8,128)(2,1)} %param.14) | data formatting | bytes 6291456 | tf_op args[3]
  26.4 3.9 %bitcast_select_fusion = bf16[8,12,128,128]{2,3,1,0:T(8,128)(2,1)} fusion(bf16[8,1,12,128,128]{3,4,2,0,1:T(8,128)(2,1)} %copy.13, pred[8,12]{1,0:T(8,128)(4,1)S(1)} %iota_compare_fusion), kind=kLoop, calls=%fused_computation | loop fusion | flops 1572864 | bytes 6291552 | tf_op jit(solution)/shard_map/jit(_where)/select_n | solution.py:92
  30.3 4.7 %copy.14.tiles_ref = bf16[8,128,1536]{2,1,0:T(8,128)(2,1)} copy(bf16[8,128,1536]{1,2,0:T(8,128)(2,1)} %bitcast.77) | data formatting | bytes 6291456 | tf_op jit(solution)/shard_map/reshape | solution.py:93
  35.6 93.5 %all-gather.2.cloned.1.call-done = bf16[8192,512]{1,0:T(8,128)(2,1)} async-done(((bf16[256,512]{1,0:T(8,128)(2,1)}), bf16[8192,512]{1,0:T(8,128)(2,1)}) %all-gather.2.cloned.1.call-update) | async-done | bytes 8388624 | tf_op jit(solution)/shard_map/all_gather | solution.py:128
  129.1 11.0 %shard_map.97 = f32[8,128,512]{2,1,0:T(8,128)} custom-call(s32[96]{0:T(128)} %fusion.5.cols_ref, bf16[8,128,1536]{2,1,0:T(8,128)(2,1)} %copy.14.tiles_ref, bf16[64,128,512]{2,1,0:T(8,128)(2,1)} %bitcast.78), custom_call_target="tpu_custom_call" | custom-call | flops 1610612736 | bytes 17825792 | tf_op jit(solution)/shard_map/pallas_call | solution.py:96
  142.5 3.4 %collective-permute-start = (f32[4,128,512]{2,1,0:T(8,128)}, f32[4,128,512]{2,1,0:T(8,128)}, u32[]{:S(2)}, u32[]{:S(2)}) collective-permute-start(f32[4,128,512]{2,1,0:T(8,128)} %dynamic-slice_bitcast_fusion), channel_id=1, source_target_pairs={{0,1},{1,0},{2,3},{3,2},{4,5},{5,4},{6,7},{7,6},{8,9},{9,8},{10,11... | collective-permute-start | bytes 3145736 | tf_op jit(solution)/shard_map/ppermute | solution.py:33
  146.0 2.6 collective-permute-done
  151.0 3.0 %collective-permute-start.1 = (bf16[2,128,512]{2,1,0:T(8,128)(2,1)S(1)}, bf16[2,128,512]{2,1,0:T(8,128)(2,1)S(1)}, u32[]{:S(2)}, u32[]{:S(2)}) collective-permute-start(bf16[2,128,512]{2,1,0:T(8,128)(2,1)S(1)} %fusion), channel_id=1, source_target_pairs={{0,2},{2,0},{4,6},{6,4},{1,3},{3,1},{5,7},{7,5},{8,10},{10,8},{12,... | collective-permute-start | bytes 786440 | tf_op jit(solution)/shard_map/ppermute | solution.py:33
  154.1 6.3 %collective-permute-done.1 = bf16[2,128,512]{2,1,0:T(8,128)(2,1)S(1)} collective-permute-done((bf16[2,128,512]{2,1,0:T(8,128)(2,1)S(1)}, bf16[2,128,512]{2,1,0:T(8,128)(2,1)S(1)}, u32[]{:S(2)}, u32[]{:S(2)}) %collective-permute-start.1) | collective-permute-done | bytes 262176 | tf_op jit(solution)/shard_map/ppermute | solution.py:33
  161.5 3.7 %collective-permute-start.2 = (bf16[128,512]{1,0:T(8,128)(2,1)S(1)}, bf16[128,512]{1,0:T(8,128)(2,1)S(1)}, u32[]{:S(2)}, u32[]{:S(2)}) collective-permute-start(bf16[128,512]{1,0:T(8,128)(2,1)S(1)} %fusion.2), channel_id=1, source_target_pairs={{0,4},{2,6},{4,0},{6,2},{1,5},{3,7},{5,1},{7,3},{8,12},{10,14},{12... | collective-permute-start | bytes 393224 | tf_op jit(solution)/shard_map/ppermute | solution.py:33
  165.2 6.5 %collective-permute-done.2 = bf16[128,512]{1,0:T(8,128)(2,1)S(1)} collective-permute-done((bf16[128,512]{1,0:T(8,128)(2,1)S(1)}, bf16[128,512]{1,0:T(8,128)(2,1)S(1)}, u32[]{:S(2)}, u32[]{:S(2)}) %collective-permute-start.2) | collective-permute-done | bytes 131104 | tf_op jit(solution)/shard_map/ppermute | solution.py:33
  173.3 3.2 %collective-permute-start.3 = (f32[272,512]{1,0:T(8,128)S(1)}, f32[272,512]{1,0:T(8,128)S(1)}, u32[]{:S(2)}, u32[]{:S(2)}) collective-permute-start(f32[272,512]{1,0:T(8,128)S(1)} %dynamic-slice_bitcast_fusion.1), channel_id=1, source_target_pairs={{0,1},{1,0},{2,3},{3,2},{4,5},{5,4},{6,7},{7,6},{8,9},{9,8},{10,11... | collective-permute-start | bytes 1671176 | tf_op jit(solution)/shard_map/ppermute | solution.py:33
  180.3 8.1 %collective-permute-done.4 = f32[2,68,512]{2,1,0:T(8,128)S(1)} collective-permute-done((f32[2,68,512]{2,1,0:T(8,128)S(1)}, f32[2,68,512]{2,1,0:T(8,128)S(1)}, u32[]{:S(2)}, u32[]{:S(2)}) %collective-permute-start.4) | collective-permute-done | bytes 278560 | tf_op jit(solution)/shard_map/ppermute | solution.py:33
  188.5 2.9 collective-permute-start.5
  191.4 4.5 %collective-permute-done.5 = f32[68,512]{1,0:T(8,128)S(1)} collective-permute-done((f32[68,512]{1,0:T(8,128)S(1)}, f32[68,512]{1,0:T(8,128)S(1)}, u32[]{:S(2)}, u32[]{:S(2)}) %collective-permute-start.5) | collective-permute-done | bytes 139296 | tf_op jit(solution)/shard_map/ppermute | solution.py:33
  197.9 3.4 %collective-permute-done.6 = f32[2,17,512]{2,1,0:T(8,128)S(1)} collective-permute-done((f32[2,17,512]{2,1,0:T(8,128)S(1)}, f32[2,17,512]{2,1,0:T(8,128)S(1)}, u32[]{:S(2)}, u32[]{:S(2)}) %collective-permute-start.6) | collective-permute-done | bytes 69664 | tf_op jit(solution)/shard_map/ppermute | solution.py:33
  201.4 3.4 %collective-permute-start.7 = (f32[17,512]{1,0:T(8,128)S(1)}, f32[17,512]{1,0:T(8,128)S(1)}, u32[]{:S(2)}, u32[]{:S(2)}) collective-permute-start(f32[17,512]{1,0:T(8,128)S(1)} %dynamic-slice_bitcast_fusion.5), channel_id=1, source_target_pairs={{0,4},{2,6},{4,0},{6,2},{1,5},{3,7},{5,1},{7,3},{8,12},{10,14},{12... | collective-permute-start | bytes 104456 | tf_op jit(solution)/shard_map/ppermute | solution.py:33
  204.8 2.9 collective-permute-done.7
  209.6 2.9 %collective-permute-done.8 = f32[17,512]{1,0:T(8,128)S(1)} collective-permute-done((f32[17,512]{1,0:T(8,128)S(1)}, f32[17,512]{1,0:T(8,128)S(1)}, u32[]{:S(2)}, u32[]{:S(2)}) %collective-permute-start.8) | collective-permute-done | bytes 34848 | tf_op jit(solution)/shard_map/ppermute | solution.py:57
  212.5 3.3 %collective-permute-start.9 = (f32[17,512]{1,0:T(8,128)S(1)}, f32[17,512]{1,0:T(8,128)S(1)}, u32[]{:S(2)}, u32[]{:S(2)}) collective-permute-start(f32[17,512]{1,0:T(8,128)S(1)} %add.185), channel_id=1, source_target_pairs={{0,64},{32,96},{64,0},{96,32},{128,192},{160,224},{192,128},{224,1... | collective-permute-start | bytes 104456 | tf_op jit(solution)/shard_map/ppermute | solution.py:57
  215.7 2.8 collective-permute-done.9
  218.6 3.7 %collective-permute-start.10 = (f32[17,512]{1,0:T(8,128)S(1)}, f32[17,512]{1,0:T(8,128)S(1)}, u32[]{:S(2)}, u32[]{:S(2)}) collective-permute-start(f32[17,512]{1,0:T(8,128)S(1)} %add.186), channel_id=1, source_target_pairs={{0,128},{32,160},{64,192},{96,224},{128,0},{160,32},{192,64},{224,... | collective-permute-start | bytes 104456 | tf_op jit(solution)/shard_map/ppermute | solution.py:57
  222.3 5.1 %collective-permute-done.10 = f32[17,512]{1,0:T(8,128)S(1)} collective-permute-done((f32[17,512]{1,0:T(8,128)S(1)}, f32[17,512]{1,0:T(8,128)S(1)}, u32[]{:S(2)}, u32[]{:S(2)}) %collective-permute-start.10) | collective-permute-done | bytes 34848 | tf_op jit(solution)/shard_map/ppermute | solution.py:57
  227.4 6.8 %collective-permute-start.11 = (f32[17,512]{1,0:T(8,128)S(1)}, f32[17,512]{1,0:T(8,128)S(1)}, u32[]{:S(2)}, u32[]{:S(2)}) collective-permute-start(f32[17,512]{1,0:T(8,128)S(1)} %add.187), channel_id=1, source_target_pairs={{0,256},{256,0},{1,257},{257,1},{2,258},{258,2},{3,259},{259,3},{4... | collective-permute-start | bytes 104456 | tf_op jit(solution)/shard_map/ppermute | solution.py:57
  236.1 2.7 collective-permute-start.12
  238.9 3.4 %collective-permute-done.12 = f32[17,512]{1,0:T(8,128)S(1)} collective-permute-done((f32[17,512]{1,0:T(8,128)S(1)}, f32[17,512]{1,0:T(8,128)S(1)}, u32[]{:S(2)}, u32[]{:S(2)}) %collective-permute-start.12) | collective-permute-done | bytes 34848 | tf_op jit(solution)/shard_map/ppermute | solution.py:43
  244.2 3.4 %collective-permute-done.13 = f32[2,17,512]{2,1,0:T(8,128)S(1)} collective-permute-done((f32[2,17,512]{2,1,0:T(8,128)S(1)}, f32[2,17,512]{2,1,0:T(8,128)S(1)}, u32[]{:S(2)}, u32[]{:S(2)}) %collective-permute-start.13) | collective-permute-done | bytes 69664 | tf_op jit(solution)/shard_map/ppermute | solution.py:43
  247.8 2.7 collective-permute-start.14
  250.5 4.7 %collective-permute-done.14 = f32[68,512]{1,0:T(8,128)S(1)} collective-permute-done((f32[68,512]{1,0:T(8,128)S(1)}, f32[68,512]{1,0:T(8,128)S(1)}, u32[]{:S(2)}, u32[]{:S(2)}) %collective-permute-start.14) | collective-permute-done | bytes 139296 | tf_op jit(solution)/shard_map/ppermute | solution.py:43
  257.3 5.4 %collective-permute-done.15 = f32[2,68,512]{2,1,0:T(8,128)S(1)} collective-permute-done((f32[2,68,512]{2,1,0:T(8,128)S(1)}, f32[2,68,512]{2,1,0:T(8,128)S(1)}, u32[]{:S(2)}, u32[]{:S(2)}) %collective-permute-start.15) | collective-permute-done | bytes 278560 | tf_op jit(solution)/shard_map/ppermute | solution.py:43
  262.9 15.9 %collective-permute-start.16 = (f32[272,512]{1,0:T(8,128)S(1)}, f32[272,512]{1,0:T(8,128)S(1)}, u32[]{:S(2)}, u32[]{:S(2)}) collective-permute-start(f32[272,512]{1,0:T(8,128)S(1)} %reshape.121), channel_id=1, source_target_pairs={{0,1},{1,0},{2,3},{3,2},{4,5},{5,4},{6,7},{7,6},{8,9},{9,8},{10,11... | collective-permute-start | bytes 1671176 | tf_op jit(solution)/shard_map/ppermute | solution.py:43
  (68 shorter events, 27.5 us)
Async XLA Ops:
  7.2 164.6 %copy-start = (bf16[512,512]{1,0:T(8,128)(2,1)S(1)}, bf16[512,512]{1,0:T(8,128)(2,1)}, u32[]{:S(2)}) copy-start(bf16[512,512]{1,0:T(8,128)(2,1)} %param.15) | copy-start | bytes 1572868
  7.2 121.9 %all-gather.2.cloned.1.call-start = ((), (), s32[]{:S(2)}) async-start(), calls=%async_computation | async-start | bytes 8650752 | tf_op jit(solution)/shard_map/all_gather | solution.py:128
  21.6 4.7 %copy-start.5 = (s32[8,1]{0,1:T(1,128)S(1)}, s32[8,1]{0,1:T(1,128)}, u32[]{:S(2)}) copy-start(s32[8,1]{0,1:T(1,128)} %param.13) | copy-start | bytes 100
  140.1 8.4 %copy-start.1 = (f32[8,128,512]{2,1,0:T(8,128)S(1)}, f32[8,128,512]{2,1,0:T(8,128)}, u32[]{:S(2)}) copy-start(f32[8,128,512]{2,1,0:T(8,128)} %shard_map.97) | copy-start | bytes 6291460
  142.5 6.0 %collective-permute-start = (f32[4,128,512]{2,1,0:T(8,128)}, f32[4,128,512]{2,1,0:T(8,128)}, u32[]{:S(2)}, u32[]{:S(2)}) collective-permute-start(f32[4,128,512]{2,1,0:T(8,128)} %dynamic-slice_bitcast_fusion), channel_id=1, source_target_pairs={{0,1},{1,0},{2,3},{3,2},{4,5},{5,4},{6,7},{7,6},{8,9},{9,8},{10,11... | collective-permute-start | bytes 3145736 | tf_op jit(solution)/shard_map/ppermute | solution.py:33
  150.0 1.0 copy-start.2
  150.0 21.8 %copy-start.3 = (bf16[128,512]{1,0:T(8,128)(2,1)S(1)}, bf16[128,512]{1,0:T(8,128)(2,1)}, u32[]{:S(2)}) copy-start(bf16[128,512]{1,0:T(8,128)(2,1)} %param.17) | copy-start | bytes 393220
  150.0 21.8 %copy-start.4 = (f32[512]{0:T(512)S(1)}, f32[512]{0:T(512)}, u32[]{:S(2)}) copy-start(f32[512]{0:T(512)} %param.16) | copy-start | bytes 6148
  151.0 9.4 %collective-permute-start.1 = (bf16[2,128,512]{2,1,0:T(8,128)(2,1)S(1)}, bf16[2,128,512]{2,1,0:T(8,128)(2,1)S(1)}, u32[]{:S(2)}, u32[]{:S(2)}) collective-permute-start(bf16[2,128,512]{2,1,0:T(8,128)(2,1)S(1)} %fusion), channel_id=1, source_target_pairs={{0,2},{2,0},{4,6},{6,4},{1,3},{3,1},{5,7},{7,5},{8,10},{10,8},{12,... | collective-permute-start | bytes 786440 | tf_op jit(solution)/shard_map/ppermute | solution.py:33
  161.5 10.2 %collective-permute-start.2 = (bf16[128,512]{1,0:T(8,128)(2,1)S(1)}, bf16[128,512]{1,0:T(8,128)(2,1)S(1)}, u32[]{:S(2)}, u32[]{:S(2)}) collective-permute-start(bf16[128,512]{1,0:T(8,128)(2,1)S(1)} %fusion.2), channel_id=1, source_target_pairs={{0,4},{2,6},{4,0},{6,2},{1,5},{3,7},{5,1},{7,3},{8,12},{10,14},{12... | collective-permute-start | bytes 393224 | tf_op jit(solution)/shard_map/ppermute | solution.py:33
  173.3 4.8 %collective-permute-start.3 = (f32[272,512]{1,0:T(8,128)S(1)}, f32[272,512]{1,0:T(8,128)S(1)}, u32[]{:S(2)}, u32[]{:S(2)}) collective-permute-start(f32[272,512]{1,0:T(8,128)S(1)} %dynamic-slice_bitcast_fusion.1), channel_id=1, source_target_pairs={{0,1},{1,0},{2,3},{3,2},{4,5},{5,4},{6,7},{7,6},{8,9},{9,8},{10,11... | collective-permute-start | bytes 1671176 | tf_op jit(solution)/shard_map/ppermute | solution.py:33
  178.3 10.1 %collective-permute-start.4 = (f32[2,68,512]{2,1,0:T(8,128)S(1)}, f32[2,68,512]{2,1,0:T(8,128)S(1)}, u32[]{:S(2)}, u32[]{:S(2)}) collective-permute-start(f32[2,68,512]{2,1,0:T(8,128)S(1)} %dynamic-slice_bitcast_fusion.2), channel_id=1, source_target_pairs={{0,8},{8,0},{16,24},{24,16},{1,9},{9,1},{17,25},{25,17},{2,10},{10... | collective-permute-start | bytes 835592 | tf_op jit(solution)/shard_map/ppermute | solution.py:33
  188.5 7.4 %collective-permute-start.5 = (f32[68,512]{1,0:T(8,128)S(1)}, f32[68,512]{1,0:T(8,128)S(1)}, u32[]{:S(2)}, u32[]{:S(2)}) collective-permute-start(f32[68,512]{1,0:T(8,128)S(1)} %dynamic-slice_bitcast_fusion.3), channel_id=1, source_target_pairs={{0,16},{8,24},{16,0},{24,8},{1,17},{9,25},{17,1},{25,9},{2,18},{10... | collective-permute-start | bytes 417800 | tf_op jit(solution)/shard_map/ppermute | solution.py:33
  196.0 5.4 %collective-permute-start.6 = (f32[2,17,512]{2,1,0:T(8,128)S(1)}, f32[2,17,512]{2,1,0:T(8,128)S(1)}, u32[]{:S(2)}, u32[]{:S(2)}) collective-permute-start(f32[2,17,512]{2,1,0:T(8,128)S(1)} %dynamic-slice_bitcast_fusion.4), channel_id=1, source_target_pairs={{0,2},{2,0},{4,6},{6,4},{1,3},{3,1},{5,7},{7,5},{8,10},{10,8},{12,... | collective-permute-start | bytes 208904 | tf_op jit(solution)/shard_map/ppermute | solution.py:33
  201.4 6.3 %collective-permute-start.7 = (f32[17,512]{1,0:T(8,128)S(1)}, f32[17,512]{1,0:T(8,128)S(1)}, u32[]{:S(2)}, u32[]{:S(2)}) collective-permute-start(f32[17,512]{1,0:T(8,128)S(1)} %dynamic-slice_bitcast_fusion.5), channel_id=1, source_target_pairs={{0,4},{2,6},{4,0},{6,2},{1,5},{3,7},{5,1},{7,3},{8,12},{10,14},{12... | collective-permute-start | bytes 104456 | tf_op jit(solution)/shard_map/ppermute | solution.py:33
  207.6 4.8 %collective-permute-start.8 = (f32[17,512]{1,0:T(8,128)S(1)}, f32[17,512]{1,0:T(8,128)S(1)}, u32[]{:S(2)}, u32[]{:S(2)}) collective-permute-start(f32[17,512]{1,0:T(8,128)S(1)} %bitcast_add_fusion.7), channel_id=1, source_target_pairs={{0,32},{32,0},{64,96},{96,64},{128,160},{160,128},{192,224},{224,1... | collective-permute-start | bytes 104456 | tf_op jit(solution)/shard_map/ppermute | solution.py:57
  212.5 6.1 %collective-permute-start.9 = (f32[17,512]{1,0:T(8,128)S(1)}, f32[17,512]{1,0:T(8,128)S(1)}, u32[]{:S(2)}, u32[]{:S(2)}) collective-permute-start(f32[17,512]{1,0:T(8,128)S(1)} %add.185), channel_id=1, source_target_pairs={{0,64},{32,96},{64,0},{96,32},{128,192},{160,224},{192,128},{224,1... | collective-permute-start | bytes 104456 | tf_op jit(solution)/shard_map/ppermute | solution.py:57
  218.6 8.8 %collective-permute-start.10 = (f32[17,512]{1,0:T(8,128)S(1)}, f32[17,512]{1,0:T(8,128)S(1)}, u32[]{:S(2)}, u32[]{:S(2)}) collective-permute-start(f32[17,512]{1,0:T(8,128)S(1)} %add.186), channel_id=1, source_target_pairs={{0,128},{32,160},{64,192},{96,224},{128,0},{160,32},{192,64},{224,... | collective-permute-start | bytes 104456 | tf_op jit(solution)/shard_map/ppermute | solution.py:57
  227.4 8.7 %collective-permute-start.11 = (f32[17,512]{1,0:T(8,128)S(1)}, f32[17,512]{1,0:T(8,128)S(1)}, u32[]{:S(2)}, u32[]{:S(2)}) collective-permute-start(f32[17,512]{1,0:T(8,128)S(1)} %add.187), channel_id=1, source_target_pairs={{0,256},{256,0},{1,257},{257,1},{2,258},{258,2},{3,259},{259,3},{4... | collective-permute-start | bytes 104456 | tf_op jit(solution)/shard_map/ppermute | solution.py:57
  236.1 6.2 %collective-permute-start.12 = (f32[17,512]{1,0:T(8,128)S(1)}, f32[17,512]{1,0:T(8,128)S(1)}, u32[]{:S(2)}, u32[]{:S(2)}) collective-permute-start(f32[17,512]{1,0:T(8,128)S(1)} %add.188), channel_id=1, source_target_pairs={{0,4},{2,6},{4,0},{6,2},{1,5},{3,7},{5,1},{7,3},{8,12},{10,14},{12... | collective-permute-start | bytes 104456 | tf_op jit(solution)/shard_map/ppermute | solution.py:43
  242.3 5.4 %collective-permute-start.13 = (f32[2,17,512]{2,1,0:T(8,128)S(1)}, f32[2,17,512]{2,1,0:T(8,128)S(1)}, u32[]{:S(2)}, u32[]{:S(2)}) collective-permute-start(f32[2,17,512]{2,1,0:T(8,128)S(1)} %pad_maximum_fusion.2), channel_id=1, source_target_pairs={{0,2},{2,0},{4,6},{6,4},{1,3},{3,1},{5,7},{7,5},{8,10},{10,8},{12,... | collective-permute-start | bytes 208904 | tf_op jit(solution)/shard_map/ppermute | solution.py:43
  247.8 7.4 %collective-permute-start.14 = (f32[68,512]{1,0:T(8,128)S(1)}, f32[68,512]{1,0:T(8,128)S(1)}, u32[]{:S(2)}, u32[]{:S(2)}) collective-permute-start(f32[68,512]{1,0:T(8,128)S(1)} %reshape.120), channel_id=1, source_target_pairs={{0,16},{8,24},{16,0},{24,8},{1,17},{9,25},{17,1},{25,9},{2,18},{10... | collective-permute-start | bytes 417800 | tf_op jit(solution)/shard_map/ppermute | solution.py:43
  255.2 7.5 %collective-permute-start.15 = (f32[2,68,512]{2,1,0:T(8,128)S(1)}, f32[2,68,512]{2,1,0:T(8,128)S(1)}, u32[]{:S(2)}, u32[]{:S(2)}) collective-permute-start(f32[2,68,512]{2,1,0:T(8,128)S(1)} %pad_maximum_fusion.1), channel_id=1, source_target_pairs={{0,8},{8,0},{16,24},{24,16},{1,9},{9,1},{17,25},{25,17},{2,10},{10... | collective-permute-start | bytes 835592 | tf_op jit(solution)/shard_map/ppermute | solution.py:43
  262.9 17.5 %collective-permute-start.16 = (f32[272,512]{1,0:T(8,128)S(1)}, f32[272,512]{1,0:T(8,128)S(1)}, u32[]{:S(2)}, u32[]{:S(2)}) collective-permute-start(f32[272,512]{1,0:T(8,128)S(1)} %reshape.121), channel_id=1, source_target_pairs={{0,1},{1,0},{2,3},{3,2},{4,5},{5,4},{6,7},{7,6},{8,9},{9,8},{10,11... | collective-permute-start | bytes 1671176 | tf_op jit(solution)/shard_map/ppermute | solution.py:43
Sparse Core Ops, SparseCore 0:
  19.8 109.2 all-gather.1

commit v7 on v5

--- a/solution.py
+++ b/solution.py
@@ -57,35 +57,39 @@
     return piece
 
 
-def _aggregate_kernel(cols_ref, tiles_ref, panels_hbm, out_ref, buf, sems):
+def _aggregate_kernel(cols_ref, tiles_ref, near_hbm, far_hbm, out_ref, buf, sems):
     groups, slots = out_ref.shape[0], buf.shape[1]
+    half = near_hbm.shape[0]
 
-    def copies(g, slot):
-        return [
-            pltpu.make_async_copy(panels_hbm.at[cols_ref[g * slots + k]], buf.at[slot, k], sems.at[slot, k])
-            for k in range(slots)
-        ]
+    def start(g, slot):
+        for k in range(slots):
+            col = cols_ref[g * slots + k]
 
-    pending = copies(0, 0)
-    for c in pending:
-        c.start()
+            @pl.when(col < half)
+            def _near(col=col, k=k):
+                pltpu.make_async_copy(near_hbm.at[col], buf.at[slot, k], sems.at[slot, k]).start()
+
+            @pl.when(col >= half)
+            def _far(col=col, k=k):
+                pltpu.make_async_copy(far_hbm.at[col - half], buf.at[slot, k], sems.at[slot, k]).start()
+
+    def wait(slot):
+        for k in range(slots):
+            pltpu.make_async_copy(near_hbm.at[0], buf.at[slot, k], sems.at[slot, k]).wait()
+
+    start(0, 0)
     for g in range(groups):
         slot = g % 2
         if g + 1 < groups:
-            ahead = copies(g + 1, 1 - slot)
-            for c in ahead:
-                c.start()
-        for c in pending:
-            c.wait()
+            start(g + 1, 1 - slot)
+        wait(slot)
         rhs = buf[slot].reshape(slots * buf.shape[2], buf.shape[3])
         out_ref[g] = jnp.dot(tiles_ref[g], rhs, preferred_element_type=jnp.float32)
-        if g + 1 < groups:
-            pending = ahead
 
 
-def _aggregate(cols, counts, tiles, panels):
+def _aggregate(cols, counts, tiles, near, far):
     groups, slots, tile_size, _ = tiles.shape
-    feat_width = panels.shape[-1]
+    feat_width = near.shape[-1]
     live = jnp.arange(slots, dtype=jnp.int32)[None, :] < counts[:, None]
     wide = jnp.where(live[:, :, None, None], tiles, jnp.zeros((), tiles.dtype))
     wide = wide.transpose(0, 2, 1, 3).reshape(groups, tile_size, slots * tile_size)
@@ -98,14 +102,15 @@
             pl.BlockSpec(memory_space=pltpu.SMEM),
             pl.BlockSpec(memory_space=pltpu.VMEM),
             pl.BlockSpec(memory_space=pl.ANY),
+            pl.BlockSpec(memory_space=pl.ANY),
         ],
         out_specs=pl.BlockSpec(memory_space=pltpu.VMEM),
         scratch_shapes=[
-            pltpu.VMEM((2, slots, tile_size, feat_width), panels.dtype),
+            pltpu.VMEM((2, slots, tile_size, feat_width), near.dtype),
             pltpu.SemaphoreType.DMA((2, slots)),
         ],
         cost_estimate=pl.CostEstimate(flops=flops, bytes_accessed=moved, transcendentals=0),
-    )(jnp.clip(cols, 0, panels.shape[0] - 1).reshape(-1), wide, panels)
+    )(jnp.clip(cols, 0, 2 * near.shape[0] - 1).reshape(-1), wide, near, far)
 
 
 def shards(features, col_panels, block_counts, block_values, weight, bias, cotangent):
@@ -118,14 +123,16 @@
     global_cols = col_panels[:, 0, :]
     section_of = global_cols // (own_panels * rep_count)
     low = sizes["z"] * sizes["x"]
-    gathered_pos = (section_of % low) * sizes["y_hi"] + section_of // low
-    local_cols = gathered_pos * own_panels + global_cols % own_panels
+    far_side = (section_of // low != lax.axis_index("y_hi")).astype(jnp.int32)
+    local_cols = (far_side * low + section_of % low) * own_panels + global_cols % own_panels
     live_counts = block_counts[:, 0]
     tiles = block_values[:, 0]
-    gathered = lax.all_gather(features, "y_hi", axis=0, tiled=True)
-    gathered = lax.all_gather(gathered, ("z", "x"), axis=0, tiled=True)
-    all_panels = gathered.reshape(-1, tile_size, feat_width)
-    gathered_sum = _aggregate(local_cols, live_counts, tiles, all_panels)
+    near = lax.all_gather(features, ("z", "x"), axis=0, tiled=True)
+    partner = lax.ppermute(features, "y_hi", _xor_perm(sizes["y_hi"], 1))
+    far = lax.all_gather(partner, ("z", "x"), axis=0, tiled=True)
+    near = near.reshape(-1, tile_size, feat_width)
+    far = far.reshape(-1, tile_size, feat_width)
+    gathered_sum = _aggregate(local_cols, live_counts, tiles, near, far)
     cores = sizes["core"]
     by_core = gathered_sum.reshape(row_panels // cores, cores, tile_size, feat_width)
     by_core = jnp.moveaxis(by_core, 1, 0)

time: 297 us -> 361 us (1.22)
  waiting for transfers between devices: 172 us -> 233 us
  starting transfers between devices: 59.9 us -> 75.7 us
  blocking collectives: 12.4 us -> 0 us
    all_gather x1 -> x2, waiting for transfers between devices: 93.5 us -> 151 us  [the longest x1 88.1 us: shards(): far = lax.all_gather(partner, ('z', 'x'), axis=0, tiled=True)]
    all_gather x1 -> x0, blocking collectives: 12.4 us -> none  [shards(): gathered = lax.all_gather(features, 'y_hi', axis=0, tiled=True)]
    ppermute x0 -> x1, starting transfers between devices: none -> 8.27 us  [shards(): partner = lax.ppermute(features, 'y_hi', _xor_perm(sizes['y_hi'], 1))]
    ppermute x0 -> x1, waiting for transfers between devices: none -> 5.2 us  [shards(): partner = lax.ppermute(features, 'y_hi', _xor_perm(sizes['y_hi'], 1))]
  transfers between devices with their start and end apart: 16 -> 18, of which waited for: 16 -> 18; matrix products, arithmetic and copies ran while one was open for 5% -> 4% of each run, Pallas kernels for 0% -> 0%
where the time goes in v7:
time: 361 us; the launch traced here: 360 us
  waiting for transfers between devices  233 us (65%)
  starting transfers between devices  75.7 us (21%)
  between operations  14.6 us (4%)
  local copies, waits for them, and re-layouts  14.4 us (4%)
  Pallas kernels  10.9 us (3%)
  other arithmetic  10.7 us (3%)
    all_gather x1, waiting for transfers between devices, shards(): far = lax.all_gather(partner, ('z', 'x'), axis=0, tiled=True)  88.1 us
    all_gather x1, waiting for transfers between devices, shards(): near = lax.all_gather(features, ('z', 'x'), axis=0, tiled=True)  63 us
    ppermute x6, waiting for transfers between devices, _halving_scatter(): blocks = keep + lax.ppermute(send, axis, _xor_perm(n, 1 << bit))  40 us
    ppermute x6, waiting for transfers between devices, _doubling_sum(): piece = piece + lax.ppermute(piece, axis, _xor_perm(n, bit))  24.8 us
    ppermute x6, starting transfers between devices, _doubling_sum(): piece = piece + lax.ppermute(piece, axis, _xor_perm(n, bit))  23.8 us
    ppermute x6, starting transfers between devices, _halving_scatter(): blocks = keep + lax.ppermute(send, axis, _xor_perm(n, 1 << bit))  21.8 us
    ppermute x3, starting transfers between devices, _doubling_gather(): other = lax.ppermute(piece, axis, _xor_perm(n, 1 << bit))  21.8 us
    pallas_call x1, Pallas kernels, _aggregate(): pl.pallas_call(_aggregate_kernel, out_shape=jax.ShapeDtypeStruct((groups,...  10.9 us
  transfers between devices with their start and end apart: 18, of which 18 were waited for; matrix products, arithmetic and copies ran while one was open for 4% of the time, Pallas kernels for 0%

profile of v7, /device:TPU:1, one launch (start us, length us, event | category | flops | bytes accessed | tf_op | source)
XLA Modules:
  0.0 360.3 jit_solution(5060990699426354675)
XLA Ops:
  8.0 8.3 %collective-permute-start = (bf16[128,512]{1,0:T(8,128)(2,1)}, bf16[128,512]{1,0:T(8,128)(2,1)S(1)}, u32[]{:S(2)}, u32[]{:S(2)}) collective-permute-start(bf16[128,512]{1,0:T(8,128)(2,1)} %param.11), channel_id=1, source_target_pairs={{0,256},{256,0},{1,257},{257,1},{2,258},{258,2},{3,259},{259,3},{4... | collective-permute-start | bytes 393224 | tf_op jit(solution)/shard_map/ppermute | solution.py:131
  16.2 5.2 %collective-permute-done = bf16[128,512]{1,0:T(8,128)(2,1)S(1)} collective-permute-done((bf16[128,512]{1,0:T(8,128)(2,1)}, bf16[128,512]{1,0:T(8,128)(2,1)S(1)}, u32[]{:S(2)}, u32[]{:S(2)}) %collective-permute-start) | collective-permute-done | bytes 131104 | tf_op jit(solution)/shard_map/ppermute | solution.py:131
  24.1 4.7 %copy.12 = bf16[8,1,12,128,128]{3,4,2,0,1:T(8,128)(2,1)} copy(bf16[8,1,12,128,128]{4,3,2,1,0:T(8,128)(2,1)} %param.14) | data formatting | bytes 6291456 | tf_op args[3]
  28.8 3.9 %bitcast_select_fusion = bf16[8,12,128,128]{2,3,1,0:T(8,128)(2,1)} fusion(bf16[8,1,12,128,128]{3,4,2,0,1:T(8,128)(2,1)} %copy.12, pred[8,12]{1,0:T(8,128)(4,1)S(1)} %iota_compare_fusion), kind=kLoop, calls=%fused_computation | loop fusion | flops 1572864 | bytes 6291552 | tf_op jit(solution)/shard_map/jit(_where)/select_n | solution.py:94
  32.7 4.7 %copy.13.tiles_ref = bf16[8,128,1536]{2,1,0:T(8,128)(2,1)} copy(bf16[8,128,1536]{1,2,0:T(8,128)(2,1)} %bitcast.64) | data formatting | bytes 6291456 | tf_op jit(solution)/shard_map/reshape | solution.py:95
  38.0 63.0 %all-gather.3.cloned.1.call-done = bf16[4096,512]{1,0:T(8,128)(2,1)} async-done(((bf16[128,512]{1,0:T(8,128)(2,1)}), bf16[4096,512]{1,0:T(8,128)(2,1)}) %all-gather.3.cloned.1.call-update) | async-done | bytes 4194320 | tf_op jit(solution)/shard_map/all_gather | solution.py:130
  101.0 88.1 %all-gather.5.cloned.1.call-done = bf16[4096,512]{1,0:T(8,128)(2,1)} async-done(((bf16[128,512]{1,0:T(8,128)(2,1)}), bf16[4096,512]{1,0:T(8,128)(2,1)}) %all-gather.5.cloned.1.call-update) | async-done | bytes 4194320 | tf_op jit(solution)/shard_map/all_gather | solution.py:132
  189.1 10.9 %shard_map.97 = f32[8,128,512]{2,1,0:T(8,128)} custom-call(s32[96]{0:T(128)} %fusion.2.cols_ref, bf16[8,128,1536]{2,1,0:T(8,128)(2,1)} %copy.13.tiles_ref, bf16[32,128,512]{2,1,0:T(8,128)(2,1)} %bitcast.73, bf16[32,128,512]{2,1,0:T(8,128)(2,1)} %bitcast.74), custom_call_target="tpu_custom_call" | custom-call | flops 1610612736 | bytes 17825792 | tf_op jit(solution)/shard_map/pallas_call | solution.py:98
  202.5 6.2 %collective-permute-start.1 = (f32[4,128,512]{2,1,0:T(8,128)}, f32[4,128,512]{2,1,0:T(8,128)}, u32[]{:S(2)}, u32[]{:S(2)}) collective-permute-start(f32[4,128,512]{2,1,0:T(8,128)} %dynamic-slice_bitcast_fusion), channel_id=1, source_target_pairs={{0,1},{1,0},{2,3},{3,2},{4,5},{5,4},{6,7},{7,6},{8,9},{9,8},{10,11... | collective-permute-start | bytes 3145736 | tf_op jit(solution)/shard_map/ppermute | solution.py:31
  213.8 3.1 collective-permute-start.2
  216.9 11.9 %collective-permute-done.2 = f32[2,128,512]{2,1,0:T(8,128)S(1)} collective-permute-done((f32[2,128,512]{2,1,0:T(8,128)S(1)}, f32[2,128,512]{2,1,0:T(8,128)S(1)}, u32[]{:S(2)}, u32[]{:S(2)}) %collective-permute-start.2) | collective-permute-done | bytes 524320 | tf_op jit(solution)/shard_map/ppermute | solution.py:31
  229.9 4.2 %collective-permute-start.3 = (f32[128,512]{1,0:T(8,128)S(1)}, f32[128,512]{1,0:T(8,128)S(1)}, u32[]{:S(2)}, u32[]{:S(2)}) collective-permute-start(f32[128,512]{1,0:T(8,128)S(1)} %dynamic-slice_bitcast_fusion.4), channel_id=1, source_target_pairs={{0,4},{2,6},{4,0},{6,2},{1,5},{3,7},{5,1},{7,3},{8,12},{10,14},{12... | collective-permute-start | bytes 786440 | tf_op jit(solution)/shard_map/ppermute | solution.py:31
  234.1 11.6 %collective-permute-done.3 = f32[128,512]{1,0:T(8,128)S(1)} collective-permute-done((f32[128,512]{1,0:T(8,128)S(1)}, f32[128,512]{1,0:T(8,128)S(1)}, u32[]{:S(2)}, u32[]{:S(2)}) %collective-permute-start.3) | collective-permute-done | bytes 262176 | tf_op jit(solution)/shard_map/ppermute | solution.py:31
  247.3 3.3 collective-permute-start.4
  254.3 8.1 %collective-permute-done.5 = f32[2,72,512]{2,1,0:T(8,128)S(1)} collective-permute-done((f32[2,72,512]{2,1,0:T(8,128)S(1)}, f32[2,72,512]{2,1,0:T(8,128)S(1)}, u32[]{:S(2)}, u32[]{:S(2)}) %collective-permute-start.5) | collective-permute-done | bytes 294944 | tf_op jit(solution)/shard_map/ppermute | solution.py:31
  262.5 3.1 collective-permute-start.6
  265.6 4.3 %collective-permute-done.6 = f32[72,512]{1,0:T(8,128)S(1)} collective-permute-done((f32[72,512]{1,0:T(8,128)S(1)}, f32[72,512]{1,0:T(8,128)S(1)}, u32[]{:S(2)}, u32[]{:S(2)}) %collective-permute-start.6) | collective-permute-done | bytes 147488 | tf_op jit(solution)/shard_map/ppermute | solution.py:31
  272.2 3.7 %collective-permute-done.7 = f32[72,512]{1,0:T(8,128)S(1)} collective-permute-done((f32[72,512]{1,0:T(8,128)S(1)}, f32[72,512]{1,0:T(8,128)S(1)}, u32[]{:S(2)}, u32[]{:S(2)}) %collective-permute-start.7) | collective-permute-done | bytes 147488 | tf_op jit(solution)/shard_map/ppermute | solution.py:55
  275.8 3.9 %collective-permute-start.8 = (f32[72,512]{1,0:T(8,128)S(1)}, f32[72,512]{1,0:T(8,128)S(1)}, u32[]{:S(2)}, u32[]{:S(2)}) collective-permute-start(f32[72,512]{1,0:T(8,128)S(1)} %add.173), channel_id=1, source_target_pairs={{0,4},{2,6},{4,0},{6,2},{1,5},{3,7},{5,1},{7,3},{8,12},{10,14},{12... | collective-permute-start | bytes 442376 | tf_op jit(solution)/shard_map/ppermute | solution.py:55
  279.7 4.5 %collective-permute-done.8 = f32[72,512]{1,0:T(8,128)S(1)} collective-permute-done((f32[72,512]{1,0:T(8,128)S(1)}, f32[72,512]{1,0:T(8,128)S(1)}, u32[]{:S(2)}, u32[]{:S(2)}) %collective-permute-start.8) | collective-permute-done | bytes 147488 | tf_op jit(solution)/shard_map/ppermute | solution.py:55
  284.2 2.7 collective-permute-start.9
  286.9 3.2 collective-permute-done.9
  290.1 3.0 collective-permute-start.10
  293.2 5.3 %collective-permute-done.10 = f32[72,512]{1,0:T(8,128)S(1)} collective-permute-done((f32[72,512]{1,0:T(8,128)S(1)}, f32[72,512]{1,0:T(8,128)S(1)}, u32[]{:S(2)}, u32[]{:S(2)}) %collective-permute-start.10) | collective-permute-done | bytes 147488 | tf_op jit(solution)/shard_map/ppermute | solution.py:55
  298.5 4.4 %collective-permute-start.11 = (f32[72,512]{1,0:T(8,128)S(1)}, f32[72,512]{1,0:T(8,128)S(1)}, u32[]{:S(2)}, u32[]{:S(2)}) collective-permute-start(f32[72,512]{1,0:T(8,128)S(1)} %add.176), channel_id=1, source_target_pairs={{0,128},{32,160},{64,192},{96,224},{128,0},{160,32},{192,64},{224,... | collective-permute-start | bytes 442376 | tf_op jit(solution)/shard_map/ppermute | solution.py:55
  303.0 5.5 %collective-permute-done.11 = f32[72,512]{1,0:T(8,128)S(1)} collective-permute-done((f32[72,512]{1,0:T(8,128)S(1)}, f32[72,512]{1,0:T(8,128)S(1)}, u32[]{:S(2)}, u32[]{:S(2)}) %collective-permute-start.11) | collective-permute-done | bytes 147488 | tf_op jit(solution)/shard_map/ppermute | solution.py:55
  308.5 7.6 %collective-permute-start.12 = (f32[72,512]{1,0:T(8,128)S(1)}, f32[72,512]{1,0:T(8,128)S(1)}, u32[]{:S(2)}, u32[]{:S(2)}) collective-permute-start(f32[72,512]{1,0:T(8,128)S(1)} %add.177), channel_id=1, source_target_pairs={{0,256},{256,0},{1,257},{257,1},{2,258},{258,2},{3,259},{259,3},{4... | collective-permute-start | bytes 442376 | tf_op jit(solution)/shard_map/ppermute | solution.py:55
  316.0 2.6 collective-permute-done.12
  318.7 3.6 collective-permute-start.13
  322.3 3.8 %collective-permute-done.13 = f32[72,512]{1,0:T(8,128)S(1)} collective-permute-done((f32[72,512]{1,0:T(8,128)S(1)}, f32[72,512]{1,0:T(8,128)S(1)}, u32[]{:S(2)}, u32[]{:S(2)}) %collective-permute-start.13) | collective-permute-done | bytes 147488 | tf_op jit(solution)/shard_map/ppermute | solution.py:41
  328.1 5.5 %collective-permute-done.14 = f32[2,72,512]{2,1,0:T(8,128)S(1)} collective-permute-done((f32[2,72,512]{2,1,0:T(8,128)S(1)}, f32[2,72,512]{2,1,0:T(8,128)S(1)}, u32[]{:S(2)}, u32[]{:S(2)}) %collective-permute-start.14) | collective-permute-done | bytes 294944 | tf_op jit(solution)/shard_map/ppermute | solution.py:41
  333.7 16.2 %collective-permute-start.15 = (f32[288,512]{1,0:T(8,128)S(1)}, f32[288,512]{1,0:T(8,128)S(1)}, u32[]{:S(2)}, u32[]{:S(2)}) collective-permute-start(f32[288,512]{1,0:T(8,128)S(1)} %bitcast.75), channel_id=1, source_target_pairs={{0,1},{1,0},{2,3},{3,2},{4,5},{5,4},{6,7},{7,6},{8,9},{9,8},{10,11... | collective-permute-start | bytes 1769480 | tf_op jit(solution)/shard_map/ppermute | solution.py:41
  (59 shorter events, 25.8 us)
Async XLA Ops:
  7.2 238.6 %copy-start = (bf16[512,512]{1,0:T(8,128)(2,1)S(1)}, bf16[512,512]{1,0:T(8,128)(2,1)}, u32[]{:S(2)}) copy-start(bf16[512,512]{1,0:T(8,128)(2,1)} %param.15) | copy-start | bytes 1572868
  7.2 93.8 %all-gather.3.cloned.1.call-start = ((), (), s32[]{:S(2)}) async-start(), calls=%async_computation | async-start | bytes 4325376 | tf_op jit(solution)/shard_map/all_gather | solution.py:130
  7.9 181.2 %all-gather.5.cloned.1.call-start = ((), (), s32[]{:S(2)}) async-start(), calls=%async_computation.1 | async-start | bytes 4325376 | tf_op jit(solution)/shard_map/all_gather | solution.py:132
  8.0 13.5 %collective-permute-start = (bf16[128,512]{1,0:T(8,128)(2,1)}, bf16[128,512]{1,0:T(8,128)(2,1)S(1)}, u32[]{:S(2)}, u32[]{:S(2)}) collective-permute-start(bf16[128,512]{1,0:T(8,128)(2,1)} %param.11), channel_id=1, source_target_pairs={{0,256},{256,0},{1,257},{257,1},{2,258},{258,2},{3,259},{259,3},{4... | collective-permute-start | bytes 393224 | tf_op jit(solution)/shard_map/ppermute | solution.py:131
  21.4 0.7 copy-start.3
  24.1 4.7 %copy-start.6 = (s32[8,1]{0,1:T(1,128)S(1)}, s32[8,1]{0,1:T(1,128)}, u32[]{:S(2)}) copy-start(s32[8,1]{0,1:T(1,128)} %param.13) | copy-start | bytes 100
  200.0 11.3 %copy-start.1 = (f32[8,128,512]{2,1,0:T(8,128)S(1)}, f32[8,128,512]{2,1,0:T(8,128)}, u32[]{:S(2)}) copy-start(f32[8,128,512]{2,1,0:T(8,128)} %shard_map.97) | copy-start | bytes 6291460
  202.5 8.8 %collective-permute-start.1 = (f32[4,128,512]{2,1,0:T(8,128)}, f32[4,128,512]{2,1,0:T(8,128)}, u32[]{:S(2)}, u32[]{:S(2)}) collective-permute-start(f32[4,128,512]{2,1,0:T(8,128)} %dynamic-slice_bitcast_fusion), channel_id=1, source_target_pairs={{0,1},{1,0},{2,3},{3,2},{4,5},{5,4},{6,7},{7,6},{8,9},{9,8},{10,11... | collective-permute-start | bytes 3145736 | tf_op jit(solution)/shard_map/ppermute | solution.py:31
  212.8 1.0 copy-start.2
  212.8 33.0 %copy-start.4 = (bf16[128,512]{1,0:T(8,128)(2,1)S(1)}, bf16[128,512]{1,0:T(8,128)(2,1)}, u32[]{:S(2)}) copy-start(bf16[128,512]{1,0:T(8,128)(2,1)} %param.17) | copy-start | bytes 393220
  212.8 33.0 %copy-start.5 = (f32[512]{0:T(512)S(1)}, f32[512]{0:T(512)}, u32[]{:S(2)}) copy-start(f32[512]{0:T(512)} %param.16) | copy-start | bytes 6148
  213.8 15.0 %collective-permute-start.2 = (f32[2,128,512]{2,1,0:T(8,128)S(1)}, f32[2,128,512]{2,1,0:T(8,128)S(1)}, u32[]{:S(2)}, u32[]{:S(2)}) collective-permute-start(f32[2,128,512]{2,1,0:T(8,128)S(1)} %dynamic-slice_bitcast_fusion.2), channel_id=1, source_target_pairs={{0,2},{2,0},{4,6},{6,4},{1,3},{3,1},{5,7},{7,5},{8,10},{10,8},{12,... | collective-permute-start | bytes 1572872 | tf_op jit(solution)/shard_map/ppermute | solution.py:31
  229.9 15.7 %collective-permute-start.3 = (f32[128,512]{1,0:T(8,128)S(1)}, f32[128,512]{1,0:T(8,128)S(1)}, u32[]{:S(2)}, u32[]{:S(2)}) collective-permute-start(f32[128,512]{1,0:T(8,128)S(1)} %dynamic-slice_bitcast_fusion.4), channel_id=1, source_target_pairs={{0,4},{2,6},{4,0},{6,2},{1,5},{3,7},{5,1},{7,3},{8,12},{10,14},{12... | collective-permute-start | bytes 786440 | tf_op jit(solution)/shard_map/ppermute | solution.py:31
  247.3 4.9 %collective-permute-start.4 = (f32[288,512]{1,0:T(8,128)S(1)}, f32[288,512]{1,0:T(8,128)S(1)}, u32[]{:S(2)}, u32[]{:S(2)}) collective-permute-start(f32[288,512]{1,0:T(8,128)S(1)} %dynamic-slice_bitcast_fusion.1), channel_id=1, source_target_pairs={{0,1},{1,0},{2,3},{3,2},{4,5},{5,4},{6,7},{7,6},{8,9},{9,8},{10,11... | collective-permute-start | bytes 1769480 | tf_op jit(solution)/shard_map/ppermute | solution.py:31
  252.4 10.1 %collective-permute-start.5 = (f32[2,72,512]{2,1,0:T(8,128)S(1)}, f32[2,72,512]{2,1,0:T(8,128)S(1)}, u32[]{:S(2)}, u32[]{:S(2)}) collective-permute-start(f32[2,72,512]{2,1,0:T(8,128)S(1)} %dynamic-slice_bitcast_fusion.3), channel_id=1, source_target_pairs={{0,8},{8,0},{16,24},{24,16},{1,9},{9,1},{17,25},{25,17},{2,10},{10... | collective-permute-start | bytes 884744 | tf_op jit(solution)/shard_map/ppermute | solution.py:31
  262.5 7.4 %collective-permute-start.6 = (f32[72,512]{1,0:T(8,128)S(1)}, f32[72,512]{1,0:T(8,128)S(1)}, u32[]{:S(2)}, u32[]{:S(2)}) collective-permute-start(f32[72,512]{1,0:T(8,128)S(1)} %dynamic-slice_bitcast_fusion.5), channel_id=1, source_target_pairs={{0,16},{8,24},{16,0},{24,8},{1,17},{9,25},{17,1},{25,9},{2,18},{10... | collective-permute-start | bytes 442376 | tf_op jit(solution)/shard_map/ppermute | solution.py:31
  269.9 5.9 %collective-permute-start.7 = (f32[72,512]{1,0:T(8,128)S(1)}, f32[72,512]{1,0:T(8,128)S(1)}, u32[]{:S(2)}, u32[]{:S(2)}) collective-permute-start(f32[72,512]{1,0:T(8,128)S(1)} %bitcast_add_fusion.5), channel_id=1, source_target_pairs={{0,2},{2,0},{4,6},{6,4},{1,3},{3,1},{5,7},{7,5},{8,10},{10,8},{12,... | collective-permute-start | bytes 442376 | tf_op jit(solution)/shard_map/ppermute | solution.py:55
  275.8 8.4 %collective-permute-start.8 = (f32[72,512]{1,0:T(8,128)S(1)}, f32[72,512]{1,0:T(8,128)S(1)}, u32[]{:S(2)}, u32[]{:S(2)}) collective-permute-start(f32[72,512]{1,0:T(8,128)S(1)} %add.173), channel_id=1, source_target_pairs={{0,4},{2,6},{4,0},{6,2},{1,5},{3,7},{5,1},{7,3},{8,12},{10,14},{12... | collective-permute-start | bytes 442376 | tf_op jit(solution)/shard_map/ppermute | solution.py:55
  284.2 5.9 %collective-permute-start.9 = (f32[72,512]{1,0:T(8,128)S(1)}, f32[72,512]{1,0:T(8,128)S(1)}, u32[]{:S(2)}, u32[]{:S(2)}) collective-permute-start(f32[72,512]{1,0:T(8,128)S(1)} %add.174), channel_id=1, source_target_pairs={{0,32},{32,0},{64,96},{96,64},{128,160},{160,128},{192,224},{224,1... | collective-permute-start | bytes 442376 | tf_op jit(solution)/shard_map/ppermute | solution.py:55
  290.1 8.4 %collective-permute-start.10 = (f32[72,512]{1,0:T(8,128)S(1)}, f32[72,512]{1,0:T(8,128)S(1)}, u32[]{:S(2)}, u32[]{:S(2)}) collective-permute-start(f32[72,512]{1,0:T(8,128)S(1)} %add.175), channel_id=1, source_target_pairs={{0,64},{32,96},{64,0},{96,32},{128,192},{160,224},{192,128},{224,1... | collective-permute-start | bytes 442376 | tf_op jit(solution)/shard_map/ppermute | solution.py:55
  298.5 9.9 %collective-permute-start.11 = (f32[72,512]{1,0:T(8,128)S(1)}, f32[72,512]{1,0:T(8,128)S(1)}, u32[]{:S(2)}, u32[]{:S(2)}) collective-permute-start(f32[72,512]{1,0:T(8,128)S(1)} %add.176), channel_id=1, source_target_pairs={{0,128},{32,160},{64,192},{96,224},{128,0},{160,32},{192,64},{224,... | collective-permute-start | bytes 442376 | tf_op jit(solution)/shard_map/ppermute | solution.py:55
  308.5 10.2 %collective-permute-start.12 = (f32[72,512]{1,0:T(8,128)S(1)}, f32[72,512]{1,0:T(8,128)S(1)}, u32[]{:S(2)}, u32[]{:S(2)}) collective-permute-start(f32[72,512]{1,0:T(8,128)S(1)} %add.177), channel_id=1, source_target_pairs={{0,256},{256,0},{1,257},{257,1},{2,258},{258,2},{3,259},{259,3},{4... | collective-permute-start | bytes 442376 | tf_op jit(solution)/shard_map/ppermute | solution.py:55
  318.7 7.4 %collective-permute-start.13 = (f32[72,512]{1,0:T(8,128)S(1)}, f32[72,512]{1,0:T(8,128)S(1)}, u32[]{:S(2)}, u32[]{:S(2)}) collective-permute-start(f32[72,512]{1,0:T(8,128)S(1)} %add.178), channel_id=1, source_target_pairs={{0,16},{8,24},{16,0},{24,8},{1,17},{9,25},{17,1},{25,9},{2,18},{10... | collective-permute-start | bytes 442376 | tf_op jit(solution)/shard_map/ppermute | solution.py:41
  326.1 7.5 %collective-permute-start.14 = (f32[2,72,512]{2,1,0:T(8,128)S(1)}, f32[2,72,512]{2,1,0:T(8,128)S(1)}, u32[]{:S(2)}, u32[]{:S(2)}) collective-permute-start(f32[2,72,512]{2,1,0:T(8,128)S(1)} %pad_maximum_fusion.2), channel_id=1, source_target_pairs={{0,8},{8,0},{16,24},{24,16},{1,9},{9,1},{17,25},{25,17},{2,10},{10... | collective-permute-start | bytes 884744 | tf_op jit(solution)/shard_map/ppermute | solution.py:41
  333.7 17.8 %collective-permute-start.15 = (f32[288,512]{1,0:T(8,128)S(1)}, f32[288,512]{1,0:T(8,128)S(1)}, u32[]{:S(2)}, u32[]{:S(2)}) collective-permute-start(f32[288,512]{1,0:T(8,128)S(1)} %bitcast.75), channel_id=1, source_target_pairs={{0,1},{1,0},{2,3},{3,2},{4,5},{5,4},{6,7},{7,6},{8,9},{9,8},{10,11... | collective-permute-start | bytes 1769480 | tf_op jit(solution)/shard_map/ppermute | solution.py:41
Sparse Core Ops, SparseCore 0:
  11.2 89.7 all-gather.2
  104.7 84.3 all-gather.4

commit v8 on v5

--- a/solution.py
+++ b/solution.py
@@ -97,7 +97,7 @@
         in_specs=[
             pl.BlockSpec(memory_space=pltpu.SMEM),
             pl.BlockSpec(memory_space=pltpu.VMEM),
-            pl.BlockSpec(memory_space=pl.ANY),
+            pl.BlockSpec(memory_space=pltpu.VMEM),
         ],
         out_specs=pl.BlockSpec(memory_space=pltpu.VMEM),
         scratch_shapes=[

time: 297 us -> 311 us (1.047)
  Pallas kernels: 11.1 us -> 25.3 us
    pallas_call x1, Pallas kernels: 11.1 us -> 25.3 us  [_aggregate(): pl.pallas_call(_aggregate_kernel, out_shape=jax.ShapeDtypeStruct((groups,...]
where the time goes in v8:
time: 311 us; the launch traced here: 310 us
  waiting for transfers between devices  171 us (55%)
  starting transfers between devices  60.5 us (19%)
  Pallas kernels  25.3 us (8%)
  between operations  14.5 us (5%)
  local copies, waits for them, and re-layouts  13.7 us (4%)
  blocking collectives  12.4 us (4%)
  other arithmetic  10.8 us (3%)
    all_gather x1, waiting for transfers between devices, shards(): gathered = lax.all_gather(gathered, ('z', 'x'), axis=0, tiled=True)  93.5 us
    ppermute x6, waiting for transfers between devices, _halving_scatter(): blocks = keep + lax.ppermute(send, axis, _xor_perm(n, 1 << bit))  40.1 us
    ppermute x6, waiting for transfers between devices, _doubling_sum(): piece = piece + lax.ppermute(piece, axis, _xor_perm(n, bit))  26.3 us
    pallas_call x1, Pallas kernels, _aggregate(): pl.pallas_call(_aggregate_kernel, out_shape=jax.ShapeDtypeStruct((groups,...  25.3 us
    ppermute x6, starting transfers between devices, _doubling_sum(): piece = piece + lax.ppermute(piece, axis, _xor_perm(n, bit))  22.1 us
    ppermute x3, starting transfers between devices, _doubling_gather(): other = lax.ppermute(piece, axis, _xor_perm(n, 1 << bit))  19.6 us
    ppermute x6, starting transfers between devices, _halving_scatter(): blocks = keep + lax.ppermute(send, axis, _xor_perm(n, 1 << bit))  18.8 us
    all_gather x1, blocking collectives, shards(): gathered = lax.all_gather(features, 'y_hi', axis=0, tiled=True)  12.4 us
  transfers between devices with their start and end apart: 16, of which 16 were waited for; matrix products, arithmetic and copies ran while one was open for 5% of the time, Pallas kernels for 0%

profile of v8, /device:TPU:1, one launch (start us, length us, event | category | flops | bytes accessed | tf_op | source)
XLA Modules:
  0.0 310.0 jit_solution(5482806572555134859)
XLA Ops:
  7.2 12.4 %all_gather.6 = bf16[256,512]{1,0:T(8,128)(2,1)} all-gather(bf16[128,512]{1,0:T(8,128)(2,1)} %param.11), channel_id=1, replica_groups=mesh['y_hi'=2,'z'=8,'x'=4,'y_lo'=4,'core'=2] {'y_hi'}, dimensions={0}, use_global_device_ids=true | all-gather | bytes 393216 | tf_op jit(solution)/shard_map/all_gather | solution.py:125
  21.6 4.7 %copy.12 = bf16[8,1,12,128,128]{3,4,2,0,1:T(8,128)(2,1)} copy(bf16[8,1,12,128,128]{4,3,2,1,0:T(8,128)(2,1)} %param.14) | data formatting | bytes 6291456 | tf_op args[3]
  26.4 3.9 %bitcast_select_fusion = bf16[8,12,128,128]{2,3,1,0:T(8,128)(2,1)} fusion(bf16[8,1,12,128,128]{3,4,2,0,1:T(8,128)(2,1)} %copy.12, pred[8,12]{1,0:T(8,128)(4,1)S(1)} %iota_compare_fusion), kind=kLoop, calls=%fused_computation | loop fusion | flops 1572864 | bytes 6291552 | tf_op jit(solution)/shard_map/jit(_where)/select_n | solution.py:90
  30.3 4.7 %copy.13.tiles_ref = bf16[8,128,1536]{2,1,0:T(8,128)(2,1)} copy(bf16[8,128,1536]{1,2,0:T(8,128)(2,1)} %bitcast.63) | data formatting | bytes 6291456 | tf_op jit(solution)/shard_map/reshape | solution.py:91
  35.6 93.5 %all-gather.2.cloned.1.call-done = bf16[8192,512]{1,0:T(8,128)(2,1)} async-done(((bf16[256,512]{1,0:T(8,128)(2,1)}), bf16[8192,512]{1,0:T(8,128)(2,1)}) %all-gather.2.cloned.1.call-update) | async-done | bytes 8388624 | tf_op jit(solution)/shard_map/all_gather | solution.py:126
  129.1 25.3 %shard_map.97 = f32[8,128,512]{2,1,0:T(8,128)} custom-call(s32[96]{0:T(128)} %fusion.3.cols_ref, bf16[8,128,1536]{2,1,0:T(8,128)(2,1)} %copy.13.tiles_ref, bf16[64,128,512]{2,1,0:T(8,128)(2,1)} %bitcast.64), custom_call_target="tpu_custom_call" | custom-call | flops 1610612736 | bytes 17825792 | tf_op jit(solution)/shard_map/pallas_call | solution.py:94
  154.4 2.4 dynamic-slice_bitcast_fusion
  156.9 3.3 %collective-permute-start = (f32[4,128,512]{2,1,0:T(8,128)}, f32[4,128,512]{2,1,0:T(8,128)}, u32[]{:S(2)}, u32[]{:S(2)}) collective-permute-start(f32[4,128,512]{2,1,0:T(8,128)} %dynamic-slice_bitcast_fusion), channel_id=1, source_target_pairs={{0,1},{1,0},{2,3},{3,2},{4,5},{5,4},{6,7},{7,6},{8,9},{9,8},{10,11... | collective-permute-start | bytes 3145736 | tf_op jit(solution)/shard_map/ppermute | solution.py:31
  160.2 2.6 collective-permute-done
  165.2 3.1 %collective-permute-start.1 = (f32[2,128,512]{2,1,0:T(8,128)S(1)}, f32[2,128,512]{2,1,0:T(8,128)S(1)}, u32[]{:S(2)}, u32[]{:S(2)}) collective-permute-start(f32[2,128,512]{2,1,0:T(8,128)S(1)} %dynamic-slice_bitcast_fusion.2), channel_id=1, source_target_pairs={{0,2},{2,0},{4,6},{6,4},{1,3},{3,1},{5,7},{7,5},{8,10},{10,8},{12,... | collective-permute-start | bytes 1572872 | tf_op jit(solution)/shard_map/ppermute | solution.py:31
  168.4 11.8 %collective-permute-done.1 = f32[2,128,512]{2,1,0:T(8,128)S(1)} collective-permute-done((f32[2,128,512]{2,1,0:T(8,128)S(1)}, f32[2,128,512]{2,1,0:T(8,128)S(1)}, u32[]{:S(2)}, u32[]{:S(2)}) %collective-permute-start.1) | collective-permute-done | bytes 524320 | tf_op jit(solution)/shard_map/ppermute | solution.py:31
  181.4 4.0 %collective-permute-start.2 = (f32[128,512]{1,0:T(8,128)S(1)}, f32[128,512]{1,0:T(8,128)S(1)}, u32[]{:S(2)}, u32[]{:S(2)}) collective-permute-start(f32[128,512]{1,0:T(8,128)S(1)} %dynamic-slice_bitcast_fusion.4), channel_id=1, source_target_pairs={{0,4},{2,6},{4,0},{6,2},{1,5},{3,7},{5,1},{7,3},{8,12},{10,14},{12... | collective-permute-start | bytes 786440 | tf_op jit(solution)/shard_map/ppermute | solution.py:31
  185.4 11.7 %collective-permute-done.2 = f32[128,512]{1,0:T(8,128)S(1)} collective-permute-done((f32[128,512]{1,0:T(8,128)S(1)}, f32[128,512]{1,0:T(8,128)S(1)}, u32[]{:S(2)}, u32[]{:S(2)}) %collective-permute-start.2) | collective-permute-done | bytes 262176 | tf_op jit(solution)/shard_map/ppermute | solution.py:31
  198.7 3.3 %collective-permute-start.3 = (f32[288,512]{1,0:T(8,128)S(1)}, f32[288,512]{1,0:T(8,128)S(1)}, u32[]{:S(2)}, u32[]{:S(2)}) collective-permute-start(f32[288,512]{1,0:T(8,128)S(1)} %dynamic-slice_bitcast_fusion.1), channel_id=1, source_target_pairs={{0,1},{1,0},{2,3},{3,2},{4,5},{5,4},{6,7},{7,6},{8,9},{9,8},{10,11... | collective-permute-start | bytes 1769480 | tf_op jit(solution)/shard_map/ppermute | solution.py:31
  205.8 8.1 %collective-permute-done.4 = f32[2,72,512]{2,1,0:T(8,128)S(1)} collective-permute-done((f32[2,72,512]{2,1,0:T(8,128)S(1)}, f32[2,72,512]{2,1,0:T(8,128)S(1)}, u32[]{:S(2)}, u32[]{:S(2)}) %collective-permute-start.4) | collective-permute-done | bytes 294944 | tf_op jit(solution)/shard_map/ppermute | solution.py:31
  214.0 3.1 collective-permute-start.5
  217.0 4.3 %collective-permute-done.5 = f32[72,512]{1,0:T(8,128)S(1)} collective-permute-done((f32[72,512]{1,0:T(8,128)S(1)}, f32[72,512]{1,0:T(8,128)S(1)}, u32[]{:S(2)}, u32[]{:S(2)}) %collective-permute-start.5) | collective-permute-done | bytes 147488 | tf_op jit(solution)/shard_map/ppermute | solution.py:31
  221.4 2.1 collective-permute-start.6
  223.5 3.8 %collective-permute-done.6 = f32[72,512]{1,0:T(8,128)S(1)} collective-permute-done((f32[72,512]{1,0:T(8,128)S(1)}, f32[72,512]{1,0:T(8,128)S(1)}, u32[]{:S(2)}, u32[]{:S(2)}) %collective-permute-start.6) | collective-permute-done | bytes 147488 | tf_op jit(solution)/shard_map/ppermute | solution.py:55
  227.3 3.8 %collective-permute-start.7 = (f32[72,512]{1,0:T(8,128)S(1)}, f32[72,512]{1,0:T(8,128)S(1)}, u32[]{:S(2)}, u32[]{:S(2)}) collective-permute-start(f32[72,512]{1,0:T(8,128)S(1)} %add.173), channel_id=1, source_target_pairs={{0,4},{2,6},{4,0},{6,2},{1,5},{3,7},{5,1},{7,3},{8,12},{10,14},{12... | collective-permute-start | bytes 442376 | tf_op jit(solution)/shard_map/ppermute | solution.py:55
  231.1 4.6 %collective-permute-done.7 = f32[72,512]{1,0:T(8,128)S(1)} collective-permute-done((f32[72,512]{1,0:T(8,128)S(1)}, f32[72,512]{1,0:T(8,128)S(1)}, u32[]{:S(2)}, u32[]{:S(2)}) %collective-permute-start.7) | collective-permute-done | bytes 147488 | tf_op jit(solution)/shard_map/ppermute | solution.py:55
  237.6 4.0 %collective-permute-done.8 = f32[72,512]{1,0:T(8,128)S(1)} collective-permute-done((f32[72,512]{1,0:T(8,128)S(1)}, f32[72,512]{1,0:T(8,128)S(1)}, u32[]{:S(2)}, u32[]{:S(2)}) %collective-permute-start.8) | collective-permute-done | bytes 147488 | tf_op jit(solution)/shard_map/ppermute | solution.py:55
  241.6 3.2 %collective-permute-start.9 = (f32[72,512]{1,0:T(8,128)S(1)}, f32[72,512]{1,0:T(8,128)S(1)}, u32[]{:S(2)}, u32[]{:S(2)}) collective-permute-start(f32[72,512]{1,0:T(8,128)S(1)} %add.175), channel_id=1, source_target_pairs={{0,64},{32,96},{64,0},{96,32},{128,192},{160,224},{192,128},{224,1... | collective-permute-start | bytes 442376 | tf_op jit(solution)/shard_map/ppermute | solution.py:55
  244.8 5.2 %collective-permute-done.9 = f32[72,512]{1,0:T(8,128)S(1)} collective-permute-done((f32[72,512]{1,0:T(8,128)S(1)}, f32[72,512]{1,0:T(8,128)S(1)}, u32[]{:S(2)}, u32[]{:S(2)}) %collective-permute-start.9) | collective-permute-done | bytes 147488 | tf_op jit(solution)/shard_map/ppermute | solution.py:55
  250.0 4.5 %collective-permute-start.10 = (f32[72,512]{1,0:T(8,128)S(1)}, f32[72,512]{1,0:T(8,128)S(1)}, u32[]{:S(2)}, u32[]{:S(2)}) collective-permute-start(f32[72,512]{1,0:T(8,128)S(1)} %add.176), channel_id=1, source_target_pairs={{0,128},{32,160},{64,192},{96,224},{128,0},{160,32},{192,64},{224,... | collective-permute-start | bytes 442376 | tf_op jit(solution)/shard_map/ppermute | solution.py:55
  254.5 5.6 %collective-permute-done.10 = f32[72,512]{1,0:T(8,128)S(1)} collective-permute-done((f32[72,512]{1,0:T(8,128)S(1)}, f32[72,512]{1,0:T(8,128)S(1)}, u32[]{:S(2)}, u32[]{:S(2)}) %collective-permute-start.10) | collective-permute-done | bytes 147488 | tf_op jit(solution)/shard_map/ppermute | solution.py:55
  260.1 6.6 %collective-permute-start.11 = (f32[72,512]{1,0:T(8,128)S(1)}, f32[72,512]{1,0:T(8,128)S(1)}, u32[]{:S(2)}, u32[]{:S(2)}) collective-permute-start(f32[72,512]{1,0:T(8,128)S(1)} %add.177), channel_id=1, source_target_pairs={{0,256},{256,0},{1,257},{257,1},{2,258},{258,2},{3,259},{259,3},{4... | collective-permute-start | bytes 442376 | tf_op jit(solution)/shard_map/ppermute | solution.py:55
  266.7 3.2 %collective-permute-done.11 = f32[72,512]{1,0:T(8,128)S(1)} collective-permute-done((f32[72,512]{1,0:T(8,128)S(1)}, f32[72,512]{1,0:T(8,128)S(1)}, u32[]{:S(2)}, u32[]{:S(2)}) %collective-permute-start.11) | collective-permute-done | bytes 147488 | tf_op jit(solution)/shard_map/ppermute | solution.py:55
  269.9 3.1 collective-permute-start.12
  273.0 4.3 %collective-permute-done.12 = f32[72,512]{1,0:T(8,128)S(1)} collective-permute-done((f32[72,512]{1,0:T(8,128)S(1)}, f32[72,512]{1,0:T(8,128)S(1)}, u32[]{:S(2)}, u32[]{:S(2)}) %collective-permute-start.12) | collective-permute-done | bytes 147488 | tf_op jit(solution)/shard_map/ppermute | solution.py:41
  279.3 5.6 %collective-permute-done.13 = f32[2,72,512]{2,1,0:T(8,128)S(1)} collective-permute-done((f32[2,72,512]{2,1,0:T(8,128)S(1)}, f32[2,72,512]{2,1,0:T(8,128)S(1)}, u32[]{:S(2)}, u32[]{:S(2)}) %collective-permute-start.13) | collective-permute-done | bytes 294944 | tf_op jit(solution)/shard_map/ppermute | solution.py:41
  285.0 14.6 %collective-permute-start.14 = (f32[288,512]{1,0:T(8,128)S(1)}, f32[288,512]{1,0:T(8,128)S(1)}, u32[]{:S(2)}, u32[]{:S(2)}) collective-permute-start(f32[288,512]{1,0:T(8,128)S(1)} %bitcast.73), channel_id=1, source_target_pairs={{0,1},{1,0},{2,3},{3,2},{4,5},{5,4},{6,7},{7,6},{8,9},{9,8},{10,11... | collective-permute-start | bytes 1769480 | tf_op jit(solution)/shard_map/ppermute | solution.py:41
  (53 shorter events, 19.1 us)
Async XLA Ops:
  7.2 190.0 %copy-start = (bf16[512,512]{1,0:T(8,128)(2,1)S(1)}, bf16[512,512]{1,0:T(8,128)(2,1)}, u32[]{:S(2)}) copy-start(bf16[512,512]{1,0:T(8,128)(2,1)} %param.15) | copy-start | bytes 1572868
  7.2 121.9 %all-gather.2.cloned.1.call-start = ((), (), s32[]{:S(2)}) async-start(), calls=%async_computation | async-start | bytes 8650752 | tf_op jit(solution)/shard_map/all_gather | solution.py:126
  21.6 4.7 %copy-start.5 = (s32[8,1]{0,1:T(1,128)S(1)}, s32[8,1]{0,1:T(1,128)}, u32[]{:S(2)}) copy-start(s32[8,1]{0,1:T(1,128)} %param.13) | copy-start | bytes 100
  154.4 8.3 %copy-start.1 = (f32[8,128,512]{2,1,0:T(8,128)S(1)}, f32[8,128,512]{2,1,0:T(8,128)}, u32[]{:S(2)}) copy-start(f32[8,128,512]{2,1,0:T(8,128)} %shard_map.97) | copy-start | bytes 6291460
  156.9 5.9 %collective-permute-start = (f32[4,128,512]{2,1,0:T(8,128)}, f32[4,128,512]{2,1,0:T(8,128)}, u32[]{:S(2)}, u32[]{:S(2)}) collective-permute-start(f32[4,128,512]{2,1,0:T(8,128)} %dynamic-slice_bitcast_fusion), channel_id=1, source_target_pairs={{0,1},{1,0},{2,3},{3,2},{4,5},{5,4},{6,7},{7,6},{8,9},{9,8},{10,11... | collective-permute-start | bytes 3145736 | tf_op jit(solution)/shard_map/ppermute | solution.py:31
  164.2 1.0 copy-start.2
  164.2 32.9 %copy-start.3 = (bf16[128,512]{1,0:T(8,128)(2,1)S(1)}, bf16[128,512]{1,0:T(8,128)(2,1)}, u32[]{:S(2)}) copy-start(bf16[128,512]{1,0:T(8,128)(2,1)} %param.17) | copy-start | bytes 393220
  164.2 32.9 %copy-start.4 = (f32[512]{0:T(512)S(1)}, f32[512]{0:T(512)}, u32[]{:S(2)}) copy-start(f32[512]{0:T(512)} %param.16) | copy-start | bytes 6148
  165.2 15.0 %collective-permute-start.1 = (f32[2,128,512]{2,1,0:T(8,128)S(1)}, f32[2,128,512]{2,1,0:T(8,128)S(1)}, u32[]{:S(2)}, u32[]{:S(2)}) collective-permute-start(f32[2,128,512]{2,1,0:T(8,128)S(1)} %dynamic-slice_bitcast_fusion.2), channel_id=1, source_target_pairs={{0,2},{2,0},{4,6},{6,4},{1,3},{3,1},{5,7},{7,5},{8,10},{10,8},{12,... | collective-permute-start | bytes 1572872 | tf_op jit(solution)/shard_map/ppermute | solution.py:31
  181.4 15.7 %collective-permute-start.2 = (f32[128,512]{1,0:T(8,128)S(1)}, f32[128,512]{1,0:T(8,128)S(1)}, u32[]{:S(2)}, u32[]{:S(2)}) collective-permute-start(f32[128,512]{1,0:T(8,128)S(1)} %dynamic-slice_bitcast_fusion.4), channel_id=1, source_target_pairs={{0,4},{2,6},{4,0},{6,2},{1,5},{3,7},{5,1},{7,3},{8,12},{10,14},{12... | collective-permute-start | bytes 786440 | tf_op jit(solution)/shard_map/ppermute | solution.py:31
  198.7 4.9 %collective-permute-start.3 = (f32[288,512]{1,0:T(8,128)S(1)}, f32[288,512]{1,0:T(8,128)S(1)}, u32[]{:S(2)}, u32[]{:S(2)}) collective-permute-start(f32[288,512]{1,0:T(8,128)S(1)} %dynamic-slice_bitcast_fusion.1), channel_id=1, source_target_pairs={{0,1},{1,0},{2,3},{3,2},{4,5},{5,4},{6,7},{7,6},{8,9},{9,8},{10,11... | collective-permute-start | bytes 1769480 | tf_op jit(solution)/shard_map/ppermute | solution.py:31
  203.8 10.1 %collective-permute-start.4 = (f32[2,72,512]{2,1,0:T(8,128)S(1)}, f32[2,72,512]{2,1,0:T(8,128)S(1)}, u32[]{:S(2)}, u32[]{:S(2)}) collective-permute-start(f32[2,72,512]{2,1,0:T(8,128)S(1)} %dynamic-slice_bitcast_fusion.3), channel_id=1, source_target_pairs={{0,8},{8,0},{16,24},{24,16},{1,9},{9,1},{17,25},{25,17},{2,10},{10... | collective-permute-start | bytes 884744 | tf_op jit(solution)/shard_map/ppermute | solution.py:31
  214.0 7.4 %collective-permute-start.5 = (f32[72,512]{1,0:T(8,128)S(1)}, f32[72,512]{1,0:T(8,128)S(1)}, u32[]{:S(2)}, u32[]{:S(2)}) collective-permute-start(f32[72,512]{1,0:T(8,128)S(1)} %dynamic-slice_bitcast_fusion.5), channel_id=1, source_target_pairs={{0,16},{8,24},{16,0},{24,8},{1,17},{9,25},{17,1},{25,9},{2,18},{10... | collective-permute-start | bytes 442376 | tf_op jit(solution)/shard_map/ppermute | solution.py:31
  221.4 5.9 %collective-permute-start.6 = (f32[72,512]{1,0:T(8,128)S(1)}, f32[72,512]{1,0:T(8,128)S(1)}, u32[]{:S(2)}, u32[]{:S(2)}) collective-permute-start(f32[72,512]{1,0:T(8,128)S(1)} %bitcast_add_fusion.5), channel_id=1, source_target_pairs={{0,2},{2,0},{4,6},{6,4},{1,3},{3,1},{5,7},{7,5},{8,10},{10,8},{12,... | collective-permute-start | bytes 442376 | tf_op jit(solution)/shard_map/ppermute | solution.py:55
  227.3 8.4 %collective-permute-start.7 = (f32[72,512]{1,0:T(8,128)S(1)}, f32[72,512]{1,0:T(8,128)S(1)}, u32[]{:S(2)}, u32[]{:S(2)}) collective-permute-start(f32[72,512]{1,0:T(8,128)S(1)} %add.173), channel_id=1, source_target_pairs={{0,4},{2,6},{4,0},{6,2},{1,5},{3,7},{5,1},{7,3},{8,12},{10,14},{12... | collective-permute-start | bytes 442376 | tf_op jit(solution)/shard_map/ppermute | solution.py:55
  235.7 5.9 %collective-permute-start.8 = (f32[72,512]{1,0:T(8,128)S(1)}, f32[72,512]{1,0:T(8,128)S(1)}, u32[]{:S(2)}, u32[]{:S(2)}) collective-permute-start(f32[72,512]{1,0:T(8,128)S(1)} %add.174), channel_id=1, source_target_pairs={{0,32},{32,0},{64,96},{96,64},{128,160},{160,128},{192,224},{224,1... | collective-permute-start | bytes 442376 | tf_op jit(solution)/shard_map/ppermute | solution.py:55
  241.6 8.4 %collective-permute-start.9 = (f32[72,512]{1,0:T(8,128)S(1)}, f32[72,512]{1,0:T(8,128)S(1)}, u32[]{:S(2)}, u32[]{:S(2)}) collective-permute-start(f32[72,512]{1,0:T(8,128)S(1)} %add.175), channel_id=1, source_target_pairs={{0,64},{32,96},{64,0},{96,32},{128,192},{160,224},{192,128},{224,1... | collective-permute-start | bytes 442376 | tf_op jit(solution)/shard_map/ppermute | solution.py:55
  250.0 10.1 %collective-permute-start.10 = (f32[72,512]{1,0:T(8,128)S(1)}, f32[72,512]{1,0:T(8,128)S(1)}, u32[]{:S(2)}, u32[]{:S(2)}) collective-permute-start(f32[72,512]{1,0:T(8,128)S(1)} %add.176), channel_id=1, source_target_pairs={{0,128},{32,160},{64,192},{96,224},{128,0},{160,32},{192,64},{224,... | collective-permute-start | bytes 442376 | tf_op jit(solution)/shard_map/ppermute | solution.py:55
  260.1 9.8 %collective-permute-start.11 = (f32[72,512]{1,0:T(8,128)S(1)}, f32[72,512]{1,0:T(8,128)S(1)}, u32[]{:S(2)}, u32[]{:S(2)}) collective-permute-start(f32[72,512]{1,0:T(8,128)S(1)} %add.177), channel_id=1, source_target_pairs={{0,256},{256,0},{1,257},{257,1},{2,258},{258,2},{3,259},{259,3},{4... | collective-permute-start | bytes 442376 | tf_op jit(solution)/shard_map/ppermute | solution.py:55
  269.9 7.4 %collective-permute-start.12 = (f32[72,512]{1,0:T(8,128)S(1)}, f32[72,512]{1,0:T(8,128)S(1)}, u32[]{:S(2)}, u32[]{:S(2)}) collective-permute-start(f32[72,512]{1,0:T(8,128)S(1)} %add.178), channel_id=1, source_target_pairs={{0,16},{8,24},{16,0},{24,8},{1,17},{9,25},{17,1},{25,9},{2,18},{10... | collective-permute-start | bytes 442376 | tf_op jit(solution)/shard_map/ppermute | solution.py:41
  277.4 7.5 %collective-permute-start.13 = (f32[2,72,512]{2,1,0:T(8,128)S(1)}, f32[2,72,512]{2,1,0:T(8,128)S(1)}, u32[]{:S(2)}, u32[]{:S(2)}) collective-permute-start(f32[2,72,512]{2,1,0:T(8,128)S(1)} %pad_maximum_fusion.2), channel_id=1, source_target_pairs={{0,8},{8,0},{16,24},{24,16},{1,9},{9,1},{17,25},{25,17},{2,10},{10... | collective-permute-start | bytes 884744 | tf_op jit(solution)/shard_map/ppermute | solution.py:41
  285.0 16.2 %collective-permute-start.14 = (f32[288,512]{1,0:T(8,128)S(1)}, f32[288,512]{1,0:T(8,128)S(1)}, u32[]{:S(2)}, u32[]{:S(2)}) collective-permute-start(f32[288,512]{1,0:T(8,128)S(1)} %bitcast.73), channel_id=1, source_target_pairs={{0,1},{1,0},{2,3},{3,2},{4,5},{5,4},{6,7},{7,6},{8,9},{9,8},{10,11... | collective-permute-start | bytes 1769480 | tf_op jit(solution)/shard_map/ppermute | solution.py:41
Sparse Core Ops, SparseCore 0:
  19.8 109.2 all-gather.1

commit v9 on v5

--- a/solution.py
+++ b/solution.py
@@ -125,11 +125,15 @@
     gathered = lax.all_gather(features, "y_hi", axis=0, tiled=True)
     gathered = lax.all_gather(gathered, ("z", "x"), axis=0, tiled=True)
     all_panels = gathered.reshape(-1, tile_size, feat_width)
-    gathered_sum = _aggregate(local_cols, live_counts, tiles, all_panels)
     cores = sizes["core"]
-    by_core = gathered_sum.reshape(row_panels // cores, cores, tile_size, feat_width)
-    by_core = jnp.moveaxis(by_core, 1, 0)
-    half = _halving_scatter(by_core, "core", cores, (0,))
+    me_core = lax.axis_index("core")
+    split = lambda a: a.reshape((row_panels // cores, cores) + a.shape[1:])
+    pick = lambda a, c: lax.dynamic_index_in_dim(split(a), c, 1, keepdims=False)
+    other = 1 - me_core
+    sent = _aggregate(pick(local_cols, other), pick(live_counts, other), pick(tiles, other), all_panels)
+    arrived = lax.ppermute(sent, "core", _xor_perm(cores, 1))
+    kept = _aggregate(pick(local_cols, me_core), pick(live_counts, me_core), pick(tiles, me_core), all_panels)
+    half = kept + arrived
     summed_own = _halving_scatter(half, "y_lo", sizes["y_lo"], (0, 1))
     own_rows = own_panels * tile_size
     aggregated = summed_own.reshape(own_rows, feat_width).astype(jnp.bfloat16)

time: 297 us -> 300 us (1.010)
    dynamic_slice x0 -> x2, local copies, waits for them, and re-layouts: none -> 4.19 us  [shards(): pick = lambda a, c: lax.dynamic_index_in_dim(split(a), c, 1, keepdims=False)]
    ppermute x0 -> x1, starting transfers between devices: none -> 3.21 us  [shards(): arrived = lax.ppermute(sent, 'core', _xor_perm(cores, 1))]
    all_gather x1, waiting for transfers between devices: 93.5 us -> 96.6 us  [shards(): gathered = lax.all_gather(gathered, ('z', 'x'), axis=0, tiled=True)]
    ppermute x6 -> x5, starting transfers between devices: 18.9 us -> 16.2 us  [_halving_scatter(): blocks = keep + lax.ppermute(send, axis, _xor_perm(n, 1 << bit))]
    pallas_call x1 -> x2, Pallas kernels: 11.1 us -> 13.4 us  [_aggregate(): pl.pallas_call(_aggregate_kernel, out_shape=jax.ShapeDtypeStruct((groups,...]
    ppermute x6 -> x5, waiting for transfers between devices: 39.8 us -> 37.5 us  [_halving_scatter(): blocks = keep + lax.ppermute(send, axis, _xor_perm(n, 1 << bit))]
    unnamed x14 -> x11, local copies, waits for them, and re-layouts: 6.2 us -> 4.36 us
  transfers between devices with their start and end apart: 16 -> 16, of which waited for: 16 -> 15; matrix products, arithmetic and copies ran while one was open for 5% -> 6% of each run, Pallas kernels for 0% -> 2%
where the time goes in v9:
time: 300 us; the launch traced here: 299 us
  waiting for transfers between devices  173 us (58%)
  starting transfers between devices  60.8 us (20%)
  local copies, waits for them, and re-layouts  15.4 us (5%)
  between operations  14.6 us (5%)
  Pallas kernels  13.4 us (4%)
  blocking collectives  12.4 us (4%)
  other arithmetic  8.04 us (3%)
    all_gather x1, waiting for transfers between devices, shards(): gathered = lax.all_gather(gathered, ('z', 'x'), axis=0, tiled=True)  96.6 us
    ppermute x5, waiting for transfers between devices, _halving_scatter(): blocks = keep + lax.ppermute(send, axis, _xor_perm(n, 1 << bit))  37.5 us
    ppermute x6, waiting for transfers between devices, _doubling_sum(): piece = piece + lax.ppermute(piece, axis, _xor_perm(n, bit))  27.4 us
    ppermute x6, starting transfers between devices, _doubling_sum(): piece = piece + lax.ppermute(piece, axis, _xor_perm(n, bit))  21.2 us
    ppermute x3, starting transfers between devices, _doubling_gather(): other = lax.ppermute(piece, axis, _xor_perm(n, 1 << bit))  20.1 us
    ppermute x5, starting transfers between devices, _halving_scatter(): blocks = keep + lax.ppermute(send, axis, _xor_perm(n, 1 << bit))  16.2 us
    pallas_call x2, Pallas kernels, _aggregate(): pl.pallas_call(_aggregate_kernel, out_shape=jax.ShapeDtypeStruct((groups,...  13.4 us
    all_gather x1, blocking collectives, shards(): gathered = lax.all_gather(features, 'y_hi', axis=0, tiled=True)  12.4 us
  transfers between devices with their start and end apart: 16, of which 15 were waited for; matrix products, arithmetic and copies ran while one was open for 6% of the time, Pallas kernels for 2%

profile of v9, /device:TPU:1, one launch (start us, length us, event | category | flops | bytes accessed | tf_op | source)
XLA Modules:
  0.0 298.9 jit_solution(17072920515647166370)
XLA Ops:
  7.2 12.4 %all_gather.6 = bf16[256,512]{1,0:T(8,128)(2,1)} all-gather(bf16[128,512]{1,0:T(8,128)(2,1)} %param.11), channel_id=1, replica_groups=mesh['y_hi'=2,'z'=8,'x'=4,'y_lo'=4,'core'=2] {'y_hi'}, dimensions={0}, use_global_device_ids=true | all-gather | bytes 393216 | tf_op jit(solution)/shard_map/all_gather | solution.py:125
  21.6 4.0 %constant_dynamic-slice_fusion = (bf16[4,1,12,128,128]{4,3,2,1,0:T(8,128)(2,1)}, bf16[4,1,12,128,128]{4,3,2,1,0:T(8,128)(2,1)}) fusion(bf16[4,2,12,128,128]{4,3,2,1,0:T(8,128)(2,1)} %bitcast.75, s32[]{:T(128)S(6)} %select_n.158, s32[]{:T(128)S(6)} %select_n.156), kind=kLoop, calls=%fused_computation.39 | loop fusion | bytes 6291464 | tf_op jit(solution)/shard_map/jit(dynamic_index_in_dim)/dynamic_slice | solution.py:131
  29.2 2.6 copy.16.tiles_ref
  32.5 96.6 %all-gather.2.cloned.1.call-done = bf16[8192,512]{1,0:T(8,128)(2,1)} async-done(((bf16[256,512]{1,0:T(8,128)(2,1)}), bf16[8192,512]{1,0:T(8,128)(2,1)}) %all-gather.2.cloned.1.call-update) | async-done | bytes 8388624 | tf_op jit(solution)/shard_map/all_gather | solution.py:126
  129.1 6.8 %shard_map.95 = f32[4,128,512]{2,1,0:T(8,128)} custom-call(s32[48]{0:T(128)} %min.20.cols_ref, bf16[4,128,1536]{2,1,0:T(8,128)(2,1)} %copy.16.tiles_ref, bf16[64,128,512]{2,1,0:T(8,128)(2,1)} %bitcast.65), custom_call_target="tpu_custom_call" | custom-call | flops 805306368 | bytes 8912896 | tf_op jit(solution)/shard_map/pallas_call | solution.py:94
  135.8 3.2 %collective-permute-start = (f32[4,128,512]{2,1,0:T(8,128)}, f32[4,128,512]{2,1,0:T(8,128)S(1)}, u32[]{:S(2)}, u32[]{:S(2)}) collective-permute-start(f32[4,128,512]{2,1,0:T(8,128)} %shard_map.95), channel_id=1, source_target_pairs={{0,1},{1,0},{2,3},{3,2},{4,5},{5,4},{6,7},{7,6},{8,9},{9,8},{10,11... | collective-permute-start | bytes 3145736 | tf_op jit(solution)/shard_map/ppermute | solution.py:134
  142.3 2.6 copy.14.tiles_ref
  145.5 6.7 %shard_map.94 = f32[4,128,512]{2,1,0:T(8,128)} custom-call(s32[48]{0:T(128)} %min.18.cols_ref, bf16[4,128,1536]{2,1,0:T(8,128)(2,1)} %copy.14.tiles_ref, bf16[64,128,512]{2,1,0:T(8,128)(2,1)} %bitcast.66), custom_call_target="tpu_custom_call" | custom-call | flops 805306368 | bytes 8912896 | tf_op jit(solution)/shard_map/pallas_call | solution.py:94
  153.7 3.4 %collective-permute-start.1 = (f32[2,128,512]{2,1,0:T(8,128)S(1)}, f32[2,128,512]{2,1,0:T(8,128)S(1)}, u32[]{:S(2)}, u32[]{:S(2)}) collective-permute-start(f32[2,128,512]{2,1,0:T(8,128)S(1)} %dynamic-slice_bitcast_fusion.1), channel_id=1, source_target_pairs={{0,2},{2,0},{4,6},{6,4},{1,3},{3,1},{5,7},{7,5},{8,10},{10,8},{12,... | collective-permute-start | bytes 1572872 | tf_op jit(solution)/shard_map/ppermute | solution.py:31
  157.2 12.0 %collective-permute-done.1 = f32[2,128,512]{2,1,0:T(8,128)S(1)} collective-permute-done((f32[2,128,512]{2,1,0:T(8,128)S(1)}, f32[2,128,512]{2,1,0:T(8,128)S(1)}, u32[]{:S(2)}, u32[]{:S(2)}) %collective-permute-start.1) | collective-permute-done | bytes 524320 | tf_op jit(solution)/shard_map/ppermute | solution.py:31
  169.3 4.6 %collective-permute-start.2 = (f32[128,512]{1,0:T(8,128)S(1)}, f32[128,512]{1,0:T(8,128)S(1)}, u32[]{:S(2)}, u32[]{:S(2)}) collective-permute-start(f32[128,512]{1,0:T(8,128)S(1)} %dynamic-slice_bitcast_fusion.3), channel_id=1, source_target_pairs={{0,4},{2,6},{4,0},{6,2},{1,5},{3,7},{5,1},{7,3},{8,12},{10,14},{12... | collective-permute-start | bytes 786440 | tf_op jit(solution)/shard_map/ppermute | solution.py:31
  173.9 11.5 %collective-permute-done.2 = f32[128,512]{1,0:T(8,128)S(1)} collective-permute-done((f32[128,512]{1,0:T(8,128)S(1)}, f32[128,512]{1,0:T(8,128)S(1)}, u32[]{:S(2)}, u32[]{:S(2)}) %collective-permute-start.2) | collective-permute-done | bytes 262176 | tf_op jit(solution)/shard_map/ppermute | solution.py:31
  187.0 3.3 %collective-permute-start.3 = (f32[288,512]{1,0:T(8,128)S(1)}, f32[288,512]{1,0:T(8,128)S(1)}, u32[]{:S(2)}, u32[]{:S(2)}) collective-permute-start(f32[288,512]{1,0:T(8,128)S(1)} %dynamic-slice_bitcast_fusion), channel_id=1, source_target_pairs={{0,1},{1,0},{2,3},{3,2},{4,5},{5,4},{6,7},{7,6},{8,9},{9,8},{10,11... | collective-permute-start | bytes 1769480 | tf_op jit(solution)/shard_map/ppermute | solution.py:31
  192.0 1.9 collective-permute-start.4
  194.0 8.1 %collective-permute-done.4 = f32[2,72,512]{2,1,0:T(8,128)S(1)} collective-permute-done((f32[2,72,512]{2,1,0:T(8,128)S(1)}, f32[2,72,512]{2,1,0:T(8,128)S(1)}, u32[]{:S(2)}, u32[]{:S(2)}) %collective-permute-start.4) | collective-permute-done | bytes 294944 | tf_op jit(solution)/shard_map/ppermute | solution.py:31
  202.2 3.0 %collective-permute-start.5 = (f32[72,512]{1,0:T(8,128)S(1)}, f32[72,512]{1,0:T(8,128)S(1)}, u32[]{:S(2)}, u32[]{:S(2)}) collective-permute-start(f32[72,512]{1,0:T(8,128)S(1)} %dynamic-slice_bitcast_fusion.4), channel_id=1, source_target_pairs={{0,16},{8,24},{16,0},{24,8},{1,17},{9,25},{17,1},{25,9},{2,18},{10... | collective-permute-start | bytes 442376 | tf_op jit(solution)/shard_map/ppermute | solution.py:31
  205.2 4.4 %collective-permute-done.5 = f32[72,512]{1,0:T(8,128)S(1)} collective-permute-done((f32[72,512]{1,0:T(8,128)S(1)}, f32[72,512]{1,0:T(8,128)S(1)}, u32[]{:S(2)}, u32[]{:S(2)}) %collective-permute-start.5) | collective-permute-done | bytes 147488 | tf_op jit(solution)/shard_map/ppermute | solution.py:31
  211.5 4.0 %collective-permute-done.6 = f32[72,512]{1,0:T(8,128)S(1)} collective-permute-done((f32[72,512]{1,0:T(8,128)S(1)}, f32[72,512]{1,0:T(8,128)S(1)}, u32[]{:S(2)}, u32[]{:S(2)}) %collective-permute-start.6) | collective-permute-done | bytes 147488 | tf_op jit(solution)/shard_map/ppermute | solution.py:55
  215.5 3.5 %collective-permute-start.7 = (f32[72,512]{1,0:T(8,128)S(1)}, f32[72,512]{1,0:T(8,128)S(1)}, u32[]{:S(2)}, u32[]{:S(2)}) collective-permute-start(f32[72,512]{1,0:T(8,128)S(1)} %add.185), channel_id=1, source_target_pairs={{0,4},{2,6},{4,0},{6,2},{1,5},{3,7},{5,1},{7,3},{8,12},{10,14},{12... | collective-permute-start | bytes 442376 | tf_op jit(solution)/shard_map/ppermute | solution.py:55
  219.0 4.9 %collective-permute-done.7 = f32[72,512]{1,0:T(8,128)S(1)} collective-permute-done((f32[72,512]{1,0:T(8,128)S(1)}, f32[72,512]{1,0:T(8,128)S(1)}, u32[]{:S(2)}, u32[]{:S(2)}) %collective-permute-start.7) | collective-permute-done | bytes 147488 | tf_op jit(solution)/shard_map/ppermute | solution.py:55
  225.8 4.0 %collective-permute-done.8 = f32[72,512]{1,0:T(8,128)S(1)} collective-permute-done((f32[72,512]{1,0:T(8,128)S(1)}, f32[72,512]{1,0:T(8,128)S(1)}, u32[]{:S(2)}, u32[]{:S(2)}) %collective-permute-start.8) | collective-permute-done | bytes 147488 | tf_op jit(solution)/shard_map/ppermute | solution.py:55
  229.8 3.1 %collective-permute-start.9 = (f32[72,512]{1,0:T(8,128)S(1)}, f32[72,512]{1,0:T(8,128)S(1)}, u32[]{:S(2)}, u32[]{:S(2)}) collective-permute-start(f32[72,512]{1,0:T(8,128)S(1)} %add.187), channel_id=1, source_target_pairs={{0,64},{32,96},{64,0},{96,32},{128,192},{160,224},{192,128},{224,1... | collective-permute-start | bytes 442376 | tf_op jit(solution)/shard_map/ppermute | solution.py:55
  232.9 5.3 %collective-permute-done.9 = f32[72,512]{1,0:T(8,128)S(1)} collective-permute-done((f32[72,512]{1,0:T(8,128)S(1)}, f32[72,512]{1,0:T(8,128)S(1)}, u32[]{:S(2)}, u32[]{:S(2)}) %collective-permute-start.9) | collective-permute-done | bytes 147488 | tf_op jit(solution)/shard_map/ppermute | solution.py:55
  238.2 4.3 %collective-permute-start.10 = (f32[72,512]{1,0:T(8,128)S(1)}, f32[72,512]{1,0:T(8,128)S(1)}, u32[]{:S(2)}, u32[]{:S(2)}) collective-permute-start(f32[72,512]{1,0:T(8,128)S(1)} %add.188), channel_id=1, source_target_pairs={{0,128},{32,160},{64,192},{96,224},{128,0},{160,32},{192,64},{224,... | collective-permute-start | bytes 442376 | tf_op jit(solution)/shard_map/ppermute | solution.py:55
  242.6 6.0 %collective-permute-done.10 = f32[72,512]{1,0:T(8,128)S(1)} collective-permute-done((f32[72,512]{1,0:T(8,128)S(1)}, f32[72,512]{1,0:T(8,128)S(1)}, u32[]{:S(2)}, u32[]{:S(2)}) %collective-permute-start.10) | collective-permute-done | bytes 147488 | tf_op jit(solution)/shard_map/ppermute | solution.py:55
  248.6 6.5 %collective-permute-start.11 = (f32[72,512]{1,0:T(8,128)S(1)}, f32[72,512]{1,0:T(8,128)S(1)}, u32[]{:S(2)}, u32[]{:S(2)}) collective-permute-start(f32[72,512]{1,0:T(8,128)S(1)} %add.189), channel_id=1, source_target_pairs={{0,256},{256,0},{1,257},{257,1},{2,258},{258,2},{3,259},{259,3},{4... | collective-permute-start | bytes 442376 | tf_op jit(solution)/shard_map/ppermute | solution.py:55
  255.1 3.3 %collective-permute-done.11 = f32[72,512]{1,0:T(8,128)S(1)} collective-permute-done((f32[72,512]{1,0:T(8,128)S(1)}, f32[72,512]{1,0:T(8,128)S(1)}, u32[]{:S(2)}, u32[]{:S(2)}) %collective-permute-start.11) | collective-permute-done | bytes 147488 | tf_op jit(solution)/shard_map/ppermute | solution.py:55
  258.4 3.1 %collective-permute-start.12 = (f32[72,512]{1,0:T(8,128)S(1)}, f32[72,512]{1,0:T(8,128)S(1)}, u32[]{:S(2)}, u32[]{:S(2)}) collective-permute-start(f32[72,512]{1,0:T(8,128)S(1)} %add.190), channel_id=1, source_target_pairs={{0,16},{8,24},{16,0},{24,8},{1,17},{9,25},{17,1},{25,9},{2,18},{10... | collective-permute-start | bytes 442376 | tf_op jit(solution)/shard_map/ppermute | solution.py:41
  261.6 4.3 %collective-permute-done.12 = f32[72,512]{1,0:T(8,128)S(1)} collective-permute-done((f32[72,512]{1,0:T(8,128)S(1)}, f32[72,512]{1,0:T(8,128)S(1)}, u32[]{:S(2)}, u32[]{:S(2)}) %collective-permute-start.12) | collective-permute-done | bytes 147488 | tf_op jit(solution)/shard_map/ppermute | solution.py:41
  265.9 1.9 collective-permute-start.13
  267.8 5.5 %collective-permute-done.13 = f32[2,72,512]{2,1,0:T(8,128)S(1)} collective-permute-done((f32[2,72,512]{2,1,0:T(8,128)S(1)}, f32[2,72,512]{2,1,0:T(8,128)S(1)}, u32[]{:S(2)}, u32[]{:S(2)}) %collective-permute-start.13) | collective-permute-done | bytes 294944 | tf_op jit(solution)/shard_map/ppermute | solution.py:41
  273.5 15.1 %collective-permute-start.14 = (f32[288,512]{1,0:T(8,128)S(1)}, f32[288,512]{1,0:T(8,128)S(1)}, u32[]{:S(2)}, u32[]{:S(2)}) collective-permute-start(f32[288,512]{1,0:T(8,128)S(1)} %bitcast.76), channel_id=1, source_target_pairs={{0,1},{1,0},{2,3},{3,2},{4,5},{5,4},{6,7},{7,6},{8,9},{9,8},{10,11... | collective-permute-start | bytes 1769480 | tf_op jit(solution)/shard_map/ppermute | solution.py:41
  (57 shorter events, 22.6 us)
Async XLA Ops:
  7.2 178.2 %copy-start = (bf16[512,512]{1,0:T(8,128)(2,1)S(1)}, bf16[512,512]{1,0:T(8,128)(2,1)}, u32[]{:S(2)}) copy-start(bf16[512,512]{1,0:T(8,128)(2,1)} %param.15) | copy-start | bytes 1572868
  7.2 121.9 %all-gather.2.cloned.1.call-start = ((), (), s32[]{:S(2)}) async-start(), calls=%async_computation | async-start | bytes 8650752 | tf_op jit(solution)/shard_map/all_gather | solution.py:126
  29.2 2.6 copy-start.1
  135.8 16.4 %collective-permute-start = (f32[4,128,512]{2,1,0:T(8,128)}, f32[4,128,512]{2,1,0:T(8,128)S(1)}, u32[]{:S(2)}, u32[]{:S(2)}) collective-permute-start(f32[4,128,512]{2,1,0:T(8,128)} %shard_map.95), channel_id=1, source_target_pairs={{0,1},{1,0},{2,3},{3,2},{4,5},{5,4},{6,7},{7,6},{8,9},{9,8},{10,11... | collective-permute-start | bytes 3145736 | tf_op jit(solution)/shard_map/ppermute | solution.py:134
  153.7 31.7 %copy-start.2 = (bf16[128,512]{1,0:T(8,128)(2,1)S(1)}, bf16[128,512]{1,0:T(8,128)(2,1)}, u32[]{:S(2)}) copy-start(bf16[128,512]{1,0:T(8,128)(2,1)} %param.17) | copy-start | bytes 393220
  153.7 31.7 %copy-start.3 = (f32[512]{0:T(512)S(1)}, f32[512]{0:T(512)}, u32[]{:S(2)}) copy-start(f32[512]{0:T(512)} %param.16) | copy-start | bytes 6148
  153.7 15.4 %collective-permute-start.1 = (f32[2,128,512]{2,1,0:T(8,128)S(1)}, f32[2,128,512]{2,1,0:T(8,128)S(1)}, u32[]{:S(2)}, u32[]{:S(2)}) collective-permute-start(f32[2,128,512]{2,1,0:T(8,128)S(1)} %dynamic-slice_bitcast_fusion.1), channel_id=1, source_target_pairs={{0,2},{2,0},{4,6},{6,4},{1,3},{3,1},{5,7},{7,5},{8,10},{10,8},{12,... | collective-permute-start | bytes 1572872 | tf_op jit(solution)/shard_map/ppermute | solution.py:31
  169.3 16.1 %collective-permute-start.2 = (f32[128,512]{1,0:T(8,128)S(1)}, f32[128,512]{1,0:T(8,128)S(1)}, u32[]{:S(2)}, u32[]{:S(2)}) collective-permute-start(f32[128,512]{1,0:T(8,128)S(1)} %dynamic-slice_bitcast_fusion.3), channel_id=1, source_target_pairs={{0,4},{2,6},{4,0},{6,2},{1,5},{3,7},{5,1},{7,3},{8,12},{10,14},{12... | collective-permute-start | bytes 786440 | tf_op jit(solution)/shard_map/ppermute | solution.py:31
  187.0 4.9 %collective-permute-start.3 = (f32[288,512]{1,0:T(8,128)S(1)}, f32[288,512]{1,0:T(8,128)S(1)}, u32[]{:S(2)}, u32[]{:S(2)}) collective-permute-start(f32[288,512]{1,0:T(8,128)S(1)} %dynamic-slice_bitcast_fusion), channel_id=1, source_target_pairs={{0,1},{1,0},{2,3},{3,2},{4,5},{5,4},{6,7},{7,6},{8,9},{9,8},{10,11... | collective-permute-start | bytes 1769480 | tf_op jit(solution)/shard_map/ppermute | solution.py:31
  192.0 10.1 %collective-permute-start.4 = (f32[2,72,512]{2,1,0:T(8,128)S(1)}, f32[2,72,512]{2,1,0:T(8,128)S(1)}, u32[]{:S(2)}, u32[]{:S(2)}) collective-permute-start(f32[2,72,512]{2,1,0:T(8,128)S(1)} %dynamic-slice_bitcast_fusion.2), channel_id=1, source_target_pairs={{0,8},{8,0},{16,24},{24,16},{1,9},{9,1},{17,25},{25,17},{2,10},{10... | collective-permute-start | bytes 884744 | tf_op jit(solution)/shard_map/ppermute | solution.py:31
  202.2 7.4 %collective-permute-start.5 = (f32[72,512]{1,0:T(8,128)S(1)}, f32[72,512]{1,0:T(8,128)S(1)}, u32[]{:S(2)}, u32[]{:S(2)}) collective-permute-start(f32[72,512]{1,0:T(8,128)S(1)} %dynamic-slice_bitcast_fusion.4), channel_id=1, source_target_pairs={{0,16},{8,24},{16,0},{24,8},{1,17},{9,25},{17,1},{25,9},{2,18},{10... | collective-permute-start | bytes 442376 | tf_op jit(solution)/shard_map/ppermute | solution.py:31
  209.6 5.9 %collective-permute-start.6 = (f32[72,512]{1,0:T(8,128)S(1)}, f32[72,512]{1,0:T(8,128)S(1)}, u32[]{:S(2)}, u32[]{:S(2)}) collective-permute-start(f32[72,512]{1,0:T(8,128)S(1)} %bitcast_add_fusion.4), channel_id=1, source_target_pairs={{0,2},{2,0},{4,6},{6,4},{1,3},{3,1},{5,7},{7,5},{8,10},{10,8},{12,... | collective-permute-start | bytes 442376 | tf_op jit(solution)/shard_map/ppermute | solution.py:55
  215.5 8.4 %collective-permute-start.7 = (f32[72,512]{1,0:T(8,128)S(1)}, f32[72,512]{1,0:T(8,128)S(1)}, u32[]{:S(2)}, u32[]{:S(2)}) collective-permute-start(f32[72,512]{1,0:T(8,128)S(1)} %add.185), channel_id=1, source_target_pairs={{0,4},{2,6},{4,0},{6,2},{1,5},{3,7},{5,1},{7,3},{8,12},{10,14},{12... | collective-permute-start | bytes 442376 | tf_op jit(solution)/shard_map/ppermute | solution.py:55
  223.9 5.9 %collective-permute-start.8 = (f32[72,512]{1,0:T(8,128)S(1)}, f32[72,512]{1,0:T(8,128)S(1)}, u32[]{:S(2)}, u32[]{:S(2)}) collective-permute-start(f32[72,512]{1,0:T(8,128)S(1)} %add.186), channel_id=1, source_target_pairs={{0,32},{32,0},{64,96},{96,64},{128,160},{160,128},{192,224},{224,1... | collective-permute-start | bytes 442376 | tf_op jit(solution)/shard_map/ppermute | solution.py:55
  229.8 8.4 %collective-permute-start.9 = (f32[72,512]{1,0:T(8,128)S(1)}, f32[72,512]{1,0:T(8,128)S(1)}, u32[]{:S(2)}, u32[]{:S(2)}) collective-permute-start(f32[72,512]{1,0:T(8,128)S(1)} %add.187), channel_id=1, source_target_pairs={{0,64},{32,96},{64,0},{96,32},{128,192},{160,224},{192,128},{224,1... | collective-permute-start | bytes 442376 | tf_op jit(solution)/shard_map/ppermute | solution.py:55
  238.2 10.4 %collective-permute-start.10 = (f32[72,512]{1,0:T(8,128)S(1)}, f32[72,512]{1,0:T(8,128)S(1)}, u32[]{:S(2)}, u32[]{:S(2)}) collective-permute-start(f32[72,512]{1,0:T(8,128)S(1)} %add.188), channel_id=1, source_target_pairs={{0,128},{32,160},{64,192},{96,224},{128,0},{160,32},{192,64},{224,... | collective-permute-start | bytes 442376 | tf_op jit(solution)/shard_map/ppermute | solution.py:55
  248.6 9.8 %collective-permute-start.11 = (f32[72,512]{1,0:T(8,128)S(1)}, f32[72,512]{1,0:T(8,128)S(1)}, u32[]{:S(2)}, u32[]{:S(2)}) collective-permute-start(f32[72,512]{1,0:T(8,128)S(1)} %add.189), channel_id=1, source_target_pairs={{0,256},{256,0},{1,257},{257,1},{2,258},{258,2},{3,259},{259,3},{4... | collective-permute-start | bytes 442376 | tf_op jit(solution)/shard_map/ppermute | solution.py:55
  258.4 7.4 %collective-permute-start.12 = (f32[72,512]{1,0:T(8,128)S(1)}, f32[72,512]{1,0:T(8,128)S(1)}, u32[]{:S(2)}, u32[]{:S(2)}) collective-permute-start(f32[72,512]{1,0:T(8,128)S(1)} %add.190), channel_id=1, source_target_pairs={{0,16},{8,24},{16,0},{24,8},{1,17},{9,25},{17,1},{25,9},{2,18},{10... | collective-permute-start | bytes 442376 | tf_op jit(solution)/shard_map/ppermute | solution.py:41
  265.9 7.5 %collective-permute-start.13 = (f32[2,72,512]{2,1,0:T(8,128)S(1)}, f32[2,72,512]{2,1,0:T(8,128)S(1)}, u32[]{:S(2)}, u32[]{:S(2)}) collective-permute-start(f32[2,72,512]{2,1,0:T(8,128)S(1)} %pad_maximum_fusion.2), channel_id=1, source_target_pairs={{0,8},{8,0},{16,24},{24,16},{1,9},{9,1},{17,25},{25,17},{2,10},{10... | collective-permute-start | bytes 884744 | tf_op jit(solution)/shard_map/ppermute | solution.py:41
  273.5 16.7 %collective-permute-start.14 = (f32[288,512]{1,0:T(8,128)S(1)}, f32[288,512]{1,0:T(8,128)S(1)}, u32[]{:S(2)}, u32[]{:S(2)}) collective-permute-start(f32[288,512]{1,0:T(8,128)S(1)} %bitcast.76), channel_id=1, source_target_pairs={{0,1},{1,0},{2,3},{3,2},{4,5},{5,4},{6,7},{7,6},{8,9},{9,8},{10,11... | collective-permute-start | bytes 1769480 | tf_op jit(solution)/shard_map/ppermute | solution.py:41
Sparse Core Ops, SparseCore 0:
  19.8 109.2 all-gather.1

commit v10 on v9

--- a/solution.py
+++ b/solution.py
@@ -57,10 +57,13 @@
     return piece
 
 
-def _aggregate_kernel(cols_ref, tiles_ref, panels_hbm, out_ref, buf, sems):
+def _aggregate_kernel(parity_ref, cols_ref, tiles_ref, panels_hbm, out_ref, buf, sems):
     groups, slots = out_ref.shape[0], buf.shape[1]
+    stride = tiles_ref.shape[0] // groups
+    parity = parity_ref[0]
 
-    def copies(g, slot):
+    def copies(j, slot):
+        g = stride * j + parity
         return [
             pltpu.make_async_copy(panels_hbm.at[cols_ref[g * slots + k]], buf.at[slot, k], sems.at[slot, k])
             for k in range(slots)
@@ -69,32 +72,40 @@
     pending = copies(0, 0)
     for c in pending:
         c.start()
-    for g in range(groups):
-        slot = g % 2
-        if g + 1 < groups:
-            ahead = copies(g + 1, 1 - slot)
+    for j in range(groups):
+        slot = j % 2
+        if j + 1 < groups:
+            ahead = copies(j + 1, 1 - slot)
             for c in ahead:
                 c.start()
         for c in pending:
             c.wait()
         rhs = buf[slot].reshape(slots * buf.shape[2], buf.shape[3])
-        out_ref[g] = jnp.dot(tiles_ref[g], rhs, preferred_element_type=jnp.float32)
-        if g + 1 < groups:
+        out_ref[j] = jnp.dot(tiles_ref[stride * j + parity], rhs, preferred_element_type=jnp.float32)
+        if j + 1 < groups:
             pending = ahead
 
 
-def _aggregate(cols, counts, tiles, panels):
+def _widen(counts, tiles):
     groups, slots, tile_size, _ = tiles.shape
-    feat_width = panels.shape[-1]
     live = jnp.arange(slots, dtype=jnp.int32)[None, :] < counts[:, None]
     wide = jnp.where(live[:, :, None, None], tiles, jnp.zeros((), tiles.dtype))
-    wide = wide.transpose(0, 2, 1, 3).reshape(groups, tile_size, slots * tile_size)
-    flops = 2 * groups * slots * tile_size * tile_size * feat_width
-    moved = tiles.size * 2 + groups * slots * tile_size * feat_width * 2 + groups * tile_size * feat_width * 4
+    return wide.transpose(0, 2, 1, 3).reshape(groups, tile_size, slots * tile_size)
+
+
+def _aggregate(cols, wide, panels, parity, stride):
+    groups, tile_size, width = wide.shape
+    slots = width // tile_size
+    feat_width = panels.shape[-1]
+    picked = groups // stride
+    flops = 2 * picked * slots * tile_size * tile_size * feat_width
+    moved = (picked * tile_size * width * 2 + picked * slots * tile_size * feat_width * 2
+             + picked * tile_size * feat_width * 4)
     return pl.pallas_call(
         _aggregate_kernel,
-        out_shape=jax.ShapeDtypeStruct((groups, tile_size, feat_width), jnp.float32),
+        out_shape=jax.ShapeDtypeStruct((picked, tile_size, feat_width), jnp.float32),
         in_specs=[
+            pl.BlockSpec(memory_space=pltpu.SMEM),
             pl.BlockSpec(memory_space=pltpu.SMEM),
             pl.BlockSpec(memory_space=pltpu.VMEM),
             pl.BlockSpec(memory_space=pl.ANY),
@@ -105,7 +116,7 @@
             pltpu.SemaphoreType.DMA((2, slots)),
         ],
         cost_estimate=pl.CostEstimate(flops=flops, bytes_accessed=moved, transcendentals=0),
-    )(jnp.clip(cols, 0, panels.shape[0] - 1).reshape(-1), wide, panels)
+    )(jnp.reshape(parity, (1,)).astype(jnp.int32), cols, wide, panels)
 
 
 def shards(features, col_panels, block_counts, block_values, weight, bias, cotangent):
@@ -125,14 +136,13 @@
     gathered = lax.all_gather(features, "y_hi", axis=0, tiled=True)
     gathered = lax.all_gather(gathered, ("z", "x"), axis=0, tiled=True)
     all_panels = gathered.reshape(-1, tile_size, feat_width)
+    wide = _widen(live_counts, tiles)
+    cols = jnp.clip(local_cols, 0, all_panels.shape[0] - 1).reshape(-1)
     cores = sizes["core"]
     me_core = lax.axis_index("core")
-    split = lambda a: a.reshape((row_panels // cores, cores) + a.shape[1:])
-    pick = lambda a, c: lax.dynamic_index_in_dim(split(a), c, 1, keepdims=False)
-    other = 1 - me_core
-    sent = _aggregate(pick(local_cols, other), pick(live_counts, other), pick(tiles, other), all_panels)
+    sent = _aggregate(cols, wide, all_panels, cores - 1 - me_core, cores)
     arrived = lax.ppermute(sent, "core", _xor_perm(cores, 1))
-    kept = _aggregate(pick(local_cols, me_core), pick(live_counts, me_core), pick(tiles, me_core), all_panels)
+    kept = _aggregate(cols, wide, all_panels, me_core, cores)
     half = kept + arrived
     summed_own = _halving_scatter(half, "y_lo", sizes["y_lo"], (0, 1))
     own_rows = own_panels * tile_size

time: 300 us -> 295 us (0.983)
  starting transfers between devices: 60.8 us -> 53 us
  local copies, waits for them, and re-layouts: 15.4 us -> 10.4 us
  waiting for transfers between devices: 173 us -> 178 us
    dynamic_slice x2 -> x0, local copies, waits for them, and re-layouts: 4.19 us -> none  [shards(): pick = lambda a, c: lax.dynamic_index_in_dim(split(a), c, 1, keepdims=False)]
    ppermute x3, starting transfers between devices: 20.1 us -> 15.9 us  [_doubling_gather(): other = lax.ppermute(piece, axis, _xor_perm(n, 1 << bit))]
    ppermute x3, waiting for transfers between devices: 11.4 us -> 14.8 us  [_doubling_gather(): other = lax.ppermute(piece, axis, _xor_perm(n, 1 << bit))]
    all_gather x1, waiting for transfers between devices: 96.6 us -> 93.5 us  [shards(): gathered = lax.all_gather(gathered, ('z', 'x'), axis=0, tiled=True)]
  transfers between devices with their start and end apart: 16 -> 16, of which waited for: 15 -> 15; matrix products, arithmetic and copies ran while one was open for 6% -> 5% of each run, Pallas kernels for 2% -> 2%
where the time goes in v10:
time: 295 us; the launch traced here: 294 us
  waiting for transfers between devices  178 us (60%)
  starting transfers between devices  53 us (18%)
  Pallas kernels  14.6 us (5%)
  between operations  14.6 us (5%)
  blocking collectives  12.4 us (4%)
  local copies, waits for them, and re-layouts  10.4 us (4%)
  other arithmetic  9.73 us (3%)
    all_gather x1, waiting for transfers between devices, shards(): gathered = lax.all_gather(gathered, ('z', 'x'), axis=0, tiled=True)  93.5 us
    ppermute x5, waiting for transfers between devices, _halving_scatter(): blocks = keep + lax.ppermute(send, axis, _xor_perm(n, 1 << bit))  39.6 us
    ppermute x6, waiting for transfers between devices, _doubling_sum(): piece = piece + lax.ppermute(piece, axis, _xor_perm(n, bit))  30.2 us
    ppermute x6, starting transfers between devices, _doubling_sum(): piece = piece + lax.ppermute(piece, axis, _xor_perm(n, bit))  19.8 us
    ppermute x3, starting transfers between devices, _doubling_gather(): other = lax.ppermute(piece, axis, _xor_perm(n, 1 << bit))  15.9 us
    ppermute x3, waiting for transfers between devices, _doubling_gather(): other = lax.ppermute(piece, axis, _xor_perm(n, 1 << bit))  14.8 us
    pallas_call x2, Pallas kernels, _aggregate(): pl.pallas_call(_aggregate_kernel, out_shape=jax.ShapeDtypeStruct((picked,...  14.6 us
    ppermute x5, starting transfers between devices, _halving_scatter(): blocks = keep + lax.ppermute(send, axis, _xor_perm(n, 1 << bit))  14.1 us
  transfers between devices with their start and end apart: 16, of which 15 were waited for; matrix products, arithmetic and copies ran while one was open for 5% of the time, Pallas kernels for 2%

profile of v10, /device:TPU:1, one launch (start us, length us, event | category | flops | bytes accessed | tf_op | source)
XLA Modules:
  0.0 294.1 jit_solution(7760303215706642507)
XLA Ops:
  7.2 12.4 %all_gather.6 = bf16[256,512]{1,0:T(8,128)(2,1)} all-gather(bf16[128,512]{1,0:T(8,128)(2,1)} %param.11), channel_id=1, replica_groups=mesh['y_hi'=2,'z'=8,'x'=4,'y_lo'=4,'core'=2] {'y_hi'}, dimensions={0}, use_global_device_ids=true | all-gather | bytes 393216 | tf_op jit(solution)/shard_map/all_gather | solution.py:136
  21.6 4.7 %copy.12 = bf16[8,1,12,128,128]{3,4,2,0,1:T(8,128)(2,1)} copy(bf16[8,1,12,128,128]{4,3,2,1,0:T(8,128)(2,1)} %param.14) | data formatting | bytes 6291456 | tf_op args[3]
  26.4 3.9 %bitcast_select_fusion = bf16[8,12,128,128]{2,3,1,0:T(8,128)(2,1)} fusion(bf16[8,1,12,128,128]{3,4,2,0,1:T(8,128)(2,1)} %copy.12, pred[8,12]{1,0:T(8,128)(4,1)S(1)} %iota_compare_fusion), kind=kLoop, calls=%fused_computation | loop fusion | flops 1572864 | bytes 6291552 | tf_op jit(solution)/shard_map/jit(_where)/select_n | solution.py:92
  30.3 4.7 %copy.13.tiles_ref = bf16[8,128,1536]{2,1,0:T(8,128)(2,1)} copy(bf16[8,128,1536]{1,2,0:T(8,128)(2,1)} %bitcast.62) | data formatting | bytes 6291456 | tf_op jit(solution)/shard_map/reshape | solution.py:93
  35.6 93.5 %all-gather.2.cloned.1.call-done = bf16[8192,512]{1,0:T(8,128)(2,1)} async-done(((bf16[256,512]{1,0:T(8,128)(2,1)}), bf16[8192,512]{1,0:T(8,128)(2,1)}) %all-gather.2.cloned.1.call-update) | async-done | bytes 8388624 | tf_op jit(solution)/shard_map/all_gather | solution.py:137
  129.1 7.3 %shard_map.98 = f32[4,128,512]{2,1,0:T(8,128)} custom-call(s32[1]{0:T(128)} %bitcast.6.parity_ref, s32[96]{0:T(128)} %fusion.3.cols_ref, bf16[8,128,1536]{2,1,0:T(8,128)(2,1)} %copy.13.tiles_ref, bf16[64,128,512]{2,1,0:T(8,128)(2,1)} %bitcast.60), custom_call_target="tpu_custom_call" | custom-call | flops 805306368 | bytes 8912896 | tf_op jit(solution)/shard_map/pallas_call | solution.py:104
  136.4 3.2 %collective-permute-start = (f32[4,128,512]{2,1,0:T(8,128)}, f32[4,128,512]{2,1,0:T(8,128)S(1)}, u32[]{:S(2)}, u32[]{:S(2)}) collective-permute-start(f32[4,128,512]{2,1,0:T(8,128)} %shard_map.98), channel_id=1, source_target_pairs={{0,1},{1,0},{2,3},{3,2},{4,5},{5,4},{6,7},{7,6},{8,9},{9,8},{10,11... | collective-permute-start | bytes 3145736 | tf_op jit(solution)/shard_map/ppermute | solution.py:144
  139.6 7.4 %shard_map.97 = f32[4,128,512]{2,1,0:T(8,128)} custom-call(s32[1]{0:T(128)} %bitcast.parity_ref, s32[96]{0:T(128)} %fusion.3.cols_ref, bf16[8,128,1536]{2,1,0:T(8,128)(2,1)} %copy.13.tiles_ref, bf16[64,128,512]{2,1,0:T(8,128)(2,1)} %bitcast.61), custom_call_target="tpu_custom_call" | custom-call | flops 805306368 | bytes 8912896 | tf_op jit(solution)/shard_map/pallas_call | solution.py:104
  148.5 2.9 collective-permute-start.1
  151.5 12.7 %collective-permute-done.1 = f32[2,128,512]{2,1,0:T(8,128)S(1)} collective-permute-done((f32[2,128,512]{2,1,0:T(8,128)S(1)}, f32[2,128,512]{2,1,0:T(8,128)S(1)}, u32[]{:S(2)}, u32[]{:S(2)}) %collective-permute-start.1) | collective-permute-done | bytes 524320 | tf_op jit(solution)/shard_map/ppermute | solution.py:31
  164.3 3.5 %collective-permute-start.2 = (f32[128,512]{1,0:T(8,128)S(1)}, f32[128,512]{1,0:T(8,128)S(1)}, u32[]{:S(2)}, u32[]{:S(2)}) collective-permute-start(f32[128,512]{1,0:T(8,128)S(1)} %dynamic-slice_bitcast_fusion.3), channel_id=1, source_target_pairs={{0,4},{2,6},{4,0},{6,2},{1,5},{3,7},{5,1},{7,3},{8,12},{10,14},{12... | collective-permute-start | bytes 786440 | tf_op jit(solution)/shard_map/ppermute | solution.py:31
  167.9 12.7 %collective-permute-done.2 = f32[128,512]{1,0:T(8,128)S(1)} collective-permute-done((f32[128,512]{1,0:T(8,128)S(1)}, f32[128,512]{1,0:T(8,128)S(1)}, u32[]{:S(2)}, u32[]{:S(2)}) %collective-permute-start.2) | collective-permute-done | bytes 262176 | tf_op jit(solution)/shard_map/ppermute | solution.py:31
  182.1 2.8 collective-permute-start.3
  186.7 1.9 collective-permute-start.4
  188.7 8.1 %collective-permute-done.4 = f32[2,72,512]{2,1,0:T(8,128)S(1)} collective-permute-done((f32[2,72,512]{2,1,0:T(8,128)S(1)}, f32[2,72,512]{2,1,0:T(8,128)S(1)}, u32[]{:S(2)}, u32[]{:S(2)}) %collective-permute-start.4) | collective-permute-done | bytes 294944 | tf_op jit(solution)/shard_map/ppermute | solution.py:31
  196.9 2.9 collective-permute-start.5
  199.7 4.5 %collective-permute-done.5 = f32[72,512]{1,0:T(8,128)S(1)} collective-permute-done((f32[72,512]{1,0:T(8,128)S(1)}, f32[72,512]{1,0:T(8,128)S(1)}, u32[]{:S(2)}, u32[]{:S(2)}) %collective-permute-start.5) | collective-permute-done | bytes 147488 | tf_op jit(solution)/shard_map/ppermute | solution.py:31
  204.3 1.9 collective-permute-start.6
  206.2 4.0 %collective-permute-done.6 = f32[72,512]{1,0:T(8,128)S(1)} collective-permute-done((f32[72,512]{1,0:T(8,128)S(1)}, f32[72,512]{1,0:T(8,128)S(1)}, u32[]{:S(2)}, u32[]{:S(2)}) %collective-permute-start.6) | collective-permute-done | bytes 147488 | tf_op jit(solution)/shard_map/ppermute | solution.py:55
  210.2 3.2 %collective-permute-start.7 = (f32[72,512]{1,0:T(8,128)S(1)}, f32[72,512]{1,0:T(8,128)S(1)}, u32[]{:S(2)}, u32[]{:S(2)}) collective-permute-start(f32[72,512]{1,0:T(8,128)S(1)} %add.169), channel_id=1, source_target_pairs={{0,4},{2,6},{4,0},{6,2},{1,5},{3,7},{5,1},{7,3},{8,12},{10,14},{12... | collective-permute-start | bytes 442376 | tf_op jit(solution)/shard_map/ppermute | solution.py:55
  213.4 5.2 %collective-permute-done.7 = f32[72,512]{1,0:T(8,128)S(1)} collective-permute-done((f32[72,512]{1,0:T(8,128)S(1)}, f32[72,512]{1,0:T(8,128)S(1)}, u32[]{:S(2)}, u32[]{:S(2)}) %collective-permute-start.7) | collective-permute-done | bytes 147488 | tf_op jit(solution)/shard_map/ppermute | solution.py:55
  218.6 1.9 collective-permute-start.8
  220.5 4.0 %collective-permute-done.8 = f32[72,512]{1,0:T(8,128)S(1)} collective-permute-done((f32[72,512]{1,0:T(8,128)S(1)}, f32[72,512]{1,0:T(8,128)S(1)}, u32[]{:S(2)}, u32[]{:S(2)}) %collective-permute-start.8) | collective-permute-done | bytes 147488 | tf_op jit(solution)/shard_map/ppermute | solution.py:55
  224.5 2.8 collective-permute-start.9
  227.3 5.4 %collective-permute-done.9 = f32[72,512]{1,0:T(8,128)S(1)} collective-permute-done((f32[72,512]{1,0:T(8,128)S(1)}, f32[72,512]{1,0:T(8,128)S(1)}, u32[]{:S(2)}, u32[]{:S(2)}) %collective-permute-start.9) | collective-permute-done | bytes 147488 | tf_op jit(solution)/shard_map/ppermute | solution.py:55
  232.8 4.4 %collective-permute-start.10 = (f32[72,512]{1,0:T(8,128)S(1)}, f32[72,512]{1,0:T(8,128)S(1)}, u32[]{:S(2)}, u32[]{:S(2)}) collective-permute-start(f32[72,512]{1,0:T(8,128)S(1)} %add.172), channel_id=1, source_target_pairs={{0,128},{32,160},{64,192},{96,224},{128,0},{160,32},{192,64},{224,... | collective-permute-start | bytes 442376 | tf_op jit(solution)/shard_map/ppermute | solution.py:55
  237.2 5.9 %collective-permute-done.10 = f32[72,512]{1,0:T(8,128)S(1)} collective-permute-done((f32[72,512]{1,0:T(8,128)S(1)}, f32[72,512]{1,0:T(8,128)S(1)}, u32[]{:S(2)}, u32[]{:S(2)}) %collective-permute-start.10) | collective-permute-done | bytes 147488 | tf_op jit(solution)/shard_map/ppermute | solution.py:55
  243.0 5.5 %collective-permute-start.11 = (f32[72,512]{1,0:T(8,128)S(1)}, f32[72,512]{1,0:T(8,128)S(1)}, u32[]{:S(2)}, u32[]{:S(2)}) collective-permute-start(f32[72,512]{1,0:T(8,128)S(1)} %add.173), channel_id=1, source_target_pairs={{0,256},{256,0},{1,257},{257,1},{2,258},{258,2},{3,259},{259,3},{4... | collective-permute-start | bytes 442376 | tf_op jit(solution)/shard_map/ppermute | solution.py:55
  248.6 5.8 %collective-permute-done.11 = f32[72,512]{1,0:T(8,128)S(1)} collective-permute-done((f32[72,512]{1,0:T(8,128)S(1)}, f32[72,512]{1,0:T(8,128)S(1)}, u32[]{:S(2)}, u32[]{:S(2)}) %collective-permute-start.11) | collective-permute-done | bytes 147488 | tf_op jit(solution)/shard_map/ppermute | solution.py:55
  256.4 5.8 %collective-permute-done.12 = f32[72,512]{1,0:T(8,128)S(1)} collective-permute-done((f32[72,512]{1,0:T(8,128)S(1)}, f32[72,512]{1,0:T(8,128)S(1)}, u32[]{:S(2)}, u32[]{:S(2)}) %collective-permute-start.12) | collective-permute-done | bytes 147488 | tf_op jit(solution)/shard_map/ppermute | solution.py:41
  264.1 7.4 %collective-permute-done.13 = f32[2,72,512]{2,1,0:T(8,128)S(1)} collective-permute-done((f32[2,72,512]{2,1,0:T(8,128)S(1)}, f32[2,72,512]{2,1,0:T(8,128)S(1)}, u32[]{:S(2)}, u32[]{:S(2)}) %collective-permute-start.13) | collective-permute-done | bytes 294944 | tf_op jit(solution)/shard_map/ppermute | solution.py:41
  271.6 12.1 %collective-permute-start.14 = (f32[288,512]{1,0:T(8,128)S(1)}, f32[288,512]{1,0:T(8,128)S(1)}, u32[]{:S(2)}, u32[]{:S(2)}) collective-permute-start(f32[288,512]{1,0:T(8,128)S(1)} %bitcast.69), channel_id=1, source_target_pairs={{0,1},{1,0},{2,3},{3,2},{4,5},{5,4},{6,7},{7,6},{8,9},{9,8},{10,11... | collective-permute-start | bytes 1769480 | tf_op jit(solution)/shard_map/ppermute | solution.py:41
  (49 shorter events, 15.1 us)
Async XLA Ops:
  7.2 173.4 %copy-start = (bf16[512,512]{1,0:T(8,128)(2,1)S(1)}, bf16[512,512]{1,0:T(8,128)(2,1)}, u32[]{:S(2)}) copy-start(bf16[512,512]{1,0:T(8,128)(2,1)} %param.15) | copy-start | bytes 1572868
  7.2 121.9 %all-gather.2.cloned.1.call-start = ((), (), s32[]{:S(2)}) async-start(), calls=%async_computation | async-start | bytes 8650752 | tf_op jit(solution)/shard_map/all_gather | solution.py:137
  21.6 4.7 %copy-start.3 = (s32[8,1]{0,1:T(1,128)S(1)}, s32[8,1]{0,1:T(1,128)}, u32[]{:S(2)}) copy-start(s32[8,1]{0,1:T(1,128)} %param.13) | copy-start | bytes 100
  136.4 10.6 %collective-permute-start = (f32[4,128,512]{2,1,0:T(8,128)}, f32[4,128,512]{2,1,0:T(8,128)S(1)}, u32[]{:S(2)}, u32[]{:S(2)}) collective-permute-start(f32[4,128,512]{2,1,0:T(8,128)} %shard_map.98), channel_id=1, source_target_pairs={{0,1},{1,0},{2,3},{3,2},{4,5},{5,4},{6,7},{7,6},{8,9},{9,8},{10,11... | collective-permute-start | bytes 3145736 | tf_op jit(solution)/shard_map/ppermute | solution.py:144
  148.5 15.7 %collective-permute-start.1 = (f32[2,128,512]{2,1,0:T(8,128)S(1)}, f32[2,128,512]{2,1,0:T(8,128)S(1)}, u32[]{:S(2)}, u32[]{:S(2)}) collective-permute-start(f32[2,128,512]{2,1,0:T(8,128)S(1)} %dynamic-slice_bitcast_fusion.1), channel_id=1, source_target_pairs={{0,2},{2,0},{4,6},{6,4},{1,3},{3,1},{5,7},{7,5},{8,10},{10,8},{12,... | collective-permute-start | bytes 1572872 | tf_op jit(solution)/shard_map/ppermute | solution.py:31
  151.5 29.1 %copy-start.1 = (bf16[128,512]{1,0:T(8,128)(2,1)S(1)}, bf16[128,512]{1,0:T(8,128)(2,1)}, u32[]{:S(2)}) copy-start(bf16[128,512]{1,0:T(8,128)(2,1)} %param.17) | copy-start | bytes 393220
  151.5 29.1 %copy-start.2 = (f32[512]{0:T(512)S(1)}, f32[512]{0:T(512)}, u32[]{:S(2)}) copy-start(f32[512]{0:T(512)} %param.16) | copy-start | bytes 6148
  164.3 16.2 %collective-permute-start.2 = (f32[128,512]{1,0:T(8,128)S(1)}, f32[128,512]{1,0:T(8,128)S(1)}, u32[]{:S(2)}, u32[]{:S(2)}) collective-permute-start(f32[128,512]{1,0:T(8,128)S(1)} %dynamic-slice_bitcast_fusion.3), channel_id=1, source_target_pairs={{0,4},{2,6},{4,0},{6,2},{1,5},{3,7},{5,1},{7,3},{8,12},{10,14},{12... | collective-permute-start | bytes 786440 | tf_op jit(solution)/shard_map/ppermute | solution.py:31
  182.1 4.4 %collective-permute-start.3 = (f32[288,512]{1,0:T(8,128)S(1)}, f32[288,512]{1,0:T(8,128)S(1)}, u32[]{:S(2)}, u32[]{:S(2)}) collective-permute-start(f32[288,512]{1,0:T(8,128)S(1)} %dynamic-slice_bitcast_fusion), channel_id=1, source_target_pairs={{0,1},{1,0},{2,3},{3,2},{4,5},{5,4},{6,7},{7,6},{8,9},{9,8},{10,11... | collective-permute-start | bytes 1769480 | tf_op jit(solution)/shard_map/ppermute | solution.py:31
  186.7 10.1 %collective-permute-start.4 = (f32[2,72,512]{2,1,0:T(8,128)S(1)}, f32[2,72,512]{2,1,0:T(8,128)S(1)}, u32[]{:S(2)}, u32[]{:S(2)}) collective-permute-start(f32[2,72,512]{2,1,0:T(8,128)S(1)} %dynamic-slice_bitcast_fusion.2), channel_id=1, source_target_pairs={{0,8},{8,0},{16,24},{24,16},{1,9},{9,1},{17,25},{25,17},{2,10},{10... | collective-permute-start | bytes 884744 | tf_op jit(solution)/shard_map/ppermute | solution.py:31
  196.9 7.4 %collective-permute-start.5 = (f32[72,512]{1,0:T(8,128)S(1)}, f32[72,512]{1,0:T(8,128)S(1)}, u32[]{:S(2)}, u32[]{:S(2)}) collective-permute-start(f32[72,512]{1,0:T(8,128)S(1)} %dynamic-slice_bitcast_fusion.4), channel_id=1, source_target_pairs={{0,16},{8,24},{16,0},{24,8},{1,17},{9,25},{17,1},{25,9},{2,18},{10... | collective-permute-start | bytes 442376 | tf_op jit(solution)/shard_map/ppermute | solution.py:31
  204.3 5.9 %collective-permute-start.6 = (f32[72,512]{1,0:T(8,128)S(1)}, f32[72,512]{1,0:T(8,128)S(1)}, u32[]{:S(2)}, u32[]{:S(2)}) collective-permute-start(f32[72,512]{1,0:T(8,128)S(1)} %bitcast_add_fusion.4), channel_id=1, source_target_pairs={{0,2},{2,0},{4,6},{6,4},{1,3},{3,1},{5,7},{7,5},{8,10},{10,8},{12,... | collective-permute-start | bytes 442376 | tf_op jit(solution)/shard_map/ppermute | solution.py:55
  210.2 8.4 %collective-permute-start.7 = (f32[72,512]{1,0:T(8,128)S(1)}, f32[72,512]{1,0:T(8,128)S(1)}, u32[]{:S(2)}, u32[]{:S(2)}) collective-permute-start(f32[72,512]{1,0:T(8,128)S(1)} %add.169), channel_id=1, source_target_pairs={{0,4},{2,6},{4,0},{6,2},{1,5},{3,7},{5,1},{7,3},{8,12},{10,14},{12... | collective-permute-start | bytes 442376 | tf_op jit(solution)/shard_map/ppermute | solution.py:55
  218.6 5.9 %collective-permute-start.8 = (f32[72,512]{1,0:T(8,128)S(1)}, f32[72,512]{1,0:T(8,128)S(1)}, u32[]{:S(2)}, u32[]{:S(2)}) collective-permute-start(f32[72,512]{1,0:T(8,128)S(1)} %add.170), channel_id=1, source_target_pairs={{0,32},{32,0},{64,96},{96,64},{128,160},{160,128},{192,224},{224,1... | collective-permute-start | bytes 442376 | tf_op jit(solution)/shard_map/ppermute | solution.py:55
  224.5 8.2 %collective-permute-start.9 = (f32[72,512]{1,0:T(8,128)S(1)}, f32[72,512]{1,0:T(8,128)S(1)}, u32[]{:S(2)}, u32[]{:S(2)}) collective-permute-start(f32[72,512]{1,0:T(8,128)S(1)} %add.171), channel_id=1, source_target_pairs={{0,64},{32,96},{64,0},{96,32},{128,192},{160,224},{192,128},{224,1... | collective-permute-start | bytes 442376 | tf_op jit(solution)/shard_map/ppermute | solution.py:55
  232.8 10.3 %collective-permute-start.10 = (f32[72,512]{1,0:T(8,128)S(1)}, f32[72,512]{1,0:T(8,128)S(1)}, u32[]{:S(2)}, u32[]{:S(2)}) collective-permute-start(f32[72,512]{1,0:T(8,128)S(1)} %add.172), channel_id=1, source_target_pairs={{0,128},{32,160},{64,192},{96,224},{128,0},{160,32},{192,64},{224,... | collective-permute-start | bytes 442376 | tf_op jit(solution)/shard_map/ppermute | solution.py:55
  243.0 11.4 %collective-permute-start.11 = (f32[72,512]{1,0:T(8,128)S(1)}, f32[72,512]{1,0:T(8,128)S(1)}, u32[]{:S(2)}, u32[]{:S(2)}) collective-permute-start(f32[72,512]{1,0:T(8,128)S(1)} %add.173), channel_id=1, source_target_pairs={{0,256},{256,0},{1,257},{257,1},{2,258},{258,2},{3,259},{259,3},{4... | collective-permute-start | bytes 442376 | tf_op jit(solution)/shard_map/ppermute | solution.py:55
  254.4 7.7 %collective-permute-start.12 = (f32[72,512]{1,0:T(8,128)S(1)}, f32[72,512]{1,0:T(8,128)S(1)}, u32[]{:S(2)}, u32[]{:S(2)}) collective-permute-start(f32[72,512]{1,0:T(8,128)S(1)} %add.174), channel_id=1, source_target_pairs={{0,16},{8,24},{16,0},{24,8},{1,17},{9,25},{17,1},{25,9},{2,18},{10... | collective-permute-start | bytes 442376 | tf_op jit(solution)/shard_map/ppermute | solution.py:41
  262.2 9.3 %collective-permute-start.13 = (f32[2,72,512]{2,1,0:T(8,128)S(1)}, f32[2,72,512]{2,1,0:T(8,128)S(1)}, u32[]{:S(2)}, u32[]{:S(2)}) collective-permute-start(f32[2,72,512]{2,1,0:T(8,128)S(1)} %pad_maximum_fusion.2), channel_id=1, source_target_pairs={{0,8},{8,0},{16,24},{24,16},{1,9},{9,1},{17,25},{25,17},{2,10},{10... | collective-permute-start | bytes 884744 | tf_op jit(solution)/shard_map/ppermute | solution.py:41
  271.6 13.7 %collective-permute-start.14 = (f32[288,512]{1,0:T(8,128)S(1)}, f32[288,512]{1,0:T(8,128)S(1)}, u32[]{:S(2)}, u32[]{:S(2)}) collective-permute-start(f32[288,512]{1,0:T(8,128)S(1)} %bitcast.69), channel_id=1, source_target_pairs={{0,1},{1,0},{2,3},{3,2},{4,5},{5,4},{6,7},{7,6},{8,9},{9,8},{10,11... | collective-permute-start | bytes 1769480 | tf_op jit(solution)/shard_map/ppermute | solution.py:41
Sparse Core Ops, SparseCore 0:
  19.8 109.2 all-gather.1

commit v11 on v10

--- a/solution.py
+++ b/solution.py
@@ -57,13 +57,11 @@
     return piece
 
 
-def _aggregate_kernel(parity_ref, cols_ref, tiles_ref, panels_hbm, out_ref, buf, sems):
+def _aggregate_kernel(rows_ref, cols_ref, tiles_ref, panels_hbm, out_ref, buf, sems):
     groups, slots = out_ref.shape[0], buf.shape[1]
-    stride = tiles_ref.shape[0] // groups
-    parity = parity_ref[0]
 
     def copies(j, slot):
-        g = stride * j + parity
+        g = rows_ref[j]
         return [
             pltpu.make_async_copy(panels_hbm.at[cols_ref[g * slots + k]], buf.at[slot, k], sems.at[slot, k])
             for k in range(slots)
@@ -81,7 +79,7 @@
         for c in pending:
             c.wait()
         rhs = buf[slot].reshape(slots * buf.shape[2], buf.shape[3])
-        out_ref[j] = jnp.dot(tiles_ref[stride * j + parity], rhs, preferred_element_type=jnp.float32)
+        out_ref[j] = jnp.dot(tiles_ref[rows_ref[j]], rhs, preferred_element_type=jnp.float32)
         if j + 1 < groups:
             pending = ahead
 
@@ -93,11 +91,11 @@
     return wide.transpose(0, 2, 1, 3).reshape(groups, tile_size, slots * tile_size)
 
 
-def _aggregate(cols, wide, panels, parity, stride):
+def _aggregate(cols, wide, panels, rows):
     groups, tile_size, width = wide.shape
     slots = width // tile_size
     feat_width = panels.shape[-1]
-    picked = groups // stride
+    picked = rows.shape[0]
     flops = 2 * picked * slots * tile_size * tile_size * feat_width
     moved = (picked * tile_size * width * 2 + picked * slots * tile_size * feat_width * 2
              + picked * tile_size * feat_width * 4)
@@ -116,7 +114,7 @@
             pltpu.SemaphoreType.DMA((2, slots)),
         ],
         cost_estimate=pl.CostEstimate(flops=flops, bytes_accessed=moved, transcendentals=0),
-    )(jnp.reshape(parity, (1,)).astype(jnp.int32), cols, wide, panels)
+    )(jnp.clip(rows, 0, groups - 1).astype(jnp.int32), cols, wide, panels)
 
 
 def shards(features, col_panels, block_counts, block_values, weight, bias, cotangent):
@@ -140,11 +138,16 @@
     cols = jnp.clip(local_cols, 0, all_panels.shape[0] - 1).reshape(-1)
     cores = sizes["core"]
     me_core = lax.axis_index("core")
-    sent = _aggregate(cols, wide, all_panels, cores - 1 - me_core, cores)
+    me_y = lax.axis_index("y_lo")
+    low_bit, high_bit = me_y % 2, (me_y // 2) % 2
+    j = jnp.arange(4, dtype=jnp.int32)
+    ys = ((high_bit ^ (j % 2)) * 2 + (low_bit ^ (j // 2))).astype(jnp.int32)
+    sent = _aggregate(cols, wide, all_panels, ys * cores + (cores - 1 - me_core))
     arrived = lax.ppermute(sent, "core", _xor_perm(cores, 1))
-    kept = _aggregate(cols, wide, all_panels, me_core, cores)
+    kept = _aggregate(cols, wide, all_panels, ys * cores + me_core)
     half = kept + arrived
-    summed_own = _halving_scatter(half, "y_lo", sizes["y_lo"], (0, 1))
+    after = half[:2] + lax.ppermute(half[2:], "y_lo", _xor_perm(sizes["y_lo"], 1))
+    summed_own = after[0] + lax.ppermute(after[1], "y_lo", _xor_perm(sizes["y_lo"], 2))
     own_rows = own_panels * tile_size
     aggregated = summed_own.reshape(own_rows, feat_width).astype(jnp.bfloat16)
     pre = jnp.dot(aggregated, weight, preferred_element_type=jnp.float32) + bias

time: 295 us -> 296 us (level)
  starting transfers between devices: 53 us -> 65.8 us
  waiting for transfers between devices: 178 us -> 166 us
    ppermute x5 -> x3, waiting for transfers between devices: 39.6 us -> 13.4 us  [_halving_scatter(): blocks = keep + lax.ppermute(send, axis, _xor_perm(n, 1 << bit))]
    ppermute x0 -> x2, waiting for transfers between devices: none -> 23.3 us  [the longest x1 12.1 us: shards(): lax.ppermute(half[2:], 'y_lo', _xor_perm(sizes['y_lo'], 1))]
    ppermute x0 -> x2, starting transfers between devices: none -> 7.58 us  [the longest x1 4.19 us: shards(): lax.ppermute(after[1], 'y_lo', _xor_perm(sizes['y_lo'], 2))]
    ppermute x3, starting transfers between devices: 15.9 us -> 23.3 us  [_doubling_gather(): other = lax.ppermute(piece, axis, _xor_perm(n, 1 << bit))]
    ppermute x5 -> x3, starting transfers between devices: 14.1 us -> 9.22 us  [_halving_scatter(): blocks = keep + lax.ppermute(send, axis, _xor_perm(n, 1 << bit))]
    ppermute x3, waiting for transfers between devices: 14.8 us -> 10 us  [_doubling_gather(): other = lax.ppermute(piece, axis, _xor_perm(n, 1 << bit))]
    ppermute x6, waiting for transfers between devices: 30.2 us -> 26.2 us  [_doubling_sum(): piece = piece + lax.ppermute(piece, axis, _xor_perm(n, bit))]
  transfers between devices with their start and end apart: 16 -> 16, of which waited for: 15 -> 15; matrix products, arithmetic and copies ran while one was open for 5% -> 6% of each run, Pallas kernels for 2% -> 2%
where the time goes in v11:
time: 296 us; the launch traced here: 295 us
  waiting for transfers between devices  166 us (56%)
  starting transfers between devices  65.8 us (22%)
  between operations  14.5 us (5%)
  Pallas kernels  14.4 us (5%)
  blocking collectives  12.4 us (4%)
  other arithmetic  10.8 us (4%)
  local copies, waits for them, and re-layouts  10.4 us (4%)
    all_gather x1, waiting for transfers between devices, shards(): gathered = lax.all_gather(gathered, ('z', 'x'), axis=0, tiled=True)  93 us
    ppermute x6, waiting for transfers between devices, _doubling_sum(): piece = piece + lax.ppermute(piece, axis, _xor_perm(n, bit))  26.2 us
    ppermute x3, starting transfers between devices, _doubling_gather(): other = lax.ppermute(piece, axis, _xor_perm(n, 1 << bit))  23.3 us
    ppermute x6, starting transfers between devices, _doubling_sum(): piece = piece + lax.ppermute(piece, axis, _xor_perm(n, bit))  22.5 us
    pallas_call x2, Pallas kernels, _aggregate(): pl.pallas_call(_aggregate_kernel, out_shape=jax.ShapeDtypeStruct((picked,...  14.4 us
    ppermute x3, waiting for transfers between devices, _halving_scatter(): blocks = keep + lax.ppermute(send, axis, _xor_perm(n, 1 << bit))  13.4 us
    all_gather x1, blocking collectives, shards(): gathered = lax.all_gather(features, 'y_hi', axis=0, tiled=True)  12.4 us
    ppermute x1, waiting for transfers between devices, shards(): lax.ppermute(half[2:], 'y_lo', _xor_perm(sizes['y_lo'], 1))  12.1 us
  transfers between devices with their start and end apart: 16, of which 15 were waited for; matrix products, arithmetic and copies ran while one was open for 6% of the time, Pallas kernels for 2%

profile of v11, /device:TPU:1, one launch (start us, length us, event | category | flops | bytes accessed | tf_op | source)
XLA Modules:
  0.0 295.5 jit_solution(4624823894457669929)
XLA Ops:
  7.2 12.4 %all_gather.6 = bf16[256,512]{1,0:T(8,128)(2,1)} all-gather(bf16[128,512]{1,0:T(8,128)(2,1)} %param.11), channel_id=1, replica_groups=mesh['y_hi'=2,'z'=8,'x'=4,'y_lo'=4,'core'=2] {'y_hi'}, dimensions={0}, use_global_device_ids=true | all-gather | bytes 393216 | tf_op jit(solution)/shard_map/all_gather | solution.py:134
  21.6 4.7 %copy.12 = bf16[8,1,12,128,128]{3,4,2,0,1:T(8,128)(2,1)} copy(bf16[8,1,12,128,128]{4,3,2,1,0:T(8,128)(2,1)} %param.14) | data formatting | bytes 6291456 | tf_op args[3]
  26.4 3.9 %bitcast_select_fusion = bf16[8,12,128,128]{2,3,1,0:T(8,128)(2,1)} fusion(bf16[8,1,12,128,128]{3,4,2,0,1:T(8,128)(2,1)} %copy.12, pred[8,12]{1,0:T(8,128)(4,1)S(1)} %iota_compare_fusion), kind=kLoop, calls=%fused_computation | loop fusion | flops 1572864 | bytes 6291552 | tf_op jit(solution)/shard_map/jit(_where)/select_n | solution.py:90
  30.3 4.7 %copy.13.tiles_ref = bf16[8,128,1536]{2,1,0:T(8,128)(2,1)} copy(bf16[8,128,1536]{1,2,0:T(8,128)(2,1)} %bitcast.57) | data formatting | bytes 6291456 | tf_op jit(solution)/shard_map/reshape | solution.py:91
  36.1 93.0 %all-gather.2.cloned.1.call-done = bf16[8192,512]{1,0:T(8,128)(2,1)} async-done(((bf16[256,512]{1,0:T(8,128)(2,1)}), bf16[8192,512]{1,0:T(8,128)(2,1)}) %all-gather.2.cloned.1.call-update) | async-done | bytes 8388624 | tf_op jit(solution)/shard_map/all_gather | solution.py:135
  129.1 7.2 %shard_map.98 = f32[4,128,512]{2,1,0:T(8,128)} custom-call(s32[4]{0:T(128)} %add_clamp_fusion.rows_ref, s32[96]{0:T(128)} %fusion.9.cols_ref, bf16[8,128,1536]{2,1,0:T(8,128)(2,1)} %copy.13.tiles_ref, bf16[64,128,512]{2,1,0:T(8,128)(2,1)} %bitcast.55), custom_call_target="tpu_custom_call" | custom-call | flops 805306368 | bytes 8912896 | tf_op jit(solution)/shard_map/pallas_call | solution.py:102
  136.2 3.2 %collective-permute-start = (f32[4,128,512]{2,1,0:T(8,128)}, f32[4,128,512]{2,1,0:T(8,128)S(1)}, u32[]{:S(2)}, u32[]{:S(2)}) collective-permute-start(f32[4,128,512]{2,1,0:T(8,128)} %shard_map.98), channel_id=1, source_target_pairs={{0,1},{1,0},{2,3},{3,2},{4,5},{5,4},{6,7},{7,6},{8,9},{9,8},{10,11... | collective-permute-start | bytes 3145736 | tf_op jit(solution)/shard_map/ppermute | solution.py:146
  140.0 7.2 %shard_map.97 = f32[4,128,512]{2,1,0:T(8,128)} custom-call(s32[4]{0:T(128)} %add_clamp_fusion.1.rows_ref, s32[96]{0:T(128)} %fusion.9.cols_ref, bf16[8,128,1536]{2,1,0:T(8,128)(2,1)} %copy.13.tiles_ref, bf16[64,128,512]{2,1,0:T(8,128)(2,1)} %bitcast.56), custom_call_target="tpu_custom_call" | custom-call | flops 805306368 | bytes 8912896 | tf_op jit(solution)/shard_map/pallas_call | solution.py:102
  148.7 3.4 %collective-permute-start.1 = (f32[2,128,512]{2,1,0:T(8,128)S(1)}, f32[2,128,512]{2,1,0:T(8,128)S(1)}, u32[]{:S(2)}, u32[]{:S(2)}) collective-permute-start(f32[2,128,512]{2,1,0:T(8,128)S(1)} %slice.56), channel_id=1, source_target_pairs={{0,2},{2,0},{4,6},{6,4},{1,3},{3,1},{5,7},{7,5},{8,10},{10,8},{12,... | collective-permute-start | bytes 1572872 | tf_op jit(solution)/shard_map/ppermute | solution.py:149
  152.1 12.1 %collective-permute-done.1 = f32[2,128,512]{2,1,0:T(8,128)S(1)} collective-permute-done((f32[2,128,512]{2,1,0:T(8,128)S(1)}, f32[2,128,512]{2,1,0:T(8,128)S(1)}, u32[]{:S(2)}, u32[]{:S(2)}) %collective-permute-start.1) | collective-permute-done | bytes 524320 | tf_op jit(solution)/shard_map/ppermute | solution.py:149
  164.3 4.2 %collective-permute-start.2 = (f32[128,512]{1,0:T(8,128)S(1)}, f32[128,512]{1,0:T(8,128)S(1)}, u32[]{:S(2)}, u32[]{:S(2)}) collective-permute-start(f32[128,512]{1,0:T(8,128)S(1)} %slice_bitcast_fusion), channel_id=1, source_target_pairs={{0,4},{2,6},{4,0},{6,2},{1,5},{3,7},{5,1},{7,3},{8,12},{10,14},{12... | collective-permute-start | bytes 786440 | tf_op jit(solution)/shard_map/ppermute | solution.py:150
  168.5 11.2 %collective-permute-done.2 = f32[128,512]{1,0:T(8,128)S(1)} collective-permute-done((f32[128,512]{1,0:T(8,128)S(1)}, f32[128,512]{1,0:T(8,128)S(1)}, u32[]{:S(2)}, u32[]{:S(2)}) %collective-permute-start.2) | collective-permute-done | bytes 262176 | tf_op jit(solution)/shard_map/ppermute | solution.py:150
  181.3 3.6 %collective-permute-start.3 = (f32[288,512]{1,0:T(8,128)S(1)}, f32[288,512]{1,0:T(8,128)S(1)}, u32[]{:S(2)}, u32[]{:S(2)}) collective-permute-start(f32[288,512]{1,0:T(8,128)S(1)} %dynamic-slice_bitcast_fusion), channel_id=1, source_target_pairs={{0,1},{1,0},{2,3},{3,2},{4,5},{5,4},{6,7},{7,6},{8,9},{9,8},{10,11... | collective-permute-start | bytes 1769480 | tf_op jit(solution)/shard_map/ppermute | solution.py:31
  189.0 7.8 %collective-permute-done.4 = f32[2,72,512]{2,1,0:T(8,128)S(1)} collective-permute-done((f32[2,72,512]{2,1,0:T(8,128)S(1)}, f32[2,72,512]{2,1,0:T(8,128)S(1)}, u32[]{:S(2)}, u32[]{:S(2)}) %collective-permute-start.4) | collective-permute-done | bytes 294944 | tf_op jit(solution)/shard_map/ppermute | solution.py:31
  196.9 3.4 %collective-permute-start.5 = (f32[72,512]{1,0:T(8,128)S(1)}, f32[72,512]{1,0:T(8,128)S(1)}, u32[]{:S(2)}, u32[]{:S(2)}) collective-permute-start(f32[72,512]{1,0:T(8,128)S(1)} %dynamic-slice_bitcast_fusion.2), channel_id=1, source_target_pairs={{0,16},{8,24},{16,0},{24,8},{1,17},{9,25},{17,1},{25,9},{2,18},{10... | collective-permute-start | bytes 442376 | tf_op jit(solution)/shard_map/ppermute | solution.py:31
  200.3 4.0 %collective-permute-done.5 = f32[72,512]{1,0:T(8,128)S(1)} collective-permute-done((f32[72,512]{1,0:T(8,128)S(1)}, f32[72,512]{1,0:T(8,128)S(1)}, u32[]{:S(2)}, u32[]{:S(2)}) %collective-permute-start.5) | collective-permute-done | bytes 147488 | tf_op jit(solution)/shard_map/ppermute | solution.py:31
  204.3 2.3 collective-permute-start.6
  206.6 3.6 %collective-permute-done.6 = f32[72,512]{1,0:T(8,128)S(1)} collective-permute-done((f32[72,512]{1,0:T(8,128)S(1)}, f32[72,512]{1,0:T(8,128)S(1)}, u32[]{:S(2)}, u32[]{:S(2)}) %collective-permute-start.6) | collective-permute-done | bytes 147488 | tf_op jit(solution)/shard_map/ppermute | solution.py:55
  210.2 3.9 %collective-permute-start.7 = (f32[72,512]{1,0:T(8,128)S(1)}, f32[72,512]{1,0:T(8,128)S(1)}, u32[]{:S(2)}, u32[]{:S(2)}) collective-permute-start(f32[72,512]{1,0:T(8,128)S(1)} %add.176), channel_id=1, source_target_pairs={{0,4},{2,6},{4,0},{6,2},{1,5},{3,7},{5,1},{7,3},{8,12},{10,14},{12... | collective-permute-start | bytes 442376 | tf_op jit(solution)/shard_map/ppermute | solution.py:55
  214.1 4.4 %collective-permute-done.7 = f32[72,512]{1,0:T(8,128)S(1)} collective-permute-done((f32[72,512]{1,0:T(8,128)S(1)}, f32[72,512]{1,0:T(8,128)S(1)}, u32[]{:S(2)}, u32[]{:S(2)}) %collective-permute-start.7) | collective-permute-done | bytes 147488 | tf_op jit(solution)/shard_map/ppermute | solution.py:55
  220.5 4.0 %collective-permute-done.8 = f32[72,512]{1,0:T(8,128)S(1)} collective-permute-done((f32[72,512]{1,0:T(8,128)S(1)}, f32[72,512]{1,0:T(8,128)S(1)}, u32[]{:S(2)}, u32[]{:S(2)}) %collective-permute-start.8) | collective-permute-done | bytes 147488 | tf_op jit(solution)/shard_map/ppermute | solution.py:55
  224.5 3.6 %collective-permute-start.9 = (f32[72,512]{1,0:T(8,128)S(1)}, f32[72,512]{1,0:T(8,128)S(1)}, u32[]{:S(2)}, u32[]{:S(2)}) collective-permute-start(f32[72,512]{1,0:T(8,128)S(1)} %add.178), channel_id=1, source_target_pairs={{0,64},{32,96},{64,0},{96,32},{128,192},{160,224},{192,128},{224,1... | collective-permute-start | bytes 442376 | tf_op jit(solution)/shard_map/ppermute | solution.py:55
  228.1 4.8 %collective-permute-done.9 = f32[72,512]{1,0:T(8,128)S(1)} collective-permute-done((f32[72,512]{1,0:T(8,128)S(1)}, f32[72,512]{1,0:T(8,128)S(1)}, u32[]{:S(2)}, u32[]{:S(2)}) %collective-permute-start.9) | collective-permute-done | bytes 147488 | tf_op jit(solution)/shard_map/ppermute | solution.py:55
  232.9 4.6 %collective-permute-start.10 = (f32[72,512]{1,0:T(8,128)S(1)}, f32[72,512]{1,0:T(8,128)S(1)}, u32[]{:S(2)}, u32[]{:S(2)}) collective-permute-start(f32[72,512]{1,0:T(8,128)S(1)} %add.179), channel_id=1, source_target_pairs={{0,128},{32,160},{64,192},{96,224},{128,0},{160,32},{192,64},{224,... | collective-permute-start | bytes 442376 | tf_op jit(solution)/shard_map/ppermute | solution.py:55
  237.5 5.9 %collective-permute-done.10 = f32[72,512]{1,0:T(8,128)S(1)} collective-permute-done((f32[72,512]{1,0:T(8,128)S(1)}, f32[72,512]{1,0:T(8,128)S(1)}, u32[]{:S(2)}, u32[]{:S(2)}) %collective-permute-start.10) | collective-permute-done | bytes 147488 | tf_op jit(solution)/shard_map/ppermute | solution.py:55
  243.4 6.3 %collective-permute-start.11 = (f32[72,512]{1,0:T(8,128)S(1)}, f32[72,512]{1,0:T(8,128)S(1)}, u32[]{:S(2)}, u32[]{:S(2)}) collective-permute-start(f32[72,512]{1,0:T(8,128)S(1)} %add.180), channel_id=1, source_target_pairs={{0,256},{256,0},{1,257},{257,1},{2,258},{258,2},{3,259},{259,3},{4... | collective-permute-start | bytes 442376 | tf_op jit(solution)/shard_map/ppermute | solution.py:55
  249.7 3.5 %collective-permute-done.11 = f32[72,512]{1,0:T(8,128)S(1)} collective-permute-done((f32[72,512]{1,0:T(8,128)S(1)}, f32[72,512]{1,0:T(8,128)S(1)}, u32[]{:S(2)}, u32[]{:S(2)}) %collective-permute-start.11) | collective-permute-done | bytes 147488 | tf_op jit(solution)/shard_map/ppermute | solution.py:55
  253.2 3.1 %collective-permute-start.12 = (f32[72,512]{1,0:T(8,128)S(1)}, f32[72,512]{1,0:T(8,128)S(1)}, u32[]{:S(2)}, u32[]{:S(2)}) collective-permute-start(f32[72,512]{1,0:T(8,128)S(1)} %add.181), channel_id=1, source_target_pairs={{0,16},{8,24},{16,0},{24,8},{1,17},{9,25},{17,1},{25,9},{2,18},{10... | collective-permute-start | bytes 442376 | tf_op jit(solution)/shard_map/ppermute | solution.py:41
  256.3 4.3 %collective-permute-done.12 = f32[72,512]{1,0:T(8,128)S(1)} collective-permute-done((f32[72,512]{1,0:T(8,128)S(1)}, f32[72,512]{1,0:T(8,128)S(1)}, u32[]{:S(2)}, u32[]{:S(2)}) %collective-permute-start.12) | collective-permute-done | bytes 147488 | tf_op jit(solution)/shard_map/ppermute | solution.py:41
  260.7 3.4 %collective-permute-start.13 = (f32[2,72,512]{2,1,0:T(8,128)S(1)}, f32[2,72,512]{2,1,0:T(8,128)S(1)}, u32[]{:S(2)}, u32[]{:S(2)}) collective-permute-start(f32[2,72,512]{2,1,0:T(8,128)S(1)} %pad_maximum_fusion.2), channel_id=1, source_target_pairs={{0,8},{8,0},{16,24},{24,16},{1,9},{9,1},{17,25},{25,17},{2,10},{10... | collective-permute-start | bytes 884744 | tf_op jit(solution)/shard_map/ppermute | solution.py:41
  264.1 4.1 %collective-permute-done.13 = f32[2,72,512]{2,1,0:T(8,128)S(1)} collective-permute-done((f32[2,72,512]{2,1,0:T(8,128)S(1)}, f32[2,72,512]{2,1,0:T(8,128)S(1)}, u32[]{:S(2)}, u32[]{:S(2)}) %collective-permute-start.13) | collective-permute-done | bytes 294944 | tf_op jit(solution)/shard_map/ppermute | solution.py:41
  268.3 16.8 %collective-permute-start.14 = (f32[288,512]{1,0:T(8,128)S(1)}, f32[288,512]{1,0:T(8,128)S(1)}, u32[]{:S(2)}, u32[]{:S(2)}) collective-permute-start(f32[288,512]{1,0:T(8,128)S(1)} %bitcast.62), channel_id=1, source_target_pairs={{0,1},{1,0},{2,3},{3,2},{4,5},{5,4},{6,7},{7,6},{8,9},{9,8},{10,11... | collective-permute-start | bytes 1769480 | tf_op jit(solution)/shard_map/ppermute | solution.py:41
  (51 shorter events, 16.5 us)
Async XLA Ops:
  7.2 172.6 %copy-start = (bf16[512,512]{1,0:T(8,128)(2,1)S(1)}, bf16[512,512]{1,0:T(8,128)(2,1)}, u32[]{:S(2)}) copy-start(bf16[512,512]{1,0:T(8,128)(2,1)} %param.15) | copy-start | bytes 1572868
  7.2 121.9 %all-gather.2.cloned.1.call-start = ((), (), s32[]{:S(2)}) async-start(), calls=%async_computation | async-start | bytes 8650752 | tf_op jit(solution)/shard_map/all_gather | solution.py:135
  21.6 4.7 %copy-start.3 = (s32[8,1]{0,1:T(1,128)S(1)}, s32[8,1]{0,1:T(1,128)}, u32[]{:S(2)}) copy-start(s32[8,1]{0,1:T(1,128)} %param.13) | copy-start | bytes 100
  136.2 11.0 %collective-permute-start = (f32[4,128,512]{2,1,0:T(8,128)}, f32[4,128,512]{2,1,0:T(8,128)S(1)}, u32[]{:S(2)}, u32[]{:S(2)}) collective-permute-start(f32[4,128,512]{2,1,0:T(8,128)} %shard_map.98), channel_id=1, source_target_pairs={{0,1},{1,0},{2,3},{3,2},{4,5},{5,4},{6,7},{7,6},{8,9},{9,8},{10,11... | collective-permute-start | bytes 3145736 | tf_op jit(solution)/shard_map/ppermute | solution.py:146
  148.7 31.1 %copy-start.1 = (bf16[128,512]{1,0:T(8,128)(2,1)S(1)}, bf16[128,512]{1,0:T(8,128)(2,1)}, u32[]{:S(2)}) copy-start(bf16[128,512]{1,0:T(8,128)(2,1)} %param.17) | copy-start | bytes 393220
  148.7 31.1 %copy-start.2 = (f32[512]{0:T(512)S(1)}, f32[512]{0:T(512)}, u32[]{:S(2)}) copy-start(f32[512]{0:T(512)} %param.16) | copy-start | bytes 6148
  148.7 15.5 %collective-permute-start.1 = (f32[2,128,512]{2,1,0:T(8,128)S(1)}, f32[2,128,512]{2,1,0:T(8,128)S(1)}, u32[]{:S(2)}, u32[]{:S(2)}) collective-permute-start(f32[2,128,512]{2,1,0:T(8,128)S(1)} %slice.56), channel_id=1, source_target_pairs={{0,2},{2,0},{4,6},{6,4},{1,3},{3,1},{5,7},{7,5},{8,10},{10,8},{12,... | collective-permute-start | bytes 1572872 | tf_op jit(solution)/shard_map/ppermute | solution.py:149
  164.3 15.4 %collective-permute-start.2 = (f32[128,512]{1,0:T(8,128)S(1)}, f32[128,512]{1,0:T(8,128)S(1)}, u32[]{:S(2)}, u32[]{:S(2)}) collective-permute-start(f32[128,512]{1,0:T(8,128)S(1)} %slice_bitcast_fusion), channel_id=1, source_target_pairs={{0,4},{2,6},{4,0},{6,2},{1,5},{3,7},{5,1},{7,3},{8,12},{10,14},{12... | collective-permute-start | bytes 786440 | tf_op jit(solution)/shard_map/ppermute | solution.py:150
  181.3 5.2 %collective-permute-start.3 = (f32[288,512]{1,0:T(8,128)S(1)}, f32[288,512]{1,0:T(8,128)S(1)}, u32[]{:S(2)}, u32[]{:S(2)}) collective-permute-start(f32[288,512]{1,0:T(8,128)S(1)} %dynamic-slice_bitcast_fusion), channel_id=1, source_target_pairs={{0,1},{1,0},{2,3},{3,2},{4,5},{5,4},{6,7},{7,6},{8,9},{9,8},{10,11... | collective-permute-start | bytes 1769480 | tf_op jit(solution)/shard_map/ppermute | solution.py:31
  186.7 10.1 %collective-permute-start.4 = (f32[2,72,512]{2,1,0:T(8,128)S(1)}, f32[2,72,512]{2,1,0:T(8,128)S(1)}, u32[]{:S(2)}, u32[]{:S(2)}) collective-permute-start(f32[2,72,512]{2,1,0:T(8,128)S(1)} %dynamic-slice_bitcast_fusion.1), channel_id=1, source_target_pairs={{0,8},{8,0},{16,24},{24,16},{1,9},{9,1},{17,25},{25,17},{2,10},{10... | collective-permute-start | bytes 884744 | tf_op jit(solution)/shard_map/ppermute | solution.py:31
  196.9 7.4 %collective-permute-start.5 = (f32[72,512]{1,0:T(8,128)S(1)}, f32[72,512]{1,0:T(8,128)S(1)}, u32[]{:S(2)}, u32[]{:S(2)}) collective-permute-start(f32[72,512]{1,0:T(8,128)S(1)} %dynamic-slice_bitcast_fusion.2), channel_id=1, source_target_pairs={{0,16},{8,24},{16,0},{24,8},{1,17},{9,25},{17,1},{25,9},{2,18},{10... | collective-permute-start | bytes 442376 | tf_op jit(solution)/shard_map/ppermute | solution.py:31
  204.3 5.9 %collective-permute-start.6 = (f32[72,512]{1,0:T(8,128)S(1)}, f32[72,512]{1,0:T(8,128)S(1)}, u32[]{:S(2)}, u32[]{:S(2)}) collective-permute-start(f32[72,512]{1,0:T(8,128)S(1)} %bitcast_add_fusion.2), channel_id=1, source_target_pairs={{0,2},{2,0},{4,6},{6,4},{1,3},{3,1},{5,7},{7,5},{8,10},{10,8},{12,... | collective-permute-start | bytes 442376 | tf_op jit(solution)/shard_map/ppermute | solution.py:55
  210.2 8.4 %collective-permute-start.7 = (f32[72,512]{1,0:T(8,128)S(1)}, f32[72,512]{1,0:T(8,128)S(1)}, u32[]{:S(2)}, u32[]{:S(2)}) collective-permute-start(f32[72,512]{1,0:T(8,128)S(1)} %add.176), channel_id=1, source_target_pairs={{0,4},{2,6},{4,0},{6,2},{1,5},{3,7},{5,1},{7,3},{8,12},{10,14},{12... | collective-permute-start | bytes 442376 | tf_op jit(solution)/shard_map/ppermute | solution.py:55
  218.6 5.9 %collective-permute-start.8 = (f32[72,512]{1,0:T(8,128)S(1)}, f32[72,512]{1,0:T(8,128)S(1)}, u32[]{:S(2)}, u32[]{:S(2)}) collective-permute-start(f32[72,512]{1,0:T(8,128)S(1)} %add.177), channel_id=1, source_target_pairs={{0,32},{32,0},{64,96},{96,64},{128,160},{160,128},{192,224},{224,1... | collective-permute-start | bytes 442376 | tf_op jit(solution)/shard_map/ppermute | solution.py:55
  224.5 8.4 %collective-permute-start.9 = (f32[72,512]{1,0:T(8,128)S(1)}, f32[72,512]{1,0:T(8,128)S(1)}, u32[]{:S(2)}, u32[]{:S(2)}) collective-permute-start(f32[72,512]{1,0:T(8,128)S(1)} %add.178), channel_id=1, source_target_pairs={{0,64},{32,96},{64,0},{96,32},{128,192},{160,224},{192,128},{224,1... | collective-permute-start | bytes 442376 | tf_op jit(solution)/shard_map/ppermute | solution.py:55
  232.9 10.5 %collective-permute-start.10 = (f32[72,512]{1,0:T(8,128)S(1)}, f32[72,512]{1,0:T(8,128)S(1)}, u32[]{:S(2)}, u32[]{:S(2)}) collective-permute-start(f32[72,512]{1,0:T(8,128)S(1)} %add.179), channel_id=1, source_target_pairs={{0,128},{32,160},{64,192},{96,224},{128,0},{160,32},{192,64},{224,... | collective-permute-start | bytes 442376 | tf_op jit(solution)/shard_map/ppermute | solution.py:55
  243.4 9.8 %collective-permute-start.11 = (f32[72,512]{1,0:T(8,128)S(1)}, f32[72,512]{1,0:T(8,128)S(1)}, u32[]{:S(2)}, u32[]{:S(2)}) collective-permute-start(f32[72,512]{1,0:T(8,128)S(1)} %add.180), channel_id=1, source_target_pairs={{0,256},{256,0},{1,257},{257,1},{2,258},{258,2},{3,259},{259,3},{4... | collective-permute-start | bytes 442376 | tf_op jit(solution)/shard_map/ppermute | solution.py:55
  253.2 7.4 %collective-permute-start.12 = (f32[72,512]{1,0:T(8,128)S(1)}, f32[72,512]{1,0:T(8,128)S(1)}, u32[]{:S(2)}, u32[]{:S(2)}) collective-permute-start(f32[72,512]{1,0:T(8,128)S(1)} %add.181), channel_id=1, source_target_pairs={{0,16},{8,24},{16,0},{24,8},{1,17},{9,25},{17,1},{25,9},{2,18},{10... | collective-permute-start | bytes 442376 | tf_op jit(solution)/shard_map/ppermute | solution.py:41
  260.7 7.5 %collective-permute-start.13 = (f32[2,72,512]{2,1,0:T(8,128)S(1)}, f32[2,72,512]{2,1,0:T(8,128)S(1)}, u32[]{:S(2)}, u32[]{:S(2)}) collective-permute-start(f32[2,72,512]{2,1,0:T(8,128)S(1)} %pad_maximum_fusion.2), channel_id=1, source_target_pairs={{0,8},{8,0},{16,24},{24,16},{1,9},{9,1},{17,25},{25,17},{2,10},{10... | collective-permute-start | bytes 884744 | tf_op jit(solution)/shard_map/ppermute | solution.py:41
  268.3 18.4 %collective-permute-start.14 = (f32[288,512]{1,0:T(8,128)S(1)}, f32[288,512]{1,0:T(8,128)S(1)}, u32[]{:S(2)}, u32[]{:S(2)}) collective-permute-start(f32[288,512]{1,0:T(8,128)S(1)} %bitcast.62), channel_id=1, source_target_pairs={{0,1},{1,0},{2,3},{3,2},{4,5},{5,4},{6,7},{7,6},{8,9},{9,8},{10,11... | collective-permute-start | bytes 1769480 | tf_op jit(solution)/shard_map/ppermute | solution.py:41
Sparse Core Ops, SparseCore 0:
  19.8 109.2 all-gather.1

commit v12 on v10

--- a/solution.py
+++ b/solution.py
@@ -57,7 +57,7 @@
     return piece
 
 
-def _aggregate_kernel(parity_ref, cols_ref, tiles_ref, panels_hbm, out_ref, buf, sems):
+def _aggregate_kernel(parity_ref, cols_ref, tiles_ref, panels_hbm, out_ref, buf, sems, tbuf, tsems):
     groups, slots = out_ref.shape[0], buf.shape[1]
     stride = tiles_ref.shape[0] // groups
     parity = parity_ref[0]
@@ -67,7 +67,7 @@
         return [
             pltpu.make_async_copy(panels_hbm.at[cols_ref[g * slots + k]], buf.at[slot, k], sems.at[slot, k])
             for k in range(slots)
-        ]
+        ] + [pltpu.make_async_copy(tiles_ref.at[g], tbuf.at[slot], tsems.at[slot])]
 
     pending = copies(0, 0)
     for c in pending:
@@ -81,7 +81,7 @@
         for c in pending:
             c.wait()
         rhs = buf[slot].reshape(slots * buf.shape[2], buf.shape[3])
-        out_ref[j] = jnp.dot(tiles_ref[stride * j + parity], rhs, preferred_element_type=jnp.float32)
+        out_ref[j] = jnp.dot(tbuf[slot], rhs, preferred_element_type=jnp.float32)
         if j + 1 < groups:
             pending = ahead
 
@@ -107,13 +107,15 @@
         in_specs=[
             pl.BlockSpec(memory_space=pltpu.SMEM),
             pl.BlockSpec(memory_space=pltpu.SMEM),
-            pl.BlockSpec(memory_space=pltpu.VMEM),
+            pl.BlockSpec(memory_space=pl.ANY),
             pl.BlockSpec(memory_space=pl.ANY),
         ],
         out_specs=pl.BlockSpec(memory_space=pltpu.VMEM),
         scratch_shapes=[
             pltpu.VMEM((2, slots, tile_size, feat_width), panels.dtype),
             pltpu.SemaphoreType.DMA((2, slots)),
+            pltpu.VMEM((2, tile_size, width), wide.dtype),
+            pltpu.SemaphoreType.DMA((2,)),
         ],
         cost_estimate=pl.CostEstimate(flops=flops, bytes_accessed=moved, transcendentals=0),
     )(jnp.reshape(parity, (1,)).astype(jnp.int32), cols, wide, panels)

time: 295 us -> 294 us (level)
  starting transfers between devices: 53 us -> 62 us
  waiting for transfers between devices: 178 us -> 169 us
    ppermute x3, starting transfers between devices: 15.9 us -> 21.2 us  [_doubling_gather(): other = lax.ppermute(piece, axis, _xor_perm(n, 1 << bit))]
    ppermute x6, waiting for transfers between devices: 30.2 us -> 26.4 us  [_doubling_sum(): piece = piece + lax.ppermute(piece, axis, _xor_perm(n, bit))]
    ppermute x3, waiting for transfers between devices: 14.8 us -> 11.4 us  [_doubling_gather(): other = lax.ppermute(piece, axis, _xor_perm(n, 1 << bit))]
where the time goes in v12:
time: 294 us; the launch traced here: 293 us
  waiting for transfers between devices  169 us (57%)
  starting transfers between devices  62 us (21%)
  between operations  14.6 us (5%)
  Pallas kernels  13.3 us (5%)
  blocking collectives  12.4 us (4%)
  local copies, waits for them, and re-layouts  10.4 us (4%)
  other arithmetic  9.73 us (3%)
    all_gather x1, waiting for transfers between devices, shards(): gathered = lax.all_gather(gathered, ('z', 'x'), axis=0, tiled=True)  93.5 us
    ppermute x5, waiting for transfers between devices, _halving_scatter(): blocks = keep + lax.ppermute(send, axis, _xor_perm(n, 1 << bit))  37.9 us
    ppermute x6, waiting for transfers between devices, _doubling_sum(): piece = piece + lax.ppermute(piece, axis, _xor_perm(n, bit))  26.4 us
    ppermute x6, starting transfers between devices, _doubling_sum(): piece = piece + lax.ppermute(piece, axis, _xor_perm(n, bit))  22 us
    ppermute x3, starting transfers between devices, _doubling_gather(): other = lax.ppermute(piece, axis, _xor_perm(n, 1 << bit))  21.2 us
    ppermute x5, starting transfers between devices, _halving_scatter(): blocks = keep + lax.ppermute(send, axis, _xor_perm(n, 1 << bit))  15.4 us
    pallas_call x2, Pallas kernels, _aggregate(): pl.pallas_call(_aggregate_kernel, out_shape=jax.ShapeDtypeStruct((picked,...  13.3 us
    all_gather x1, blocking collectives, shards(): gathered = lax.all_gather(features, 'y_hi', axis=0, tiled=True)  12.4 us
  transfers between devices with their start and end apart: 16, of which 15 were waited for; matrix products, arithmetic and copies ran while one was open for 5% of the time, Pallas kernels for 2%

profile of v12, /device:TPU:1, one launch (start us, length us, event | category | flops | bytes accessed | tf_op | source)
XLA Modules:
  0.0 292.9 jit_solution(9492488675126856900)
XLA Ops:
  7.2 12.4 %all_gather.6 = bf16[256,512]{1,0:T(8,128)(2,1)} all-gather(bf16[128,512]{1,0:T(8,128)(2,1)} %param.11), channel_id=1, replica_groups=mesh['y_hi'=2,'z'=8,'x'=4,'y_lo'=4,'core'=2] {'y_hi'}, dimensions={0}, use_global_device_ids=true | all-gather | bytes 393216 | tf_op jit(solution)/shard_map/all_gather | solution.py:138
  21.6 4.7 %copy.12 = bf16[8,1,12,128,128]{3,4,2,0,1:T(8,128)(2,1)} copy(bf16[8,1,12,128,128]{4,3,2,1,0:T(8,128)(2,1)} %param.14) | data formatting | bytes 6291456 | tf_op args[3]
  26.4 3.9 %bitcast_select_fusion = bf16[8,12,128,128]{2,3,1,0:T(8,128)(2,1)} fusion(bf16[8,1,12,128,128]{3,4,2,0,1:T(8,128)(2,1)} %copy.12, pred[8,12]{1,0:T(8,128)(4,1)S(1)} %iota_compare_fusion), kind=kLoop, calls=%fused_computation | loop fusion | flops 1572864 | bytes 6291552 | tf_op jit(solution)/shard_map/jit(_where)/select_n | solution.py:92
  30.3 4.7 %copy.13.tiles_ref = bf16[8,128,1536]{2,1,0:T(8,128)(2,1)} copy(bf16[8,128,1536]{1,2,0:T(8,128)(2,1)} %bitcast.62) | data formatting | bytes 6291456 | tf_op jit(solution)/shard_map/reshape | solution.py:93
  35.6 93.5 %all-gather.2.cloned.1.call-done = bf16[8192,512]{1,0:T(8,128)(2,1)} async-done(((bf16[256,512]{1,0:T(8,128)(2,1)}), bf16[8192,512]{1,0:T(8,128)(2,1)}) %all-gather.2.cloned.1.call-update) | async-done | bytes 8388624 | tf_op jit(solution)/shard_map/all_gather | solution.py:139
  129.1 6.7 %shard_map.98 = f32[4,128,512]{2,1,0:T(8,128)} custom-call(s32[1]{0:T(128)} %bitcast.6.parity_ref, s32[96]{0:T(128)} %fusion.3.cols_ref, bf16[8,128,1536]{2,1,0:T(8,128)(2,1)} %copy.13.tiles_ref, bf16[64,128,512]{2,1,0:T(8,128)(2,1)} %bitcast.60), custom_call_target="tpu_custom_call" | custom-call | flops 805306368 | bytes 8912896 | tf_op jit(solution)/shard_map/pallas_call | solution.py:104
  135.8 3.3 %collective-permute-start = (f32[4,128,512]{2,1,0:T(8,128)}, f32[4,128,512]{2,1,0:T(8,128)S(1)}, u32[]{:S(2)}, u32[]{:S(2)}) collective-permute-start(f32[4,128,512]{2,1,0:T(8,128)} %shard_map.98), channel_id=1, source_target_pairs={{0,1},{1,0},{2,3},{3,2},{4,5},{5,4},{6,7},{7,6},{8,9},{9,8},{10,11... | collective-permute-start | bytes 3145736 | tf_op jit(solution)/shard_map/ppermute | solution.py:146
  139.1 6.7 %shard_map.97 = f32[4,128,512]{2,1,0:T(8,128)} custom-call(s32[1]{0:T(128)} %bitcast.parity_ref, s32[96]{0:T(128)} %fusion.3.cols_ref, bf16[8,128,1536]{2,1,0:T(8,128)(2,1)} %copy.13.tiles_ref, bf16[64,128,512]{2,1,0:T(8,128)(2,1)} %bitcast.61), custom_call_target="tpu_custom_call" | custom-call | flops 805306368 | bytes 8912896 | tf_op jit(solution)/shard_map/pallas_call | solution.py:104
  147.2 3.1 %collective-permute-start.1 = (f32[2,128,512]{2,1,0:T(8,128)S(1)}, f32[2,128,512]{2,1,0:T(8,128)S(1)}, u32[]{:S(2)}, u32[]{:S(2)}) collective-permute-start(f32[2,128,512]{2,1,0:T(8,128)S(1)} %dynamic-slice_bitcast_fusion.1), channel_id=1, source_target_pairs={{0,2},{2,0},{4,6},{6,4},{1,3},{3,1},{5,7},{7,5},{8,10},{10,8},{12,... | collective-permute-start | bytes 1572872 | tf_op jit(solution)/shard_map/ppermute | solution.py:31
  150.4 12.2 %collective-permute-done.1 = f32[2,128,512]{2,1,0:T(8,128)S(1)} collective-permute-done((f32[2,128,512]{2,1,0:T(8,128)S(1)}, f32[2,128,512]{2,1,0:T(8,128)S(1)}, u32[]{:S(2)}, u32[]{:S(2)}) %collective-permute-start.1) | collective-permute-done | bytes 524320 | tf_op jit(solution)/shard_map/ppermute | solution.py:31
  162.7 4.0 %collective-permute-start.2 = (f32[128,512]{1,0:T(8,128)S(1)}, f32[128,512]{1,0:T(8,128)S(1)}, u32[]{:S(2)}, u32[]{:S(2)}) collective-permute-start(f32[128,512]{1,0:T(8,128)S(1)} %dynamic-slice_bitcast_fusion.3), channel_id=1, source_target_pairs={{0,4},{2,6},{4,0},{6,2},{1,5},{3,7},{5,1},{7,3},{8,12},{10,14},{12... | collective-permute-start | bytes 786440 | tf_op jit(solution)/shard_map/ppermute | solution.py:31
  166.8 11.7 %collective-permute-done.2 = f32[128,512]{1,0:T(8,128)S(1)} collective-permute-done((f32[128,512]{1,0:T(8,128)S(1)}, f32[128,512]{1,0:T(8,128)S(1)}, u32[]{:S(2)}, u32[]{:S(2)}) %collective-permute-start.2) | collective-permute-done | bytes 262176 | tf_op jit(solution)/shard_map/ppermute | solution.py:31
  180.1 3.3 %collective-permute-start.3 = (f32[288,512]{1,0:T(8,128)S(1)}, f32[288,512]{1,0:T(8,128)S(1)}, u32[]{:S(2)}, u32[]{:S(2)}) collective-permute-start(f32[288,512]{1,0:T(8,128)S(1)} %dynamic-slice_bitcast_fusion), channel_id=1, source_target_pairs={{0,1},{1,0},{2,3},{3,2},{4,5},{5,4},{6,7},{7,6},{8,9},{9,8},{10,11... | collective-permute-start | bytes 1769480 | tf_op jit(solution)/shard_map/ppermute | solution.py:31
  187.1 8.1 %collective-permute-done.4 = f32[2,72,512]{2,1,0:T(8,128)S(1)} collective-permute-done((f32[2,72,512]{2,1,0:T(8,128)S(1)}, f32[2,72,512]{2,1,0:T(8,128)S(1)}, u32[]{:S(2)}, u32[]{:S(2)}) %collective-permute-start.4) | collective-permute-done | bytes 294944 | tf_op jit(solution)/shard_map/ppermute | solution.py:31
  195.3 3.1 %collective-permute-start.5 = (f32[72,512]{1,0:T(8,128)S(1)}, f32[72,512]{1,0:T(8,128)S(1)}, u32[]{:S(2)}, u32[]{:S(2)}) collective-permute-start(f32[72,512]{1,0:T(8,128)S(1)} %dynamic-slice_bitcast_fusion.4), channel_id=1, source_target_pairs={{0,16},{8,24},{16,0},{24,8},{1,17},{9,25},{17,1},{25,9},{2,18},{10... | collective-permute-start | bytes 442376 | tf_op jit(solution)/shard_map/ppermute | solution.py:31
  198.4 4.3 %collective-permute-done.5 = f32[72,512]{1,0:T(8,128)S(1)} collective-permute-done((f32[72,512]{1,0:T(8,128)S(1)}, f32[72,512]{1,0:T(8,128)S(1)}, u32[]{:S(2)}, u32[]{:S(2)}) %collective-permute-start.5) | collective-permute-done | bytes 147488 | tf_op jit(solution)/shard_map/ppermute | solution.py:31
  202.7 2.1 collective-permute-start.6
  204.9 3.8 %collective-permute-done.6 = f32[72,512]{1,0:T(8,128)S(1)} collective-permute-done((f32[72,512]{1,0:T(8,128)S(1)}, f32[72,512]{1,0:T(8,128)S(1)}, u32[]{:S(2)}, u32[]{:S(2)}) %collective-permute-start.6) | collective-permute-done | bytes 147488 | tf_op jit(solution)/shard_map/ppermute | solution.py:55
  208.7 3.8 %collective-permute-start.7 = (f32[72,512]{1,0:T(8,128)S(1)}, f32[72,512]{1,0:T(8,128)S(1)}, u32[]{:S(2)}, u32[]{:S(2)}) collective-permute-start(f32[72,512]{1,0:T(8,128)S(1)} %add.169), channel_id=1, source_target_pairs={{0,4},{2,6},{4,0},{6,2},{1,5},{3,7},{5,1},{7,3},{8,12},{10,14},{12... | collective-permute-start | bytes 442376 | tf_op jit(solution)/shard_map/ppermute | solution.py:55
  212.4 4.6 %collective-permute-done.7 = f32[72,512]{1,0:T(8,128)S(1)} collective-permute-done((f32[72,512]{1,0:T(8,128)S(1)}, f32[72,512]{1,0:T(8,128)S(1)}, u32[]{:S(2)}, u32[]{:S(2)}) %collective-permute-start.7) | collective-permute-done | bytes 147488 | tf_op jit(solution)/shard_map/ppermute | solution.py:55
  219.0 4.0 %collective-permute-done.8 = f32[72,512]{1,0:T(8,128)S(1)} collective-permute-done((f32[72,512]{1,0:T(8,128)S(1)}, f32[72,512]{1,0:T(8,128)S(1)}, u32[]{:S(2)}, u32[]{:S(2)}) %collective-permute-start.8) | collective-permute-done | bytes 147488 | tf_op jit(solution)/shard_map/ppermute | solution.py:55
  223.0 3.2 %collective-permute-start.9 = (f32[72,512]{1,0:T(8,128)S(1)}, f32[72,512]{1,0:T(8,128)S(1)}, u32[]{:S(2)}, u32[]{:S(2)}) collective-permute-start(f32[72,512]{1,0:T(8,128)S(1)} %add.171), channel_id=1, source_target_pairs={{0,64},{32,96},{64,0},{96,32},{128,192},{160,224},{192,128},{224,1... | collective-permute-start | bytes 442376 | tf_op jit(solution)/shard_map/ppermute | solution.py:55
  226.1 5.2 %collective-permute-done.9 = f32[72,512]{1,0:T(8,128)S(1)} collective-permute-done((f32[72,512]{1,0:T(8,128)S(1)}, f32[72,512]{1,0:T(8,128)S(1)}, u32[]{:S(2)}, u32[]{:S(2)}) %collective-permute-start.9) | collective-permute-done | bytes 147488 | tf_op jit(solution)/shard_map/ppermute | solution.py:55
  231.3 4.5 %collective-permute-start.10 = (f32[72,512]{1,0:T(8,128)S(1)}, f32[72,512]{1,0:T(8,128)S(1)}, u32[]{:S(2)}, u32[]{:S(2)}) collective-permute-start(f32[72,512]{1,0:T(8,128)S(1)} %add.172), channel_id=1, source_target_pairs={{0,128},{32,160},{64,192},{96,224},{128,0},{160,32},{192,64},{224,... | collective-permute-start | bytes 442376 | tf_op jit(solution)/shard_map/ppermute | solution.py:55
  235.9 5.6 %collective-permute-done.10 = f32[72,512]{1,0:T(8,128)S(1)} collective-permute-done((f32[72,512]{1,0:T(8,128)S(1)}, f32[72,512]{1,0:T(8,128)S(1)}, u32[]{:S(2)}, u32[]{:S(2)}) %collective-permute-start.10) | collective-permute-done | bytes 147488 | tf_op jit(solution)/shard_map/ppermute | solution.py:55
  241.5 6.6 %collective-permute-start.11 = (f32[72,512]{1,0:T(8,128)S(1)}, f32[72,512]{1,0:T(8,128)S(1)}, u32[]{:S(2)}, u32[]{:S(2)}) collective-permute-start(f32[72,512]{1,0:T(8,128)S(1)} %add.173), channel_id=1, source_target_pairs={{0,256},{256,0},{1,257},{257,1},{2,258},{258,2},{3,259},{259,3},{4... | collective-permute-start | bytes 442376 | tf_op jit(solution)/shard_map/ppermute | solution.py:55
  248.1 3.2 %collective-permute-done.11 = f32[72,512]{1,0:T(8,128)S(1)} collective-permute-done((f32[72,512]{1,0:T(8,128)S(1)}, f32[72,512]{1,0:T(8,128)S(1)}, u32[]{:S(2)}, u32[]{:S(2)}) %collective-permute-start.11) | collective-permute-done | bytes 147488 | tf_op jit(solution)/shard_map/ppermute | solution.py:55
  251.3 3.1 %collective-permute-start.12 = (f32[72,512]{1,0:T(8,128)S(1)}, f32[72,512]{1,0:T(8,128)S(1)}, u32[]{:S(2)}, u32[]{:S(2)}) collective-permute-start(f32[72,512]{1,0:T(8,128)S(1)} %add.174), channel_id=1, source_target_pairs={{0,16},{8,24},{16,0},{24,8},{1,17},{9,25},{17,1},{25,9},{2,18},{10... | collective-permute-start | bytes 442376 | tf_op jit(solution)/shard_map/ppermute | solution.py:41
  254.4 4.3 %collective-permute-done.12 = f32[72,512]{1,0:T(8,128)S(1)} collective-permute-done((f32[72,512]{1,0:T(8,128)S(1)}, f32[72,512]{1,0:T(8,128)S(1)}, u32[]{:S(2)}, u32[]{:S(2)}) %collective-permute-start.12) | collective-permute-done | bytes 147488 | tf_op jit(solution)/shard_map/ppermute | solution.py:41
  258.8 1.9 collective-permute-start.13
  260.7 5.5 %collective-permute-done.13 = f32[2,72,512]{2,1,0:T(8,128)S(1)} collective-permute-done((f32[2,72,512]{2,1,0:T(8,128)S(1)}, f32[2,72,512]{2,1,0:T(8,128)S(1)}, u32[]{:S(2)}, u32[]{:S(2)}) %collective-permute-start.13) | collective-permute-done | bytes 294944 | tf_op jit(solution)/shard_map/ppermute | solution.py:41
  266.3 16.2 %collective-permute-start.14 = (f32[288,512]{1,0:T(8,128)S(1)}, f32[288,512]{1,0:T(8,128)S(1)}, u32[]{:S(2)}, u32[]{:S(2)}) collective-permute-start(f32[288,512]{1,0:T(8,128)S(1)} %bitcast.69), channel_id=1, source_target_pairs={{0,1},{1,0},{2,3},{3,2},{4,5},{5,4},{6,7},{7,6},{8,9},{9,8},{10,11... | collective-permute-start | bytes 1769480 | tf_op jit(solution)/shard_map/ppermute | solution.py:41
  (49 shorter events, 15.1 us)
Async XLA Ops:
  7.2 171.4 %copy-start = (bf16[512,512]{1,0:T(8,128)(2,1)S(1)}, bf16[512,512]{1,0:T(8,128)(2,1)}, u32[]{:S(2)}) copy-start(bf16[512,512]{1,0:T(8,128)(2,1)} %param.15) | copy-start | bytes 1572868
  7.2 121.9 %all-gather.2.cloned.1.call-start = ((), (), s32[]{:S(2)}) async-start(), calls=%async_computation | async-start | bytes 8650752 | tf_op jit(solution)/shard_map/all_gather | solution.py:139
  21.6 4.7 %copy-start.3 = (s32[8,1]{0,1:T(1,128)S(1)}, s32[8,1]{0,1:T(1,128)}, u32[]{:S(2)}) copy-start(s32[8,1]{0,1:T(1,128)} %param.13) | copy-start | bytes 100
  135.8 10.0 %collective-permute-start = (f32[4,128,512]{2,1,0:T(8,128)}, f32[4,128,512]{2,1,0:T(8,128)S(1)}, u32[]{:S(2)}, u32[]{:S(2)}) collective-permute-start(f32[4,128,512]{2,1,0:T(8,128)} %shard_map.98), channel_id=1, source_target_pairs={{0,1},{1,0},{2,3},{3,2},{4,5},{5,4},{6,7},{7,6},{8,9},{9,8},{10,11... | collective-permute-start | bytes 3145736 | tf_op jit(solution)/shard_map/ppermute | solution.py:146
  147.2 15.4 %collective-permute-start.1 = (f32[2,128,512]{2,1,0:T(8,128)S(1)}, f32[2,128,512]{2,1,0:T(8,128)S(1)}, u32[]{:S(2)}, u32[]{:S(2)}) collective-permute-start(f32[2,128,512]{2,1,0:T(8,128)S(1)} %dynamic-slice_bitcast_fusion.1), channel_id=1, source_target_pairs={{0,2},{2,0},{4,6},{6,4},{1,3},{3,1},{5,7},{7,5},{8,10},{10,8},{12,... | collective-permute-start | bytes 1572872 | tf_op jit(solution)/shard_map/ppermute | solution.py:31
  150.4 28.1 %copy-start.1 = (bf16[128,512]{1,0:T(8,128)(2,1)S(1)}, bf16[128,512]{1,0:T(8,128)(2,1)}, u32[]{:S(2)}) copy-start(bf16[128,512]{1,0:T(8,128)(2,1)} %param.17) | copy-start | bytes 393220
  150.4 28.1 %copy-start.2 = (f32[512]{0:T(512)S(1)}, f32[512]{0:T(512)}, u32[]{:S(2)}) copy-start(f32[512]{0:T(512)} %param.16) | copy-start | bytes 6148
  162.7 15.7 %collective-permute-start.2 = (f32[128,512]{1,0:T(8,128)S(1)}, f32[128,512]{1,0:T(8,128)S(1)}, u32[]{:S(2)}, u32[]{:S(2)}) collective-permute-start(f32[128,512]{1,0:T(8,128)S(1)} %dynamic-slice_bitcast_fusion.3), channel_id=1, source_target_pairs={{0,4},{2,6},{4,0},{6,2},{1,5},{3,7},{5,1},{7,3},{8,12},{10,14},{12... | collective-permute-start | bytes 786440 | tf_op jit(solution)/shard_map/ppermute | solution.py:31
  180.1 4.9 %collective-permute-start.3 = (f32[288,512]{1,0:T(8,128)S(1)}, f32[288,512]{1,0:T(8,128)S(1)}, u32[]{:S(2)}, u32[]{:S(2)}) collective-permute-start(f32[288,512]{1,0:T(8,128)S(1)} %dynamic-slice_bitcast_fusion), channel_id=1, source_target_pairs={{0,1},{1,0},{2,3},{3,2},{4,5},{5,4},{6,7},{7,6},{8,9},{9,8},{10,11... | collective-permute-start | bytes 1769480 | tf_op jit(solution)/shard_map/ppermute | solution.py:31
  185.2 10.1 %collective-permute-start.4 = (f32[2,72,512]{2,1,0:T(8,128)S(1)}, f32[2,72,512]{2,1,0:T(8,128)S(1)}, u32[]{:S(2)}, u32[]{:S(2)}) collective-permute-start(f32[2,72,512]{2,1,0:T(8,128)S(1)} %dynamic-slice_bitcast_fusion.2), channel_id=1, source_target_pairs={{0,8},{8,0},{16,24},{24,16},{1,9},{9,1},{17,25},{25,17},{2,10},{10... | collective-permute-start | bytes 884744 | tf_op jit(solution)/shard_map/ppermute | solution.py:31
  195.3 7.4 %collective-permute-start.5 = (f32[72,512]{1,0:T(8,128)S(1)}, f32[72,512]{1,0:T(8,128)S(1)}, u32[]{:S(2)}, u32[]{:S(2)}) collective-permute-start(f32[72,512]{1,0:T(8,128)S(1)} %dynamic-slice_bitcast_fusion.4), channel_id=1, source_target_pairs={{0,16},{8,24},{16,0},{24,8},{1,17},{9,25},{17,1},{25,9},{2,18},{10... | collective-permute-start | bytes 442376 | tf_op jit(solution)/shard_map/ppermute | solution.py:31
  202.7 5.9 %collective-permute-start.6 = (f32[72,512]{1,0:T(8,128)S(1)}, f32[72,512]{1,0:T(8,128)S(1)}, u32[]{:S(2)}, u32[]{:S(2)}) collective-permute-start(f32[72,512]{1,0:T(8,128)S(1)} %bitcast_add_fusion.4), channel_id=1, source_target_pairs={{0,2},{2,0},{4,6},{6,4},{1,3},{3,1},{5,7},{7,5},{8,10},{10,8},{12,... | collective-permute-start | bytes 442376 | tf_op jit(solution)/shard_map/ppermute | solution.py:55
  208.7 8.4 %collective-permute-start.7 = (f32[72,512]{1,0:T(8,128)S(1)}, f32[72,512]{1,0:T(8,128)S(1)}, u32[]{:S(2)}, u32[]{:S(2)}) collective-permute-start(f32[72,512]{1,0:T(8,128)S(1)} %add.169), channel_id=1, source_target_pairs={{0,4},{2,6},{4,0},{6,2},{1,5},{3,7},{5,1},{7,3},{8,12},{10,14},{12... | collective-permute-start | bytes 442376 | tf_op jit(solution)/shard_map/ppermute | solution.py:55
  217.0 5.9 %collective-permute-start.8 = (f32[72,512]{1,0:T(8,128)S(1)}, f32[72,512]{1,0:T(8,128)S(1)}, u32[]{:S(2)}, u32[]{:S(2)}) collective-permute-start(f32[72,512]{1,0:T(8,128)S(1)} %add.170), channel_id=1, source_target_pairs={{0,32},{32,0},{64,96},{96,64},{128,160},{160,128},{192,224},{224,1... | collective-permute-start | bytes 442376 | tf_op jit(solution)/shard_map/ppermute | solution.py:55
  223.0 8.4 %collective-permute-start.9 = (f32[72,512]{1,0:T(8,128)S(1)}, f32[72,512]{1,0:T(8,128)S(1)}, u32[]{:S(2)}, u32[]{:S(2)}) collective-permute-start(f32[72,512]{1,0:T(8,128)S(1)} %add.171), channel_id=1, source_target_pairs={{0,64},{32,96},{64,0},{96,32},{128,192},{160,224},{192,128},{224,1... | collective-permute-start | bytes 442376 | tf_op jit(solution)/shard_map/ppermute | solution.py:55
  231.3 10.1 %collective-permute-start.10 = (f32[72,512]{1,0:T(8,128)S(1)}, f32[72,512]{1,0:T(8,128)S(1)}, u32[]{:S(2)}, u32[]{:S(2)}) collective-permute-start(f32[72,512]{1,0:T(8,128)S(1)} %add.172), channel_id=1, source_target_pairs={{0,128},{32,160},{64,192},{96,224},{128,0},{160,32},{192,64},{224,... | collective-permute-start | bytes 442376 | tf_op jit(solution)/shard_map/ppermute | solution.py:55
  241.5 9.8 %collective-permute-start.11 = (f32[72,512]{1,0:T(8,128)S(1)}, f32[72,512]{1,0:T(8,128)S(1)}, u32[]{:S(2)}, u32[]{:S(2)}) collective-permute-start(f32[72,512]{1,0:T(8,128)S(1)} %add.173), channel_id=1, source_target_pairs={{0,256},{256,0},{1,257},{257,1},{2,258},{258,2},{3,259},{259,3},{4... | collective-permute-start | bytes 442376 | tf_op jit(solution)/shard_map/ppermute | solution.py:55
  251.3 7.4 %collective-permute-start.12 = (f32[72,512]{1,0:T(8,128)S(1)}, f32[72,512]{1,0:T(8,128)S(1)}, u32[]{:S(2)}, u32[]{:S(2)}) collective-permute-start(f32[72,512]{1,0:T(8,128)S(1)} %add.174), channel_id=1, source_target_pairs={{0,16},{8,24},{16,0},{24,8},{1,17},{9,25},{17,1},{25,9},{2,18},{10... | collective-permute-start | bytes 442376 | tf_op jit(solution)/shard_map/ppermute | solution.py:41
  258.8 7.5 %collective-permute-start.13 = (f32[2,72,512]{2,1,0:T(8,128)S(1)}, f32[2,72,512]{2,1,0:T(8,128)S(1)}, u32[]{:S(2)}, u32[]{:S(2)}) collective-permute-start(f32[2,72,512]{2,1,0:T(8,128)S(1)} %pad_maximum_fusion.2), channel_id=1, source_target_pairs={{0,8},{8,0},{16,24},{24,16},{1,9},{9,1},{17,25},{25,17},{2,10},{10... | collective-permute-start | bytes 884744 | tf_op jit(solution)/shard_map/ppermute | solution.py:41
  266.3 17.8 %collective-permute-start.14 = (f32[288,512]{1,0:T(8,128)S(1)}, f32[288,512]{1,0:T(8,128)S(1)}, u32[]{:S(2)}, u32[]{:S(2)}) collective-permute-start(f32[288,512]{1,0:T(8,128)S(1)} %bitcast.69), channel_id=1, source_target_pairs={{0,1},{1,0},{2,3},{3,2},{4,5},{5,4},{6,7},{7,6},{8,9},{9,8},{10,11... | collective-permute-start | bytes 1769480 | tf_op jit(solution)/shard_map/ppermute | solution.py:41
Sparse Core Ops, SparseCore 0:
  19.8 109.2 all-gather.1

commit v13 on v10

--- a/solution.py
+++ b/solution.py
@@ -157,7 +157,7 @@
     local_bias = jnp.sum(slope.astype(jnp.float32), axis=0)
     width = weight.shape[0]
     scatter_ways = sizes["core"] * sizes["x"]
-    padded_rows = -(-(width + 1) // (scatter_ways * 8)) * scatter_ways * 8
+    padded_rows = -(-(width + 1) // scatter_ways) * scatter_ways
     combined = jnp.zeros((padded_rows, feat_width), jnp.float32)
     combined = combined.at[:width].set(local_weight).at[width].set(local_bias)
     chunk = _halving_scatter(combined.reshape(sizes["core"], -1, feat_width), "core", sizes["core"], (0,))

time: 295 us -> 295 us (level)
  waiting for transfers between devices: 178 us -> 168 us
  starting transfers between devices: 53 us -> 62.4 us
    ppermute x3, starting transfers between devices: 15.9 us -> 22.3 us  [_doubling_gather(): other = lax.ppermute(piece, axis, _xor_perm(n, 1 << bit))]
    ppermute x3, waiting for transfers between devices: 14.8 us -> 9.76 us  [_doubling_gather(): other = lax.ppermute(piece, axis, _xor_perm(n, 1 << bit))]
where the time goes in v13:
time: 295 us; the launch traced here: 294 us
  waiting for transfers between devices  168 us (57%)
  starting transfers between devices  62.4 us (21%)
  between operations  14.6 us (5%)
  Pallas kernels  14.4 us (5%)
  blocking collectives  12.4 us (4%)
  local copies, waits for them, and re-layouts  10.7 us (4%)
  other arithmetic  9.68 us (3%)
    all_gather x1, waiting for transfers between devices, shards(): gathered = lax.all_gather(gathered, ('z', 'x'), axis=0, tiled=True)  93.5 us
    ppermute x5, waiting for transfers between devices, _halving_scatter(): blocks = keep + lax.ppermute(send, axis, _xor_perm(n, 1 << bit))  37.8 us
    ppermute x6, waiting for transfers between devices, _doubling_sum(): piece = piece + lax.ppermute(piece, axis, _xor_perm(n, bit))  27.3 us
    ppermute x3, starting transfers between devices, _doubling_gather(): other = lax.ppermute(piece, axis, _xor_perm(n, 1 << bit))  22.3 us
    ppermute x6, starting transfers between devices, _doubling_sum(): piece = piece + lax.ppermute(piece, axis, _xor_perm(n, bit))  21.3 us
    ppermute x5, starting transfers between devices, _halving_scatter(): blocks = keep + lax.ppermute(send, axis, _xor_perm(n, 1 << bit))  15.4 us
    pallas_call x2, Pallas kernels, _aggregate(): pl.pallas_call(_aggregate_kernel, out_shape=jax.ShapeDtypeStruct((picked,...  14.4 us
    all_gather x1, blocking collectives, shards(): gathered = lax.all_gather(features, 'y_hi', axis=0, tiled=True)  12.4 us
  transfers between devices with their start and end apart: 16, of which 15 were waited for; matrix products, arithmetic and copies ran while one was open for 5% of the time, Pallas kernels for 2%

profile of v13, /device:TPU:1, one launch (start us, length us, event | category | flops | bytes accessed | tf_op | source)
XLA Modules:
  0.0 293.9 jit_solution(2405134446842609492)
XLA Ops:
  7.2 12.4 %all_gather.6 = bf16[256,512]{1,0:T(8,128)(2,1)} all-gather(bf16[128,512]{1,0:T(8,128)(2,1)} %param.11), channel_id=1, replica_groups=mesh['y_hi'=2,'z'=8,'x'=4,'y_lo'=4,'core'=2] {'y_hi'}, dimensions={0}, use_global_device_ids=true | all-gather | bytes 393216 | tf_op jit(solution)/shard_map/all_gather | solution.py:136
  21.6 4.7 %copy.12 = bf16[8,1,12,128,128]{3,4,2,0,1:T(8,128)(2,1)} copy(bf16[8,1,12,128,128]{4,3,2,1,0:T(8,128)(2,1)} %param.14) | data formatting | bytes 6291456 | tf_op args[3]
  26.4 3.9 %bitcast_select_fusion = bf16[8,12,128,128]{2,3,1,0:T(8,128)(2,1)} fusion(bf16[8,1,12,128,128]{3,4,2,0,1:T(8,128)(2,1)} %copy.12, pred[8,12]{1,0:T(8,128)(4,1)S(1)} %iota_compare_fusion), kind=kLoop, calls=%fused_computation | loop fusion | flops 1572864 | bytes 6291552 | tf_op jit(solution)/shard_map/jit(_where)/select_n | solution.py:92
  30.3 4.7 %copy.13.tiles_ref = bf16[8,128,1536]{2,1,0:T(8,128)(2,1)} copy(bf16[8,128,1536]{1,2,0:T(8,128)(2,1)} %bitcast.56) | data formatting | bytes 6291456 | tf_op jit(solution)/shard_map/reshape | solution.py:93
  35.6 93.5 %all-gather.2.cloned.1.call-done = bf16[8192,512]{1,0:T(8,128)(2,1)} async-done(((bf16[256,512]{1,0:T(8,128)(2,1)}), bf16[8192,512]{1,0:T(8,128)(2,1)}) %all-gather.2.cloned.1.call-update) | async-done | bytes 8388624 | tf_op jit(solution)/shard_map/all_gather | solution.py:137
  129.1 7.2 %shard_map.98 = f32[4,128,512]{2,1,0:T(8,128)} custom-call(s32[1]{0:T(128)} %bitcast.6.parity_ref, s32[96]{0:T(128)} %fusion.3.cols_ref, bf16[8,128,1536]{2,1,0:T(8,128)(2,1)} %copy.13.tiles_ref, bf16[64,128,512]{2,1,0:T(8,128)(2,1)} %bitcast.54), custom_call_target="tpu_custom_call" | custom-call | flops 805306368 | bytes 8912896 | tf_op jit(solution)/shard_map/pallas_call | solution.py:104
  136.3 3.4 %collective-permute-start = (f32[4,128,512]{2,1,0:T(8,128)}, f32[4,128,512]{2,1,0:T(8,128)S(1)}, u32[]{:S(2)}, u32[]{:S(2)}) collective-permute-start(f32[4,128,512]{2,1,0:T(8,128)} %shard_map.98), channel_id=1, source_target_pairs={{0,1},{1,0},{2,3},{3,2},{4,5},{5,4},{6,7},{7,6},{8,9},{9,8},{10,11... | collective-permute-start | bytes 3145736 | tf_op jit(solution)/shard_map/ppermute | solution.py:144
  139.7 7.2 %shard_map.97 = f32[4,128,512]{2,1,0:T(8,128)} custom-call(s32[1]{0:T(128)} %bitcast.parity_ref, s32[96]{0:T(128)} %fusion.3.cols_ref, bf16[8,128,1536]{2,1,0:T(8,128)(2,1)} %copy.13.tiles_ref, bf16[64,128,512]{2,1,0:T(8,128)(2,1)} %bitcast.55), custom_call_target="tpu_custom_call" | custom-call | flops 805306368 | bytes 8912896 | tf_op jit(solution)/shard_map/pallas_call | solution.py:104
  148.4 3.2 %collective-permute-start.1 = (f32[2,128,512]{2,1,0:T(8,128)S(1)}, f32[2,128,512]{2,1,0:T(8,128)S(1)}, u32[]{:S(2)}, u32[]{:S(2)}) collective-permute-start(f32[2,128,512]{2,1,0:T(8,128)S(1)} %dynamic-slice_bitcast_fusion.1), channel_id=1, source_target_pairs={{0,2},{2,0},{4,6},{6,4},{1,3},{3,1},{5,7},{7,5},{8,10},{10,8},{12,... | collective-permute-start | bytes 1572872 | tf_op jit(solution)/shard_map/ppermute | solution.py:31
  151.7 12.1 %collective-permute-done.1 = f32[2,128,512]{2,1,0:T(8,128)S(1)} collective-permute-done((f32[2,128,512]{2,1,0:T(8,128)S(1)}, f32[2,128,512]{2,1,0:T(8,128)S(1)}, u32[]{:S(2)}, u32[]{:S(2)}) %collective-permute-start.1) | collective-permute-done | bytes 524320 | tf_op jit(solution)/shard_map/ppermute | solution.py:31
  163.9 3.9 %collective-permute-start.2 = (f32[128,512]{1,0:T(8,128)S(1)}, f32[128,512]{1,0:T(8,128)S(1)}, u32[]{:S(2)}, u32[]{:S(2)}) collective-permute-start(f32[128,512]{1,0:T(8,128)S(1)} %dynamic-slice_bitcast_fusion.3), channel_id=1, source_target_pairs={{0,4},{2,6},{4,0},{6,2},{1,5},{3,7},{5,1},{7,3},{8,12},{10,14},{12... | collective-permute-start | bytes 786440 | tf_op jit(solution)/shard_map/ppermute | solution.py:31
  167.8 11.6 %collective-permute-done.2 = f32[128,512]{1,0:T(8,128)S(1)} collective-permute-done((f32[128,512]{1,0:T(8,128)S(1)}, f32[128,512]{1,0:T(8,128)S(1)}, u32[]{:S(2)}, u32[]{:S(2)}) %collective-permute-start.2) | collective-permute-done | bytes 262176 | tf_op jit(solution)/shard_map/ppermute | solution.py:31
  181.1 3.5 %collective-permute-start.3 = (f32[260,512]{1,0:T(8,128)S(1)}, f32[260,512]{1,0:T(8,128)S(1)}, u32[]{:S(2)}, u32[]{:S(2)}) collective-permute-start(f32[260,512]{1,0:T(8,128)S(1)} %dynamic-slice_bitcast_fusion), channel_id=1, source_target_pairs={{0,1},{1,0},{2,3},{3,2},{4,5},{5,4},{6,7},{7,6},{8,9},{9,8},{10,11... | collective-permute-start | bytes 1597448 | tf_op jit(solution)/shard_map/ppermute | solution.py:31
  188.3 8.1 %collective-permute-done.4 = f32[2,65,512]{2,1,0:T(8,128)S(1)} collective-permute-done((f32[2,65,512]{2,1,0:T(8,128)S(1)}, f32[2,65,512]{2,1,0:T(8,128)S(1)}, u32[]{:S(2)}, u32[]{:S(2)}) %collective-permute-start.4) | collective-permute-done | bytes 266272 | tf_op jit(solution)/shard_map/ppermute | solution.py:31
  196.5 2.9 collective-permute-start.5
  199.4 4.5 %collective-permute-done.5 = f32[65,512]{1,0:T(8,128)S(1)} collective-permute-done((f32[65,512]{1,0:T(8,128)S(1)}, f32[65,512]{1,0:T(8,128)S(1)}, u32[]{:S(2)}, u32[]{:S(2)}) %collective-permute-start.5) | collective-permute-done | bytes 133152 | tf_op jit(solution)/shard_map/ppermute | solution.py:31
  203.9 2.0 collective-permute-start.6
  205.9 3.9 %collective-permute-done.6 = f32[65,512]{1,0:T(8,128)S(1)} collective-permute-done((f32[65,512]{1,0:T(8,128)S(1)}, f32[65,512]{1,0:T(8,128)S(1)}, u32[]{:S(2)}, u32[]{:S(2)}) %collective-permute-start.6) | collective-permute-done | bytes 133152 | tf_op jit(solution)/shard_map/ppermute | solution.py:55
  209.8 3.6 %collective-permute-start.7 = (f32[65,512]{1,0:T(8,128)S(1)}, f32[65,512]{1,0:T(8,128)S(1)}, u32[]{:S(2)}, u32[]{:S(2)}) collective-permute-start(f32[65,512]{1,0:T(8,128)S(1)} %add.169), channel_id=1, source_target_pairs={{0,4},{2,6},{4,0},{6,2},{1,5},{3,7},{5,1},{7,3},{8,12},{10,14},{12... | collective-permute-start | bytes 399368 | tf_op jit(solution)/shard_map/ppermute | solution.py:55
  213.5 4.7 %collective-permute-done.7 = f32[65,512]{1,0:T(8,128)S(1)} collective-permute-done((f32[65,512]{1,0:T(8,128)S(1)}, f32[65,512]{1,0:T(8,128)S(1)}, u32[]{:S(2)}, u32[]{:S(2)}) %collective-permute-start.7) | collective-permute-done | bytes 133152 | tf_op jit(solution)/shard_map/ppermute | solution.py:55
  220.2 4.0 %collective-permute-done.8 = f32[65,512]{1,0:T(8,128)S(1)} collective-permute-done((f32[65,512]{1,0:T(8,128)S(1)}, f32[65,512]{1,0:T(8,128)S(1)}, u32[]{:S(2)}, u32[]{:S(2)}) %collective-permute-start.8) | collective-permute-done | bytes 133152 | tf_op jit(solution)/shard_map/ppermute | solution.py:55
  224.1 2.9 collective-permute-start.9
  227.1 5.3 %collective-permute-done.9 = f32[65,512]{1,0:T(8,128)S(1)} collective-permute-done((f32[65,512]{1,0:T(8,128)S(1)}, f32[65,512]{1,0:T(8,128)S(1)}, u32[]{:S(2)}, u32[]{:S(2)}) %collective-permute-start.9) | collective-permute-done | bytes 133152 | tf_op jit(solution)/shard_map/ppermute | solution.py:55
  232.4 4.6 %collective-permute-start.10 = (f32[65,512]{1,0:T(8,128)S(1)}, f32[65,512]{1,0:T(8,128)S(1)}, u32[]{:S(2)}, u32[]{:S(2)}) collective-permute-start(f32[65,512]{1,0:T(8,128)S(1)} %add.172), channel_id=1, source_target_pairs={{0,128},{32,160},{64,192},{96,224},{128,0},{160,32},{192,64},{224,... | collective-permute-start | bytes 399368 | tf_op jit(solution)/shard_map/ppermute | solution.py:55
  237.0 5.9 %collective-permute-done.10 = f32[65,512]{1,0:T(8,128)S(1)} collective-permute-done((f32[65,512]{1,0:T(8,128)S(1)}, f32[65,512]{1,0:T(8,128)S(1)}, u32[]{:S(2)}, u32[]{:S(2)}) %collective-permute-start.10) | collective-permute-done | bytes 133152 | tf_op jit(solution)/shard_map/ppermute | solution.py:55
  242.9 6.2 %collective-permute-start.11 = (f32[65,512]{1,0:T(8,128)S(1)}, f32[65,512]{1,0:T(8,128)S(1)}, u32[]{:S(2)}, u32[]{:S(2)}) collective-permute-start(f32[65,512]{1,0:T(8,128)S(1)} %add.173), channel_id=1, source_target_pairs={{0,256},{256,0},{1,257},{257,1},{2,258},{258,2},{3,259},{259,3},{4... | collective-permute-start | bytes 399368 | tf_op jit(solution)/shard_map/ppermute | solution.py:55
  249.2 3.5 %collective-permute-done.11 = f32[65,512]{1,0:T(8,128)S(1)} collective-permute-done((f32[65,512]{1,0:T(8,128)S(1)}, f32[65,512]{1,0:T(8,128)S(1)}, u32[]{:S(2)}, u32[]{:S(2)}) %collective-permute-start.11) | collective-permute-done | bytes 133152 | tf_op jit(solution)/shard_map/ppermute | solution.py:55
  252.7 4.7 %collective-permute-start.12 = (f32[65,512]{1,0:T(8,128)S(1)}, f32[65,512]{1,0:T(8,128)S(1)}, u32[]{:S(2)}, u32[]{:S(2)}) collective-permute-start(f32[65,512]{1,0:T(8,128)S(1)} %add.174), channel_id=1, source_target_pairs={{0,16},{8,24},{16,0},{24,8},{1,17},{9,25},{17,1},{25,9},{2,18},{10... | collective-permute-start | bytes 399368 | tf_op jit(solution)/shard_map/ppermute | solution.py:41
  257.4 2.7 collective-permute-done.12
  260.2 1.9 collective-permute-start.13
  262.1 5.5 %collective-permute-done.13 = f32[2,65,512]{2,1,0:T(8,128)S(1)} collective-permute-done((f32[2,65,512]{2,1,0:T(8,128)S(1)}, f32[2,65,512]{2,1,0:T(8,128)S(1)}, u32[]{:S(2)}, u32[]{:S(2)}) %collective-permute-start.13) | collective-permute-done | bytes 266272 | tf_op jit(solution)/shard_map/ppermute | solution.py:41
  267.8 15.7 %collective-permute-start.14 = (f32[260,512]{1,0:T(8,128)S(1)}, f32[260,512]{1,0:T(8,128)S(1)}, u32[]{:S(2)}, u32[]{:S(2)}) collective-permute-start(f32[260,512]{1,0:T(8,128)S(1)} %reshape.115), channel_id=1, source_target_pairs={{0,1},{1,0},{2,3},{3,2},{4,5},{5,4},{6,7},{7,6},{8,9},{9,8},{10,11... | collective-permute-start | bytes 1597448 | tf_op jit(solution)/shard_map/ppermute | solution.py:41
  (53 shorter events, 15.3 us)
Async XLA Ops:
  7.2 172.3 %copy-start = (bf16[512,512]{1,0:T(8,128)(2,1)S(1)}, bf16[512,512]{1,0:T(8,128)(2,1)}, u32[]{:S(2)}) copy-start(bf16[512,512]{1,0:T(8,128)(2,1)} %param.15) | copy-start | bytes 1572868
  7.2 121.9 %all-gather.2.cloned.1.call-start = ((), (), s32[]{:S(2)}) async-start(), calls=%async_computation | async-start | bytes 8650752 | tf_op jit(solution)/shard_map/all_gather | solution.py:137
  21.6 4.7 %copy-start.3 = (s32[8,1]{0,1:T(1,128)S(1)}, s32[8,1]{0,1:T(1,128)}, u32[]{:S(2)}) copy-start(s32[8,1]{0,1:T(1,128)} %param.13) | copy-start | bytes 100
  136.3 10.7 %collective-permute-start = (f32[4,128,512]{2,1,0:T(8,128)}, f32[4,128,512]{2,1,0:T(8,128)S(1)}, u32[]{:S(2)}, u32[]{:S(2)}) collective-permute-start(f32[4,128,512]{2,1,0:T(8,128)} %shard_map.98), channel_id=1, source_target_pairs={{0,1},{1,0},{2,3},{3,2},{4,5},{5,4},{6,7},{7,6},{8,9},{9,8},{10,11... | collective-permute-start | bytes 3145736 | tf_op jit(solution)/shard_map/ppermute | solution.py:144
  148.4 15.3 %collective-permute-start.1 = (f32[2,128,512]{2,1,0:T(8,128)S(1)}, f32[2,128,512]{2,1,0:T(8,128)S(1)}, u32[]{:S(2)}, u32[]{:S(2)}) collective-permute-start(f32[2,128,512]{2,1,0:T(8,128)S(1)} %dynamic-slice_bitcast_fusion.1), channel_id=1, source_target_pairs={{0,2},{2,0},{4,6},{6,4},{1,3},{3,1},{5,7},{7,5},{8,10},{10,8},{12,... | collective-permute-start | bytes 1572872 | tf_op jit(solution)/shard_map/ppermute | solution.py:31
  151.7 27.8 %copy-start.1 = (bf16[128,512]{1,0:T(8,128)(2,1)S(1)}, bf16[128,512]{1,0:T(8,128)(2,1)}, u32[]{:S(2)}) copy-start(bf16[128,512]{1,0:T(8,128)(2,1)} %param.17) | copy-start | bytes 393220
  151.7 27.8 %copy-start.2 = (f32[512]{0:T(512)S(1)}, f32[512]{0:T(512)}, u32[]{:S(2)}) copy-start(f32[512]{0:T(512)} %param.16) | copy-start | bytes 6148
  163.9 15.6 %collective-permute-start.2 = (f32[128,512]{1,0:T(8,128)S(1)}, f32[128,512]{1,0:T(8,128)S(1)}, u32[]{:S(2)}, u32[]{:S(2)}) collective-permute-start(f32[128,512]{1,0:T(8,128)S(1)} %dynamic-slice_bitcast_fusion.3), channel_id=1, source_target_pairs={{0,4},{2,6},{4,0},{6,2},{1,5},{3,7},{5,1},{7,3},{8,12},{10,14},{12... | collective-permute-start | bytes 786440 | tf_op jit(solution)/shard_map/ppermute | solution.py:31
  181.1 5.0 %collective-permute-start.3 = (f32[260,512]{1,0:T(8,128)S(1)}, f32[260,512]{1,0:T(8,128)S(1)}, u32[]{:S(2)}, u32[]{:S(2)}) collective-permute-start(f32[260,512]{1,0:T(8,128)S(1)} %dynamic-slice_bitcast_fusion), channel_id=1, source_target_pairs={{0,1},{1,0},{2,3},{3,2},{4,5},{5,4},{6,7},{7,6},{8,9},{9,8},{10,11... | collective-permute-start | bytes 1597448 | tf_op jit(solution)/shard_map/ppermute | solution.py:31
  186.4 10.1 %collective-permute-start.4 = (f32[2,65,512]{2,1,0:T(8,128)S(1)}, f32[2,65,512]{2,1,0:T(8,128)S(1)}, u32[]{:S(2)}, u32[]{:S(2)}) collective-permute-start(f32[2,65,512]{2,1,0:T(8,128)S(1)} %dynamic-slice_bitcast_fusion.2), channel_id=1, source_target_pairs={{0,8},{8,0},{16,24},{24,16},{1,9},{9,1},{17,25},{25,17},{2,10},{10... | collective-permute-start | bytes 798728 | tf_op jit(solution)/shard_map/ppermute | solution.py:31
  196.5 7.4 %collective-permute-start.5 = (f32[65,512]{1,0:T(8,128)S(1)}, f32[65,512]{1,0:T(8,128)S(1)}, u32[]{:S(2)}, u32[]{:S(2)}) collective-permute-start(f32[65,512]{1,0:T(8,128)S(1)} %dynamic-slice_bitcast_fusion.4), channel_id=1, source_target_pairs={{0,16},{8,24},{16,0},{24,8},{1,17},{9,25},{17,1},{25,9},{2,18},{10... | collective-permute-start | bytes 399368 | tf_op jit(solution)/shard_map/ppermute | solution.py:31
  203.9 5.9 %collective-permute-start.6 = (f32[65,512]{1,0:T(8,128)S(1)}, f32[65,512]{1,0:T(8,128)S(1)}, u32[]{:S(2)}, u32[]{:S(2)}) collective-permute-start(f32[65,512]{1,0:T(8,128)S(1)} %bitcast_add_fusion.4), channel_id=1, source_target_pairs={{0,2},{2,0},{4,6},{6,4},{1,3},{3,1},{5,7},{7,5},{8,10},{10,8},{12,... | collective-permute-start | bytes 399368 | tf_op jit(solution)/shard_map/ppermute | solution.py:55
  209.8 8.4 %collective-permute-start.7 = (f32[65,512]{1,0:T(8,128)S(1)}, f32[65,512]{1,0:T(8,128)S(1)}, u32[]{:S(2)}, u32[]{:S(2)}) collective-permute-start(f32[65,512]{1,0:T(8,128)S(1)} %add.169), channel_id=1, source_target_pairs={{0,4},{2,6},{4,0},{6,2},{1,5},{3,7},{5,1},{7,3},{8,12},{10,14},{12... | collective-permute-start | bytes 399368 | tf_op jit(solution)/shard_map/ppermute | solution.py:55
  218.2 5.9 %collective-permute-start.8 = (f32[65,512]{1,0:T(8,128)S(1)}, f32[65,512]{1,0:T(8,128)S(1)}, u32[]{:S(2)}, u32[]{:S(2)}) collective-permute-start(f32[65,512]{1,0:T(8,128)S(1)} %add.170), channel_id=1, source_target_pairs={{0,32},{32,0},{64,96},{96,64},{128,160},{160,128},{192,224},{224,1... | collective-permute-start | bytes 399368 | tf_op jit(solution)/shard_map/ppermute | solution.py:55
  224.1 8.3 %collective-permute-start.9 = (f32[65,512]{1,0:T(8,128)S(1)}, f32[65,512]{1,0:T(8,128)S(1)}, u32[]{:S(2)}, u32[]{:S(2)}) collective-permute-start(f32[65,512]{1,0:T(8,128)S(1)} %add.171), channel_id=1, source_target_pairs={{0,64},{32,96},{64,0},{96,32},{128,192},{160,224},{192,128},{224,1... | collective-permute-start | bytes 399368 | tf_op jit(solution)/shard_map/ppermute | solution.py:55
  232.4 10.4 %collective-permute-start.10 = (f32[65,512]{1,0:T(8,128)S(1)}, f32[65,512]{1,0:T(8,128)S(1)}, u32[]{:S(2)}, u32[]{:S(2)}) collective-permute-start(f32[65,512]{1,0:T(8,128)S(1)} %add.172), channel_id=1, source_target_pairs={{0,128},{32,160},{64,192},{96,224},{128,0},{160,32},{192,64},{224,... | collective-permute-start | bytes 399368 | tf_op jit(solution)/shard_map/ppermute | solution.py:55
  242.9 9.8 %collective-permute-start.11 = (f32[65,512]{1,0:T(8,128)S(1)}, f32[65,512]{1,0:T(8,128)S(1)}, u32[]{:S(2)}, u32[]{:S(2)}) collective-permute-start(f32[65,512]{1,0:T(8,128)S(1)} %add.173), channel_id=1, source_target_pairs={{0,256},{256,0},{1,257},{257,1},{2,258},{258,2},{3,259},{259,3},{4... | collective-permute-start | bytes 399368 | tf_op jit(solution)/shard_map/ppermute | solution.py:55
  252.7 7.4 %collective-permute-start.12 = (f32[65,512]{1,0:T(8,128)S(1)}, f32[65,512]{1,0:T(8,128)S(1)}, u32[]{:S(2)}, u32[]{:S(2)}) collective-permute-start(f32[65,512]{1,0:T(8,128)S(1)} %add.174), channel_id=1, source_target_pairs={{0,16},{8,24},{16,0},{24,8},{1,17},{9,25},{17,1},{25,9},{2,18},{10... | collective-permute-start | bytes 399368 | tf_op jit(solution)/shard_map/ppermute | solution.py:41
  260.2 7.5 %collective-permute-start.13 = (f32[2,65,512]{2,1,0:T(8,128)S(1)}, f32[2,65,512]{2,1,0:T(8,128)S(1)}, u32[]{:S(2)}, u32[]{:S(2)}) collective-permute-start(f32[2,65,512]{2,1,0:T(8,128)S(1)} %pad_maximum_fusion.1), channel_id=1, source_target_pairs={{0,8},{8,0},{16,24},{24,16},{1,9},{9,1},{17,25},{25,17},{2,10},{10... | collective-permute-start | bytes 798728 | tf_op jit(solution)/shard_map/ppermute | solution.py:41
  267.8 17.2 %collective-permute-start.14 = (f32[260,512]{1,0:T(8,128)S(1)}, f32[260,512]{1,0:T(8,128)S(1)}, u32[]{:S(2)}, u32[]{:S(2)}) collective-permute-start(f32[260,512]{1,0:T(8,128)S(1)} %reshape.115), channel_id=1, source_target_pairs={{0,1},{1,0},{2,3},{3,2},{4,5},{5,4},{6,7},{7,6},{8,9},{9,8},{10,11... | collective-permute-start | bytes 1597448 | tf_op jit(solution)/shard_map/ppermute | solution.py:41
Sparse Core Ops, SparseCore 0:
  19.8 109.2 all-gather.1
